TPU v7x, 512 devices: a whole 4x4x16 slice. The times are simulated.
512 devices in a mesh: ctx: 64 (over z_lo, x, core), tp: 8 (over y, z_hi).
Axes of the slice: x: 4, y: 4, z: 16 (z_hi: 2, z_lo: 8; z = z_hi * 8 + z_lo), core: 2. Of those that a mesh axis runs over, the one named last changes fastest.
Arguments:
- u_query: bfloat16 [8192, 4096], P('ctx', 'tp'), may hold values from -6 to 6
- u_key: bfloat16 [8192, 4096], P('ctx', 'tp'), may hold values from -6 to 6
- u_value: bfloat16 [8192, 4096], P('ctx', 'tp'), may hold values from -6 to 6
- short_filter: float32 [3, 7, 4096], P(None, None, 'tp'), may hold values from -2 to 2
- decay_rate: float32 [256, 16], P('tp'), may hold values from 3.6621094e-05 to 0.0333333333
- residue: float32 [256, 16], P('tp'), may hold values from -1.8 to 1.8
- grad_out: bfloat16 [8192, 4096], P('ctx', 'tp'), may hold values from -6 to 6
Outputs:
- mixer_out: bfloat16 [8192, 4096], P('ctx', 'tp')
- grad_query: bfloat16 [8192, 4096], P('ctx', 'tp')
- grad_key: bfloat16 [8192, 4096], P('ctx', 'tp')
- grad_value: bfloat16 [8192, 4096], P('ctx', 'tp')
All inputs are finite; a program needn't handle non-finite values.
Results may differ from a plain program's by a relative error of at most 0.0076.
Values may be sent and summed in bfloat16 or wider, within the bound.
No kernel may reach another device: no remote copies, remote signals or barrier semaphores. Data moves between devices by JAX's collectives and lax.ppermute only.
A program may use at most 128 MiB of HBM per device.

v0:
```python
import jax
import jax.numpy as jnp
from jax import lax
from jax.sharding import PartitionSpec as P

GROUP = 16
SHORT = 7


precise = lax.Precision.HIGHEST


def from_behind(value, axis, steps):
    count = lax.axis_size(axis)
    leading, last = (max(0, -steps), min(count, count - steps))
    return lax.ppermute(value, axis, [(source, source + steps) for source in range(leading, last)])


def rounded(values):
    return lax.optimization_barrier(values.astype(jnp.bfloat16))


def modal_tables(rate_rows, residue, block_len):
    lag_steps = jnp.arange(block_len).astype(jnp.float32)
    powers = jnp.exp(-rate_rows[:, :, None] * lag_steps)
    weights = residue * jnp.sqrt(-jnp.expm1(-2.0 * rate_rows))
    impulse = jnp.einsum("gm,gmk->gk", weights, powers, precision=precise)
    return (weights, powers, impulse)


def toeplitz_of(impulse_row, block_len, backward):
    lag_grid = jnp.arange(block_len)[:, None] - jnp.arange(block_len)[None, :]
    matrix = jnp.where(lag_grid >= 0, impulse_row[jnp.clip(lag_grid, 0, block_len - 1)], 0.0)
    if backward:
        return matrix.T
    return matrix


def short_causal(prior_rows, inputs, filter_taps):
    length = inputs.shape[0]
    padded = jnp.concatenate([prior_rows.astype(jnp.float32), inputs.astype(jnp.float32)], axis=0)
    summed = jnp.zeros(inputs.shape, jnp.float32)
    for offset in range(SHORT):
        summed = (
            summed + filter_taps[offset] * padded[SHORT - 1 - offset : SHORT - 1 - offset + length]
        )
    return summed


def short_reverse(grad_rows, next_rows, filter_taps):
    length = grad_rows.shape[0]
    padded = jnp.concatenate([grad_rows.astype(jnp.float32), next_rows.astype(jnp.float32)], axis=0)
    summed = jnp.zeros(grad_rows.shape, jnp.float32)
    for offset in range(SHORT):
        summed = summed + filter_taps[offset] * padded[offset : offset + length]
    return summed


def block_pass(across, picked, ctx_count, block_len, per_group, backward):
    rate_rows, weight_rows, power_table, impulse_rows = picked
    group_count = rate_rows.shape[0]
    grouped_rows = across.reshape(group_count, per_group, ctx_count, block_len)

    def one_group(group_item):
        rate_row, weight_row, power_rows, impulse_row, piece_rows = group_item
        toeplitz = toeplitz_of(impulse_row, block_len, backward)
        values = piece_rows.astype(jnp.float32)
        local_part = jnp.einsum("ts,cns->cnt", toeplitz, values, precision=precise)
        index_rows = jnp.arange(ctx_count).astype(jnp.float32)
        if backward:
            gap_grid = index_rows[None, :] - index_rows[:, None] - 1.0
            sweep = power_rows
            lead_source = power_rows[:, ::-1]
        else:
            gap_grid = index_rows[:, None] - index_rows[None, :] - 1.0
            sweep = power_rows[:, ::-1]
            lead_source = power_rows
        states = jnp.einsum("ms,cns->cnm", sweep, values, precision=precise)
        decay_mat = jnp.where(
            gap_grid[None] >= 0,
            jnp.exp(-rate_row[:, None, None] * block_len * jnp.maximum(gap_grid, 0.0)[None]),
            0.0,
        )
        entering = jnp.einsum("mnk,ckm->cnm", decay_mat, states, precision=precise)
        lead_rows = weight_row[:, None] * lead_source * jnp.exp(-rate_row)[:, None]
        return local_part + jnp.einsum("mt,cnm->cnt", lead_rows, entering, precision=precise)

    result = lax.map(one_group, (rate_rows, weight_rows, power_table, impulse_rows, grouped_rows))
    return result.reshape(group_count * per_group, ctx_count * block_len).astype(jnp.bfloat16)


def shards(u_query, u_key, u_value, short_filter, decay_rate, residue, grad_out):
    block_len, channels = u_query.shape
    ctx_count = lax.axis_size("ctx")
    position = lax.axis_index("ctx")
    rim_rows = jnp.stack(
        [
            u_query[block_len - SHORT + 1 :],
            u_key[block_len - SHORT + 1 :],
            u_value[block_len - SHORT + 1 :],
        ]
    )
    before = from_behind(rim_rows, "ctx", 1)
    q_short = rounded(short_causal(before[0], u_query, short_filter[0]))
    k_short = rounded(short_causal(before[1], u_key, short_filter[1]))
    v_short = rounded(short_causal(before[2], u_value, short_filter[2]))
    product = rounded(k_short.astype(jnp.float32) * v_short.astype(jnp.float32))
    grad_conv = rounded(grad_out.astype(jnp.float32) * q_short.astype(jnp.float32))
    weights, powers, impulse = modal_tables(decay_rate, residue, block_len)
    chan_count = channels // ctx_count
    per_group = min(chan_count, GROUP)
    first_group = position * chan_count // GROUP
    picked = tuple(
        (
            lax.dynamic_slice_in_dim(table_rows, first_group, chan_count // per_group, 0)
            for table_rows in (decay_rate, weights, powers, impulse)
        )
    )
    across = lax.all_to_all(product.T, "ctx", split_axis=0, concat_axis=1, tiled=True)
    conv_rows = block_pass(across, picked, ctx_count, block_len, per_group, False)
    conv_out = lax.all_to_all(conv_rows, "ctx", split_axis=1, concat_axis=0, tiled=True).T
    across_back = lax.all_to_all(grad_conv.T, "ctx", split_axis=0, concat_axis=1, tiled=True)
    grad_rows = block_pass(across_back, picked, ctx_count, block_len, per_group, True)
    grad_prod = lax.all_to_all(grad_rows, "ctx", split_axis=1, concat_axis=0, tiled=True).T
    mixer_out = (q_short.astype(jnp.float32) * conv_out.astype(jnp.float32)).astype(jnp.bfloat16)
    grad_qshort = rounded(grad_out.astype(jnp.float32) * conv_out.astype(jnp.float32))
    grad_kshort = rounded(grad_prod.astype(jnp.float32) * v_short.astype(jnp.float32))
    grad_vshort = rounded(grad_prod.astype(jnp.float32) * k_short.astype(jnp.float32))
    head_rows = jnp.stack(
        [grad_qshort[: SHORT - 1], grad_kshort[: SHORT - 1], grad_vshort[: SHORT - 1]]
    )
    next_rows = from_behind(head_rows, "ctx", -1)
    grad_query = short_reverse(grad_qshort, next_rows[0], short_filter[0]).astype(jnp.bfloat16)
    grad_key = short_reverse(grad_kshort, next_rows[1], short_filter[1]).astype(jnp.bfloat16)
    grad_value = short_reverse(grad_vshort, next_rows[2], short_filter[2]).astype(jnp.bfloat16)
    return (mixer_out, grad_query, grad_key, grad_value)


def solution(mesh):
    return jax.shard_map(
        shards,
        mesh=mesh,
        in_specs=(
            P("ctx", "tp"),
            P("ctx", "tp"),
            P("ctx", "tp"),
            P(None, None, "tp"),
            P("tp", None),
            P("tp", None),
            P("ctx", "tp"),
        ),
        out_specs=(P("ctx", "tp"), P("ctx", "tp"), P("ctx", "tp"), P("ctx", "tp")),
        check_vma=False,
    )
```

profile of v0, /device:TPU:1, one launch (start us, length us, event | category | flops | bytes accessed | tf_op | source)
XLA Modules:
  0.0 223.5 jit_solution(17923716505941237007)
XLA Ops:
  0.6 0.7 slice_bitcast_fusion.11
  1.3 0.7 slice_bitcast_fusion.9
  2.1 0.3 copy.51
  2.4 4.5 %collective-permute-start = (bf16[3,6,512]{1,2,0:T(8,128)(2,1)S(1)}, bf16[3,6,512]{1,2,0:T(8,128)(2,1)S(1)}, u32[]{:S(2)}, u32[]{:S(2)}) collective-permute-start(bf16[3,6,512]{1,2,0:T(8,128)(2,1)S(1)} %copy.51), channel_id=1, source_target_pairs={{0,8},{8,16},{16,24},{24,32},{32,40},{40,48},{48,56},{56,64},{64,7... | collective-permute-start | bytes 55304 | tf_op jit(solution)/shard_map/ppermute | solution.py:16
  6.9 0.0 copy-start.4
  7.0 0.7 copy-done.4
  7.7 0.7 copy-done.5
  8.4 0.0 copy-done.6
  8.4 0.1 copy.55
  8.5 0.1 copy.68
  8.6 0.1 multiply_exponential_fusion
  8.7 0.0 copy-start
  8.7 0.4 fusion.146
  9.2 0.4 copy-done
  9.6 0.1 copy.50
  9.8 0.0 copy-start.3
  9.8 0.9 copy-done.3
  10.7 0.1 copy.59
  10.8 0.1 rev.6
  10.9 97.2 %gather_fusion = f32[16384]{0:T(1024)S(1)} fusion(f32[128]{0:T(128)S(1)} %fusion.181, s32[16384]{0:T(1024)S(1)} %fusion.148), kind=kCustom, calls=%fused_computation | custom fusion | bytes 196608 | tf_op jit(solution)/shard_map/while/body/eval_jaxpr/gather | solution.py:33
  108.1 0.2 exponential_reduce_fusion
  108.3 0.0 collective-permute-done
  108.3 0.1 fusion.134
  108.4 1.3 fusion.103
  109.7 0.7 fusion.13
  110.4 15.4 %all-to-all-start.2 = ((bf16[64,8,128]{2,1,0:T(8,128)(2,1)}), bf16[64,8,128]{2,1,0:T(8,128)(2,1)S(1)}, u32[]{:S(2)}, u32[]{:S(2)}) async-start(bf16[64,8,128]{2,1,0:T(8,128)(2,1)} %bitcast.48), calls=%async_computation.2 | async-start | bytes 262144 | tf_op jit(solution)/shard_map/all_to_all | solution.py:122
  125.8 0.1 fusion.158
  125.8 0.1 fusion.157
  125.9 14.4 %all-to-all-done.2 = bf16[64,8,128]{2,1,0:T(8,128)(2,1)S(1)} async-done(((bf16[64,8,128]{2,1,0:T(8,128)(2,1)}), bf16[64,8,128]{2,1,0:T(8,128)(2,1)S(1)}, u32[]{:S(2)}, u32[]{:S(2)}) %all-to-all-start.2) | async-done | bytes 131104 | tf_op jit(solution)/shard_map/all_to_all | solution.py:122
  140.4 0.4 fusion.136
  140.8 1.0 convolution_bitcast_fusion
  141.8 0.6 fusion.151
  142.4 0.3 fusion.1
  142.7 0.7 copy.63
  143.5 5.9 %all-to-all-start.3 = ((bf16[8,64,128]{2,0,1:T(8,128)(2,1)}), bf16[8,64,128]{2,0,1:T(8,128)(2,1)S(1)}, u32[]{:S(2)}, u32[]{:S(2)}) async-start(bf16[8,64,128]{2,0,1:T(8,128)(2,1)} %copy.63), calls=%async_computation.3 | async-start | bytes 262144 | tf_op jit(solution)/shard_map/all_to_all | solution.py:124
  149.4 0.0 copy-done.1
  149.4 0.0 copy-start.2
  149.4 0.1 copy.52
  149.5 0.8 copy-done.2
  150.3 0.1 copy.53
  150.5 1.3 fusion.86
  151.8 1.3 fusion.69
  153.1 10.9 %all-to-all-done.3 = bf16[8,64,128]{2,0,1:T(8,128)(2,1)S(1)} async-done(((bf16[8,64,128]{2,0,1:T(8,128)(2,1)}), bf16[8,64,128]{2,0,1:T(8,128)(2,1)S(1)}, u32[]{:S(2)}, u32[]{:S(2)}) %all-to-all-start.3) | async-done | bytes 131104 | tf_op jit(solution)/shard_map/all_to_all | solution.py:124
  164.0 0.1 fusion.11
  164.1 20.2 %all_to_all.46 = bf16[64,8,128]{2,1,0:T(8,128)(2,1)S(1)} all-to-all(bf16[64,8,128]{2,1,0:T(8,128)(2,1)S(1)} %bitcast.134), channel_id=1, replica_groups=mesh['ctx'=64,'tp'=8] {'ctx'}, dimensions={0} | all-to-all | bytes 262144 | tf_op jit(solution)/shard_map/all_to_all | solution.py:119
  184.3 0.4 fusion.139
  184.7 1.0 convolution_bitcast_fusion.1
  185.7 0.6 fusion.154
  186.3 0.3 fusion
  186.6 0.7 copy.58
  187.4 5.8 %all-to-all-start.1 = ((bf16[8,64,128]{2,0,1:T(8,128)(2,1)}), bf16[8,64,128]{2,0,1:T(8,128)(2,1)S(1)}, u32[]{:S(2)}, u32[]{:S(2)}) async-start(bf16[8,64,128]{2,0,1:T(8,128)(2,1)} %copy.58), calls=%async_computation.1 | async-start | bytes 262144 | tf_op jit(solution)/shard_map/all_to_all | solution.py:121
  193.2 14.6 %all-to-all-done.1 = bf16[8,64,128]{2,0,1:T(8,128)(2,1)S(1)} async-done(((bf16[8,64,128]{2,0,1:T(8,128)(2,1)}), bf16[8,64,128]{2,0,1:T(8,128)(2,1)S(1)}, u32[]{:S(2)}, u32[]{:S(2)}) %all-to-all-start.1) | async-done | bytes 131104 | tf_op jit(solution)/shard_map/all_to_all | solution.py:121
  207.8 0.1 fusion.12
  207.9 0.1 pad_maximum_fusion
  208.0 2.3 %collective-permute-start.1 = (bf16[3,6,512]{1,2,0:T(8,128)(2,1)S(1)}, bf16[3,6,512]{1,2,0:T(8,128)(2,1)S(1)}, u32[]{:S(2)}, u32[]{:S(2)}) collective-permute-start(bf16[3,6,512]{1,2,0:T(8,128)(2,1)S(1)} %pad_maximum_fusion), channel_id=1, source_target_pairs={{8,0},{16,8},{24,16},{32,24},{40,32},{48,40},{56,48},{64,56},{72,6... | collective-permute-start | bytes 55304 | tf_op jit(solution)/shard_map/ppermute | solution.py:16
  210.4 0.8 copy.64
  211.1 5.9 %collective-permute-done.1 = bf16[3,6,512]{1,2,0:T(8,128)(2,1)S(1)} collective-permute-done((bf16[3,6,512]{1,2,0:T(8,128)(2,1)S(1)}, bf16[3,6,512]{1,2,0:T(8,128)(2,1)S(1)}, u32[]{:S(2)}, u32[]{:S(2)}) %collective-permute-start.1) | collective-permute-done | bytes 18464 | tf_op jit(solution)/shard_map/ppermute | solution.py:16
  217.1 0.1 fusion.130
  217.1 1.4 fusion.18
  218.5 0.8 copy.67
  219.2 1.3 fusion.35
  220.6 0.8 copy.66
  221.4 1.3 fusion.52
  222.7 0.8 copy.65
  (21 shorter events, 0.3 us)
Async XLA Ops:
  2.4 105.9 %collective-permute-start = (bf16[3,6,512]{1,2,0:T(8,128)(2,1)S(1)}, bf16[3,6,512]{1,2,0:T(8,128)(2,1)S(1)}, u32[]{:S(2)}, u32[]{:S(2)}) collective-permute-start(bf16[3,6,512]{1,2,0:T(8,128)(2,1)S(1)} %copy.51), channel_id=1, source_target_pairs={{0,8},{8,16},{16,24},{24,32},{32,40},{40,48},{48,56},{56,64},{64,7... | collective-permute-start | bytes 55304 | tf_op jit(solution)/shard_map/ppermute | solution.py:16
  6.9 0.8 copy-start.4
  7.7 0.7 copy-start.5
  7.7 0.7 copy-start.6
  8.7 0.9 copy-start
  9.8 0.9 copy-start.3
  110.4 30.0 %all-to-all-start.2 = ((bf16[64,8,128]{2,1,0:T(8,128)(2,1)}), bf16[64,8,128]{2,1,0:T(8,128)(2,1)S(1)}, u32[]{:S(2)}, u32[]{:S(2)}) async-start(bf16[64,8,128]{2,1,0:T(8,128)(2,1)} %bitcast.48), calls=%async_computation.2 | async-start | bytes 262144 | tf_op jit(solution)/shard_map/all_to_all | solution.py:122
  143.5 5.9 %copy-start.1 = (bf16[128,512]{1,0:T(8,128)(2,1)S(1)}, bf16[128,512]{1,0:T(8,128)(2,1)}, u32[]{:S(2)}) copy-start(bf16[128,512]{1,0:T(8,128)(2,1)} %param.8) | copy-start | bytes 393220
  143.5 20.5 %all-to-all-start.3 = ((bf16[8,64,128]{2,0,1:T(8,128)(2,1)}), bf16[8,64,128]{2,0,1:T(8,128)(2,1)S(1)}, u32[]{:S(2)}, u32[]{:S(2)}) async-start(bf16[8,64,128]{2,0,1:T(8,128)(2,1)} %copy.63), calls=%async_computation.3 | async-start | bytes 262144 | tf_op jit(solution)/shard_map/all_to_all | solution.py:124
  149.4 0.9 copy-start.2
  187.4 20.4 %all-to-all-start.1 = ((bf16[8,64,128]{2,0,1:T(8,128)(2,1)}), bf16[8,64,128]{2,0,1:T(8,128)(2,1)S(1)}, u32[]{:S(2)}, u32[]{:S(2)}) async-start(bf16[8,64,128]{2,0,1:T(8,128)(2,1)} %copy.58), calls=%async_computation.1 | async-start | bytes 262144 | tf_op jit(solution)/shard_map/all_to_all | solution.py:121
  208.0 9.1 %collective-permute-start.1 = (bf16[3,6,512]{1,2,0:T(8,128)(2,1)S(1)}, bf16[3,6,512]{1,2,0:T(8,128)(2,1)S(1)}, u32[]{:S(2)}, u32[]{:S(2)}) collective-permute-start(bf16[3,6,512]{1,2,0:T(8,128)(2,1)S(1)} %pad_maximum_fusion), channel_id=1, source_target_pairs={{8,0},{16,8},{24,16},{32,24},{40,32},{48,40},{56,48},{64,56},{72,6... | collective-permute-start | bytes 55304 | tf_op jit(solution)/shard_map/ppermute | solution.py:16
where the time goes:
time: 224 us; the launch traced here: 223 us
  local copies, waits for them, and re-layouts  108 us (48%)
  waiting for transfers between devices  45.9 us (20%)
  starting transfers between devices  33.8 us (15%)
  blocking collectives  20.2 us (9%)
  other arithmetic  9.66 us (4%)
  matrix products  5.13 us (2%)
    gather x1, local copies, waits for them, and re-layouts, toeplitz_of(): impulse_row[jnp.clip(lag_grid, 0, block_len - 1)]  97.2 us
    all_to_all x1, blocking collectives, shards(): lax.all_to_all(product.T, 'ctx', split_axis=0, concat_axis=1, tiled=True)  20.2 us
    all_to_all x1, starting transfers between devices, shards(): lax.all_to_all(grad_conv.T, 'ctx', split_axis=0, concat_axis=1, tiled=True)  15.4 us
    all_to_all x1, waiting for transfers between devices, shards(): lax.all_to_all(conv_rows, 'ctx', split_axis=1, concat_axis=0, tiled=True)  14.6 us
    all_to_all x1, waiting for transfers between devices, shards(): lax.all_to_all(grad_conv.T, 'ctx', split_axis=0, concat_axis=1, tiled=True)  14.4 us
    all_to_all x1, waiting for transfers between devices, shards(): lax.all_to_all(grad_rows, 'ctx', split_axis=1, concat_axis=0, tiled=True)  10.9 us
    unnamed x22, local copies, waits for them, and re-layouts  7.04 us
    ppermute x2, starting transfers between devices, from_behind(): lax.ppermute(value, axis, [(source, source + steps) for source in range(l...  6.81 us
  transfers between devices with their start and end apart: 5, of which 4 were waited for; matrix products, arithmetic and copies ran while one was open for 46% of the time, Pallas kernels for 0%

commit v1 on v0

v1 whole, which is shorter than its diff:
```python
import jax
import jax.numpy as jnp
from jax import lax
from jax.sharding import PartitionSpec as P

GROUP = 16
SHORT = 7


precise = lax.Precision.HIGHEST


def from_behind(value, axis, steps):
    count = lax.axis_size(axis)
    leading, last = (max(0, -steps), min(count, count - steps))
    return lax.ppermute(value, axis, [(source, source + steps) for source in range(leading, last)])


def rounded(values):
    return lax.optimization_barrier(values.astype(jnp.bfloat16))


def short_causal(prior_rows, inputs, filter_taps):
    length = inputs.shape[0]
    padded = jnp.concatenate([prior_rows.astype(jnp.float32), inputs.astype(jnp.float32)], axis=0)
    summed = jnp.zeros(inputs.shape, jnp.float32)
    for offset in range(SHORT):
        summed = (
            summed + filter_taps[offset] * padded[SHORT - 1 - offset : SHORT - 1 - offset + length]
        )
    return summed


def short_reverse(grad_rows, next_rows, filter_taps):
    length = grad_rows.shape[0]
    padded = jnp.concatenate([grad_rows.astype(jnp.float32), next_rows.astype(jnp.float32)], axis=0)
    summed = jnp.zeros(grad_rows.shape, jnp.float32)
    for offset in range(SHORT):
        summed = summed + filter_taps[offset] * padded[offset : offset + length]
    return summed


def split_dot(spec, table, values):
    high = table.astype(jnp.bfloat16)
    low = (table - high.astype(jnp.float32)).astype(jnp.bfloat16)
    lhs = jnp.einsum(spec, high, values, preferred_element_type=jnp.float32)
    return lhs + jnp.einsum(spec, low, values, preferred_element_type=jnp.float32)


def modal_scan(local_state, decay_step, axis, forward):
    count = lax.axis_size(axis)
    entering = jnp.zeros_like(local_state)
    window = local_state
    shift = 1
    while shift < count:
        if forward:
            pairs = [(source, source + shift) for source in range(count - shift)]
        else:
            pairs = [(source, source - shift) for source in range(shift, count)]
        arrived = lax.ppermute(window, axis, pairs)
        entering = entering + jnp.exp(-decay_step * (shift - 1)) * arrived
        if shift * 2 < count:
            window = window + jnp.exp(-decay_step * shift) * arrived
        shift *= 2
    return entering


def shards(u_query, u_key, u_value, short_filter, decay_rate, residue, grad_out):
    block_len, channels = u_query.shape
    group_count = channels // GROUP
    rim_rows = jnp.stack(
        [
            u_query[block_len - SHORT + 1 :],
            u_key[block_len - SHORT + 1 :],
            u_value[block_len - SHORT + 1 :],
        ]
    )
    before = from_behind(rim_rows, "ctx", 1)
    q_short = rounded(short_causal(before[0], u_query, short_filter[0]))
    k_short = rounded(short_causal(before[1], u_key, short_filter[1]))
    v_short = rounded(short_causal(before[2], u_value, short_filter[2]))
    product = rounded(k_short.astype(jnp.float32) * v_short.astype(jnp.float32))
    grad_conv = rounded(grad_out.astype(jnp.float32) * q_short.astype(jnp.float32))

    rates = decay_rate
    weights = residue * jnp.sqrt(-jnp.expm1(-2.0 * rates))
    lags = jnp.arange(block_len + 1).astype(jnp.float32)
    powers = jnp.exp(-rates[:, :, None] * lags)
    centred = jnp.arange(block_len).astype(jnp.float32) - block_len // 2
    falling = weights[:, None, :] * jnp.exp(-centred[None, :, None] * rates[:, None, :])
    rising = jnp.exp(centred[None, None, :] * rates[:, :, None])
    toeplitz = jnp.einsum("gtm,gms->gts", falling, rising, precision=precise)
    lower = jnp.arange(block_len)[:, None] >= jnp.arange(block_len)[None, :]
    toeplitz = jnp.where(lower[None], toeplitz, 0.0)

    signal = product.reshape(block_len, group_count, GROUP)
    cotangent = grad_conv.reshape(block_len, group_count, GROUP)
    end_state = split_dot("gms,sgc->gmc", powers[:, :, block_len - 1 :: -1], signal)
    start_state = split_dot("gms,sgc->gmc", powers[:, :, :block_len], cotangent)
    decay_step = (rates * block_len)[:, :, None]
    entering = modal_scan(end_state, decay_step, "ctx", True)
    leaving = modal_scan(start_state, decay_step, "ctx", False)

    local_conv = split_dot("gts,sgc->tgc", toeplitz, signal)
    local_grad = split_dot("gts,tgc->sgc", toeplitz, cotangent)
    lead_fwd = weights[:, None, :] * jnp.swapaxes(powers[:, :, 1:], 1, 2)
    lead_bwd = weights[:, None, :] * jnp.swapaxes(powers[:, :, block_len:0:-1], 1, 2)
    carried_conv = jnp.einsum("gtm,gmc->tgc", lead_fwd, entering, precision=precise)
    carried_grad = jnp.einsum("gsm,gmc->sgc", lead_bwd, leaving, precision=precise)
    conv_out = rounded((local_conv + carried_conv).reshape(block_len, channels))
    grad_prod = rounded((local_grad + carried_grad).reshape(block_len, channels))

    mixer_out = (q_short.astype(jnp.float32) * conv_out.astype(jnp.float32)).astype(jnp.bfloat16)
    grad_qshort = rounded(grad_out.astype(jnp.float32) * conv_out.astype(jnp.float32))
    grad_kshort = rounded(grad_prod.astype(jnp.float32) * v_short.astype(jnp.float32))
    grad_vshort = rounded(grad_prod.astype(jnp.float32) * k_short.astype(jnp.float32))
    head_rows = jnp.stack(
        [grad_qshort[: SHORT - 1], grad_kshort[: SHORT - 1], grad_vshort[: SHORT - 1]]
    )
    next_rows = from_behind(head_rows, "ctx", -1)
    grad_query = short_reverse(grad_qshort, next_rows[0], short_filter[0]).astype(jnp.bfloat16)
    grad_key = short_reverse(grad_kshort, next_rows[1], short_filter[1]).astype(jnp.bfloat16)
    grad_value = short_reverse(grad_vshort, next_rows[2], short_filter[2]).astype(jnp.bfloat16)
    return (mixer_out, grad_query, grad_key, grad_value)


def solution(mesh):
    return jax.shard_map(
        shards,
        mesh=mesh,
        in_specs=(
            P("ctx", "tp"),
            P("ctx", "tp"),
            P("ctx", "tp"),
            P(None, None, "tp"),
            P("tp", None),
            P("tp", None),
            P("ctx", "tp"),
        ),
        out_specs=(P("ctx", "tp"), P("ctx", "tp"), P("ctx", "tp"), P("ctx", "tp")),
        check_vma=False,
    )
```

time: 224 us -> 217 us (0.969)
  the two profiles are of different devices: /device:TPU:1 before, /device:TPU:407 now
where the time goes in v1:
time: 217 us; the launch traced here: 216 us
  waiting for transfers between devices  105 us (48%)
  starting transfers between devices  55.2 us (25%)
  local copies, waits for them, and re-layouts  27.2 us (13%)
  other arithmetic  17 us (8%)
  matrix products  9.86 us (5%)
    ppermute x12, waiting for transfers between devices, modal_scan(): arrived = lax.ppermute(window, axis, pairs)  91.3 us
    ppermute x12, starting transfers between devices, modal_scan(): arrived = lax.ppermute(window, axis, pairs)  31.3 us
    ppermute x2, starting transfers between devices, from_behind(): lax.ppermute(value, axis, [(source, source + steps) for source in range(l...  23.9 us
    ppermute x2, waiting for transfers between devices, from_behind(): lax.ppermute(value, axis, [(source, source + steps) for source in range(l...  13.6 us
    exp x6, local copies, waits for them, and re-layouts, modal_scan(): entering = entering + jnp.exp(-decay_step * (shift - 1)) * arrived  7.62 us
    unnamed x129, local copies, waits for them, and re-layouts  6.41 us
    exp x4, local copies, waits for them, and re-layouts, modal_scan(): window = window + jnp.exp(-decay_step * shift) * arrived  5.5 us
    convert_element_type x6, other arithmetic, rounded(): return lax.optimization_barrier(values.astype(jnp.bfloat16))  4.72 us
  transfers between devices with their start and end apart: 14, of which 12 were waited for; matrix products, arithmetic and copies ran while one was open for 16% of the time, Pallas kernels for 0%

profile of v1, /device:TPU:407, one launch (start us, length us, event | category | flops | bytes accessed | tf_op | source)
XLA Modules:
  0.0 215.9 jit_solution(1914771671786607331)
XLA Ops:
  0.6 0.7 slice_bitcast_fusion.11
  1.3 0.7 slice_bitcast_fusion.9
  2.4 3.3 %collective-permute-start = (bf16[3,6,512]{1,2,0:T(8,128)(2,1)S(1)}, bf16[3,6,512]{1,2,0:T(8,128)(2,1)}, u32[]{:S(2)}, u32[]{:S(2)}) collective-permute-start(bf16[3,6,512]{1,2,0:T(8,128)(2,1)S(1)} %copy.97), channel_id=1, source_target_pairs={{0,8},{8,16},{16,24},{24,32},{32,40},{40,48},{48,56},{56,64},{64,7... | collective-permute-start | bytes 55304 | tf_op jit(solution)/shard_map/ppermute | solution.py:16
  5.6 0.8 copy.101
  6.4 1.4 multiply_exponential_fusion.9
  8.1 0.9 fusion.188
  9.0 3.7 %fusion.142 = f32[32,128,128]{2,1,0:T(8,128)S(1)} fusion(f32[32,16]{1,0:T(8,128)S(1)} %copy.101, f32[128]{0:T(128)S(1)} %get-tuple-element.64, f32[128]{0:T(128)S(1)} %get-tuple-element.65, f32[32,16]{1,0:T(8,128)S(1)} %copy.100), kind=kOutput, calls=%fused_computation.236 | convolution fusion | flops 100859904 | bytes 2102272 | tf_op jit(solution)/shard_map/gtm,gms->gts/dot_general | solution.py:92
  13.6 1.9 fusion.153
  15.5 2.0 fusion.99
  18.0 1.9 collective-permute-start.7
  19.9 1.4 fusion.190
  21.3 0.8 copy.105
  22.1 5.7 %collective-permute-done.7 = f32[32,16,16]{2,1,0:T(8,128)S(1)} collective-permute-done((f32[32,16,16]{2,1,0:T(8,128)S(1)}, f32[32,16,16]{2,1,0:T(8,128)S(1)}, u32[]{:S(2)}, u32[]{:S(2)}) %collective-permute-start.7) | collective-permute-done | bytes 32800 | tf_op jit(solution)/shard_map/ppermute | solution.py:60
  27.8 0.8 multiply_add_fusion.4
  28.6 1.9 collective-permute-start.8
  30.6 1.0 copy.98
  31.6 1.0 copy.99
  32.6 1.4 copy.103
  34.0 1.4 copy.106
  35.4 1.4 copy.107
  36.7 1.4 copy.108
  38.1 1.4 copy.109
  39.5 1.4 copy.110
  40.9 1.4 copy.111
  42.2 1.4 copy.112
  43.6 1.4 copy.113
  45.0 0.7 convert_element_type.187
  45.7 0.7 convert_element_type.192
  46.4 1.8 rev.7
  48.3 1.1 rev.6
  49.4 1.2 multiply_add_fusion.3
  50.5 1.9 collective-permute-start.9
  52.9 8.4 %collective-permute-done.9 = f32[32,16,16]{2,1,0:T(8,128)S(1)} collective-permute-done((f32[32,16,16]{2,1,0:T(8,128)S(1)}, f32[32,16,16]{2,1,0:T(8,128)S(1)}, u32[]{:S(2)}, u32[]{:S(2)}) %collective-permute-start.9) | collective-permute-done | bytes 32800 | tf_op jit(solution)/shard_map/ppermute | solution.py:60
  61.6 5.2 %collective-permute-start.10 = (f32[32,16,16]{2,1,0:T(8,128)S(1)}, f32[32,16,16]{2,1,0:T(8,128)S(1)}, u32[]{:S(2)}, u32[]{:S(2)}) collective-permute-start(f32[32,16,16]{2,1,0:T(8,128)S(1)} %multiply_add_fusion.2), channel_id=1, source_target_pairs={{64,0},{72,8},{80,16},{88,24},{96,32},{104,40},{112,48},{120,56},{... | collective-permute-start | bytes 98312 | tf_op jit(solution)/shard_map/ppermute | solution.py:60
  67.2 4.0 %collective-permute-done.10 = f32[32,16,16]{2,1,0:T(8,128)S(1)} collective-permute-done((f32[32,16,16]{2,1,0:T(8,128)S(1)}, f32[32,16,16]{2,1,0:T(8,128)S(1)}, u32[]{:S(2)}, u32[]{:S(2)}) %collective-permute-start.10) | collective-permute-done | bytes 32800 | tf_op jit(solution)/shard_map/ppermute | solution.py:60
  71.3 4.3 %collective-permute-start.11 = (f32[32,16,16]{2,1,0:T(8,128)S(1)}, f32[32,16,16]{2,1,0:T(8,128)S(1)}, u32[]{:S(2)}, u32[]{:S(2)}) collective-permute-start(f32[32,16,16]{2,1,0:T(8,128)S(1)} %multiply_add_fusion.1), channel_id=1, source_target_pairs={{128,0},{136,8},{144,16},{152,24},{160,32},{168,40},{176,48},{184,... | collective-permute-start | bytes 98312 | tf_op jit(solution)/shard_map/ppermute | solution.py:60
  75.7 1.3 fusion.82
  77.0 10.7 %collective-permute-done.11 = f32[32,16,16]{2,1,0:T(8,128)S(1)} collective-permute-done((f32[32,16,16]{2,1,0:T(8,128)S(1)}, f32[32,16,16]{2,1,0:T(8,128)S(1)}, u32[]{:S(2)}, u32[]{:S(2)}) %collective-permute-start.11) | collective-permute-done | bytes 32800 | tf_op jit(solution)/shard_map/ppermute | solution.py:60
  87.8 5.2 %collective-permute-start.12 = (f32[32,16,16]{2,1,0:T(8,128)S(1)}, f32[32,16,16]{2,1,0:T(8,128)S(1)}, u32[]{:S(2)}, u32[]{:S(2)}) collective-permute-start(f32[32,16,16]{2,1,0:T(8,128)S(1)} %multiply_add_fusion), channel_id=1, source_target_pairs={{256,0},{264,8},{272,16},{280,24},{288,32},{296,40},{304,48},{312,... | collective-permute-start | bytes 98312 | tf_op jit(solution)/shard_map/ppermute | solution.py:60
  93.1 1.3 fusion.65
  94.4 17.9 %collective-permute-done.12 = f32[32,16,16]{2,1,0:T(8,128)S(1)} collective-permute-done((f32[32,16,16]{2,1,0:T(8,128)S(1)}, f32[32,16,16]{2,1,0:T(8,128)S(1)}, u32[]{:S(2)}, u32[]{:S(2)}) %collective-permute-start.12) | collective-permute-done | bytes 32800 | tf_op jit(solution)/shard_map/ppermute | solution.py:60
  112.3 2.1 fusion.1
  114.9 1.9 collective-permute-start.1
  116.9 3.3 %collective-permute-done.1 = f32[32,16,16]{2,1,0:T(8,128)S(1)} collective-permute-done((f32[32,16,16]{2,1,0:T(8,128)S(1)}, f32[32,16,16]{2,1,0:T(8,128)S(1)}, u32[]{:S(2)}, u32[]{:S(2)}) %collective-permute-start.1) | collective-permute-done | bytes 32800 | tf_op jit(solution)/shard_map/ppermute | solution.py:60
  120.3 1.9 collective-permute-start.2
  122.2 5.6 %collective-permute-done.2 = f32[32,16,16]{2,1,0:T(8,128)S(1)} collective-permute-done((f32[32,16,16]{2,1,0:T(8,128)S(1)}, f32[32,16,16]{2,1,0:T(8,128)S(1)}, u32[]{:S(2)}, u32[]{:S(2)}) %collective-permute-start.2) | collective-permute-done | bytes 32800 | tf_op jit(solution)/shard_map/ppermute | solution.py:60
  127.9 1.9 collective-permute-start.3
  130.5 6.1 %collective-permute-done.3 = f32[32,16,16]{2,1,0:T(8,128)S(1)} collective-permute-done((f32[32,16,16]{2,1,0:T(8,128)S(1)}, f32[32,16,16]{2,1,0:T(8,128)S(1)}, u32[]{:S(2)}, u32[]{:S(2)}) %collective-permute-start.3) | collective-permute-done | bytes 32800 | tf_op jit(solution)/shard_map/ppermute | solution.py:60
  136.7 1.9 collective-permute-start.4
  139.3 8.2 %collective-permute-done.4 = f32[32,16,16]{2,1,0:T(8,128)S(1)} collective-permute-done((f32[32,16,16]{2,1,0:T(8,128)S(1)}, f32[32,16,16]{2,1,0:T(8,128)S(1)}, u32[]{:S(2)}, u32[]{:S(2)}) %collective-permute-start.4) | collective-permute-done | bytes 32800 | tf_op jit(solution)/shard_map/ppermute | solution.py:60
  147.6 1.9 collective-permute-start.5
  149.6 11.6 %collective-permute-done.5 = f32[32,16,16]{2,1,0:T(8,128)S(1)} collective-permute-done((f32[32,16,16]{2,1,0:T(8,128)S(1)}, f32[32,16,16]{2,1,0:T(8,128)S(1)}, u32[]{:S(2)}, u32[]{:S(2)}) %collective-permute-start.5) | collective-permute-done | bytes 32800 | tf_op jit(solution)/shard_map/ppermute | solution.py:60
  161.3 1.3 collective-permute-start.6
  162.6 9.9 %collective-permute-done.6 = f32[32,16,16]{2,1,0:T(8,128)S(1)} collective-permute-done((f32[32,16,16]{2,1,0:T(8,128)S(1)}, f32[32,16,16]{2,1,0:T(8,128)S(1)}, u32[]{:S(2)}, u32[]{:S(2)}) %collective-permute-start.6) | collective-permute-done | bytes 32800 | tf_op jit(solution)/shard_map/ppermute | solution.py:60
  172.5 1.2 fusion
  174.1 20.6 %collective-permute-start.13 = (bf16[3,6,512]{1,2,0:T(8,128)(2,1)S(1)}, bf16[3,6,512]{1,2,0:T(8,128)(2,1)S(1)}, u32[]{:S(2)}, u32[]{:S(2)}) collective-permute-start(bf16[3,6,512]{1,2,0:T(8,128)(2,1)S(1)} %pad_maximum_fusion), channel_id=1, source_target_pairs={{8,0},{16,8},{24,16},{32,24},{40,32},{48,40},{56,48},{64,56},{72,6... | collective-permute-start | bytes 55304 | tf_op jit(solution)/shard_map/ppermute | solution.py:16
  194.9 0.8 copy.118
  195.7 13.6 %collective-permute-done.13 = bf16[3,6,512]{1,2,0:T(8,128)(2,1)S(1)} collective-permute-done((bf16[3,6,512]{1,2,0:T(8,128)(2,1)S(1)}, bf16[3,6,512]{1,2,0:T(8,128)(2,1)S(1)}, u32[]{:S(2)}, u32[]{:S(2)}) %collective-permute-start.13) | collective-permute-done | bytes 18464 | tf_op jit(solution)/shard_map/ppermute | solution.py:16
  209.4 1.4 fusion.48
  210.8 0.8 copy.119
  211.6 1.4 fusion.31
  212.9 0.8 copy.120
  213.8 1.4 fusion.14
  215.1 0.8 copy.121
  (161 shorter events, 6.1 us)
Async XLA Ops:
  2.4 11.3 %collective-permute-start = (bf16[3,6,512]{1,2,0:T(8,128)(2,1)S(1)}, bf16[3,6,512]{1,2,0:T(8,128)(2,1)}, u32[]{:S(2)}, u32[]{:S(2)}) collective-permute-start(bf16[3,6,512]{1,2,0:T(8,128)(2,1)S(1)} %copy.97), channel_id=1, source_target_pairs={{0,8},{8,16},{16,24},{24,32},{32,40},{40,48},{48,56},{56,64},{64,7... | collective-permute-start | bytes 55304 | tf_op jit(solution)/shard_map/ppermute | solution.py:16
  18.0 9.8 %collective-permute-start.7 = (f32[32,16,16]{2,1,0:T(8,128)S(1)}, f32[32,16,16]{2,1,0:T(8,128)S(1)}, u32[]{:S(2)}, u32[]{:S(2)}) collective-permute-start(f32[32,16,16]{2,1,0:T(8,128)S(1)} %convolution_add_fusion.1), channel_id=1, source_target_pairs={{8,0},{16,8},{24,16},{32,24},{40,32},{48,40},{56,48},{64,56},{72,6... | collective-permute-start | bytes 98312 | tf_op jit(solution)/shard_map/ppermute | solution.py:60
  28.6 20.7 %collective-permute-start.8 = (f32[32,16,16]{2,1,0:T(8,128)}, f32[32,16,16]{2,1,0:T(8,128)}, u32[]{:S(2)}, u32[]{:S(2)}) collective-permute-start(f32[32,16,16]{2,1,0:T(8,128)} %multiply_add_fusion.4), channel_id=1, source_target_pairs={{16,0},{24,8},{32,16},{40,24},{48,32},{56,40},{64,48},{72,56},{80,... | collective-permute-start | bytes 98312 | tf_op jit(solution)/shard_map/ppermute | solution.py:60
  50.5 10.8 %collective-permute-start.9 = (f32[32,16,16]{2,1,0:T(8,128)S(1)}, f32[32,16,16]{2,1,0:T(8,128)S(1)}, u32[]{:S(2)}, u32[]{:S(2)}) collective-permute-start(f32[32,16,16]{2,1,0:T(8,128)S(1)} %multiply_add_fusion.3), channel_id=1, source_target_pairs={{32,0},{40,8},{48,16},{56,24},{64,32},{72,40},{80,48},{88,56},{96,... | collective-permute-start | bytes 98312 | tf_op jit(solution)/shard_map/ppermute | solution.py:60
  52.8 18.4 %copy-start.16 = (f32[32,16]{1,0:T(8,128)S(1)}, f32[32,16]{1,0:T(8,128)}, u32[]{:S(2)}) copy-start(f32[32,16]{1,0:T(8,128)} %copy.111) | copy-start | bytes 6148
  52.8 22.8 %copy-start.2 = (f32[128,512]{0,1:T(8,128)S(1)}, f32[128,512]{0,1:T(8,128)}, u32[]{:S(2)}) copy-start(f32[128,512]{0,1:T(8,128)} %convert_element_type.187) | copy-start | bytes 786436
  52.8 22.8 %copy-start.4 = (f32[6,512]{0,1:T(8,128)S(1)}, f32[6,512]{0,1:T(8,128)}, u32[]{:S(2)}) copy-start(f32[6,512]{0,1:T(8,128)} %get-tuple-element.23) | copy-start | bytes 36868
  52.8 22.8 %copy-start.31 = (f32[1,1,512]{2,1,0:T(1,128)S(1)}, f32[1,1,512]{2,1,0:T(1,128)}, u32[]{:S(2)}) copy-start(f32[1,1,512]{2,1,0:T(1,128)} %get-tuple-element.35) | copy-start | bytes 6148
  52.9 22.8 %copy-start.33 = (f32[1,1,512]{2,1,0:T(1,128)S(1)}, f32[1,1,512]{2,1,0:T(1,128)}, u32[]{:S(2)}) copy-start(f32[1,1,512]{2,1,0:T(1,128)} %get-tuple-element.36) | copy-start | bytes 6148
  52.9 22.8 %copy-start.35 = (f32[1,1,512]{2,1,0:T(1,128)S(1)}, f32[1,1,512]{2,1,0:T(1,128)}, u32[]{:S(2)}) copy-start(f32[1,1,512]{2,1,0:T(1,128)} %get-tuple-element.37) | copy-start | bytes 6148
  52.9 22.8 %copy-start.37 = (f32[1,1,512]{2,1,0:T(1,128)S(1)}, f32[1,1,512]{2,1,0:T(1,128)}, u32[]{:S(2)}) copy-start(f32[1,1,512]{2,1,0:T(1,128)} %get-tuple-element.38) | copy-start | bytes 6148
  52.9 22.8 %copy-start.39 = (f32[1,1,512]{2,1,0:T(1,128)S(1)}, f32[1,1,512]{2,1,0:T(1,128)}, u32[]{:S(2)}) copy-start(f32[1,1,512]{2,1,0:T(1,128)} %get-tuple-element.39) | copy-start | bytes 6148
  52.9 22.8 %copy-start.41 = (f32[1,1,512]{2,1,0:T(1,128)S(1)}, f32[1,1,512]{2,1,0:T(1,128)}, u32[]{:S(2)}) copy-start(f32[1,1,512]{2,1,0:T(1,128)} %get-tuple-element.40) | copy-start | bytes 6148
  52.9 22.8 %copy-start.43 = (f32[1,1,512]{2,1,0:T(1,128)S(1)}, f32[1,1,512]{2,1,0:T(1,128)}, u32[]{:S(2)}) copy-start(f32[1,1,512]{2,1,0:T(1,128)} %get-tuple-element.41) | copy-start | bytes 6148
  61.5 26.2 %copy-start.15 = (f32[32,16]{1,0:T(8,128)S(1)}, f32[32,16]{1,0:T(8,128)}, u32[]{:S(2)}) copy-start(f32[32,16]{1,0:T(8,128)} %copy.113) | copy-start | bytes 6148
  61.5 31.5 %copy-start.1 = (f32[128,512]{0,1:T(8,128)S(1)}, f32[128,512]{0,1:T(8,128)}, u32[]{:S(2)}) copy-start(f32[128,512]{0,1:T(8,128)} %convert_element_type.192) | copy-start | bytes 786436
  61.5 31.5 %copy-start.3 = (f32[6,512]{0,1:T(8,128)S(1)}, f32[6,512]{0,1:T(8,128)}, u32[]{:S(2)}) copy-start(f32[6,512]{0,1:T(8,128)} %get-tuple-element.22) | copy-start | bytes 36868
  61.5 31.5 %copy-start.21 = (f32[1,1,512]{2,1,0:T(1,128)S(1)}, f32[1,1,512]{2,1,0:T(1,128)}, u32[]{:S(2)}) copy-start(f32[1,1,512]{2,1,0:T(1,128)} %get-tuple-element.30) | copy-start | bytes 6148
  61.5 31.5 %copy-start.23 = (f32[1,1,512]{2,1,0:T(1,128)S(1)}, f32[1,1,512]{2,1,0:T(1,128)}, u32[]{:S(2)}) copy-start(f32[1,1,512]{2,1,0:T(1,128)} %get-tuple-element.31) | copy-start | bytes 6148
  61.5 31.5 %copy-start.25 = (f32[1,1,512]{2,1,0:T(1,128)S(1)}, f32[1,1,512]{2,1,0:T(1,128)}, u32[]{:S(2)}) copy-start(f32[1,1,512]{2,1,0:T(1,128)} %get-tuple-element.32) | copy-start | bytes 6148
  61.5 31.5 %copy-start.27 = (f32[1,1,512]{2,1,0:T(1,128)S(1)}, f32[1,1,512]{2,1,0:T(1,128)}, u32[]{:S(2)}) copy-start(f32[1,1,512]{2,1,0:T(1,128)} %get-tuple-element.33) | copy-start | bytes 6148
  61.5 31.5 %copy-start.29 = (f32[1,1,512]{2,1,0:T(1,128)S(1)}, f32[1,1,512]{2,1,0:T(1,128)}, u32[]{:S(2)}) copy-start(f32[1,1,512]{2,1,0:T(1,128)} %get-tuple-element.34) | copy-start | bytes 6148
  61.5 31.5 %copy-start.56 = (f32[1,1,512]{2,1,0:T(1,128)S(1)}, f32[1,1,512]{2,1,0:T(1,128)}, u32[]{:S(2)}) copy-start(f32[1,1,512]{2,1,0:T(1,128)} %get-tuple-element.48) | copy-start | bytes 6148
  61.6 31.5 %copy-start.58 = (f32[1,1,512]{2,1,0:T(1,128)S(1)}, f32[1,1,512]{2,1,0:T(1,128)}, u32[]{:S(2)}) copy-start(f32[1,1,512]{2,1,0:T(1,128)} %get-tuple-element.49) | copy-start | bytes 6148
  61.6 9.6 %collective-permute-start.10 = (f32[32,16,16]{2,1,0:T(8,128)S(1)}, f32[32,16,16]{2,1,0:T(8,128)S(1)}, u32[]{:S(2)}, u32[]{:S(2)}) collective-permute-start(f32[32,16,16]{2,1,0:T(8,128)S(1)} %multiply_add_fusion.2), channel_id=1, source_target_pairs={{64,0},{72,8},{80,16},{88,24},{96,32},{104,40},{112,48},{120,56},{... | collective-permute-start | bytes 98312 | tf_op jit(solution)/shard_map/ppermute | solution.py:60
  67.2 45.1 %copy-start = (f32[32,16,128]{2,1,0:T(8,128)S(1)}, f32[32,16,128]{2,1,0:T(8,128)}, u32[]{:S(2)}) copy-start(f32[32,16,128]{2,1,0:T(8,128)} %rev.7) | copy-start | bytes 786436
  67.2 45.1 %copy-start.6 = (f32[32,16]{1,0:T(8,128)S(1)}, f32[32,16]{1,0:T(8,128)}, u32[]{:S(2)}) copy-start(f32[32,16]{1,0:T(8,128)} %copy-done.5) | copy-start | bytes 6148
  67.2 45.1 %copy-start.8 = (f32[32,16]{1,0:T(8,128)S(1)}, f32[32,16]{1,0:T(8,128)}, u32[]{:S(2)}) copy-start(f32[32,16]{1,0:T(8,128)} %copy-done.7) | copy-start | bytes 6148
  67.2 45.1 %copy-start.10 = (f32[32,16]{1,0:T(8,128)S(1)}, f32[32,16]{1,0:T(8,128)}, u32[]{:S(2)}) copy-start(f32[32,16]{1,0:T(8,128)} %copy.103) | copy-start | bytes 6148
  67.2 45.1 %copy-start.11 = (f32[32,16]{1,0:T(8,128)S(1)}, f32[32,16]{1,0:T(8,128)}, u32[]{:S(2)}) copy-start(f32[32,16]{1,0:T(8,128)} %copy.106) | copy-start | bytes 6148
  67.2 45.1 %copy-start.12 = (f32[32,16]{1,0:T(8,128)S(1)}, f32[32,16]{1,0:T(8,128)}, u32[]{:S(2)}) copy-start(f32[32,16]{1,0:T(8,128)} %copy.108) | copy-start | bytes 6148
  67.2 45.1 %copy-start.13 = (f32[32,16]{1,0:T(8,128)S(1)}, f32[32,16]{1,0:T(8,128)}, u32[]{:S(2)}) copy-start(f32[32,16]{1,0:T(8,128)} %copy.110) | copy-start | bytes 6148
  67.2 45.1 %copy-start.14 = (f32[32,16]{1,0:T(8,128)S(1)}, f32[32,16]{1,0:T(8,128)}, u32[]{:S(2)}) copy-start(f32[32,16]{1,0:T(8,128)} %copy.112) | copy-start | bytes 6148
  71.3 16.3 %collective-permute-start.11 = (f32[32,16,16]{2,1,0:T(8,128)S(1)}, f32[32,16,16]{2,1,0:T(8,128)S(1)}, u32[]{:S(2)}, u32[]{:S(2)}) collective-permute-start(f32[32,16,16]{2,1,0:T(8,128)S(1)} %multiply_add_fusion.1), channel_id=1, source_target_pairs={{128,0},{136,8},{144,16},{152,24},{160,32},{168,40},{176,48},{184,... | collective-permute-start | bytes 98312 | tf_op jit(solution)/shard_map/ppermute | solution.py:60
  87.8 24.5 %collective-permute-start.12 = (f32[32,16,16]{2,1,0:T(8,128)S(1)}, f32[32,16,16]{2,1,0:T(8,128)S(1)}, u32[]{:S(2)}, u32[]{:S(2)}) collective-permute-start(f32[32,16,16]{2,1,0:T(8,128)S(1)} %multiply_add_fusion), channel_id=1, source_target_pairs={{256,0},{264,8},{272,16},{280,24},{288,32},{296,40},{304,48},{312,... | collective-permute-start | bytes 98312 | tf_op jit(solution)/shard_map/ppermute | solution.py:60
  114.4 13.4 %copy-start.18 = (f32[32,16]{1,0:T(8,128)S(1)}, f32[32,16]{1,0:T(8,128)}, u32[]{:S(2)}) copy-start(f32[32,16]{1,0:T(8,128)} %copy.107) | copy-start | bytes 6148
  114.9 5.2 %collective-permute-start.1 = (f32[32,16,16]{2,1,0:T(8,128)S(1)}, f32[32,16,16]{2,1,0:T(8,128)S(1)}, u32[]{:S(2)}, u32[]{:S(2)}) collective-permute-start(f32[32,16,16]{2,1,0:T(8,128)S(1)} %convolution_add_fusion.3), channel_id=1, source_target_pairs={{0,8},{8,16},{16,24},{24,32},{32,40},{40,48},{48,56},{56,64},{64,7... | collective-permute-start | bytes 98312 | tf_op jit(solution)/shard_map/ppermute | solution.py:60
  120.3 7.5 %collective-permute-start.2 = (f32[32,16,16]{2,1,0:T(8,128)S(1)}, f32[32,16,16]{2,1,0:T(8,128)S(1)}, u32[]{:S(2)}, u32[]{:S(2)}) collective-permute-start(f32[32,16,16]{2,1,0:T(8,128)S(1)} %multiply_add_fusion.9), channel_id=1, source_target_pairs={{0,16},{8,24},{16,32},{24,40},{32,48},{40,56},{48,64},{56,72},{64,... | collective-permute-start | bytes 98312 | tf_op jit(solution)/shard_map/ppermute | solution.py:60
  127.9 8.6 %collective-permute-start.3 = (f32[32,16,16]{2,1,0:T(8,128)S(1)}, f32[32,16,16]{2,1,0:T(8,128)S(1)}, u32[]{:S(2)}, u32[]{:S(2)}) collective-permute-start(f32[32,16,16]{2,1,0:T(8,128)S(1)} %multiply_add_fusion.8), channel_id=1, source_target_pairs={{0,32},{8,40},{16,48},{24,56},{32,64},{40,72},{48,80},{56,88},{64,... | collective-permute-start | bytes 98312 | tf_op jit(solution)/shard_map/ppermute | solution.py:60
  136.7 10.8 %collective-permute-start.4 = (f32[32,16,16]{2,1,0:T(8,128)S(1)}, f32[32,16,16]{2,1,0:T(8,128)S(1)}, u32[]{:S(2)}, u32[]{:S(2)}) collective-permute-start(f32[32,16,16]{2,1,0:T(8,128)S(1)} %multiply_add_fusion.7), channel_id=1, source_target_pairs={{0,64},{8,72},{16,80},{24,88},{32,96},{40,104},{48,112},{56,120},{... | collective-permute-start | bytes 98312 | tf_op jit(solution)/shard_map/ppermute | solution.py:60
  147.6 13.5 %collective-permute-start.5 = (f32[32,16,16]{2,1,0:T(8,128)S(1)}, f32[32,16,16]{2,1,0:T(8,128)S(1)}, u32[]{:S(2)}, u32[]{:S(2)}) collective-permute-start(f32[32,16,16]{2,1,0:T(8,128)S(1)} %multiply_add_fusion.6), channel_id=1, source_target_pairs={{0,128},{8,136},{16,144},{24,152},{32,160},{40,168},{48,176},{56,1... | collective-permute-start | bytes 98312 | tf_op jit(solution)/shard_map/ppermute | solution.py:60
  161.3 11.2 %collective-permute-start.6 = (f32[32,16,16]{2,1,0:T(8,128)S(1)}, f32[32,16,16]{2,1,0:T(8,128)S(1)}, u32[]{:S(2)}, u32[]{:S(2)}) collective-permute-start(f32[32,16,16]{2,1,0:T(8,128)S(1)} %multiply_add_fusion.5), channel_id=1, source_target_pairs={{0,256},{8,264},{16,272},{24,280},{32,288},{40,296},{48,304},{56,3... | collective-permute-start | bytes 98312 | tf_op jit(solution)/shard_map/ppermute | solution.py:60
  173.8 35.6 %copy-start.46 = (f32[1,1,512]{2,1,0:T(1,128)S(1)}, f32[1,1,512]{2,1,0:T(1,128)}, u32[]{:S(2)}) copy-start(f32[1,1,512]{2,1,0:T(1,128)} %copy-done.45) | copy-start | bytes 6148
  173.8 35.6 %copy-start.48 = (f32[1,1,512]{2,1,0:T(1,128)S(1)}, f32[1,1,512]{2,1,0:T(1,128)}, u32[]{:S(2)}) copy-start(f32[1,1,512]{2,1,0:T(1,128)} %copy-done.47) | copy-start | bytes 6148
  173.8 35.6 %copy-start.50 = (f32[1,1,512]{2,1,0:T(1,128)S(1)}, f32[1,1,512]{2,1,0:T(1,128)}, u32[]{:S(2)}) copy-start(f32[1,1,512]{2,1,0:T(1,128)} %copy-done.49) | copy-start | bytes 6148
  173.8 35.6 %copy-start.52 = (f32[1,1,512]{2,1,0:T(1,128)S(1)}, f32[1,1,512]{2,1,0:T(1,128)}, u32[]{:S(2)}) copy-start(f32[1,1,512]{2,1,0:T(1,128)} %copy-done.51) | copy-start | bytes 6148
  173.8 35.6 %copy-start.53 = (f32[1,1,512]{2,1,0:T(1,128)S(1)}, f32[1,1,512]{2,1,0:T(1,128)}, u32[]{:S(2)}) copy-start(f32[1,1,512]{2,1,0:T(1,128)} %get-tuple-element.45) | copy-start | bytes 6148
  173.8 35.6 %copy-start.54 = (f32[1,1,512]{2,1,0:T(1,128)S(1)}, f32[1,1,512]{2,1,0:T(1,128)}, u32[]{:S(2)}) copy-start(f32[1,1,512]{2,1,0:T(1,128)} %get-tuple-element.46) | copy-start | bytes 6148
  173.8 35.6 %copy-start.55 = (f32[1,1,512]{2,1,0:T(1,128)S(1)}, f32[1,1,512]{2,1,0:T(1,128)}, u32[]{:S(2)}) copy-start(f32[1,1,512]{2,1,0:T(1,128)} %get-tuple-element.47) | copy-start | bytes 6148
  173.9 37.6 %copy-start.32 = (f32[1,1,512]{2,1,0:T(1,128)S(1)}, f32[1,1,512]{2,1,0:T(1,128)}, u32[]{:S(2)}) copy-start(f32[1,1,512]{2,1,0:T(1,128)} %get-tuple-element.35) | copy-start | bytes 6148
  173.9 37.6 %copy-start.34 = (f32[1,1,512]{2,1,0:T(1,128)S(1)}, f32[1,1,512]{2,1,0:T(1,128)}, u32[]{:S(2)}) copy-start(f32[1,1,512]{2,1,0:T(1,128)} %get-tuple-element.36) | copy-start | bytes 6148
  173.9 37.6 %copy-start.36 = (f32[1,1,512]{2,1,0:T(1,128)S(1)}, f32[1,1,512]{2,1,0:T(1,128)}, u32[]{:S(2)}) copy-start(f32[1,1,512]{2,1,0:T(1,128)} %get-tuple-element.37) | copy-start | bytes 6148
  173.9 37.6 %copy-start.38 = (f32[1,1,512]{2,1,0:T(1,128)S(1)}, f32[1,1,512]{2,1,0:T(1,128)}, u32[]{:S(2)}) copy-start(f32[1,1,512]{2,1,0:T(1,128)} %get-tuple-element.38) | copy-start | bytes 6148
  174.0 37.6 %copy-start.40 = (f32[1,1,512]{2,1,0:T(1,128)S(1)}, f32[1,1,512]{2,1,0:T(1,128)}, u32[]{:S(2)}) copy-start(f32[1,1,512]{2,1,0:T(1,128)} %get-tuple-element.39) | copy-start | bytes 6148
  174.0 37.6 %copy-start.42 = (f32[1,1,512]{2,1,0:T(1,128)S(1)}, f32[1,1,512]{2,1,0:T(1,128)}, u32[]{:S(2)}) copy-start(f32[1,1,512]{2,1,0:T(1,128)} %get-tuple-element.40) | copy-start | bytes 6148
  174.0 37.6 %copy-start.44 = (f32[1,1,512]{2,1,0:T(1,128)S(1)}, f32[1,1,512]{2,1,0:T(1,128)}, u32[]{:S(2)}) copy-start(f32[1,1,512]{2,1,0:T(1,128)} %get-tuple-element.41) | copy-start | bytes 6148
  174.1 35.2 %collective-permute-start.13 = (bf16[3,6,512]{1,2,0:T(8,128)(2,1)S(1)}, bf16[3,6,512]{1,2,0:T(8,128)(2,1)S(1)}, u32[]{:S(2)}, u32[]{:S(2)}) collective-permute-start(bf16[3,6,512]{1,2,0:T(8,128)(2,1)S(1)} %pad_maximum_fusion), channel_id=1, source_target_pairs={{8,0},{16,8},{24,16},{32,24},{40,32},{48,40},{56,48},{64,56},{72,6... | collective-permute-start | bytes 55304 | tf_op jit(solution)/shard_map/ppermute | solution.py:16
  194.8 19.0 %copy-start.22 = (f32[1,1,512]{2,1,0:T(1,128)S(1)}, f32[1,1,512]{2,1,0:T(1,128)}, u32[]{:S(2)}) copy-start(f32[1,1,512]{2,1,0:T(1,128)} %get-tuple-element.30) | copy-start | bytes 6148
  194.8 18.9 %copy-start.24 = (f32[1,1,512]{2,1,0:T(1,128)S(1)}, f32[1,1,512]{2,1,0:T(1,128)}, u32[]{:S(2)}) copy-start(f32[1,1,512]{2,1,0:T(1,128)} %get-tuple-element.31) | copy-start | bytes 6148
  194.8 18.9 %copy-start.26 = (f32[1,1,512]{2,1,0:T(1,128)S(1)}, f32[1,1,512]{2,1,0:T(1,128)}, u32[]{:S(2)}) copy-start(f32[1,1,512]{2,1,0:T(1,128)} %get-tuple-element.32) | copy-start | bytes 6148
  194.8 18.9 %copy-start.28 = (f32[1,1,512]{2,1,0:T(1,128)S(1)}, f32[1,1,512]{2,1,0:T(1,128)}, u32[]{:S(2)}) copy-start(f32[1,1,512]{2,1,0:T(1,128)} %get-tuple-element.33) | copy-start | bytes 6148
  194.8 18.9 %copy-start.30 = (f32[1,1,512]{2,1,0:T(1,128)S(1)}, f32[1,1,512]{2,1,0:T(1,128)}, u32[]{:S(2)}) copy-start(f32[1,1,512]{2,1,0:T(1,128)} %get-tuple-element.34) | copy-start | bytes 6148
  194.8 18.9 %copy-start.57 = (f32[1,1,512]{2,1,0:T(1,128)S(1)}, f32[1,1,512]{2,1,0:T(1,128)}, u32[]{:S(2)}) copy-start(f32[1,1,512]{2,1,0:T(1,128)} %get-tuple-element.48) | copy-start | bytes 6148
  194.8 18.9 %copy-start.59 = (f32[1,1,512]{2,1,0:T(1,128)S(1)}, f32[1,1,512]{2,1,0:T(1,128)}, u32[]{:S(2)}) copy-start(f32[1,1,512]{2,1,0:T(1,128)} %get-tuple-element.49) | copy-start | bytes 6148
  (10 other events, 61.3 us)

commit v2 on v1

--- a/solution.py
+++ b/solution.py
@@ -1,10 +1,13 @@
+import math
+
 import jax
 import jax.numpy as jnp
 from jax import lax
-from jax.sharding import PartitionSpec as P
+from jax.sharding import Mesh, PartitionSpec as P
 
 GROUP = 16
 SHORT = 7
+INNER = 8
 
 
 precise = lax.Precision.HIGHEST
@@ -41,31 +44,33 @@
 
 
 def split_dot(spec, table, values):
-    high = table.astype(jnp.bfloat16)
-    low = (table - high.astype(jnp.float32)).astype(jnp.bfloat16)
-    lhs = jnp.einsum(spec, high, values, preferred_element_type=jnp.float32)
+    high = lax.reduce_precision(table, exponent_bits=8, mantissa_bits=7)
+    low = (table - high).astype(jnp.bfloat16)
+    lhs = jnp.einsum(spec, high.astype(jnp.bfloat16), values, preferred_element_type=jnp.float32)
     return lhs + jnp.einsum(spec, low, values, preferred_element_type=jnp.float32)
 
 
-def modal_scan(local_state, decay_step, axis, forward):
-    count = lax.axis_size(axis)
-    entering = jnp.zeros_like(local_state)
-    window = local_state
+def cube_scan(tot_fwd, tot_bwd, unit_decay, axis, size, index):
+    pre_fwd = jnp.zeros_like(tot_fwd)
+    pre_bwd = jnp.zeros_like(tot_bwd)
     shift = 1
-    while shift < count:
-        if forward:
-            pairs = [(source, source + shift) for source in range(count - shift)]
-        else:
-            pairs = [(source, source - shift) for source in range(shift, count)]
-        arrived = lax.ppermute(window, axis, pairs)
-        entering = entering + jnp.exp(-decay_step * (shift - 1)) * arrived
-        if shift * 2 < count:
-            window = window + jnp.exp(-decay_step * shift) * arrived
+    while shift < size:
+        pairs = [(source, source ^ shift) for source in range(size)]
+        got = lax.ppermute(jnp.stack([tot_fwd, tot_bwd]), axis, pairs)
+        upper = (index & shift) != 0
+        offset = (index % shift).astype(jnp.float32)
+        span = jnp.exp(-unit_decay * shift)
+        pre_fwd = jnp.where(upper, pre_fwd + jnp.exp(-unit_decay * offset) * got[0], pre_fwd)
+        pre_bwd = jnp.where(
+            upper, pre_bwd, pre_bwd + jnp.exp(-unit_decay * (shift - 1 - offset)) * got[1]
+        )
+        tot_fwd = jnp.where(upper, span * got[0] + tot_fwd, span * tot_fwd + got[0])
+        tot_bwd = jnp.where(upper, got[1] + span * tot_bwd, tot_bwd + span * got[1])
         shift *= 2
-    return entering
+    return pre_fwd, tot_fwd, pre_bwd, tot_bwd
 
 
-def shards(u_query, u_key, u_value, short_filter, decay_rate, residue, grad_out):
+def shards(inner, u_query, u_key, u_value, short_filter, decay_rate, residue, grad_out):
     block_len, channels = u_query.shape
     group_count = channels // GROUP
     rim_rows = jnp.stack(
@@ -75,7 +80,7 @@
             u_value[block_len - SHORT + 1 :],
         ]
     )
-    before = from_behind(rim_rows, "ctx", 1)
+    before = from_behind(rim_rows, ("zl", "xc"), 1)
     q_short = rounded(short_causal(before[0], u_query, short_filter[0]))
     k_short = rounded(short_causal(before[1], u_key, short_filter[1]))
     v_short = rounded(short_causal(before[2], u_value, short_filter[2]))
@@ -98,8 +103,16 @@
     end_state = split_dot("gms,sgc->gmc", powers[:, :, block_len - 1 :: -1], signal)
     start_state = split_dot("gms,sgc->gmc", powers[:, :, :block_len], cotangent)
     decay_step = (rates * block_len)[:, :, None]
-    entering = modal_scan(end_state, decay_step, "ctx", True)
-    leaving = modal_scan(start_state, decay_step, "ctx", False)
+    member = lax.axis_index("xc")
+    pre_fwd, group_fwd, pre_bwd, group_bwd = cube_scan(
+        end_state, start_state, decay_step, "xc", inner, member
+    )
+    outer_fwd, _, outer_bwd, _ = cube_scan(
+        group_fwd, group_bwd, decay_step * inner, "zl", lax.axis_size("zl"), lax.axis_index("zl")
+    )
+    place = member.astype(jnp.float32)
+    entering = pre_fwd + jnp.exp(-decay_step * place) * outer_fwd
+    leaving = pre_bwd + jnp.exp(-decay_step * (inner - 1 - place)) * outer_bwd
 
     local_conv = split_dot("gts,sgc->tgc", toeplitz, signal)
     local_grad = split_dot("gts,tgc->sgc", toeplitz, cotangent)
@@ -117,7 +130,7 @@
     head_rows = jnp.stack(
         [grad_qshort[: SHORT - 1], grad_kshort[: SHORT - 1], grad_vshort[: SHORT - 1]]
     )
-    next_rows = from_behind(head_rows, "ctx", -1)
+    next_rows = from_behind(head_rows, ("zl", "xc"), -1)
     grad_query = short_reverse(grad_qshort, next_rows[0], short_filter[0]).astype(jnp.bfloat16)
     grad_key = short_reverse(grad_kshort, next_rows[1], short_filter[1]).astype(jnp.bfloat16)
     grad_value = short_reverse(grad_vshort, next_rows[2], short_filter[2]).astype(jnp.bfloat16)
@@ -125,18 +138,16 @@
 
 
 def solution(mesh):
+    ctx_count = mesh.shape["ctx"]
+    inner = math.gcd(INNER, ctx_count)
+    grid = Mesh(
+        mesh.devices.reshape(ctx_count // inner, inner, mesh.shape["tp"]), ("zl", "xc", "tp")
+    )
+    rows = P(("zl", "xc"), "tp")
     return jax.shard_map(
-        shards,
-        mesh=mesh,
-        in_specs=(
-            P("ctx", "tp"),
-            P("ctx", "tp"),
-            P("ctx", "tp"),
-            P(None, None, "tp"),
-            P("tp", None),
-            P("tp", None),
-            P("ctx", "tp"),
-        ),
-        out_specs=(P("ctx", "tp"), P("ctx", "tp"), P("ctx", "tp"), P("ctx", "tp")),
+        lambda *arrays: shards(inner, *arrays),
+        mesh=grid,
+        in_specs=(rows, rows, rows, P(None, None, "tp"), P("tp", None), P("tp", None), rows),
+        out_specs=(rows, rows, rows, rows),
         check_vma=False,
     )

time: 217 us -> 206 us (0.949)
  the two profiles are of different devices: /device:TPU:407 before, /device:TPU:1 now
where the time goes in v2:
time: 206 us; the launch traced here: 204 us
  waiting for transfers between devices  113 us (55%)
  local copies, waits for them, and re-layouts  35.2 us (17%)
  starting transfers between devices  28.3 us (14%)
  other arithmetic  14.7 us (7%)
  matrix products  11 us (5%)
  between operations  2.11 us (1%)
    ppermute x6, waiting for transfers between devices, cube_scan(): got = lax.ppermute(jnp.stack([tot_fwd, tot_bwd]), axis, pairs)  108 us
    ppermute x6, starting transfers between devices, cube_scan(): got = lax.ppermute(jnp.stack([tot_fwd, tot_bwd]), axis, pairs)  21.3 us
    exp x6, local copies, waits for them, and re-layouts, cube_scan(): jnp.exp(-unit_decay * offset) * got[0]  8.22 us
    ppermute x2, starting transfers between devices, from_behind(): lax.ppermute(value, axis, [(source, source + steps) for source in range(l...  6.98 us
    exp x5, local copies, waits for them, and re-layouts, cube_scan(): span = jnp.exp(-unit_decay * shift)  6.25 us
    ppermute x2, waiting for transfers between devices, from_behind(): lax.ppermute(value, axis, [(source, source + steps) for source in range(l...  5.69 us
    exp x4, local copies, waits for them, and re-layouts, cube_scan(): jnp.exp(-unit_decay * (shift - 1 - offset)) * got[1]  5.47 us
    unnamed x157, local copies, waits for them, and re-layouts  5.16 us
  transfers between devices with their start and end apart: 8, of which 6 were waited for; matrix products, arithmetic and copies ran while one was open for 18% of the time, Pallas kernels for 0%

profile of v2, /device:TPU:1, one launch (start us, length us, event | category | flops | bytes accessed | tf_op | source)
XLA Modules:
  0.0 204.4 jit_solution(10353968602678728607)
XLA Ops:
  0.7 0.8 slice_bitcast_fusion.33
  1.5 0.7 slice_bitcast_fusion.31
  2.2 0.3 copy.118
  2.5 4.5 %collective-permute-start = (bf16[3,6,512]{1,2,0:T(8,128)(2,1)S(1)}, bf16[3,6,512]{1,2,0:T(8,128)(2,1)S(1)}, u32[]{:S(2)}, u32[]{:S(2)}) collective-permute-start(bf16[3,6,512]{1,2,0:T(8,128)(2,1)S(1)} %copy.118), channel_id=1, source_target_pairs={{0,8},{8,16},{16,24},{24,32},{32,40},{40,48},{48,56},{56,64},{64,7... | collective-permute-start | bytes 55304 | tf_op jit(solution)/shard_map/ppermute | solution.py:19
  7.0 1.2 fusion.219
  8.4 0.8 fusion.220
  9.2 1.5 multiply_exponential_fusion.5
  10.9 0.9 fusion.218
  11.8 0.6 convert_add_fusion
  13.2 0.7 copy.121
  14.0 1.3 fusion.110
  15.3 0.6 copy-done
  16.5 1.3 fusion.93
  17.8 1.3 fusion.76
  19.2 0.6 copy-done.4
  20.2 0.8 pad_maximum_fusion
  21.0 5.6 %collective-permute-start.1 = (f32[2,32,16,16]{3,2,1,0:T(8,128)}, f32[2,32,16,16]{3,2,1,0:T(8,128)}, u32[]{:S(2)}, u32[]{:S(2)}) collective-permute-start(f32[2,32,16,16]{3,2,1,0:T(8,128)} %pad_maximum_fusion), channel_id=1, source_target_pairs={{0,8},{8,0},{16,24},{24,16},{32,40},{40,32},{48,56},{56,48},{1,9},... | collective-permute-start | bytes 196616 | tf_op jit(solution)/shard_map/ppermute | solution.py:59
  26.6 3.7 %fusion.149 = f32[32,128,128]{2,1,0:T(8,128)S(1)} fusion(f32[32,16]{1,0:T(8,128)S(1)} %copy.122, f32[128]{0:T(128)S(1)} %copy-done.72, f32[128]{0:T(128)S(1)} %copy-done.73, f32[32,16]{1,0:T(8,128)S(1)} %copy-done.12), kind=kOutput, calls=%fused_computation.265 | convolution fusion | flops 100859904 | bytes 2102272 | tf_op jit(solution)/shard_map/gtm,gms->gts/dot_general | solution.py:97
  30.3 1.4 copy.128
  31.7 1.4 copy.130
  33.0 0.8 copy.133
  33.8 1.4 copy.135
  35.2 1.4 copy.137
  36.6 1.8 rev.7
  38.4 1.4 copy.124
  39.7 1.4 copy.132
  41.1 1.4 copy.140
  42.5 1.4 copy.141
  43.8 1.4 copy.142
  45.2 1.4 copy.143
  46.6 1.4 copy.144
  47.9 1.4 copy.127
  49.3 1.4 copy.129
  50.7 1.4 copy.131
  52.1 1.4 copy.134
  53.4 1.4 copy.136
  54.8 1.2 fusion.202
  56.1 1.9 collective-permute-start.2
  58.0 13.5 %collective-permute-done.2 = f32[2,32,16,16]{3,2,1,0:T(8,128)S(1)} collective-permute-done((f32[2,32,16,16]{3,2,1,0:T(8,128)S(1)}, f32[2,32,16,16]{3,2,1,0:T(8,128)S(1)}, u32[]{:S(2)}, u32[]{:S(2)}) %collective-permute-start.2) | collective-permute-done | bytes 65568 | tf_op jit(solution)/shard_map/ppermute | solution.py:59
  71.5 1.3 add_select_fusion.13
  72.8 1.9 collective-permute-start.3
  74.8 0.4 fusion.3
  75.1 13.8 %collective-permute-done.3 = f32[2,32,16,16]{3,2,1,0:T(8,128)S(1)} collective-permute-done((f32[2,32,16,16]{3,2,1,0:T(8,128)S(1)}, f32[2,32,16,16]{3,2,1,0:T(8,128)S(1)}, u32[]{:S(2)}, u32[]{:S(2)}) %collective-permute-start.3) | collective-permute-done | bytes 65568 | tf_op jit(solution)/shard_map/ppermute | solution.py:59
  89.1 1.9 collective-permute-start.4
  91.0 0.4 convolution_add_fusion.4
  91.4 11.3 %collective-permute-done.4 = f32[2,32,16,16]{3,2,1,0:T(8,128)S(1)} collective-permute-done((f32[2,32,16,16]{3,2,1,0:T(8,128)S(1)}, f32[2,32,16,16]{3,2,1,0:T(8,128)S(1)}, u32[]{:S(2)}, u32[]{:S(2)}) %collective-permute-start.4) | collective-permute-done | bytes 65568 | tf_op jit(solution)/shard_map/ppermute | solution.py:59
  102.7 0.2 add_select_fusion.9
  103.0 2.9 %collective-permute-start.5 = (f32[2,32,16,16]{3,2,1,0:T(8,128)S(1)}, f32[2,32,16,16]{3,2,1,0:T(8,128)S(1)}, u32[]{:S(2)}, u32[]{:S(2)}) collective-permute-start(f32[2,32,16,16]{3,2,1,0:T(8,128)S(1)} %pad_maximum_fusion.4), channel_id=1, source_target_pairs={{0,128},{64,192},{128,0},{192,64},{256,384},{320,448},{384,256},{4... | collective-permute-start | bytes 196616 | tf_op jit(solution)/shard_map/ppermute | solution.py:59
  105.9 0.6 fusion.4
  106.6 24.3 %collective-permute-done.5 = f32[2,32,16,16]{3,2,1,0:T(8,128)S(1)} collective-permute-done((f32[2,32,16,16]{3,2,1,0:T(8,128)S(1)}, f32[2,32,16,16]{3,2,1,0:T(8,128)S(1)}, u32[]{:S(2)}, u32[]{:S(2)}) %collective-permute-start.5) | collective-permute-done | bytes 65568 | tf_op jit(solution)/shard_map/ppermute | solution.py:59
  131.2 7.1 %collective-permute-start.6 = (f32[2,32,16,16]{3,2,1,0:T(8,128)S(1)}, f32[2,32,16,16]{3,2,1,0:T(8,128)S(1)}, u32[]{:S(2)}, u32[]{:S(2)}) collective-permute-start(f32[2,32,16,16]{3,2,1,0:T(8,128)S(1)} %pad_maximum_fusion.5), channel_id=1, source_target_pairs={{0,256},{64,320},{128,384},{192,448},{256,0},{320,64},{384,128},{4... | collective-permute-start | bytes 196616 | tf_op jit(solution)/shard_map/ppermute | solution.py:59
  138.4 0.7 convolution_add_fusion.5
  139.1 44.6 %collective-permute-done.6 = f32[2,32,16,16]{3,2,1,0:T(8,128)S(1)} collective-permute-done((f32[2,32,16,16]{3,2,1,0:T(8,128)S(1)}, f32[2,32,16,16]{3,2,1,0:T(8,128)S(1)}, u32[]{:S(2)}, u32[]{:S(2)}) %collective-permute-start.6) | collective-permute-done | bytes 65568 | tf_op jit(solution)/shard_map/ppermute | solution.py:59
  183.8 2.2 %fusion.2 = bf16[32,16,128]{2,1,0:T(8,128)(2,1)S(1)} fusion(f32[32,16,128]{2,1,0:T(8,128)S(1)} %convolution_add_fusion.4, f32[2,32,16,16]{3,2,1,0:T(8,128)S(1)} %collective-permute-done.6, f32[32,16,128]{2,1,0:T(8,128)S(1)} %copy-done.6, f32[2,32,16,16]{3,2,1,0:T(8,128)} %collective-permute-done.1, f32[2,32,16,16]{3,2,1,0:T(8,128)S(1)} %collective-permute-done.2, ...), kind=kOutput, calls=%fused_computation.10 | convolution fusion | flops 12926976 | bytes 2359302 | tf_op jit(solution)/shard_map/gsm,gmc->sgc/dot_general | solution.py:122
  186.2 2.2 %fusion.1 = bf16[32,16,128]{2,1,0:T(8,128)(2,1)S(1)} fusion(f32[32,16,128]{2,1,0:T(8,128)S(1)} %convolution_add_fusion.5, f32[2,32,16,16]{3,2,1,0:T(8,128)S(1)} %collective-permute-done.6, f32[2,32,16,16]{3,2,1,0:T(8,128)} %collective-permute-done.1, f32[2,32,16,16]{3,2,1,0:T(8,128)S(1)} %collective-permute-done.2, ...), kind=kOutput, calls=%fused_computation.9 | convolution fusion | flops 12926976 | bytes 2359302 | tf_op jit(solution)/shard_map/gtm,gmc->tgc/dot_general | solution.py:121
  188.8 2.5 %collective-permute-start.7 = (bf16[3,6,512]{1,2,0:T(8,128)(2,1)S(1)}, bf16[3,6,512]{1,2,0:T(8,128)(2,1)S(1)}, u32[]{:S(2)}, u32[]{:S(2)}) collective-permute-start(bf16[3,6,512]{1,2,0:T(8,128)(2,1)S(1)} %pad_maximum_fusion.6), channel_id=1, source_target_pairs={{8,0},{16,8},{24,16},{32,24},{40,32},{48,40},{56,48},{64,56},{72,6... | collective-permute-start | bytes 55304 | tf_op jit(solution)/shard_map/ppermute | solution.py:19
  191.4 0.8 copy.146
  192.2 5.7 %collective-permute-done.7 = bf16[3,6,512]{1,2,0:T(8,128)(2,1)S(1)} collective-permute-done((bf16[3,6,512]{1,2,0:T(8,128)(2,1)S(1)}, bf16[3,6,512]{1,2,0:T(8,128)(2,1)S(1)}, u32[]{:S(2)}, u32[]{:S(2)}) %collective-permute-start.7) | collective-permute-done | bytes 18464 | tf_op jit(solution)/shard_map/ppermute | solution.py:19
  198.0 1.4 fusion.25
  199.3 0.8 copy.149
  200.1 1.4 fusion.42
  201.5 0.8 copy.148
  202.3 1.4 fusion.59
  203.7 0.8 copy.147
  (186 shorter events, 3.1 us)
Async XLA Ops:
  0.6 11.7 %copy-start.7 = (bf16[128,512]{1,0:T(8,128)(2,1)S(1)}, bf16[128,512]{1,0:T(8,128)(2,1)}, u32[]{:S(2)}) copy-start(bf16[128,512]{1,0:T(8,128)(2,1)} %param.7) | copy-start | bytes 393220
  0.6 11.8 %copy-start.8 = (bf16[128,512]{1,0:T(8,128)(2,1)S(1)}, bf16[128,512]{1,0:T(8,128)(2,1)}, u32[]{:S(2)}) copy-start(bf16[128,512]{1,0:T(8,128)(2,1)} %param.8) | copy-start | bytes 393220
  0.7 12.0 %copy-start.9 = (bf16[128,512]{1,0:T(8,128)(2,1)S(1)}, bf16[128,512]{1,0:T(8,128)(2,1)}, u32[]{:S(2)}) copy-start(bf16[128,512]{1,0:T(8,128)(2,1)} %param.9) | copy-start | bytes 393220
  0.7 12.1 %copy-start.17 = (f32[32,16]{0,1:T(8,128)S(1)}, f32[32,16]{0,1:T(8,128)}, u32[]{:S(2)}) copy-start(f32[32,16]{0,1:T(8,128)} %param.11) | copy-start | bytes 6148
  0.7 12.2 %copy-start.11 = (bf16[128,512]{1,0:T(8,128)(2,1)S(1)}, bf16[128,512]{1,0:T(8,128)(2,1)}, u32[]{:S(2)}) copy-start(bf16[128,512]{1,0:T(8,128)(2,1)} %param.13) | copy-start | bytes 393220
  2.5 11.4 %collective-permute-start = (bf16[3,6,512]{1,2,0:T(8,128)(2,1)S(1)}, bf16[3,6,512]{1,2,0:T(8,128)(2,1)S(1)}, u32[]{:S(2)}, u32[]{:S(2)}) collective-permute-start(bf16[3,6,512]{1,2,0:T(8,128)(2,1)S(1)} %copy.118), channel_id=1, source_target_pairs={{0,8},{8,16},{16,24},{24,32},{32,40},{40,48},{48,56},{56,64},{64,7... | collective-permute-start | bytes 55304 | tf_op jit(solution)/shard_map/ppermute | solution.py:19
  8.3 9.4 %copy-start.46 = (f32[1,1,512]{2,1,0:T(1,128)}, f32[1,1,512]{2,1,0:T(1,128)S(1)}, u32[]{:S(2)}) copy-start(f32[1,1,512]{2,1,0:T(1,128)S(1)} %get-tuple-element.39) | copy-start | bytes 6148
  8.3 9.4 %copy-start.48 = (f32[1,1,512]{2,1,0:T(1,128)}, f32[1,1,512]{2,1,0:T(1,128)S(1)}, u32[]{:S(2)}) copy-start(f32[1,1,512]{2,1,0:T(1,128)S(1)} %get-tuple-element.40) | copy-start | bytes 6148
  8.3 9.4 %copy-start.50 = (f32[1,1,512]{2,1,0:T(1,128)}, f32[1,1,512]{2,1,0:T(1,128)S(1)}, u32[]{:S(2)}) copy-start(f32[1,1,512]{2,1,0:T(1,128)S(1)} %get-tuple-element.41) | copy-start | bytes 6148
  8.4 9.4 %copy-start.52 = (f32[1,1,512]{2,1,0:T(1,128)}, f32[1,1,512]{2,1,0:T(1,128)S(1)}, u32[]{:S(2)}) copy-start(f32[1,1,512]{2,1,0:T(1,128)S(1)} %get-tuple-element.42) | copy-start | bytes 6148
  8.4 9.4 %copy-start.54 = (f32[1,1,512]{2,1,0:T(1,128)}, f32[1,1,512]{2,1,0:T(1,128)S(1)}, u32[]{:S(2)}) copy-start(f32[1,1,512]{2,1,0:T(1,128)S(1)} %get-tuple-element.43) | copy-start | bytes 6148
  9.2 8.6 %copy-start.56 = (f32[1,1,512]{2,1,0:T(1,128)}, f32[1,1,512]{2,1,0:T(1,128)S(1)}, u32[]{:S(2)}) copy-start(f32[1,1,512]{2,1,0:T(1,128)S(1)} %get-tuple-element.57) | copy-start | bytes 6148
  9.2 8.6 %copy-start.58 = (f32[1,1,512]{2,1,0:T(1,128)}, f32[1,1,512]{2,1,0:T(1,128)S(1)}, u32[]{:S(2)}) copy-start(f32[1,1,512]{2,1,0:T(1,128)S(1)} %get-tuple-element.58) | copy-start | bytes 6148
  16.4 10.2 %copy-start.12 = (f32[32,16]{1,0:T(8,128)S(1)}, f32[32,16]{1,0:T(8,128)}, u32[]{:S(2)}) copy-start(f32[32,16]{1,0:T(8,128)} %copy.121) | copy-start | bytes 6148
  16.4 10.2 %copy-start.72 = (f32[128]{0:T(128)S(1)}, f32[128]{0:T(128)}, u32[]{:S(2)}) copy-start(f32[128]{0:T(128)} %get-tuple-element.80) | copy-start | bytes 1540
  16.4 10.2 %copy-start.73 = (f32[128]{0:T(128)S(1)}, f32[128]{0:T(128)}, u32[]{:S(2)}) copy-start(f32[128]{0:T(128)} %get-tuple-element.81) | copy-start | bytes 1540
  21.0 33.8 %collective-permute-start.1 = (f32[2,32,16,16]{3,2,1,0:T(8,128)}, f32[2,32,16,16]{3,2,1,0:T(8,128)}, u32[]{:S(2)}, u32[]{:S(2)}) collective-permute-start(f32[2,32,16,16]{3,2,1,0:T(8,128)} %pad_maximum_fusion), channel_id=1, source_target_pairs={{0,8},{8,0},{16,24},{24,16},{32,40},{40,32},{48,56},{56,48},{1,9},... | collective-permute-start | bytes 196616 | tf_op jit(solution)/shard_map/ppermute | solution.py:59
  54.8 16.7 %copy-start.10 = (f32[32,16]{1,0:T(8,128)S(1)}, f32[32,16]{1,0:T(8,128)}, u32[]{:S(2)}) copy-start(f32[32,16]{1,0:T(8,128)} %copy.128) | copy-start | bytes 6148
  54.8 16.7 %copy-start.16 = (f32[32,16]{1,0:T(8,128)S(1)}, f32[32,16]{1,0:T(8,128)}, u32[]{:S(2)}) copy-start(f32[32,16]{1,0:T(8,128)} %copy.130) | copy-start | bytes 6148
  56.1 15.4 %collective-permute-start.2 = (f32[2,32,16,16]{3,2,1,0:T(8,128)S(1)}, f32[2,32,16,16]{3,2,1,0:T(8,128)S(1)}, u32[]{:S(2)}, u32[]{:S(2)}) collective-permute-start(f32[2,32,16,16]{3,2,1,0:T(8,128)S(1)} %pad_maximum_fusion.1), channel_id=1, source_target_pairs={{0,16},{8,24},{16,0},{24,8},{32,48},{40,56},{48,32},{56,40},{1,17}... | collective-permute-start | bytes 196616 | tf_op jit(solution)/shard_map/ppermute | solution.py:59
  72.8 16.1 %collective-permute-start.3 = (f32[2,32,16,16]{3,2,1,0:T(8,128)S(1)}, f32[2,32,16,16]{3,2,1,0:T(8,128)S(1)}, u32[]{:S(2)}, u32[]{:S(2)}) collective-permute-start(f32[2,32,16,16]{3,2,1,0:T(8,128)S(1)} %pad_maximum_fusion.2), channel_id=1, source_target_pairs={{0,32},{8,40},{16,48},{24,56},{32,0},{40,8},{48,16},{56,24},{1,33}... | collective-permute-start | bytes 196616 | tf_op jit(solution)/shard_map/ppermute | solution.py:59
  89.1 13.7 %copy-start.15 = (f32[32,16]{1,0:T(8,128)S(1)}, f32[32,16]{1,0:T(8,128)}, u32[]{:S(2)}) copy-start(f32[32,16]{1,0:T(8,128)} %copy.135) | copy-start | bytes 6148
  89.1 13.6 %collective-permute-start.4 = (f32[2,32,16,16]{3,2,1,0:T(8,128)S(1)}, f32[2,32,16,16]{3,2,1,0:T(8,128)S(1)}, u32[]{:S(2)}, u32[]{:S(2)}) collective-permute-start(f32[2,32,16,16]{3,2,1,0:T(8,128)S(1)} %pad_maximum_fusion.3), channel_id=1, source_target_pairs={{0,64},{64,0},{128,192},{192,128},{256,320},{320,256},{384,448},{4... | collective-permute-start | bytes 196616 | tf_op jit(solution)/shard_map/ppermute | solution.py:59
  103.0 27.9 %copy-start.14 = (f32[32,16]{1,0:T(8,128)S(1)}, f32[32,16]{1,0:T(8,128)}, u32[]{:S(2)}) copy-start(f32[32,16]{1,0:T(8,128)} %copy.137) | copy-start | bytes 6148
  103.0 27.9 %collective-permute-start.5 = (f32[2,32,16,16]{3,2,1,0:T(8,128)S(1)}, f32[2,32,16,16]{3,2,1,0:T(8,128)S(1)}, u32[]{:S(2)}, u32[]{:S(2)}) collective-permute-start(f32[2,32,16,16]{3,2,1,0:T(8,128)S(1)} %pad_maximum_fusion.4), channel_id=1, source_target_pairs={{0,128},{64,192},{128,0},{192,64},{256,384},{320,448},{384,256},{4... | collective-permute-start | bytes 196616 | tf_op jit(solution)/shard_map/ppermute | solution.py:59
  131.1 52.6 %copy-start.6 = (f32[32,16,128]{2,1,0:T(8,128)S(1)}, f32[32,16,128]{2,1,0:T(8,128)}, u32[]{:S(2)}) copy-start(f32[32,16,128]{2,1,0:T(8,128)} %rev.7) | copy-start | bytes 786436
  131.1 52.6 %copy-start.13 = (f32[32,16]{1,0:T(8,128)S(1)}, f32[32,16]{1,0:T(8,128)}, u32[]{:S(2)}) copy-start(f32[32,16]{1,0:T(8,128)} %copy.121) | copy-start | bytes 6148
  131.1 52.6 %copy-start.60 = (f32[32,16]{1,0:T(8,128)S(1)}, f32[32,16]{1,0:T(8,128)}, u32[]{:S(2)}) copy-start(f32[32,16]{1,0:T(8,128)} %copy.124) | copy-start | bytes 6148
  131.1 52.6 %copy-start.61 = (f32[32,16]{1,0:T(8,128)S(1)}, f32[32,16]{1,0:T(8,128)}, u32[]{:S(2)}) copy-start(f32[32,16]{1,0:T(8,128)} %copy.132) | copy-start | bytes 6148
  131.1 52.6 %copy-start.67 = (f32[32,16]{1,0:T(8,128)S(1)}, f32[32,16]{1,0:T(8,128)}, u32[]{:S(2)}) copy-start(f32[32,16]{1,0:T(8,128)} %copy.140) | copy-start | bytes 6148
  131.1 52.6 %copy-start.68 = (f32[32,16]{1,0:T(8,128)S(1)}, f32[32,16]{1,0:T(8,128)}, u32[]{:S(2)}) copy-start(f32[32,16]{1,0:T(8,128)} %copy.141) | copy-start | bytes 6148
  131.1 52.6 %copy-start.69 = (f32[32,16]{1,0:T(8,128)S(1)}, f32[32,16]{1,0:T(8,128)}, u32[]{:S(2)}) copy-start(f32[32,16]{1,0:T(8,128)} %copy.142) | copy-start | bytes 6148
  131.1 52.6 %copy-start.70 = (f32[32,16]{1,0:T(8,128)S(1)}, f32[32,16]{1,0:T(8,128)}, u32[]{:S(2)}) copy-start(f32[32,16]{1,0:T(8,128)} %copy.143) | copy-start | bytes 6148
  131.2 52.6 %copy-start.71 = (f32[32,16]{1,0:T(8,128)S(1)}, f32[32,16]{1,0:T(8,128)}, u32[]{:S(2)}) copy-start(f32[32,16]{1,0:T(8,128)} %copy.144) | copy-start | bytes 6148
  131.2 54.8 %copy-start.3 = (bf16[128,512]{0,1:T(8,128)(2,1)S(1)}, bf16[128,512]{0,1:T(8,128)(2,1)}, u32[]{:S(2)}) copy-start(bf16[128,512]{0,1:T(8,128)(2,1)} %copy-done.2) | copy-start | bytes 393220
  131.2 54.8 %copy-start.5 = (bf16[128,512]{0,1:T(8,128)(2,1)S(1)}, bf16[128,512]{0,1:T(8,128)(2,1)}, u32[]{:S(2)}) copy-start(bf16[128,512]{0,1:T(8,128)(2,1)} %copy-done.4) | copy-start | bytes 393220
  131.2 52.5 %collective-permute-start.6 = (f32[2,32,16,16]{3,2,1,0:T(8,128)S(1)}, f32[2,32,16,16]{3,2,1,0:T(8,128)S(1)}, u32[]{:S(2)}, u32[]{:S(2)}) collective-permute-start(f32[2,32,16,16]{3,2,1,0:T(8,128)S(1)} %pad_maximum_fusion.5), channel_id=1, source_target_pairs={{0,256},{64,320},{128,384},{192,448},{256,0},{320,64},{384,128},{4... | collective-permute-start | bytes 196616 | tf_op jit(solution)/shard_map/ppermute | solution.py:59
  139.0 47.1 %copy-start.62 = (f32[32,16]{1,0:T(8,128)S(1)}, f32[32,16]{1,0:T(8,128)}, u32[]{:S(2)}) copy-start(f32[32,16]{1,0:T(8,128)} %copy.127) | copy-start | bytes 6148
  139.0 47.1 %copy-start.63 = (f32[32,16]{1,0:T(8,128)S(1)}, f32[32,16]{1,0:T(8,128)}, u32[]{:S(2)}) copy-start(f32[32,16]{1,0:T(8,128)} %copy.129) | copy-start | bytes 6148
  139.0 47.1 %copy-start.64 = (f32[32,16]{1,0:T(8,128)S(1)}, f32[32,16]{1,0:T(8,128)}, u32[]{:S(2)}) copy-start(f32[32,16]{1,0:T(8,128)} %copy.131) | copy-start | bytes 6148
  139.0 47.1 %copy-start.65 = (f32[32,16]{1,0:T(8,128)S(1)}, f32[32,16]{1,0:T(8,128)}, u32[]{:S(2)}) copy-start(f32[32,16]{1,0:T(8,128)} %copy.134) | copy-start | bytes 6148
  139.0 47.1 %copy-start.66 = (f32[32,16]{1,0:T(8,128)S(1)}, f32[32,16]{1,0:T(8,128)}, u32[]{:S(2)}) copy-start(f32[32,16]{1,0:T(8,128)} %copy.136) | copy-start | bytes 6148
  188.4 9.5 %copy-start.47 = (f32[1,1,512]{2,1,0:T(1,128)S(1)}, f32[1,1,512]{2,1,0:T(1,128)}, u32[]{:S(2)}) copy-start(f32[1,1,512]{2,1,0:T(1,128)} %copy-done.46) | copy-start | bytes 6148
  188.4 9.5 %copy-start.49 = (f32[1,1,512]{2,1,0:T(1,128)S(1)}, f32[1,1,512]{2,1,0:T(1,128)}, u32[]{:S(2)}) copy-start(f32[1,1,512]{2,1,0:T(1,128)} %copy-done.48) | copy-start | bytes 6148
  188.4 9.5 %copy-start.51 = (f32[1,1,512]{2,1,0:T(1,128)S(1)}, f32[1,1,512]{2,1,0:T(1,128)}, u32[]{:S(2)}) copy-start(f32[1,1,512]{2,1,0:T(1,128)} %copy-done.50) | copy-start | bytes 6148
  188.4 9.5 %copy-start.53 = (f32[1,1,512]{2,1,0:T(1,128)S(1)}, f32[1,1,512]{2,1,0:T(1,128)}, u32[]{:S(2)}) copy-start(f32[1,1,512]{2,1,0:T(1,128)} %copy-done.52) | copy-start | bytes 6148
  188.5 9.5 %copy-start.55 = (f32[1,1,512]{2,1,0:T(1,128)S(1)}, f32[1,1,512]{2,1,0:T(1,128)}, u32[]{:S(2)}) copy-start(f32[1,1,512]{2,1,0:T(1,128)} %copy-done.54) | copy-start | bytes 6148
  188.5 9.5 %copy-start.57 = (f32[1,1,512]{2,1,0:T(1,128)S(1)}, f32[1,1,512]{2,1,0:T(1,128)}, u32[]{:S(2)}) copy-start(f32[1,1,512]{2,1,0:T(1,128)} %copy-done.56) | copy-start | bytes 6148
  188.5 9.5 %copy-start.59 = (f32[1,1,512]{2,1,0:T(1,128)S(1)}, f32[1,1,512]{2,1,0:T(1,128)}, u32[]{:S(2)}) copy-start(f32[1,1,512]{2,1,0:T(1,128)} %copy-done.58) | copy-start | bytes 6148
  188.6 11.5 %copy-start.33 = (f32[1,1,512]{2,1,0:T(1,128)S(1)}, f32[1,1,512]{2,1,0:T(1,128)}, u32[]{:S(2)}) copy-start(f32[1,1,512]{2,1,0:T(1,128)} %copy-done.32) | copy-start | bytes 6148
  188.6 11.5 %copy-start.35 = (f32[1,1,512]{2,1,0:T(1,128)S(1)}, f32[1,1,512]{2,1,0:T(1,128)}, u32[]{:S(2)}) copy-start(f32[1,1,512]{2,1,0:T(1,128)} %copy-done.34) | copy-start | bytes 6148
  188.6 11.5 %copy-start.37 = (f32[1,1,512]{2,1,0:T(1,128)S(1)}, f32[1,1,512]{2,1,0:T(1,128)}, u32[]{:S(2)}) copy-start(f32[1,1,512]{2,1,0:T(1,128)} %copy-done.36) | copy-start | bytes 6148
  188.6 11.5 %copy-start.39 = (f32[1,1,512]{2,1,0:T(1,128)S(1)}, f32[1,1,512]{2,1,0:T(1,128)}, u32[]{:S(2)}) copy-start(f32[1,1,512]{2,1,0:T(1,128)} %copy-done.38) | copy-start | bytes 6148
  188.6 11.5 %copy-start.41 = (f32[1,1,512]{2,1,0:T(1,128)S(1)}, f32[1,1,512]{2,1,0:T(1,128)}, u32[]{:S(2)}) copy-start(f32[1,1,512]{2,1,0:T(1,128)} %copy-done.40) | copy-start | bytes 6148
  188.6 11.5 %copy-start.43 = (f32[1,1,512]{2,1,0:T(1,128)S(1)}, f32[1,1,512]{2,1,0:T(1,128)}, u32[]{:S(2)}) copy-start(f32[1,1,512]{2,1,0:T(1,128)} %copy-done.42) | copy-start | bytes 6148
  188.6 11.5 %copy-start.45 = (f32[1,1,512]{2,1,0:T(1,128)S(1)}, f32[1,1,512]{2,1,0:T(1,128)}, u32[]{:S(2)}) copy-start(f32[1,1,512]{2,1,0:T(1,128)} %copy-done.44) | copy-start | bytes 6148
  188.8 9.1 %collective-permute-start.7 = (bf16[3,6,512]{1,2,0:T(8,128)(2,1)S(1)}, bf16[3,6,512]{1,2,0:T(8,128)(2,1)S(1)}, u32[]{:S(2)}, u32[]{:S(2)}) collective-permute-start(bf16[3,6,512]{1,2,0:T(8,128)(2,1)S(1)} %pad_maximum_fusion.6), channel_id=1, source_target_pairs={{8,0},{16,8},{24,16},{32,24},{40,32},{48,40},{56,48},{64,56},{72,6... | collective-permute-start | bytes 55304 | tf_op jit(solution)/shard_map/ppermute | solution.py:19
  191.3 11.0 %copy-start.19 = (f32[1,1,512]{2,1,0:T(1,128)S(1)}, f32[1,1,512]{2,1,0:T(1,128)}, u32[]{:S(2)}) copy-start(f32[1,1,512]{2,1,0:T(1,128)} %copy-done.18) | copy-start | bytes 6148
  191.3 11.0 %copy-start.21 = (f32[1,1,512]{2,1,0:T(1,128)S(1)}, f32[1,1,512]{2,1,0:T(1,128)}, u32[]{:S(2)}) copy-start(f32[1,1,512]{2,1,0:T(1,128)} %copy-done.20) | copy-start | bytes 6148
  191.3 11.0 %copy-start.23 = (f32[1,1,512]{2,1,0:T(1,128)S(1)}, f32[1,1,512]{2,1,0:T(1,128)}, u32[]{:S(2)}) copy-start(f32[1,1,512]{2,1,0:T(1,128)} %copy-done.22) | copy-start | bytes 6148
  191.3 11.0 %copy-start.25 = (f32[1,1,512]{2,1,0:T(1,128)S(1)}, f32[1,1,512]{2,1,0:T(1,128)}, u32[]{:S(2)}) copy-start(f32[1,1,512]{2,1,0:T(1,128)} %copy-done.24) | copy-start | bytes 6148
  191.3 11.0 %copy-start.27 = (f32[1,1,512]{2,1,0:T(1,128)S(1)}, f32[1,1,512]{2,1,0:T(1,128)}, u32[]{:S(2)}) copy-start(f32[1,1,512]{2,1,0:T(1,128)} %copy-done.26) | copy-start | bytes 6148
  191.3 11.0 %copy-start.29 = (f32[1,1,512]{2,1,0:T(1,128)S(1)}, f32[1,1,512]{2,1,0:T(1,128)}, u32[]{:S(2)}) copy-start(f32[1,1,512]{2,1,0:T(1,128)} %copy-done.28) | copy-start | bytes 6148
  191.3 11.0 %copy-start.31 = (f32[1,1,512]{2,1,0:T(1,128)S(1)}, f32[1,1,512]{2,1,0:T(1,128)}, u32[]{:S(2)}) copy-start(f32[1,1,512]{2,1,0:T(1,128)} %copy-done.30) | copy-start | bytes 6148
  (18 other events, 102.0 us)

commit v3 on v2

--- a/solution.py
+++ b/solution.py
@@ -100,9 +100,21 @@
 
     signal = product.reshape(block_len, group_count, GROUP)
     cotangent = grad_conv.reshape(block_len, group_count, GROUP)
-    end_state = split_dot("gms,sgc->gmc", powers[:, :, block_len - 1 :: -1], signal)
-    start_state = split_dot("gms,sgc->gmc", powers[:, :, :block_len], cotangent)
-    decay_step = (rates * block_len)[:, :, None]
+    order = rates.shape[1]
+    owner = (jnp.arange(channels) // GROUP)[None, :] == jnp.arange(group_count)[:, None]
+    owner = owner.astype(jnp.float32)
+
+    def own_block(full):
+        return (full.reshape(group_count, order, channels) * owner[:, None, :]).sum(0)
+
+    def spread(state):
+        return (state[None] * owner[:, None, :]).reshape(group_count * order, channels)
+
+    end_rows = powers[:, :, block_len - 1 :: -1].reshape(group_count * order, block_len)
+    start_rows = powers[:, :, :block_len].reshape(group_count * order, block_len)
+    end_state = own_block(split_dot("ks,sc->kc", end_rows, product))
+    start_state = own_block(split_dot("ks,sc->kc", start_rows, grad_conv))
+    decay_step = jnp.repeat(rates.T, GROUP, axis=1) * block_len
     member = lax.axis_index("xc")
     pre_fwd, group_fwd, pre_bwd, group_bwd = cube_scan(
         end_state, start_state, decay_step, "xc", inner, member
@@ -114,14 +126,16 @@
     entering = pre_fwd + jnp.exp(-decay_step * place) * outer_fwd
     leaving = pre_bwd + jnp.exp(-decay_step * (inner - 1 - place)) * outer_bwd
 
-    local_conv = split_dot("gts,sgc->tgc", toeplitz, signal)
-    local_grad = split_dot("gts,tgc->sgc", toeplitz, cotangent)
-    lead_fwd = weights[:, None, :] * jnp.swapaxes(powers[:, :, 1:], 1, 2)
-    lead_bwd = weights[:, None, :] * jnp.swapaxes(powers[:, :, block_len:0:-1], 1, 2)
-    carried_conv = jnp.einsum("gtm,gmc->tgc", lead_fwd, entering, precision=precise)
-    carried_grad = jnp.einsum("gsm,gmc->sgc", lead_bwd, leaving, precision=precise)
-    conv_out = rounded((local_conv + carried_conv).reshape(block_len, channels))
-    grad_prod = rounded((local_grad + carried_grad).reshape(block_len, channels))
+    local_conv = split_dot("gts,sgc->tgc", toeplitz, signal).reshape(block_len, channels)
+    local_grad = split_dot("gts,tgc->sgc", toeplitz, cotangent).reshape(block_len, channels)
+    lead_fwd = (weights[:, :, None] * powers[:, :, 1:]).reshape(group_count * order, block_len)
+    lead_bwd = (weights[:, :, None] * powers[:, :, block_len:0:-1]).reshape(
+        group_count * order, block_len
+    )
+    carried_conv = jnp.einsum("kt,kc->tc", lead_fwd, spread(entering), precision=precise)
+    carried_grad = jnp.einsum("ks,kc->sc", lead_bwd, spread(leaving), precision=precise)
+    conv_out = rounded(local_conv + carried_conv)
+    grad_prod = rounded(local_grad + carried_grad)
 
     mixer_out = (q_short.astype(jnp.float32) * conv_out.astype(jnp.float32)).astype(jnp.bfloat16)
     grad_qshort = rounded(grad_out.astype(jnp.float32) * conv_out.astype(jnp.float32))

time: 206 us -> 111 us (0.54)
  waiting for transfers between devices: 113 us -> 18.1 us
    ppermute x6, waiting for transfers between devices: 108 us -> 16.7 us  [cube_scan(): got = lax.ppermute(jnp.stack([tot_fwd, tot_bwd]), axis, pairs)]
    broadcast_in_dim x0 -> x17, local copies, waits for them, and re-layouts: none -> 12.5 us  [shards(): decay_step = jnp.repeat(rates.T, GROUP, axis=1) * block_len]
    unnamed x157 -> x121, local copies, waits for them, and re-layouts: 5.16 us -> 0.34 us
    ppermute x2, waiting for transfers between devices: 5.69 us -> 1.4 us  [from_behind(): lax.ppermute(value, axis, [(source, source + steps) for source in range(l...]
    ppermute x2, starting transfers between devices: 6.98 us -> 10.9 us  [from_behind(): lax.ppermute(value, axis, [(source, source + steps) for source in range(l...]
    exp x6, local copies, waits for them, and re-layouts: 8.22 us -> 4.57 us  [cube_scan(): jnp.exp(-unit_decay * offset) * got[0]]
    mul x0 -> x3, other arithmetic: none -> 3.08 us  [spread(): state[None] * owner[:, None, :]]
    ppermute x6, starting transfers between devices: 21.3 us -> 18.4 us  [cube_scan(): got = lax.ppermute(jnp.stack([tot_fwd, tot_bwd]), axis, pairs)]
  transfers between devices with their start and end apart: 8 -> 8, of which waited for: 6 -> 6; matrix products, arithmetic and copies ran while one was open for 18% -> 37% of each run, Pallas kernels for 0% -> 0%
where the time goes in v3:
time: 111 us; the launch traced here: 110 us
  local copies, waits for them, and re-layouts  33.6 us (30%)
  starting transfers between devices  29.3 us (26%)
  waiting for transfers between devices  18.1 us (16%)
  other arithmetic  15.4 us (14%)
  matrix products  11 us (10%)
  between operations  2.03 us (2%)
    ppermute x6, starting transfers between devices, cube_scan(): got = lax.ppermute(jnp.stack([tot_fwd, tot_bwd]), axis, pairs)  18.4 us
    ppermute x6, waiting for transfers between devices, cube_scan(): got = lax.ppermute(jnp.stack([tot_fwd, tot_bwd]), axis, pairs)  16.7 us
    broadcast_in_dim x17, local copies, waits for them, and re-layouts, shards(): decay_step = jnp.repeat(rates.T, GROUP, axis=1) * block_len  12.5 us
    ppermute x2, starting transfers between devices, from_behind(): lax.ppermute(value, axis, [(source, source + steps) for source in range(l...  10.9 us
    exp x6, local copies, waits for them, and re-layouts, cube_scan(): jnp.exp(-unit_decay * offset) * got[0]  4.57 us
    exp x5, local copies, waits for them, and re-layouts, cube_scan(): span = jnp.exp(-unit_decay * shift)  3.85 us
    dot_general x1, matrix products, shards(): toeplitz = jnp.einsum('gtm,gms->gts', falling, rising, precision=precise)  3.65 us
    mul x3, other arithmetic, spread(): state[None] * owner[:, None, :]  3.08 us
  transfers between devices with their start and end apart: 8, of which 6 were waited for; matrix products, arithmetic and copies ran while one was open for 37% of the time, Pallas kernels for 0%

profile of v3, /device:TPU:1, one launch (start us, length us, event | category | flops | bytes accessed | tf_op | source)
XLA Modules:
  0.0 109.5 jit_solution(4391621337753049608)
XLA Ops:
  2.2 4.5 %collective-permute-start = (bf16[3,6,512]{2,1,0:T(8,128)(2,1)S(1)}, bf16[3,6,512]{2,1,0:T(8,128)(2,1)S(1)}, u32[]{:S(2)}, u32[]{:S(2)}) collective-permute-start(bf16[3,6,512]{2,1,0:T(8,128)(2,1)S(1)} %pad_maximum_fusion.12), channel_id=1, source_target_pairs={{0,8},{8,16},{16,24},{24,32},{32,40},{40,48},{48,56},{56,64},{64,7... | collective-permute-start | bytes 55304 | tf_op jit(solution)/shard_map/ppermute | solution.py:19
  6.7 0.8 fusion.168
  7.5 1.2 %fusion.167 = (f32[1,1,512]{2,1,0:T(1,128)S(1)}, f32[1,1,512]{2,1,0:T(1,128)S(1)}, f32[1,1,512]{2,1,0:T(1,128)S(1)}, f32[1,1,512]{2,1,0:T(1,128)S(1)}, f32[1,1,5...) fusion(f32[3,7,512]{2,1,0:T(8,128)} %param.10), kind=kLoop, calls=%fused_computation.310 | loop fusion | bytes 77824 | tf_op jit(solution)/shard_map/slice | solution.py:32
  8.9 1.5 %exponential_bitcast_fusion.4 = (f32[16,32]{1,0:T(8,128)}, f32[16,32]{1,0:T(8,128)}, f32[16,32]{1,0:T(8,128)}, f32[16,32]{1,0:T(8,128)}, f32[16,32]{1,0:T(8,128)...) fusion(f32[]{:T(128)S(6)} %sub.50, ...), kind=kLoop, calls=%fused_computation.275 | loop fusion | flops 11776 | bytes 43048 | tf_op jit(solution)/shard_map/exp | solution.py:65
  10.6 0.9 fusion.166
  14.2 1.2 %fusion.8 = (f32[16,512]{1,0:T(8,128)S(1)}, f32[16,512]{1,0:T(8,128)S(1)}) fusion(f32[32,16,512]{2,1,0:T(8,128)S(1)} %bitcast.145, f32[32,512]{1,0:T(8,128)S(1)} %fusion.144, f32[32,16,512]{2,1,0:T(8,128)S(1)} %bitcast.146), kind=kLoop, calls=%fused_computation.18 | loop fusion | flops 1032192 | bytes 2228224 | tf_op jit(solution)/shard_map/reduce_sum | solution.py:108
  16.1 5.6 %collective-permute-start.1 = (f32[2,16,512]{2,1,0:T(8,128)}, f32[2,16,512]{2,1,0:T(8,128)}, u32[]{:S(2)}, u32[]{:S(2)}) collective-permute-start(f32[2,16,512]{2,1,0:T(8,128)} %pad_maximum_fusion.6), channel_id=1, source_target_pairs={{0,8},{8,0},{16,24},{24,16},{32,40},{40,32},{48,56},{56,48},{1,9},... | collective-permute-start | bytes 196616 | tf_op jit(solution)/shard_map/ppermute | solution.py:59
  21.7 3.7 %fusion.129 = f32[32,128,128]{2,1,0:T(8,128)S(1)} fusion(f32[32,16]{1,0:T(8,128)S(1)} %copy.24, f32[128]{0:T(128)S(1)} %get-tuple-element.76, f32[128]{0:T(128)S(1)} %get-tuple-element.77, f32[32,16]{1,0:T(8,128)S(1)} %copy.23), kind=kOutput, calls=%fused_computation.206 | convolution fusion | flops 100859904 | bytes 2102272 | tf_op jit(solution)/shard_map/gtm,gms->gts/dot_general | solution.py:97
  25.4 0.8 broadcast_in_dim.81
  27.0 0.8 broadcast_in_dim.70
  27.8 0.8 exp.298
  28.6 0.8 broadcast_in_dim.71
  29.4 0.8 exp.301
  30.2 0.8 broadcast_in_dim.72
  31.0 0.8 exp.303
  31.8 0.8 broadcast_in_dim.73
  32.6 0.8 exp.305
  33.4 0.8 broadcast_in_dim.74
  34.2 0.8 exp.307
  34.9 0.8 broadcast_in_dim.76
  35.8 0.8 exp.311
  36.5 0.8 broadcast_in_dim.82
  37.4 0.8 exp.324
  38.1 0.8 broadcast_in_dim.83
  39.7 0.8 broadcast_in_dim.77
  40.5 0.8 exp.313
  41.3 0.8 broadcast_in_dim.78
  42.1 0.8 exp.316
  42.9 0.8 broadcast_in_dim.79
  44.5 0.8 broadcast_in_dim.80
  45.3 0.8 exp.320
  46.1 0.8 broadcast_in_dim.84
  46.9 0.8 exp.328
  47.7 0.8 broadcast_in_dim.85
  48.5 0.8 exp.330
  49.4 0.8 exp.309
  50.3 0.8 exp.296
  51.0 1.8 %rev.7 = f32[32,16,128]{2,1,0:T(8,128)} reverse(f32[32,16,128]{2,1,0:T(8,128)} %get-tuple-element.6), dimensions={2} | reverse | bytes 524288 | tf_op jit(solution)/shard_map/rev | solution.py:132
  52.8 0.8 add_select_fusion.17
  54.3 1.9 %collective-permute-start.2 = (f32[2,16,512]{2,1,0:T(8,128)}, f32[2,16,512]{2,1,0:T(8,128)S(1)}, u32[]{:S(2)}, u32[]{:S(2)}) collective-permute-start(f32[2,16,512]{2,1,0:T(8,128)} %pad_maximum_fusion.7), channel_id=1, source_target_pairs={{0,16},{8,24},{16,0},{24,8},{32,48},{40,56},{48,32},{56,40},{1,17}... | collective-permute-start | bytes 196616 | tf_op jit(solution)/shard_map/ppermute | solution.py:59
  56.4 3.7 %collective-permute-done.2 = f32[2,16,512]{2,1,0:T(8,128)S(1)} collective-permute-done((f32[2,16,512]{2,1,0:T(8,128)}, f32[2,16,512]{2,1,0:T(8,128)S(1)}, u32[]{:S(2)}, u32[]{:S(2)}) %collective-permute-start.2) | collective-permute-done | bytes 65568 | tf_op jit(solution)/shard_map/ppermute | solution.py:59
  60.1 0.8 add_select_fusion.15
  60.9 2.1 %collective-permute-start.3 = (f32[2,16,512]{2,1,0:T(8,128)S(1)}, f32[2,16,512]{2,1,0:T(8,128)S(1)}, u32[]{:S(2)}, u32[]{:S(2)}) collective-permute-start(f32[2,16,512]{2,1,0:T(8,128)S(1)} %pad_maximum_fusion.8), channel_id=1, source_target_pairs={{0,32},{8,40},{16,48},{24,56},{32,0},{40,8},{48,16},{56,24},{1,33}... | collective-permute-start | bytes 196616 | tf_op jit(solution)/shard_map/ppermute | solution.py:59
  63.4 4.0 %collective-permute-done.3 = f32[2,16,512]{2,1,0:T(8,128)S(1)} collective-permute-done((f32[2,16,512]{2,1,0:T(8,128)S(1)}, f32[2,16,512]{2,1,0:T(8,128)S(1)}, u32[]{:S(2)}, u32[]{:S(2)}) %collective-permute-start.3) | collective-permute-done | bytes 65568 | tf_op jit(solution)/shard_map/ppermute | solution.py:59
  68.1 1.9 %collective-permute-start.4 = (f32[2,16,512]{2,1,0:T(8,128)}, f32[2,16,512]{2,1,0:T(8,128)}, u32[]{:S(2)}, u32[]{:S(2)}) collective-permute-start(f32[2,16,512]{2,1,0:T(8,128)} %pad_maximum_fusion.9), channel_id=1, source_target_pairs={{0,64},{64,0},{128,192},{192,128},{256,320},{320,256},{384,448},{4... | collective-permute-start | bytes 196616 | tf_op jit(solution)/shard_map/ppermute | solution.py:59
  70.0 1.1 %convolution_add_fusion.2 = f32[32,16,128]{2,1,0:T(8,128)} fusion(f32[32,16,128]{2,1,0:T(8,128)S(1)} %fusion.9, bf16[128,32,16]{0,2,1:T(8,128)(2,1)S(1)} %bitcast.150, f32[32,128,128]{2,1,0:T(8,128)S(1)} %fusion.129, pred[128,128]{1,0:T(8,128)(4,1)S(1)} %iota_compare_fusion.1), kind=kOutput, calls=%fused_computation.7 | convolution fusion | flops 18939904 | bytes 2768896 | tf_op jit(solution)/shard_map/gts,tgc->sgc/dot_general | solution.py:50
  71.2 2.1 %collective-permute-done.4 = f32[2,16,512]{2,1,0:T(8,128)} collective-permute-done((f32[2,16,512]{2,1,0:T(8,128)}, f32[2,16,512]{2,1,0:T(8,128)}, u32[]{:S(2)}, u32[]{:S(2)}) %collective-permute-start.4) | collective-permute-done | bytes 65568 | tf_op jit(solution)/shard_map/ppermute | solution.py:59
  73.4 0.8 add_select_fusion.11
  74.2 2.0 %collective-permute-start.5 = (f32[2,16,512]{2,1,0:T(8,128)S(1)}, f32[2,16,512]{2,1,0:T(8,128)S(1)}, u32[]{:S(2)}, u32[]{:S(2)}) collective-permute-start(f32[2,16,512]{2,1,0:T(8,128)S(1)} %pad_maximum_fusion.10), channel_id=1, source_target_pairs={{0,128},{64,192},{128,0},{192,64},{256,384},{320,448},{384,256},{4... | collective-permute-start | bytes 196616 | tf_op jit(solution)/shard_map/ppermute | solution.py:59
  76.8 3.7 %collective-permute-done.5 = f32[2,16,512]{2,1,0:T(8,128)S(1)} collective-permute-done((f32[2,16,512]{2,1,0:T(8,128)S(1)}, f32[2,16,512]{2,1,0:T(8,128)S(1)}, u32[]{:S(2)}, u32[]{:S(2)}) %collective-permute-start.5) | collective-permute-done | bytes 65568 | tf_op jit(solution)/shard_map/ppermute | solution.py:59
  81.2 4.9 %collective-permute-start.6 = (f32[2,16,512]{2,1,0:T(8,128)}, f32[2,16,512]{2,1,0:T(8,128)}, u32[]{:S(2)}, u32[]{:S(2)}) collective-permute-start(f32[2,16,512]{2,1,0:T(8,128)} %pad_maximum_fusion.11), channel_id=1, source_target_pairs={{0,256},{64,320},{128,384},{192,448},{256,0},{320,64},{384,128},{4... | collective-permute-start | bytes 196616 | tf_op jit(solution)/shard_map/ppermute | solution.py:59
  86.1 1.4 %convolution_add_fusion.3 = f32[32,16,128]{2,1,0:T(8,128)} fusion(f32[32,16,128]{2,1,0:T(8,128)S(1)} %fusion.10, bf16[128,32,16]{0,2,1:T(8,128)(2,1)S(1)} %bitcast.148, f32[32,128,128]{2,1,0:T(8,128)S(1)} %fusion.129, pred[128,128]{1,0:T(8,128)(4,1)S(1)} %iota_compare_fusion.1), kind=kOutput, calls=%fused_computation.8 | convolution fusion | flops 18939904 | bytes 2768896 | tf_op jit(solution)/shard_map/gts,sgc->tgc/dot_general | solution.py:50
  87.7 1.1 copy.31
  88.8 3.1 %collective-permute-done.6 = f32[2,16,512]{2,1,0:T(8,128)} collective-permute-done((f32[2,16,512]{2,1,0:T(8,128)}, f32[2,16,512]{2,1,0:T(8,128)}, u32[]{:S(2)}, u32[]{:S(2)}) %collective-permute-start.6) | collective-permute-done | bytes 65568 | tf_op jit(solution)/shard_map/ppermute | solution.py:59
  91.9 1.0 fusion.149
  92.9 1.0 fusion.146
  93.9 1.1 broadcast_multiply_fusion
  95.0 1.4 %fusion.3 = bf16[128,512]{1,0:T(8,128)(2,1)S(1)} fusion(f32[128,512]{1,0:T(8,128)S(1)} %copy.34, f32[32,16,512]{2,0,1:T(8,128)S(1)} %get-tuple-element.26, f32[32,16,128]{2,1,0:T(8,128)S(1)} %copy-done, f32[32,16]{1,0:T(8,128)S(1)} %copy-done.8), kind=kOutput, calls=%fused_computation.11 | convolution fusion | flops 402849792 | bytes 1705984 | tf_op jit(solution)/shard_map/ks,kc->sc/dot_general | solution.py:136
  96.6 1.4 %fusion.4 = bf16[128,512]{1,0:T(8,128)(2,1)S(1)} fusion(f32[128,512]{1,0:T(8,128)S(1)} %copy.31, f32[32,16,512]{2,0,1:T(8,128)S(1)} %get-tuple-element.27, f32[32,16]{1,0:T(8,128)S(1)} %copy-done.8, f32[32,16,129]{2,1,0:T(8,128)S(1)} %multiply_exponential_fusion), kind=kOutput, calls=%fused_computation.12 | convolution fusion | flops 402849792 | bytes 1720320 | tf_op jit(solution)/shard_map/kt,kc->tc/dot_general | solution.py:135
  98.8 6.4 %collective-permute-start.7 = (bf16[3,6,512]{2,1,0:T(8,128)(2,1)S(1)}, bf16[3,6,512]{2,1,0:T(8,128)(2,1)S(1)}, u32[]{:S(2)}, u32[]{:S(2)}) collective-permute-start(bf16[3,6,512]{2,1,0:T(8,128)(2,1)S(1)} %pad_maximum_fusion.13), channel_id=1, source_target_pairs={{8,0},{16,8},{24,16},{32,24},{40,32},{48,40},{56,48},{64,56},{72,6... | collective-permute-start | bytes 55304 | tf_op jit(solution)/shard_map/ppermute | solution.py:19
  105.3 1.4 %collective-permute-done.7 = bf16[3,6,512]{2,1,0:T(8,128)(2,1)S(1)} collective-permute-done((bf16[3,6,512]{2,1,0:T(8,128)(2,1)S(1)}, bf16[3,6,512]{2,1,0:T(8,128)(2,1)S(1)}, u32[]{:S(2)}, u32[]{:S(2)}) %collective-permute-start.7) | collective-permute-done | bytes 18464 | tf_op jit(solution)/shard_map/ppermute | solution.py:19
  106.8 0.9 fusion.40
  107.7 0.9 fusion.23
  108.7 0.9 fusion.57
  (178 shorter events, 11.6 us)
Async XLA Ops:
  0.6 11.2 %copy-start.12 = (bf16[128,512]{1,0:T(8,128)(2,1)S(1)}, bf16[128,512]{1,0:T(8,128)(2,1)}, u32[]{:S(2)}) copy-start(bf16[128,512]{1,0:T(8,128)(2,1)} %param.7) | copy-start | bytes 393220
  0.6 11.2 %copy-start.13 = (bf16[128,512]{1,0:T(8,128)(2,1)S(1)}, bf16[128,512]{1,0:T(8,128)(2,1)}, u32[]{:S(2)}) copy-start(bf16[128,512]{1,0:T(8,128)(2,1)} %param.8) | copy-start | bytes 393220
  0.7 11.1 %copy-start.17 = (f32[32,16]{0,1:T(8,128)S(1)}, f32[32,16]{0,1:T(8,128)}, u32[]{:S(2)}) copy-start(f32[32,16]{0,1:T(8,128)} %param.11) | copy-start | bytes 6148
  2.2 9.9 %collective-permute-start = (bf16[3,6,512]{2,1,0:T(8,128)(2,1)S(1)}, bf16[3,6,512]{2,1,0:T(8,128)(2,1)S(1)}, u32[]{:S(2)}, u32[]{:S(2)}) collective-permute-start(bf16[3,6,512]{2,1,0:T(8,128)(2,1)S(1)} %pad_maximum_fusion.12), channel_id=1, source_target_pairs={{0,8},{8,16},{16,24},{24,32},{32,40},{40,48},{48,56},{56,64},{64,7... | collective-permute-start | bytes 55304 | tf_op jit(solution)/shard_map/ppermute | solution.py:19
  7.5 5.2 %copy-start.56 = (f32[1,1,512]{2,1,0:T(1,128)}, f32[1,1,512]{2,1,0:T(1,128)S(1)}, u32[]{:S(2)}) copy-start(f32[1,1,512]{2,1,0:T(1,128)S(1)} %get-tuple-element.47) | copy-start | bytes 6148
  7.5 5.2 %copy-start.58 = (f32[1,1,512]{2,1,0:T(1,128)}, f32[1,1,512]{2,1,0:T(1,128)S(1)}, u32[]{:S(2)}) copy-start(f32[1,1,512]{2,1,0:T(1,128)S(1)} %get-tuple-element.48) | copy-start | bytes 6148
  8.7 3.3 %copy-start.18 = (f32[1,1,512]{2,1,0:T(1,128)}, f32[1,1,512]{2,1,0:T(1,128)S(1)}, u32[]{:S(2)}) copy-start(f32[1,1,512]{2,1,0:T(1,128)S(1)} %get-tuple-element.28) | copy-start | bytes 6148
  8.7 3.3 %copy-start.20 = (f32[1,1,512]{2,1,0:T(1,128)}, f32[1,1,512]{2,1,0:T(1,128)S(1)}, u32[]{:S(2)}) copy-start(f32[1,1,512]{2,1,0:T(1,128)S(1)} %get-tuple-element.41) | copy-start | bytes 6148
  8.7 3.3 %copy-start.22 = (f32[1,1,512]{2,1,0:T(1,128)}, f32[1,1,512]{2,1,0:T(1,128)S(1)}, u32[]{:S(2)}) copy-start(f32[1,1,512]{2,1,0:T(1,128)S(1)} %get-tuple-element.42) | copy-start | bytes 6148
  8.7 3.3 %copy-start.24 = (f32[1,1,512]{2,1,0:T(1,128)}, f32[1,1,512]{2,1,0:T(1,128)S(1)}, u32[]{:S(2)}) copy-start(f32[1,1,512]{2,1,0:T(1,128)S(1)} %get-tuple-element.43) | copy-start | bytes 6148
  8.7 3.3 %copy-start.26 = (f32[1,1,512]{2,1,0:T(1,128)}, f32[1,1,512]{2,1,0:T(1,128)S(1)}, u32[]{:S(2)}) copy-start(f32[1,1,512]{2,1,0:T(1,128)S(1)} %get-tuple-element.44) | copy-start | bytes 6148
  8.8 3.3 %copy-start.28 = (f32[1,1,512]{2,1,0:T(1,128)}, f32[1,1,512]{2,1,0:T(1,128)S(1)}, u32[]{:S(2)}) copy-start(f32[1,1,512]{2,1,0:T(1,128)S(1)} %get-tuple-element.45) | copy-start | bytes 6148
  8.8 3.3 %copy-start.30 = (f32[1,1,512]{2,1,0:T(1,128)}, f32[1,1,512]{2,1,0:T(1,128)S(1)}, u32[]{:S(2)}) copy-start(f32[1,1,512]{2,1,0:T(1,128)S(1)} %get-tuple-element.46) | copy-start | bytes 6148
  8.8 3.6 %copy-start.42 = (f32[1,1,512]{2,1,0:T(1,128)}, f32[1,1,512]{2,1,0:T(1,128)S(1)}, u32[]{:S(2)}) copy-start(f32[1,1,512]{2,1,0:T(1,128)S(1)} %get-tuple-element.34) | copy-start | bytes 6148
  8.8 3.6 %copy-start.44 = (f32[1,1,512]{2,1,0:T(1,128)}, f32[1,1,512]{2,1,0:T(1,128)S(1)}, u32[]{:S(2)}) copy-start(f32[1,1,512]{2,1,0:T(1,128)S(1)} %get-tuple-element.35) | copy-start | bytes 6148
  8.8 3.6 %copy-start.46 = (f32[1,1,512]{2,1,0:T(1,128)}, f32[1,1,512]{2,1,0:T(1,128)S(1)}, u32[]{:S(2)}) copy-start(f32[1,1,512]{2,1,0:T(1,128)S(1)} %get-tuple-element.36) | copy-start | bytes 6148
  8.8 3.6 %copy-start.48 = (f32[1,1,512]{2,1,0:T(1,128)}, f32[1,1,512]{2,1,0:T(1,128)S(1)}, u32[]{:S(2)}) copy-start(f32[1,1,512]{2,1,0:T(1,128)S(1)} %get-tuple-element.37) | copy-start | bytes 6148
  8.8 3.6 %copy-start.50 = (f32[1,1,512]{2,1,0:T(1,128)}, f32[1,1,512]{2,1,0:T(1,128)S(1)}, u32[]{:S(2)}) copy-start(f32[1,1,512]{2,1,0:T(1,128)S(1)} %get-tuple-element.38) | copy-start | bytes 6148
  8.8 3.6 %copy-start.52 = (f32[1,1,512]{2,1,0:T(1,128)}, f32[1,1,512]{2,1,0:T(1,128)S(1)}, u32[]{:S(2)}) copy-start(f32[1,1,512]{2,1,0:T(1,128)S(1)} %get-tuple-element.39) | copy-start | bytes 6148
  8.8 3.6 %copy-start.54 = (f32[1,1,512]{2,1,0:T(1,128)}, f32[1,1,512]{2,1,0:T(1,128)S(1)}, u32[]{:S(2)}) copy-start(f32[1,1,512]{2,1,0:T(1,128)S(1)} %get-tuple-element.40) | copy-start | bytes 6148
  8.8 3.9 %copy-start.32 = (f32[1,1,512]{2,1,0:T(1,128)}, f32[1,1,512]{2,1,0:T(1,128)S(1)}, u32[]{:S(2)}) copy-start(f32[1,1,512]{2,1,0:T(1,128)S(1)} %get-tuple-element.29) | copy-start | bytes 6148
  8.9 3.9 %copy-start.34 = (f32[1,1,512]{2,1,0:T(1,128)}, f32[1,1,512]{2,1,0:T(1,128)S(1)}, u32[]{:S(2)}) copy-start(f32[1,1,512]{2,1,0:T(1,128)S(1)} %get-tuple-element.30) | copy-start | bytes 6148
  8.9 3.9 %copy-start.36 = (f32[1,1,512]{2,1,0:T(1,128)}, f32[1,1,512]{2,1,0:T(1,128)S(1)}, u32[]{:S(2)}) copy-start(f32[1,1,512]{2,1,0:T(1,128)S(1)} %get-tuple-element.31) | copy-start | bytes 6148
  8.9 3.9 %copy-start.38 = (f32[1,1,512]{2,1,0:T(1,128)}, f32[1,1,512]{2,1,0:T(1,128)S(1)}, u32[]{:S(2)}) copy-start(f32[1,1,512]{2,1,0:T(1,128)S(1)} %get-tuple-element.32) | copy-start | bytes 6148
  8.9 3.9 %copy-start.40 = (f32[1,1,512]{2,1,0:T(1,128)}, f32[1,1,512]{2,1,0:T(1,128)S(1)}, u32[]{:S(2)}) copy-start(f32[1,1,512]{2,1,0:T(1,128)S(1)} %get-tuple-element.33) | copy-start | bytes 6148
  12.0 9.7 %copy-start.7 = (f32[32,16]{1,0:T(8,128)}, f32[32,16]{1,0:T(8,128)S(1)}, u32[]{:S(2)}) copy-start(f32[32,16]{1,0:T(8,128)S(1)} %copy.23) | copy-start | bytes 6148
  15.5 6.2 %copy-start.5 = (f32[16,512]{1,0:T(8,128)}, f32[16,512]{1,0:T(8,128)S(1)}, u32[]{:S(2)}) copy-start(f32[16,512]{1,0:T(8,128)S(1)} %get-tuple-element.4) | copy-start | bytes 98308
  15.5 6.3 %copy-start.6 = (f32[16,512]{1,0:T(8,128)}, f32[16,512]{1,0:T(8,128)S(1)}, u32[]{:S(2)}) copy-start(f32[16,512]{1,0:T(8,128)S(1)} %get-tuple-element.5) | copy-start | bytes 98308
  16.1 36.7 %collective-permute-start.1 = (f32[2,16,512]{2,1,0:T(8,128)}, f32[2,16,512]{2,1,0:T(8,128)}, u32[]{:S(2)}, u32[]{:S(2)}) collective-permute-start(f32[2,16,512]{2,1,0:T(8,128)} %pad_maximum_fusion.6), channel_id=1, source_target_pairs={{0,8},{8,0},{16,24},{24,16},{32,40},{40,32},{48,56},{56,48},{1,9},... | collective-permute-start | bytes 196616 | tf_op jit(solution)/shard_map/ppermute | solution.py:59
  54.3 5.8 %collective-permute-start.2 = (f32[2,16,512]{2,1,0:T(8,128)}, f32[2,16,512]{2,1,0:T(8,128)S(1)}, u32[]{:S(2)}, u32[]{:S(2)}) collective-permute-start(f32[2,16,512]{2,1,0:T(8,128)} %pad_maximum_fusion.7), channel_id=1, source_target_pairs={{0,16},{8,24},{16,0},{24,8},{32,48},{40,56},{48,32},{56,40},{1,17}... | collective-permute-start | bytes 196616 | tf_op jit(solution)/shard_map/ppermute | solution.py:59
  56.3 11.1 %copy-start.16 = (f32[1,16,512]{2,1,0:T(8,128)S(1)}, f32[1,16,512]{2,1,0:T(8,128)}, u32[]{:S(2)}) copy-start(f32[1,16,512]{2,1,0:T(8,128)} %exp.311) | copy-start | bytes 98308
  60.1 11.0 %copy-start.9 = (f32[2,16,512]{2,1,0:T(8,128)}, f32[2,16,512]{2,1,0:T(8,128)S(1)}, u32[]{:S(2)}) copy-start(f32[2,16,512]{2,1,0:T(8,128)S(1)} %collective-permute-done.2) | copy-start | bytes 196612
  60.9 6.5 %collective-permute-start.3 = (f32[2,16,512]{2,1,0:T(8,128)S(1)}, f32[2,16,512]{2,1,0:T(8,128)S(1)}, u32[]{:S(2)}, u32[]{:S(2)}) collective-permute-start(f32[2,16,512]{2,1,0:T(8,128)S(1)} %pad_maximum_fusion.8), channel_id=1, source_target_pairs={{0,32},{8,40},{16,48},{24,56},{32,0},{40,8},{48,16},{56,24},{1,33}... | collective-permute-start | bytes 196616 | tf_op jit(solution)/shard_map/ppermute | solution.py:59
  68.1 5.3 %collective-permute-start.4 = (f32[2,16,512]{2,1,0:T(8,128)}, f32[2,16,512]{2,1,0:T(8,128)}, u32[]{:S(2)}, u32[]{:S(2)}) collective-permute-start(f32[2,16,512]{2,1,0:T(8,128)} %pad_maximum_fusion.9), channel_id=1, source_target_pairs={{0,64},{64,0},{128,192},{192,128},{256,320},{320,256},{384,448},{4... | collective-permute-start | bytes 196616 | tf_op jit(solution)/shard_map/ppermute | solution.py:59
  71.2 9.3 %copy-start.15 = (f32[1,16,512]{2,1,0:T(8,128)S(1)}, f32[1,16,512]{2,1,0:T(8,128)}, u32[]{:S(2)}) copy-start(f32[1,16,512]{2,1,0:T(8,128)} %exp.320) | copy-start | bytes 98308
  74.2 6.3 %collective-permute-start.5 = (f32[2,16,512]{2,1,0:T(8,128)S(1)}, f32[2,16,512]{2,1,0:T(8,128)S(1)}, u32[]{:S(2)}, u32[]{:S(2)}) collective-permute-start(f32[2,16,512]{2,1,0:T(8,128)S(1)} %pad_maximum_fusion.10), channel_id=1, source_target_pairs={{0,128},{64,192},{128,0},{192,64},{256,384},{320,448},{384,256},{4... | collective-permute-start | bytes 196616 | tf_op jit(solution)/shard_map/ppermute | solution.py:59
  76.8 10.7 %copy-start.1 = (f32[32,16,128]{2,1,0:T(8,128)S(1)}, f32[32,16,128]{2,1,0:T(8,128)}, u32[]{:S(2)}) copy-start(f32[32,16,128]{2,1,0:T(8,128)} %convolution_add_fusion.2) | copy-start | bytes 786436
  80.5 7.1 %copy-start.11 = (f32[2,16,512]{2,1,0:T(8,128)}, f32[2,16,512]{2,1,0:T(8,128)S(1)}, u32[]{:S(2)}) copy-start(f32[2,16,512]{2,1,0:T(8,128)S(1)} %collective-permute-done.5) | copy-start | bytes 196612
  81.2 10.7 %collective-permute-start.6 = (f32[2,16,512]{2,1,0:T(8,128)}, f32[2,16,512]{2,1,0:T(8,128)}, u32[]{:S(2)}, u32[]{:S(2)}) collective-permute-start(f32[2,16,512]{2,1,0:T(8,128)} %pad_maximum_fusion.11), channel_id=1, source_target_pairs={{0,256},{64,320},{128,384},{192,448},{256,0},{320,64},{384,128},{4... | collective-permute-start | bytes 196616 | tf_op jit(solution)/shard_map/ppermute | solution.py:59
  87.5 7.4 %copy-start = (f32[32,16,128]{2,1,0:T(8,128)S(1)}, f32[32,16,128]{2,1,0:T(8,128)}, u32[]{:S(2)}) copy-start(f32[32,16,128]{2,1,0:T(8,128)} %rev.7) | copy-start | bytes 786436
  87.5 7.5 %copy-start.8 = (f32[32,16]{1,0:T(8,128)S(1)}, f32[32,16]{1,0:T(8,128)}, u32[]{:S(2)}) copy-start(f32[32,16]{1,0:T(8,128)} %copy-done.7) | copy-start | bytes 6148
  95.0 3.1 %copy-start.4 = (bf16[128,512]{1,0:T(8,128)(2,1)S(1)}, bf16[128,512]{1,0:T(8,128)(2,1)}, u32[]{:S(2)}) copy-start(bf16[128,512]{1,0:T(8,128)(2,1)} %param.13) | copy-start | bytes 393220
  96.3 10.4 %copy-start.43 = (f32[1,1,512]{2,1,0:T(1,128)S(1)}, f32[1,1,512]{2,1,0:T(1,128)}, u32[]{:S(2)}) copy-start(f32[1,1,512]{2,1,0:T(1,128)} %copy-done.42) | copy-start | bytes 6148
  96.4 10.4 %copy-start.45 = (f32[1,1,512]{2,1,0:T(1,128)S(1)}, f32[1,1,512]{2,1,0:T(1,128)}, u32[]{:S(2)}) copy-start(f32[1,1,512]{2,1,0:T(1,128)} %copy-done.44) | copy-start | bytes 6148
  96.4 10.4 %copy-start.47 = (f32[1,1,512]{2,1,0:T(1,128)S(1)}, f32[1,1,512]{2,1,0:T(1,128)}, u32[]{:S(2)}) copy-start(f32[1,1,512]{2,1,0:T(1,128)} %copy-done.46) | copy-start | bytes 6148
  96.4 10.4 %copy-start.49 = (f32[1,1,512]{2,1,0:T(1,128)S(1)}, f32[1,1,512]{2,1,0:T(1,128)}, u32[]{:S(2)}) copy-start(f32[1,1,512]{2,1,0:T(1,128)} %copy-done.48) | copy-start | bytes 6148
  96.4 10.4 %copy-start.51 = (f32[1,1,512]{2,1,0:T(1,128)S(1)}, f32[1,1,512]{2,1,0:T(1,128)}, u32[]{:S(2)}) copy-start(f32[1,1,512]{2,1,0:T(1,128)} %copy-done.50) | copy-start | bytes 6148
  96.4 10.4 %copy-start.53 = (f32[1,1,512]{2,1,0:T(1,128)S(1)}, f32[1,1,512]{2,1,0:T(1,128)}, u32[]{:S(2)}) copy-start(f32[1,1,512]{2,1,0:T(1,128)} %copy-done.52) | copy-start | bytes 6148
  96.4 10.4 %copy-start.55 = (f32[1,1,512]{2,1,0:T(1,128)S(1)}, f32[1,1,512]{2,1,0:T(1,128)}, u32[]{:S(2)}) copy-start(f32[1,1,512]{2,1,0:T(1,128)} %copy-done.54) | copy-start | bytes 6148
  96.5 11.2 %copy-start.33 = (f32[1,1,512]{2,1,0:T(1,128)S(1)}, f32[1,1,512]{2,1,0:T(1,128)}, u32[]{:S(2)}) copy-start(f32[1,1,512]{2,1,0:T(1,128)} %copy-done.32) | copy-start | bytes 6148
  96.5 11.2 %copy-start.35 = (f32[1,1,512]{2,1,0:T(1,128)S(1)}, f32[1,1,512]{2,1,0:T(1,128)}, u32[]{:S(2)}) copy-start(f32[1,1,512]{2,1,0:T(1,128)} %copy-done.34) | copy-start | bytes 6148
  96.5 11.2 %copy-start.37 = (f32[1,1,512]{2,1,0:T(1,128)S(1)}, f32[1,1,512]{2,1,0:T(1,128)}, u32[]{:S(2)}) copy-start(f32[1,1,512]{2,1,0:T(1,128)} %copy-done.36) | copy-start | bytes 6148
  96.5 11.2 %copy-start.39 = (f32[1,1,512]{2,1,0:T(1,128)S(1)}, f32[1,1,512]{2,1,0:T(1,128)}, u32[]{:S(2)}) copy-start(f32[1,1,512]{2,1,0:T(1,128)} %copy-done.38) | copy-start | bytes 6148
  96.5 11.2 %copy-start.41 = (f32[1,1,512]{2,1,0:T(1,128)S(1)}, f32[1,1,512]{2,1,0:T(1,128)}, u32[]{:S(2)}) copy-start(f32[1,1,512]{2,1,0:T(1,128)} %copy-done.40) | copy-start | bytes 6148
  96.5 11.2 %copy-start.57 = (f32[1,1,512]{2,1,0:T(1,128)S(1)}, f32[1,1,512]{2,1,0:T(1,128)}, u32[]{:S(2)}) copy-start(f32[1,1,512]{2,1,0:T(1,128)} %copy-done.56) | copy-start | bytes 6148
  96.5 11.2 %copy-start.59 = (f32[1,1,512]{2,1,0:T(1,128)S(1)}, f32[1,1,512]{2,1,0:T(1,128)}, u32[]{:S(2)}) copy-start(f32[1,1,512]{2,1,0:T(1,128)} %copy-done.58) | copy-start | bytes 6148
  96.6 12.0 %copy-start.19 = (f32[1,1,512]{2,1,0:T(1,128)S(1)}, f32[1,1,512]{2,1,0:T(1,128)}, u32[]{:S(2)}) copy-start(f32[1,1,512]{2,1,0:T(1,128)} %copy-done.18) | copy-start | bytes 6148
  96.6 12.0 %copy-start.21 = (f32[1,1,512]{2,1,0:T(1,128)S(1)}, f32[1,1,512]{2,1,0:T(1,128)}, u32[]{:S(2)}) copy-start(f32[1,1,512]{2,1,0:T(1,128)} %copy-done.20) | copy-start | bytes 6148
  96.6 12.0 %copy-start.23 = (f32[1,1,512]{2,1,0:T(1,128)S(1)}, f32[1,1,512]{2,1,0:T(1,128)}, u32[]{:S(2)}) copy-start(f32[1,1,512]{2,1,0:T(1,128)} %copy-done.22) | copy-start | bytes 6148
  96.6 12.0 %copy-start.25 = (f32[1,1,512]{2,1,0:T(1,128)S(1)}, f32[1,1,512]{2,1,0:T(1,128)}, u32[]{:S(2)}) copy-start(f32[1,1,512]{2,1,0:T(1,128)} %copy-done.24) | copy-start | bytes 6148
  96.6 12.0 %copy-start.27 = (f32[1,1,512]{2,1,0:T(1,128)S(1)}, f32[1,1,512]{2,1,0:T(1,128)}, u32[]{:S(2)}) copy-start(f32[1,1,512]{2,1,0:T(1,128)} %copy-done.26) | copy-start | bytes 6148
  96.6 12.0 %copy-start.29 = (f32[1,1,512]{2,1,0:T(1,128)S(1)}, f32[1,1,512]{2,1,0:T(1,128)}, u32[]{:S(2)}) copy-start(f32[1,1,512]{2,1,0:T(1,128)} %copy-done.28) | copy-start | bytes 6148
  96.6 12.0 %copy-start.31 = (f32[1,1,512]{2,1,0:T(1,128)S(1)}, f32[1,1,512]{2,1,0:T(1,128)}, u32[]{:S(2)}) copy-start(f32[1,1,512]{2,1,0:T(1,128)} %copy-done.30) | copy-start | bytes 6148
  98.8 7.9 %collective-permute-start.7 = (bf16[3,6,512]{2,1,0:T(8,128)(2,1)S(1)}, bf16[3,6,512]{2,1,0:T(8,128)(2,1)S(1)}, u32[]{:S(2)}, u32[]{:S(2)}) collective-permute-start(bf16[3,6,512]{2,1,0:T(8,128)(2,1)S(1)} %pad_maximum_fusion.13), channel_id=1, source_target_pairs={{8,0},{16,8},{24,16},{32,24},{40,32},{48,40},{56,48},{64,56},{72,6... | collective-permute-start | bytes 55304 | tf_op jit(solution)/shard_map/ppermute | solution.py:19
  (4 other events, 9.8 us)

commit v4 on v3

--- a/solution.py
+++ b/solution.py
@@ -50,23 +50,32 @@
     return lhs + jnp.einsum(spec, low, values, preferred_element_type=jnp.float32)
 
 
-def cube_scan(tot_fwd, tot_bwd, unit_decay, axis, size, index):
+def cube_coefficients(size, index):
+    terms = []
+    shift = 1
+    while shift < size:
+        offset = (index % shift).astype(jnp.float32)
+        terms += [jnp.float32(shift), offset, shift - 1 - offset]
+        shift *= 2
+    return terms
+
+
+def cube_scan(tot_fwd, tot_bwd, factors, axis, size, index):
     pre_fwd = jnp.zeros_like(tot_fwd)
     pre_bwd = jnp.zeros_like(tot_bwd)
     shift = 1
+    step = 0
     while shift < size:
         pairs = [(source, source ^ shift) for source in range(size)]
         got = lax.ppermute(jnp.stack([tot_fwd, tot_bwd]), axis, pairs)
         upper = (index & shift) != 0
-        offset = (index % shift).astype(jnp.float32)
-        span = jnp.exp(-unit_decay * shift)
-        pre_fwd = jnp.where(upper, pre_fwd + jnp.exp(-unit_decay * offset) * got[0], pre_fwd)
-        pre_bwd = jnp.where(
-            upper, pre_bwd, pre_bwd + jnp.exp(-unit_decay * (shift - 1 - offset)) * got[1]
-        )
+        span, lead, trail = factors[step], factors[step + 1], factors[step + 2]
+        pre_fwd = jnp.where(upper, pre_fwd + lead * got[0], pre_fwd)
+        pre_bwd = jnp.where(upper, pre_bwd, pre_bwd + trail * got[1])
         tot_fwd = jnp.where(upper, span * got[0] + tot_fwd, span * tot_fwd + got[0])
         tot_bwd = jnp.where(upper, got[1] + span * tot_bwd, tot_bwd + span * got[1])
         shift *= 2
+        step += 3
     return pre_fwd, tot_fwd, pre_bwd, tot_bwd
 
 
@@ -116,15 +125,21 @@
     start_state = own_block(split_dot("ks,sc->kc", start_rows, grad_conv))
     decay_step = jnp.repeat(rates.T, GROUP, axis=1) * block_len
     member = lax.axis_index("xc")
+    outer = lax.axis_size("zl")
+    band = lax.axis_index("zl")
+    place = member.astype(jnp.float32)
+    inner_terms = cube_coefficients(inner, member)
+    outer_terms = [inner * term for term in cube_coefficients(outer, band)]
+    terms = jnp.stack(inner_terms + outer_terms + [place, inner - 1 - place])
+    factors = jnp.exp(-decay_step[None] * terms[:, None, None])
     pre_fwd, group_fwd, pre_bwd, group_bwd = cube_scan(
-        end_state, start_state, decay_step, "xc", inner, member
+        end_state, start_state, factors, "xc", inner, member
     )
     outer_fwd, _, outer_bwd, _ = cube_scan(
-        group_fwd, group_bwd, decay_step * inner, "zl", lax.axis_size("zl"), lax.axis_index("zl")
+        group_fwd, group_bwd, factors[len(inner_terms) :], "zl", outer, band
     )
-    place = member.astype(jnp.float32)
-    entering = pre_fwd + jnp.exp(-decay_step * place) * outer_fwd
-    leaving = pre_bwd + jnp.exp(-decay_step * (inner - 1 - place)) * outer_bwd
+    entering = pre_fwd + factors[-2] * outer_fwd
+    leaving = pre_bwd + factors[-1] * outer_bwd
 
     local_conv = split_dot("gts,sgc->tgc", toeplitz, signal).reshape(block_len, channels)
     local_grad = split_dot("gts,tgc->sgc", toeplitz, cotangent).reshape(block_len, channels)

time: 111 us -> 94.7 us (0.85)
  local copies, waits for them, and re-layouts: 33.6 us -> 11.6 us
  other arithmetic: 15.4 us -> 22.3 us
  waiting for transfers between devices: 18.1 us -> 16.9 us
    exp x17 -> x0, local copies, waits for them, and re-layouts: 13 us -> none  [the longest x6 4.57 us: cube_scan(): jnp.exp(-unit_decay * offset) * got[0]]
    broadcast_in_dim x17 -> x1, local copies, waits for them, and re-layouts: 12.5 us -> 0.12 us  [shards(): decay_step = jnp.repeat(rates.T, GROUP, axis=1) * block_len]
    convert_element_type x7, other arithmetic: 1.54 us -> 4.97 us  [rounded(): return lax.optimization_barrier(values.astype(jnp.bfloat16))]
    ppermute x6, waiting for transfers between devices: 16.7 us -> 14.9 us  [cube_scan(): got = lax.ppermute(jnp.stack([tot_fwd, tot_bwd]), axis, pairs)]
    convert_element_type x3, other arithmetic: 0.06 us -> 1.66 us  [short_causal(): inputs.astype(jnp.float32)]
    unnamed x121 -> x109, local copies, waits for them, and re-layouts: 0.34 us -> 1.92 us
    convert_element_type x2, other arithmetic: 0.09 us -> 1.49 us  [split_dot(): low = (table - high).astype(jnp.bfloat16)]
    exp x1, other arithmetic: 1.45 us -> 0.16 us  [shards(): factors = jnp.exp(-decay_step[None] * terms[:, None, None])]
  transfers between devices with their start and end apart: 8 -> 8, of which waited for: 6 -> 6; matrix products, arithmetic and copies ran while one was open for 37% -> 23% of each run, Pallas kernels for 0% -> 0%
where the time goes in v4:
time: 94.7 us; the launch traced here: 93.6 us
  starting transfers between devices  29.3 us (31%)
  other arithmetic  22.3 us (24%)
  waiting for transfers between devices  16.9 us (18%)
  matrix products  11.9 us (13%)
  local copies, waits for them, and re-layouts  11.6 us (12%)
  between operations  1.65 us (2%)
    ppermute x6, starting transfers between devices, cube_scan(): got = lax.ppermute(jnp.stack([tot_fwd, tot_bwd]), axis, pairs)  18.5 us
    ppermute x6, waiting for transfers between devices, cube_scan(): got = lax.ppermute(jnp.stack([tot_fwd, tot_bwd]), axis, pairs)  14.9 us
    ppermute x2, starting transfers between devices, from_behind(): lax.ppermute(value, axis, [(source, source + steps) for source in range(l...  10.8 us
    convert_element_type x7, other arithmetic, rounded(): return lax.optimization_barrier(values.astype(jnp.bfloat16))  4.97 us
    dot_general x1, matrix products, shards(): toeplitz = jnp.einsum('gtm,gms->gts', falling, rising, precision=precise)  3.65 us
    dot_general x4, matrix products, split_dot(): jnp.einsum(spec, low, values, preferred_element_type=jnp.float32)  3.02 us
    another operation x6, other arithmetic, cube_scan(): got = lax.ppermute(jnp.stack([tot_fwd, tot_bwd]), axis, pairs)  2.56 us
    select_n x5, other arithmetic, cube_scan(): tot_fwd = jnp.where(upper, span * got[0] + tot_fwd, span * tot_fwd + got[0])  2.5 us
  transfers between devices with their start and end apart: 8, of which 6 were waited for; matrix products, arithmetic and copies ran while one was open for 23% of the time, Pallas kernels for 0%

profile of v4, /device:TPU:1, one launch (start us, length us, event | category | flops | bytes accessed | tf_op | source)
XLA Modules:
  0.0 93.6 jit_solution(14733096240638096814)
XLA Ops:
  0.6 0.7 slice_bitcast_fusion.11
  1.4 0.7 slice_bitcast_fusion.9
  2.1 0.6 pad_maximum_fusion.12
  2.7 4.5 %collective-permute-start = (bf16[3,6,512]{2,1,0:T(8,128)(2,1)}, bf16[3,6,512]{2,1,0:T(8,128)(2,1)}, u32[]{:S(2)}, u32[]{:S(2)}) collective-permute-start(bf16[3,6,512]{2,1,0:T(8,128)(2,1)} %pad_maximum_fusion.12), channel_id=1, source_target_pairs={{0,8},{8,16},{16,24},{24,32},{32,40},{40,48},{48,56},{56,64},{64,7... | collective-permute-start | bytes 55304 | tf_op jit(solution)/shard_map/ppermute | solution.py:19
  7.2 0.8 copy.24
  8.0 0.7 negate_bitcast_fusion
  9.0 0.8 fusion.170
  9.9 0.7 fusion.18
  10.8 0.7 fusion.171
  11.4 0.6 fusion.144
  12.1 0.7 fusion.17
  12.8 3.7 %fusion.129 = f32[32,128,128]{2,1,0:T(8,128)S(1)} fusion(f32[32,16]{1,0:T(8,128)S(1)} %copy.24, f32[128]{0:T(128)S(1)} %get-tuple-element.60, f32[128]{0:T(128)S(1)} %get-tuple-element.61, f32[32,16]{1,0:T(8,128)S(1)} %copy.23), kind=kOutput, calls=%fused_computation.207 | convolution fusion | flops 100859904 | bytes 2102272 | tf_op jit(solution)/shard_map/gtm,gms->gts/dot_general | solution.py:106
  16.5 0.6 fusion.172
  17.1 0.7 convert_element_type.195
  17.8 0.9 convert_element_type.200
  18.9 0.8 neg.35
  19.8 0.8 fusion.160
  20.6 0.9 fusion.108
  21.6 2.2 %fusion.91 = bf16[128,512]{1,0:T(8,128)(2,1)S(1)} fusion(f32[6,512]{1,0:T(8,128)S(1)} %get-tuple-element.54, f32[128,512]{1,0:T(8,128)} %convert_element_type.195, f32[512]{0:T(512)} %bitcast.157, f32[512]{0:T(512)} %bitcast.159, f32[512]{0:T(512)} %bitcast.161, f32[512]{0:T(512)} %bitcast.163, f32[512]{0:T(512)} %bitcast.165, f32[512]{0:T(512)} %bitcast.167, ...), kind=kLoop, calls=%fused_computation.145 | loop fusion | flops 1310720 | bytes 419840 | tf_op jit(solution)/shard_map/convert_element_type | solution.py:23
  23.8 1.0 %fusion.74 = bf16[128,512]{1,0:T(8,128)(2,1)S(1)} fusion(f32[6,512]{1,0:T(8,128)S(1)} %get-tuple-element.53, f32[128,512]{1,0:T(8,128)S(1)} %convert_element_type.200, f32[512]{0:T(512)} %bitcast.173, f32[512]{0:T(512)} %bitcast.171, f32[512]{0:T(512)} %bitcast.147, f32[512]{0:T(512)} %bitcast.149, f32[512]{0:T(512)} %bitcast.151, f32[512]{0:T(512)} %bitcast.153, ...), kind=kLoop, calls=%fused_computation.128 | loop fusion | flops 1310720 | bytes 419840 | tf_op jit(solution)/shard_map/convert_element_type | solution.py:23
  24.9 0.3 fusion.173
  25.2 0.3 convolution_add_fusion.1
  25.5 0.3 copy-done.13
  25.8 0.3 fusion.174
  26.1 0.3 convolution_add_fusion
  26.4 1.2 %fusion.8 = (f32[16,512]{1,0:T(8,128)S(1)}, f32[16,512]{1,0:T(8,128)S(1)}) fusion(f32[32,16,512]{2,1,0:T(8,128)S(1)} %bitcast.123, f32[32,512]{1,0:T(8,128)S(1)} %copy-done.8, f32[32,16,512]{2,1,0:T(8,128)S(1)} %bitcast.124), kind=kLoop, calls=%fused_computation.18 | loop fusion | flops 1032192 | bytes 2228224 | tf_op jit(solution)/shard_map/reduce_sum | solution.py:117
  27.7 0.6 pad_maximum_fusion.6
  28.3 6.1 %collective-permute-start.1 = (f32[2,16,512]{2,1,0:T(8,128)}, f32[2,16,512]{2,1,0:T(8,128)}, u32[]{:S(2)}, u32[]{:S(2)}) collective-permute-start(f32[2,16,512]{2,1,0:T(8,128)} %pad_maximum_fusion.6), channel_id=1, source_target_pairs={{0,8},{8,0},{16,24},{24,16},{32,40},{40,32},{48,56},{56,48},{1,9},... | collective-permute-start | bytes 196616 | tf_op jit(solution)/shard_map/ppermute | solution.py:70
  34.6 1.8 %rev.7 = f32[32,16,128]{2,1,0:T(8,128)} reverse(f32[32,16,128]{2,1,0:T(8,128)} %get-tuple-element.16), dimensions={2} | reverse | bytes 524288 | tf_op jit(solution)/shard_map/rev | solution.py:147
  36.4 0.8 add_select_fusion.17
  37.3 0.6 pad_maximum_fusion.7
  37.9 1.9 %collective-permute-start.2 = (f32[2,16,512]{2,1,0:T(8,128)}, f32[2,16,512]{2,1,0:T(8,128)}, u32[]{:S(2)}, u32[]{:S(2)}) collective-permute-start(f32[2,16,512]{2,1,0:T(8,128)} %pad_maximum_fusion.7), channel_id=1, source_target_pairs={{0,16},{8,24},{16,0},{24,8},{32,48},{40,56},{48,32},{56,40},{1,17}... | collective-permute-start | bytes 196616 | tf_op jit(solution)/shard_map/ppermute | solution.py:70
  39.9 0.8 copy.32
  40.6 3.2 %collective-permute-done.2 = f32[2,16,512]{2,1,0:T(8,128)} collective-permute-done((f32[2,16,512]{2,1,0:T(8,128)}, f32[2,16,512]{2,1,0:T(8,128)}, u32[]{:S(2)}, u32[]{:S(2)}) %collective-permute-start.2) | collective-permute-done | bytes 65568 | tf_op jit(solution)/shard_map/ppermute | solution.py:70
  43.8 0.8 add_select_fusion.15
  44.7 1.9 %collective-permute-start.3 = (f32[2,16,512]{2,1,0:T(8,128)S(1)}, f32[2,16,512]{2,1,0:T(8,128)S(1)}, u32[]{:S(2)}, u32[]{:S(2)}) collective-permute-start(f32[2,16,512]{2,1,0:T(8,128)S(1)} %pad_maximum_fusion.8), channel_id=1, source_target_pairs={{0,32},{8,40},{16,48},{24,56},{32,0},{40,8},{48,16},{56,24},{1,33}... | collective-permute-start | bytes 196616 | tf_op jit(solution)/shard_map/ppermute | solution.py:70
  46.6 1.3 %fusion.9 = f32[32,16,128]{2,1,0:T(8,128)S(1)} fusion(bf16[128,32,16]{0,2,1:T(8,128)(2,1)} %bitcast.127, f32[32,128,128]{2,1,0:T(8,128)S(1)} %fusion.129, pred[128,128]{1,0:T(8,128)(4,1)S(1)} %iota_compare_fusion.1), kind=kOutput, calls=%fused_computation.63 | convolution fusion | flops 18350080 | bytes 2506752 | tf_op jit(solution)/shard_map/gts,tgc->sgc/dot_general | solution.py:49
  47.9 3.3 %collective-permute-done.3 = f32[2,16,512]{2,1,0:T(8,128)S(1)} collective-permute-done((f32[2,16,512]{2,1,0:T(8,128)S(1)}, f32[2,16,512]{2,1,0:T(8,128)S(1)}, u32[]{:S(2)}, u32[]{:S(2)}) %collective-permute-start.3) | collective-permute-done | bytes 65568 | tf_op jit(solution)/shard_map/ppermute | solution.py:70
  51.2 0.6 copy-done.18
  51.8 0.6 pad_maximum_fusion.9
  52.5 1.9 %collective-permute-start.4 = (f32[2,16,512]{2,1,0:T(8,128)}, f32[2,16,512]{2,1,0:T(8,128)}, u32[]{:S(2)}, u32[]{:S(2)}) collective-permute-start(f32[2,16,512]{2,1,0:T(8,128)} %pad_maximum_fusion.9), channel_id=1, source_target_pairs={{0,64},{64,0},{128,192},{192,128},{256,320},{320,256},{384,448},{4... | collective-permute-start | bytes 196616 | tf_op jit(solution)/shard_map/ppermute | solution.py:70
  54.4 1.1 %convolution_add_fusion.2 = f32[32,16,128]{2,1,0:T(8,128)} fusion(f32[32,16,128]{2,1,0:T(8,128)S(1)} %fusion.9, bf16[128,32,16]{0,2,1:T(8,128)(2,1)S(1)} %bitcast.128, f32[32,128,128]{2,1,0:T(8,128)S(1)} %fusion.129, pred[128,128]{1,0:T(8,128)(4,1)S(1)} %iota_compare_fusion.1), kind=kOutput, calls=%fused_computation.7 | convolution fusion | flops 18939904 | bytes 2768896 | tf_op jit(solution)/shard_map/gts,tgc->sgc/dot_general | solution.py:50
  55.6 2.1 %collective-permute-done.4 = f32[2,16,512]{2,1,0:T(8,128)} collective-permute-done((f32[2,16,512]{2,1,0:T(8,128)}, f32[2,16,512]{2,1,0:T(8,128)}, u32[]{:S(2)}, u32[]{:S(2)}) %collective-permute-start.4) | collective-permute-done | bytes 65568 | tf_op jit(solution)/shard_map/ppermute | solution.py:70
  57.8 0.8 add_select_fusion.11
  58.6 1.9 %collective-permute-start.5 = (f32[2,16,512]{2,1,0:T(8,128)S(1)}, f32[2,16,512]{2,1,0:T(8,128)S(1)}, u32[]{:S(2)}, u32[]{:S(2)}) collective-permute-start(f32[2,16,512]{2,1,0:T(8,128)S(1)} %pad_maximum_fusion.10), channel_id=1, source_target_pairs={{0,128},{64,192},{128,0},{192,64},{256,384},{320,448},{384,256},{4... | collective-permute-start | bytes 196616 | tf_op jit(solution)/shard_map/ppermute | solution.py:70
  60.5 0.6 fusion.10
  61.2 3.8 %collective-permute-done.5 = f32[2,16,512]{2,1,0:T(8,128)S(1)} collective-permute-done((f32[2,16,512]{2,1,0:T(8,128)S(1)}, f32[2,16,512]{2,1,0:T(8,128)S(1)}, u32[]{:S(2)}, u32[]{:S(2)}) %collective-permute-start.5) | collective-permute-done | bytes 65568 | tf_op jit(solution)/shard_map/ppermute | solution.py:70
  65.0 0.6 pad_maximum_fusion.11
  65.6 4.7 %collective-permute-start.6 = (f32[2,16,512]{2,1,0:T(8,128)}, f32[2,16,512]{2,1,0:T(8,128)}, u32[]{:S(2)}, u32[]{:S(2)}) collective-permute-start(f32[2,16,512]{2,1,0:T(8,128)} %pad_maximum_fusion.11), channel_id=1, source_target_pairs={{0,256},{64,320},{128,384},{192,448},{256,0},{320,64},{384,128},{4... | collective-permute-start | bytes 196616 | tf_op jit(solution)/shard_map/ppermute | solution.py:70
  70.3 1.4 %convolution_add_fusion.3 = f32[32,16,128]{2,1,0:T(8,128)} fusion(f32[32,16,128]{2,1,0:T(8,128)S(1)} %fusion.10, bf16[128,32,16]{0,2,1:T(8,128)(2,1)S(1)} %bitcast.126, f32[32,128,128]{2,1,0:T(8,128)S(1)} %fusion.129, pred[128,128]{1,0:T(8,128)(4,1)S(1)} %iota_compare_fusion.1), kind=kOutput, calls=%fused_computation.8 | convolution fusion | flops 18939904 | bytes 2768896 | tf_op jit(solution)/shard_map/gts,sgc->tgc/dot_general | solution.py:50
  71.7 1.1 %copy.34 = f32[128,512]{1,0:T(8,128)S(1)} copy(f32[128,512]{0,1:T(8,128)} %bitcast.129) | data formatting | bytes 524288 | tf_op jit(solution)/shard_map/reshape | solution.py:145
  72.8 1.1 %copy.31 = f32[128,512]{1,0:T(8,128)S(1)} copy(f32[128,512]{0,1:T(8,128)} %bitcast.130) | data formatting | bytes 524288 | tf_op jit(solution)/shard_map/reshape | solution.py:144
  73.9 2.5 %collective-permute-done.6 = f32[2,16,512]{2,1,0:T(8,128)} collective-permute-done((f32[2,16,512]{2,1,0:T(8,128)}, f32[2,16,512]{2,1,0:T(8,128)}, u32[]{:S(2)}, u32[]{:S(2)}) %collective-permute-start.6) | collective-permute-done | bytes 65568 | tf_op jit(solution)/shard_map/ppermute | solution.py:70
  76.4 0.9 fusion.149
  77.3 0.9 fusion.146
  78.2 0.3 broadcast_multiply_fusion
  78.5 1.4 %fusion.3 = bf16[128,512]{1,0:T(8,128)(2,1)S(1)} fusion(f32[128,512]{1,0:T(8,128)S(1)} %copy.34, f32[32,16,512]{2,0,1:T(8,128)S(1)} %get-tuple-element.26, f32[32,16,128]{2,1,0:T(8,128)S(1)} %copy-done.7, f32[32,16]{1,0:T(8,128)S(1)} %copy-done.23), kind=kOutput, calls=%fused_computation.11 | convolution fusion | flops 402849792 | bytes 1705984 | tf_op jit(solution)/shard_map/ks,kc->sc/dot_general | solution.py:151
  80.2 1.4 %fusion.4 = bf16[128,512]{1,0:T(8,128)(2,1)S(1)} fusion(f32[128,512]{1,0:T(8,128)S(1)} %copy.31, f32[32,16,512]{2,0,1:T(8,128)S(1)} %get-tuple-element.27, f32[32,16]{1,0:T(8,128)S(1)} %copy-done.23, f32[32,16,129]{2,1,0:T(8,128)S(1)} %multiply_exponential_fusion.1), kind=kOutput, calls=%fused_computation.12 | convolution fusion | flops 402849792 | bytes 1720320 | tf_op jit(solution)/shard_map/kt,kc->tc/dot_general | solution.py:150
  81.7 0.7 fusion.14
  82.4 6.3 %collective-permute-start.7 = (bf16[3,6,512]{2,1,0:T(8,128)(2,1)S(1)}, bf16[3,6,512]{2,1,0:T(8,128)(2,1)S(1)}, u32[]{:S(2)}, u32[]{:S(2)}) collective-permute-start(bf16[3,6,512]{2,1,0:T(8,128)(2,1)S(1)} %pad_maximum_fusion.13), channel_id=1, source_target_pairs={{8,0},{16,8},{24,16},{32,24},{40,32},{48,40},{56,48},{64,56},{72,6... | collective-permute-start | bytes 55304 | tf_op jit(solution)/shard_map/ppermute | solution.py:19
  88.8 2.0 %collective-permute-done.7 = bf16[3,6,512]{2,1,0:T(8,128)(2,1)S(1)} collective-permute-done((bf16[3,6,512]{2,1,0:T(8,128)(2,1)S(1)}, bf16[3,6,512]{2,1,0:T(8,128)(2,1)S(1)}, u32[]{:S(2)}, u32[]{:S(2)}) %collective-permute-start.7) | collective-permute-done | bytes 18464 | tf_op jit(solution)/shard_map/ppermute | solution.py:19
  90.8 0.9 fusion.40
  91.8 0.9 fusion.23
  92.7 0.9 fusion.57
  (136 shorter events, 1.5 us)
Async XLA Ops:
  0.6 10.1 %copy-start.30 = (f32[3,7,512]{2,1,0:T(8,128)S(1)}, f32[3,7,512]{2,1,0:T(8,128)}, u32[]{:S(2)}) copy-start(f32[3,7,512]{2,1,0:T(8,128)} %param.10) | copy-start | bytes 129028
  2.7 17.1 %collective-permute-start = (bf16[3,6,512]{2,1,0:T(8,128)(2,1)}, bf16[3,6,512]{2,1,0:T(8,128)(2,1)}, u32[]{:S(2)}, u32[]{:S(2)}) collective-permute-start(bf16[3,6,512]{2,1,0:T(8,128)(2,1)} %pad_maximum_fusion.12), channel_id=1, source_target_pairs={{0,8},{8,16},{16,24},{24,32},{32,40},{40,48},{48,56},{56,64},{64,7... | collective-permute-start | bytes 55304 | tf_op jit(solution)/shard_map/ppermute | solution.py:19
  9.8 7.3 %copy-start.27 = (bf16[128,512]{1,0:T(8,128)(2,1)S(1)}, bf16[128,512]{1,0:T(8,128)(2,1)}, u32[]{:S(2)}) copy-start(bf16[128,512]{1,0:T(8,128)(2,1)} %param.7) | copy-start | bytes 393220
  9.8 7.3 %copy-start.28 = (bf16[128,512]{1,0:T(8,128)(2,1)S(1)}, bf16[128,512]{1,0:T(8,128)(2,1)}, u32[]{:S(2)}) copy-start(bf16[128,512]{1,0:T(8,128)(2,1)} %param.8) | copy-start | bytes 393220
  10.8 8.0 %copy-start.22 = (f32[32,16]{1,0:T(8,128)}, f32[32,16]{1,0:T(8,128)S(1)}, u32[]{:S(2)}) copy-start(f32[32,16]{1,0:T(8,128)S(1)} %copy.23) | copy-start | bytes 6148
  11.4 9.2 %copy-start.31 = (f32[1,1,512]{2,1,0:T(1,128)}, f32[1,1,512]{2,1,0:T(1,128)S(1)}, u32[]{:S(2)}) copy-start(f32[1,1,512]{2,1,0:T(1,128)S(1)} %get-tuple-element.28) | copy-start | bytes 6148
  11.4 9.2 %copy-start.33 = (f32[1,1,512]{2,1,0:T(1,128)}, f32[1,1,512]{2,1,0:T(1,128)S(1)}, u32[]{:S(2)}) copy-start(f32[1,1,512]{2,1,0:T(1,128)S(1)} %get-tuple-element.41) | copy-start | bytes 6148
  12.8 8.7 %copy-start.10 = (bf16[128,512]{1,0:T(8,128)(2,1)S(1)}, bf16[128,512]{1,0:T(8,128)(2,1)}, u32[]{:S(2)}) copy-start(bf16[128,512]{1,0:T(8,128)(2,1)} %param.13) | copy-start | bytes 393220
  19.8 5.1 %copy-start.15 = (bf16[512,128]{1,0:T(8,128)(2,1)S(1)}, bf16[512,128]{1,0:T(8,128)(2,1)}, u32[]{:S(2)}) copy-start(bf16[512,128]{1,0:T(8,128)(2,1)} %get-tuple-element.21) | copy-start | bytes 393220
  19.8 5.4 %copy-start.14 = (bf16[512,128]{1,0:T(8,128)(2,1)S(1)}, bf16[512,128]{1,0:T(8,128)(2,1)}, u32[]{:S(2)}) copy-start(bf16[512,128]{1,0:T(8,128)(2,1)} %get-tuple-element.20) | copy-start | bytes 393220
  21.6 3.9 %copy-start = (bf16[128,512]{1,0:T(8,128)(2,1)}, bf16[128,512]{1,0:T(8,128)(2,1)S(1)}, u32[]{:S(2)}) copy-start(bf16[128,512]{1,0:T(8,128)(2,1)S(1)} %fusion.108) | copy-start | bytes 393220
  23.8 1.6 %copy-start.2 = (bf16[128,512]{1,0:T(8,128)(2,1)}, bf16[128,512]{1,0:T(8,128)(2,1)S(1)}, u32[]{:S(2)}) copy-start(bf16[128,512]{1,0:T(8,128)(2,1)S(1)} %fusion.91) | copy-start | bytes 393220
  24.8 1.2 %copy-start.4 = (bf16[128,512]{1,0:T(8,128)(2,1)}, bf16[128,512]{1,0:T(8,128)(2,1)S(1)}, u32[]{:S(2)}) copy-start(bf16[128,512]{1,0:T(8,128)(2,1)S(1)} %fusion.74) | copy-start | bytes 393220
  24.8 1.0 %copy-start.13 = (bf16[512,128]{1,0:T(8,128)(2,1)S(1)}, bf16[512,128]{1,0:T(8,128)(2,1)}, u32[]{:S(2)}) copy-start(bf16[512,128]{1,0:T(8,128)(2,1)} %get-tuple-element.19) | copy-start | bytes 393220
  25.2 0.9 copy-start.12
  25.5 0.9 copy-start.8
  26.1 8.3 %copy-start.29 = (f32[16,512]{1,0:T(8,128)S(1)}, f32[16,512]{1,0:T(8,128)}, u32[]{:S(2)}) copy-start(f32[16,512]{1,0:T(8,128)} %neg.35) | copy-start | bytes 98308
  27.6 0.7 copy-start.16
  27.6 0.7 copy-start.17
  28.3 8.1 %collective-permute-start.1 = (f32[2,16,512]{2,1,0:T(8,128)}, f32[2,16,512]{2,1,0:T(8,128)}, u32[]{:S(2)}, u32[]{:S(2)}) collective-permute-start(f32[2,16,512]{2,1,0:T(8,128)} %pad_maximum_fusion.6), channel_id=1, source_target_pairs={{0,8},{8,0},{16,24},{24,16},{32,40},{40,32},{48,56},{56,48},{1,9},... | collective-permute-start | bytes 196616 | tf_op jit(solution)/shard_map/ppermute | solution.py:70
  37.2 0.7 copy-start.20
  37.3 2.6 %copy-start.21 = (f32[1,16,512]{2,1,0:T(8,128)}, f32[1,16,512]{2,1,0:T(8,128)S(1)}, u32[]{:S(2)}) copy-start(f32[1,16,512]{2,1,0:T(8,128)S(1)} %get-tuple-element.15) | copy-start | bytes 98308
  37.9 5.9 %collective-permute-start.2 = (f32[2,16,512]{2,1,0:T(8,128)}, f32[2,16,512]{2,1,0:T(8,128)}, u32[]{:S(2)}, u32[]{:S(2)}) collective-permute-start(f32[2,16,512]{2,1,0:T(8,128)} %pad_maximum_fusion.7), channel_id=1, source_target_pairs={{0,16},{8,24},{16,0},{24,8},{32,48},{40,56},{48,32},{56,40},{1,17}... | collective-permute-start | bytes 196616 | tf_op jit(solution)/shard_map/ppermute | solution.py:70
  40.6 13.8 %copy-start.6 = (bf16[128,512]{0,1:T(8,128)(2,1)S(1)}, bf16[128,512]{0,1:T(8,128)(2,1)}, u32[]{:S(2)}) copy-start(bf16[128,512]{0,1:T(8,128)(2,1)} %copy.32) | copy-start | bytes 393220
  44.7 6.5 %collective-permute-start.3 = (f32[2,16,512]{2,1,0:T(8,128)S(1)}, f32[2,16,512]{2,1,0:T(8,128)S(1)}, u32[]{:S(2)}, u32[]{:S(2)}) collective-permute-start(f32[2,16,512]{2,1,0:T(8,128)S(1)} %pad_maximum_fusion.8), channel_id=1, source_target_pairs={{0,32},{8,40},{16,48},{24,56},{32,0},{40,8},{48,16},{56,24},{1,33}... | collective-permute-start | bytes 196616 | tf_op jit(solution)/shard_map/ppermute | solution.py:70
  51.2 3.2 %copy-start.24 = (f32[2,16,512]{2,1,0:T(8,128)}, f32[2,16,512]{2,1,0:T(8,128)S(1)}, u32[]{:S(2)}) copy-start(f32[2,16,512]{2,1,0:T(8,128)S(1)} %collective-permute-done.3) | copy-start | bytes 196612
  51.2 0.6 copy-start.18
  51.2 1.2 %copy-start.19 = (f32[1,16,512]{2,1,0:T(8,128)}, f32[1,16,512]{2,1,0:T(8,128)S(1)}, u32[]{:S(2)}) copy-start(f32[1,16,512]{2,1,0:T(8,128)S(1)} %get-tuple-element.11) | copy-start | bytes 98308
  52.5 5.3 %collective-permute-start.4 = (f32[2,16,512]{2,1,0:T(8,128)}, f32[2,16,512]{2,1,0:T(8,128)}, u32[]{:S(2)}, u32[]{:S(2)}) collective-permute-start(f32[2,16,512]{2,1,0:T(8,128)} %pad_maximum_fusion.9), channel_id=1, source_target_pairs={{0,64},{64,0},{128,192},{192,128},{256,320},{320,256},{384,448},{4... | collective-permute-start | bytes 196616 | tf_op jit(solution)/shard_map/ppermute | solution.py:70
  58.6 6.3 %collective-permute-start.5 = (f32[2,16,512]{2,1,0:T(8,128)S(1)}, f32[2,16,512]{2,1,0:T(8,128)S(1)}, u32[]{:S(2)}, u32[]{:S(2)}) collective-permute-start(f32[2,16,512]{2,1,0:T(8,128)S(1)} %pad_maximum_fusion.10), channel_id=1, source_target_pairs={{0,128},{64,192},{128,0},{192,64},{256,384},{320,448},{384,256},{4... | collective-permute-start | bytes 196616 | tf_op jit(solution)/shard_map/ppermute | solution.py:70
  61.2 15.3 %copy-start.25 = (f32[2,16,512]{2,1,0:T(8,128)S(1)}, f32[2,16,512]{2,1,0:T(8,128)}, u32[]{:S(2)}) copy-start(f32[2,16,512]{2,1,0:T(8,128)} %copy-done.24) | copy-start | bytes 196612
  65.0 6.7 %copy-start.26 = (f32[2,16,512]{2,1,0:T(8,128)}, f32[2,16,512]{2,1,0:T(8,128)S(1)}, u32[]{:S(2)}) copy-start(f32[2,16,512]{2,1,0:T(8,128)S(1)} %collective-permute-done.5) | copy-start | bytes 196612
  65.6 12.6 %copy-start.9 = (f32[32,512]{1,0:T(8,128)S(1)}, f32[32,512]{1,0:T(8,128)}, u32[]{:S(2)}) copy-start(f32[32,512]{1,0:T(8,128)} %fusion.144) | copy-start | bytes 196612
  65.6 10.8 %collective-permute-start.6 = (f32[2,16,512]{2,1,0:T(8,128)}, f32[2,16,512]{2,1,0:T(8,128)}, u32[]{:S(2)}, u32[]{:S(2)}) collective-permute-start(f32[2,16,512]{2,1,0:T(8,128)} %pad_maximum_fusion.11), channel_id=1, source_target_pairs={{0,256},{64,320},{128,384},{192,448},{256,0},{320,64},{384,128},{4... | collective-permute-start | bytes 196616 | tf_op jit(solution)/shard_map/ppermute | solution.py:70
  71.7 6.8 %copy-start.7 = (f32[32,16,128]{2,1,0:T(8,128)S(1)}, f32[32,16,128]{2,1,0:T(8,128)}, u32[]{:S(2)}) copy-start(f32[32,16,128]{2,1,0:T(8,128)} %rev.7) | copy-start | bytes 786436
  71.7 6.8 %copy-start.23 = (f32[32,16]{1,0:T(8,128)S(1)}, f32[32,16]{1,0:T(8,128)}, u32[]{:S(2)}) copy-start(f32[32,16]{1,0:T(8,128)} %copy-done.22) | copy-start | bytes 6148
  77.3 2.6 %copy-start.3 = (bf16[128,512]{1,0:T(8,128)(2,1)S(1)}, bf16[128,512]{1,0:T(8,128)(2,1)}, u32[]{:S(2)}) copy-start(bf16[128,512]{1,0:T(8,128)(2,1)} %copy-done.2) | copy-start | bytes 393220
  77.3 2.6 %copy-start.5 = (bf16[128,512]{1,0:T(8,128)(2,1)S(1)}, bf16[128,512]{1,0:T(8,128)(2,1)}, u32[]{:S(2)}) copy-start(bf16[128,512]{1,0:T(8,128)(2,1)} %copy-done.4) | copy-start | bytes 393220
  78.5 3.2 %copy-start.1 = (bf16[128,512]{1,0:T(8,128)(2,1)S(1)}, bf16[128,512]{1,0:T(8,128)(2,1)}, u32[]{:S(2)}) copy-start(bf16[128,512]{1,0:T(8,128)(2,1)} %copy-done) | copy-start | bytes 393220
  78.5 3.2 %copy-start.11 = (bf16[128,512]{1,0:T(8,128)(2,1)S(1)}, bf16[128,512]{1,0:T(8,128)(2,1)}, u32[]{:S(2)}) copy-start(bf16[128,512]{1,0:T(8,128)(2,1)} %param.13) | copy-start | bytes 393220
  79.9 10.9 %copy-start.45 = (f32[1,1,512]{2,1,0:T(1,128)S(1)}, f32[1,1,512]{2,1,0:T(1,128)}, u32[]{:S(2)}) copy-start(f32[1,1,512]{2,1,0:T(1,128)} %get-tuple-element.34) | copy-start | bytes 6148
  79.9 10.9 %copy-start.46 = (f32[1,1,512]{2,1,0:T(1,128)S(1)}, f32[1,1,512]{2,1,0:T(1,128)}, u32[]{:S(2)}) copy-start(f32[1,1,512]{2,1,0:T(1,128)} %get-tuple-element.35) | copy-start | bytes 6148
  79.9 10.9 %copy-start.47 = (f32[1,1,512]{2,1,0:T(1,128)S(1)}, f32[1,1,512]{2,1,0:T(1,128)}, u32[]{:S(2)}) copy-start(f32[1,1,512]{2,1,0:T(1,128)} %get-tuple-element.36) | copy-start | bytes 6148
  79.9 10.9 %copy-start.48 = (f32[1,1,512]{2,1,0:T(1,128)S(1)}, f32[1,1,512]{2,1,0:T(1,128)}, u32[]{:S(2)}) copy-start(f32[1,1,512]{2,1,0:T(1,128)} %get-tuple-element.37) | copy-start | bytes 6148
  80.0 10.9 %copy-start.49 = (f32[1,1,512]{2,1,0:T(1,128)S(1)}, f32[1,1,512]{2,1,0:T(1,128)}, u32[]{:S(2)}) copy-start(f32[1,1,512]{2,1,0:T(1,128)} %get-tuple-element.38) | copy-start | bytes 6148
  80.0 10.9 %copy-start.50 = (f32[1,1,512]{2,1,0:T(1,128)S(1)}, f32[1,1,512]{2,1,0:T(1,128)}, u32[]{:S(2)}) copy-start(f32[1,1,512]{2,1,0:T(1,128)} %get-tuple-element.39) | copy-start | bytes 6148
  80.0 10.9 %copy-start.51 = (f32[1,1,512]{2,1,0:T(1,128)S(1)}, f32[1,1,512]{2,1,0:T(1,128)}, u32[]{:S(2)}) copy-start(f32[1,1,512]{2,1,0:T(1,128)} %get-tuple-element.40) | copy-start | bytes 6148
  80.0 11.7 %copy-start.40 = (f32[1,1,512]{2,1,0:T(1,128)S(1)}, f32[1,1,512]{2,1,0:T(1,128)}, u32[]{:S(2)}) copy-start(f32[1,1,512]{2,1,0:T(1,128)} %get-tuple-element.29) | copy-start | bytes 6148
  80.1 11.7 %copy-start.41 = (f32[1,1,512]{2,1,0:T(1,128)S(1)}, f32[1,1,512]{2,1,0:T(1,128)}, u32[]{:S(2)}) copy-start(f32[1,1,512]{2,1,0:T(1,128)} %get-tuple-element.30) | copy-start | bytes 6148
  80.1 11.7 %copy-start.42 = (f32[1,1,512]{2,1,0:T(1,128)S(1)}, f32[1,1,512]{2,1,0:T(1,128)}, u32[]{:S(2)}) copy-start(f32[1,1,512]{2,1,0:T(1,128)} %get-tuple-element.31) | copy-start | bytes 6148
  80.1 11.7 %copy-start.43 = (f32[1,1,512]{2,1,0:T(1,128)S(1)}, f32[1,1,512]{2,1,0:T(1,128)}, u32[]{:S(2)}) copy-start(f32[1,1,512]{2,1,0:T(1,128)} %get-tuple-element.32) | copy-start | bytes 6148
  80.1 11.7 %copy-start.44 = (f32[1,1,512]{2,1,0:T(1,128)S(1)}, f32[1,1,512]{2,1,0:T(1,128)}, u32[]{:S(2)}) copy-start(f32[1,1,512]{2,1,0:T(1,128)} %get-tuple-element.33) | copy-start | bytes 6148
  80.1 11.7 %copy-start.52 = (f32[1,1,512]{2,1,0:T(1,128)S(1)}, f32[1,1,512]{2,1,0:T(1,128)}, u32[]{:S(2)}) copy-start(f32[1,1,512]{2,1,0:T(1,128)} %get-tuple-element.47) | copy-start | bytes 6148
  80.1 11.7 %copy-start.53 = (f32[1,1,512]{2,1,0:T(1,128)S(1)}, f32[1,1,512]{2,1,0:T(1,128)}, u32[]{:S(2)}) copy-start(f32[1,1,512]{2,1,0:T(1,128)} %get-tuple-element.48) | copy-start | bytes 6148
  80.1 12.5 %copy-start.32 = (f32[1,1,512]{2,1,0:T(1,128)S(1)}, f32[1,1,512]{2,1,0:T(1,128)}, u32[]{:S(2)}) copy-start(f32[1,1,512]{2,1,0:T(1,128)} %copy-done.31) | copy-start | bytes 6148
  80.1 12.5 %copy-start.34 = (f32[1,1,512]{2,1,0:T(1,128)S(1)}, f32[1,1,512]{2,1,0:T(1,128)}, u32[]{:S(2)}) copy-start(f32[1,1,512]{2,1,0:T(1,128)} %copy-done.33) | copy-start | bytes 6148
  80.2 12.5 %copy-start.35 = (f32[1,1,512]{2,1,0:T(1,128)S(1)}, f32[1,1,512]{2,1,0:T(1,128)}, u32[]{:S(2)}) copy-start(f32[1,1,512]{2,1,0:T(1,128)} %get-tuple-element.42) | copy-start | bytes 6148
  80.2 12.5 %copy-start.36 = (f32[1,1,512]{2,1,0:T(1,128)S(1)}, f32[1,1,512]{2,1,0:T(1,128)}, u32[]{:S(2)}) copy-start(f32[1,1,512]{2,1,0:T(1,128)} %get-tuple-element.43) | copy-start | bytes 6148
  80.2 12.5 %copy-start.37 = (f32[1,1,512]{2,1,0:T(1,128)S(1)}, f32[1,1,512]{2,1,0:T(1,128)}, u32[]{:S(2)}) copy-start(f32[1,1,512]{2,1,0:T(1,128)} %get-tuple-element.44) | copy-start | bytes 6148
  80.2 12.5 %copy-start.38 = (f32[1,1,512]{2,1,0:T(1,128)S(1)}, f32[1,1,512]{2,1,0:T(1,128)}, u32[]{:S(2)}) copy-start(f32[1,1,512]{2,1,0:T(1,128)} %get-tuple-element.45) | copy-start | bytes 6148
  80.2 12.5 %copy-start.39 = (f32[1,1,512]{2,1,0:T(1,128)S(1)}, f32[1,1,512]{2,1,0:T(1,128)}, u32[]{:S(2)}) copy-start(f32[1,1,512]{2,1,0:T(1,128)} %get-tuple-element.46) | copy-start | bytes 6148
  82.4 8.4 %collective-permute-start.7 = (bf16[3,6,512]{2,1,0:T(8,128)(2,1)S(1)}, bf16[3,6,512]{2,1,0:T(8,128)(2,1)S(1)}, u32[]{:S(2)}, u32[]{:S(2)}) collective-permute-start(bf16[3,6,512]{2,1,0:T(8,128)(2,1)S(1)} %pad_maximum_fusion.13), channel_id=1, source_target_pairs={{8,0},{16,8},{24,16},{32,24},{40,32},{48,40},{56,48},{64,56},{72,6... | collective-permute-start | bytes 55304 | tf_op jit(solution)/shard_map/ppermute | solution.py:19

commit v5 on v4

--- a/solution.py
+++ b/solution.py
@@ -60,23 +60,33 @@
     return terms
 
 
-def cube_scan(tot_fwd, tot_bwd, factors, axis, size, index):
-    pre_fwd = jnp.zeros_like(tot_fwd)
-    pre_bwd = jnp.zeros_like(tot_bwd)
+def cube_weights(factors, size, index):
+    rounds = []
     shift = 1
     step = 0
     while shift < size:
-        pairs = [(source, source ^ shift) for source in range(size)]
-        got = lax.ppermute(jnp.stack([tot_fwd, tot_bwd]), axis, pairs)
         upper = (index & shift) != 0
         span, lead, trail = factors[step], factors[step + 1], factors[step + 2]
-        pre_fwd = jnp.where(upper, pre_fwd + lead * got[0], pre_fwd)
-        pre_bwd = jnp.where(upper, pre_bwd, pre_bwd + trail * got[1])
-        tot_fwd = jnp.where(upper, span * got[0] + tot_fwd, span * tot_fwd + got[0])
-        tot_bwd = jnp.where(upper, got[1] + span * tot_bwd, tot_bwd + span * got[1])
+        one = jnp.ones_like(span)
+        zero = jnp.zeros_like(span)
+        keep = jnp.stack([jnp.where(upper, one, span), jnp.where(upper, span, one)])
+        take = jnp.stack([jnp.where(upper, span, one), jnp.where(upper, one, span)])
+        add = jnp.stack([jnp.where(upper, lead, zero), jnp.where(upper, zero, trail)])
+        rounds.append((keep, take, add))
         shift *= 2
         step += 3
-    return pre_fwd, tot_fwd, pre_bwd, tot_bwd
+    return rounds
+
+
+def cube_scan(window, rounds, axis, size):
+    entering = jnp.zeros_like(window)
+    shift = 1
+    for keep, take, add in rounds:
+        arrived = lax.ppermute(window, axis, [(source, source ^ shift) for source in range(size)])
+        entering = entering + add * arrived
+        window = keep * window + take * arrived
+        shift *= 2
+    return entering, window
 
 
 def shards(inner, u_query, u_key, u_value, short_filter, decay_rate, residue, grad_out):
@@ -132,14 +142,12 @@
     outer_terms = [inner * term for term in cube_coefficients(outer, band)]
     terms = jnp.stack(inner_terms + outer_terms + [place, inner - 1 - place])
     factors = jnp.exp(-decay_step[None] * terms[:, None, None])
-    pre_fwd, group_fwd, pre_bwd, group_bwd = cube_scan(
-        end_state, start_state, factors, "xc", inner, member
-    )
-    outer_fwd, _, outer_bwd, _ = cube_scan(
-        group_fwd, group_bwd, factors[len(inner_terms) :], "zl", outer, band
-    )
-    entering = pre_fwd + factors[-2] * outer_fwd
-    leaving = pre_bwd + factors[-1] * outer_bwd
+    inner_rounds = cube_weights(factors, inner, member)
+    outer_rounds = cube_weights(factors[len(inner_terms) :], outer, band)
+    near, group = cube_scan(jnp.stack([end_state, start_state]), inner_rounds, "xc", inner)
+    far, _ = cube_scan(group, outer_rounds, "zl", outer)
+    entering = near[0] + factors[-2] * far[0]
+    leaving = near[1] + factors[-1] * far[1]
 
     local_conv = split_dot("gts,sgc->tgc", toeplitz, signal).reshape(block_len, channels)
     local_grad = split_dot("gts,tgc->sgc", toeplitz, cotangent).reshape(block_len, channels)

time: 94.7 us -> 94.6 us (level)
  other arithmetic: 22.3 us -> 19.9 us
  local copies, waits for them, and re-layouts: 11.6 us -> 12.8 us
    add x0 -> x6, other arithmetic: none -> 6.81 us  [the longest x4 4.22 us: cube_scan(): window = keep * window + take * arrived]
    convert_element_type x7, other arithmetic: 4.97 us -> 1.54 us  [rounded(): return lax.optimization_barrier(values.astype(jnp.bfloat16))]
    another operation x6 -> x1, other arithmetic: 2.56 us -> 0.63 us  [shards(): jnp.stack([end_state, start_state])]
    mul x3 -> x2, other arithmetic: 2.02 us -> 0.28 us  [spread(): state[None] * owner[:, None, :]]
    convert_element_type x3, other arithmetic: 1.66 us -> 0.06 us  [short_causal(): inputs.astype(jnp.float32)]
    unnamed x109 -> x157, local copies, waits for them, and re-layouts: 1.92 us -> 3.5 us
    select_n x5 -> x2, other arithmetic: 2.5 us -> 1.53 us  [the longest x1 0.82 us: cube_weights(): jnp.where(upper, lead, zero)]
  transfers between devices with their start and end apart: 8 -> 8, of which waited for: 6 -> 6; matrix products, arithmetic and copies ran while one was open for 23% -> 25% of each run, Pallas kernels for 0% -> 0%
where the time goes in v5:
time: 94.6 us; the launch traced here: 93.6 us
  starting transfers between devices  29.3 us (31%)
  other arithmetic  19.9 us (21%)
  waiting for transfers between devices  16.9 us (18%)
  local copies, waits for them, and re-layouts  12.8 us (14%)
  matrix products  12.7 us (13%)
  between operations  1.96 us (2%)
    ppermute x6, starting transfers between devices, cube_scan(): lax.ppermute(window, axis, [(source, source ^ shift) for source in range(...  18.5 us
    ppermute x6, waiting for transfers between devices, cube_scan(): lax.ppermute(window, axis, [(source, source ^ shift) for source in range(...  14.9 us
    ppermute x2, starting transfers between devices, from_behind(): lax.ppermute(value, axis, [(source, source + steps) for source in range(l...  10.8 us
    dot_general x1, matrix products, shards(): toeplitz = jnp.einsum('gtm,gms->gts', falling, rising, precision=precise)  4.45 us
    add x4, other arithmetic, cube_scan(): window = keep * window + take * arrived  4.22 us
    unnamed x157, local copies, waits for them, and re-layouts  3.5 us
    dot_general x4, matrix products, split_dot(): jnp.einsum(spec, low, values, preferred_element_type=jnp.float32)  3.05 us
    add x2, other arithmetic, cube_scan(): entering = entering + add * arrived  2.59 us
  transfers between devices with their start and end apart: 8, of which 6 were waited for; matrix products, arithmetic and copies ran while one was open for 25% of the time, Pallas kernels for 0%

profile of v5, /device:TPU:1, one launch (start us, length us, event | category | flops | bytes accessed | tf_op | source)
XLA Modules:
  0.0 93.6 jit_solution(6012442656413938463)
XLA Ops:
  0.6 0.7 slice_bitcast_fusion.11
  1.4 0.7 slice_bitcast_fusion.9
  2.1 0.6 pad_maximum_fusion.7
  2.7 4.5 %collective-permute-start = (bf16[3,6,512]{2,1,0:T(8,128)(2,1)}, bf16[3,6,512]{2,1,0:T(8,128)(2,1)}, u32[]{:S(2)}, u32[]{:S(2)}) collective-permute-start(bf16[3,6,512]{2,1,0:T(8,128)(2,1)} %pad_maximum_fusion.7), channel_id=1, source_target_pairs={{0,8},{8,16},{16,24},{24,32},{32,40},{40,48},{48,56},{56,64},{64,7... | collective-permute-start | bytes 55304 | tf_op jit(solution)/shard_map/ppermute | solution.py:19
  7.2 0.6 convert_add_fusion
  7.8 1.4 %copy.24 = f32[32,16]{1,0:T(8,128)} copy(f32[32,16]{0,1:T(8,128)} %param.11) | data formatting | bytes 4096 | tf_op args[4]
  9.2 0.7 fusion.176
  10.2 0.9 fusion.173
  11.1 0.7 fusion.18
  12.0 0.7 fusion.174
  12.6 0.6 fusion.153
  13.6 0.7 fusion.17
  14.7 4.4 %fusion.129 = f32[32,128,128]{2,1,0:T(8,128)S(1)} fusion(f32[32,16]{1,0:T(8,128)} %copy.24, f32[128]{0:T(128)} %get-tuple-element.76, f32[128]{0:T(128)} %get-tuple-element.77, f32[32,16]{1,0:T(8,128)S(1)} %copy.23), kind=kOutput, calls=%fused_computation.207 | convolution fusion | flops 100859904 | bytes 2102272 | tf_op jit(solution)/shard_map/gtm,gms->gts/dot_general | solution.py:116
  19.3 0.8 slice_select_fusion.7
  20.1 0.8 fusion.175
  21.0 0.7 fusion.163
  21.8 0.2 fusion.108
  22.2 0.2 fusion.91
  22.4 0.3 copy-done
  22.7 0.2 fusion.74
  23.1 0.3 fusion.177
  23.4 0.3 convolution_add_fusion.1
  23.7 0.3 copy-done.15
  23.9 0.3 fusion.178
  24.3 0.3 convolution_add_fusion
  24.6 1.2 %fusion.8 = (f32[16,512]{1,0:T(8,128)S(1)}, f32[16,512]{1,0:T(8,128)S(1)}) fusion(f32[32,16,512]{2,1,0:T(8,128)S(1)} %bitcast.121, f32[32,512]{1,0:T(8,128)S(1)} %copy-done.8, f32[32,16,512]{2,1,0:T(8,128)S(1)} %bitcast.122), kind=kLoop, calls=%fused_computation.18 | loop fusion | flops 1032192 | bytes 2228224 | tf_op jit(solution)/shard_map/reduce_sum | solution.py:127
  25.8 0.6 copy-done.10
  26.4 0.6 pad_maximum_fusion.6
  27.1 6.1 %collective-permute-start.1 = (f32[2,16,512]{2,1,0:T(8,128)}, f32[2,16,512]{2,1,0:T(8,128)}, u32[]{:S(2)}, u32[]{:S(2)}) collective-permute-start(f32[2,16,512]{2,1,0:T(8,128)} %pad_maximum_fusion.6), channel_id=1, source_target_pairs={{0,8},{8,0},{16,24},{24,16},{32,40},{40,32},{48,56},{56,48},{1,9},... | collective-permute-start | bytes 196616 | tf_op jit(solution)/shard_map/ppermute | solution.py:85
  33.2 0.7 slice_select_fusion.6
  33.9 1.8 %rev.7 = f32[32,16,128]{2,1,0:T(8,128)} reverse(f32[32,16,128]{2,1,0:T(8,128)} %get-tuple-element.30), dimensions={2} | reverse | bytes 524288 | tf_op jit(solution)/shard_map/rev | solution.py:155
  35.7 1.6 %fusion.146 = f32[2,16,512]{2,1,0:T(8,128)} fusion(f32[1,16,512]{2,1,0:T(8,128)} %get-tuple-element.9, f32[1,16,512]{2,1,0:T(8,128)} %get-tuple-element.25, f32[2,16,512]{2,1,0:T(8,128)} %collective-permute-done.1, f32[1,16,512]{2,1,0:T(8,128)} %bitcast.133, f32[1,16,512]{2,1,0:T(8,128)} %bitcast.130), kind=kLoop, calls=%fused_computation.226 | loop fusion | flops 98304 | bytes 262144 | tf_op jit(solution)/shard_map/add | solution.py:87
  37.3 1.9 %collective-permute-start.2 = (f32[2,16,512]{2,1,0:T(8,128)}, f32[2,16,512]{2,1,0:T(8,128)}, u32[]{:S(2)}, u32[]{:S(2)}) collective-permute-start(f32[2,16,512]{2,1,0:T(8,128)} %fusion.146), channel_id=1, source_target_pairs={{0,16},{8,24},{16,0},{24,8},{32,48},{40,56},{48,32},{56,40},{1,17}... | collective-permute-start | bytes 196616 | tf_op jit(solution)/shard_map/ppermute | solution.py:85
  39.2 0.8 copy.32
  40.1 3.1 %collective-permute-done.2 = f32[2,16,512]{2,1,0:T(8,128)} collective-permute-done((f32[2,16,512]{2,1,0:T(8,128)}, f32[2,16,512]{2,1,0:T(8,128)}, u32[]{:S(2)}, u32[]{:S(2)}) %collective-permute-start.2) | collective-permute-done | bytes 65568 | tf_op jit(solution)/shard_map/ppermute | solution.py:85
  43.2 1.0 %fusion.147 = f32[2,16,512]{2,1,0:T(8,128)S(1)} fusion(f32[1,16,512]{2,1,0:T(8,128)} %get-tuple-element.10, f32[1,16,512]{2,1,0:T(8,128)} %get-tuple-element.24, f32[2,16,512]{2,1,0:T(8,128)} %collective-permute-done.2, f32[2,16,512]{2,1,0:T(8,128)} %collective-permute-done.1, f32[1,16,512]{2,1,0:T(8,128)} %get-tuple-element.25, ...), kind=kLoop, calls=%fused_computation.230 | loop fusion | flops 180224 | bytes 393216 | tf_op jit(solution)/shard_map/add | solution.py:87
  44.2 1.9 %collective-permute-start.3 = (f32[2,16,512]{2,1,0:T(8,128)S(1)}, f32[2,16,512]{2,1,0:T(8,128)S(1)}, u32[]{:S(2)}, u32[]{:S(2)}) collective-permute-start(f32[2,16,512]{2,1,0:T(8,128)S(1)} %fusion.147), channel_id=1, source_target_pairs={{0,32},{8,40},{16,48},{24,56},{32,0},{40,8},{48,16},{56,24},{1,33}... | collective-permute-start | bytes 196616 | tf_op jit(solution)/shard_map/ppermute | solution.py:85
  46.2 1.3 %fusion.9 = f32[32,16,128]{2,1,0:T(8,128)S(1)} fusion(bf16[128,32,16]{0,2,1:T(8,128)(2,1)} %bitcast.123, f32[32,128,128]{2,1,0:T(8,128)S(1)} %fusion.129, pred[128,128]{1,0:T(8,128)(4,1)S(1)} %iota_compare_fusion.1), kind=kOutput, calls=%fused_computation.63 | convolution fusion | flops 18350080 | bytes 2506752 | tf_op jit(solution)/shard_map/gts,tgc->sgc/dot_general | solution.py:49
  47.4 3.3 %collective-permute-done.3 = f32[2,16,512]{2,1,0:T(8,128)S(1)} collective-permute-done((f32[2,16,512]{2,1,0:T(8,128)S(1)}, f32[2,16,512]{2,1,0:T(8,128)S(1)}, u32[]{:S(2)}, u32[]{:S(2)}) %collective-permute-start.3) | collective-permute-done | bytes 65568 | tf_op jit(solution)/shard_map/ppermute | solution.py:85
  50.8 1.6 %fusion.145 = (f32[2,16,512]{2,1,0:T(8,128)}, f32[2,16,512]{2,1,0:T(8,128)}) fusion(f32[2,16,512]{2,1,0:T(8,128)} %collective-permute-done.1, f32[1,16,512]{2,1,0:T(8,128)S(1)} %copy-done.31, f32[1,16,512]{2,1,0:T(8,128)S(1)} %copy-done.32, f32[2,16,512]{2,1,0:T(8,128)} %collective-permute-done.2, f32[1,16,512]{2,1,0:T(8,128)S(1)} %copy-done.29, ...), kind=kLoop, calls=%fused_computation.222 | loop fusion | flops 212992 | bytes 655360 | tf_op jit(solution)/shard_map/add | solution.py:86
  52.4 1.9 %collective-permute-start.4 = (f32[2,16,512]{2,1,0:T(8,128)}, f32[2,16,512]{2,1,0:T(8,128)}, u32[]{:S(2)}, u32[]{:S(2)}) collective-permute-start(f32[2,16,512]{2,1,0:T(8,128)} %get-tuple-element.43), channel_id=1, source_target_pairs={{0,64},{64,0},{128,192},{192,128},{256,320},{320,256},{384,448},{4... | collective-permute-start | bytes 196616 | tf_op jit(solution)/shard_map/ppermute | solution.py:85
  54.3 1.1 %convolution_add_fusion.2 = f32[32,16,128]{2,1,0:T(8,128)} fusion(f32[32,16,128]{2,1,0:T(8,128)S(1)} %fusion.9, bf16[128,32,16]{0,2,1:T(8,128)(2,1)S(1)} %bitcast.124, f32[32,128,128]{2,1,0:T(8,128)S(1)} %fusion.129, pred[128,128]{1,0:T(8,128)(4,1)S(1)} %iota_compare_fusion.1), kind=kOutput, calls=%fused_computation.7 | convolution fusion | flops 18939904 | bytes 2768896 | tf_op jit(solution)/shard_map/gts,tgc->sgc/dot_general | solution.py:50
  55.6 2.1 %collective-permute-done.4 = f32[2,16,512]{2,1,0:T(8,128)} collective-permute-done((f32[2,16,512]{2,1,0:T(8,128)}, f32[2,16,512]{2,1,0:T(8,128)}, u32[]{:S(2)}, u32[]{:S(2)}) %collective-permute-start.4) | collective-permute-done | bytes 65568 | tf_op jit(solution)/shard_map/ppermute | solution.py:85
  57.7 1.0 %fusion.151 = f32[2,16,512]{2,1,0:T(8,128)S(1)} fusion(f32[2,16,512]{2,1,0:T(8,128)} %get-tuple-element.43, f32[1,16,512]{2,1,0:T(8,128)} %get-tuple-element.12, f32[1,16,512]{2,1,0:T(8,128)} %get-tuple-element.17, f32[2,16,512]{2,1,0:T(8,128)} %collective-permute-done.4), kind=kLoop, calls=%fused_computation.240 | loop fusion | flops 81920 | bytes 262144 | tf_op jit(solution)/shard_map/add | solution.py:87
  58.7 1.9 %collective-permute-start.5 = (f32[2,16,512]{2,1,0:T(8,128)S(1)}, f32[2,16,512]{2,1,0:T(8,128)S(1)}, u32[]{:S(2)}, u32[]{:S(2)}) collective-permute-start(f32[2,16,512]{2,1,0:T(8,128)S(1)} %fusion.151), channel_id=1, source_target_pairs={{0,128},{64,192},{128,0},{192,64},{256,384},{320,448},{384,256},{4... | collective-permute-start | bytes 196616 | tf_op jit(solution)/shard_map/ppermute | solution.py:85
  60.6 0.6 fusion.10
  61.2 3.8 %collective-permute-done.5 = f32[2,16,512]{2,1,0:T(8,128)S(1)} collective-permute-done((f32[2,16,512]{2,1,0:T(8,128)S(1)}, f32[2,16,512]{2,1,0:T(8,128)S(1)}, u32[]{:S(2)}, u32[]{:S(2)}) %collective-permute-start.5) | collective-permute-done | bytes 65568 | tf_op jit(solution)/shard_map/ppermute | solution.py:85
  65.0 0.6 copy-done.21
  65.6 0.6 fusion.152
  66.3 4.7 %collective-permute-start.6 = (f32[2,16,512]{2,1,0:T(8,128)}, f32[2,16,512]{2,1,0:T(8,128)}, u32[]{:S(2)}, u32[]{:S(2)}) collective-permute-start(f32[2,16,512]{2,1,0:T(8,128)} %fusion.152), channel_id=1, source_target_pairs={{0,256},{64,320},{128,384},{192,448},{256,0},{320,64},{384,128},{4... | collective-permute-start | bytes 196616 | tf_op jit(solution)/shard_map/ppermute | solution.py:85
  71.0 1.4 %convolution_add_fusion.3 = f32[32,16,128]{2,1,0:T(8,128)} fusion(f32[32,16,128]{2,1,0:T(8,128)S(1)} %fusion.10, bf16[128,32,16]{0,2,1:T(8,128)(2,1)S(1)} %bitcast.126, f32[32,128,128]{2,1,0:T(8,128)S(1)} %fusion.129, pred[128,128]{1,0:T(8,128)(4,1)S(1)} %iota_compare_fusion.1), kind=kOutput, calls=%fused_computation.8 | convolution fusion | flops 18939904 | bytes 2768896 | tf_op jit(solution)/shard_map/gts,sgc->tgc/dot_general | solution.py:50
  72.4 1.1 %copy.34 = f32[128,512]{1,0:T(8,128)S(1)} copy(f32[128,512]{0,1:T(8,128)} %bitcast.127) | data formatting | bytes 524288 | tf_op jit(solution)/shard_map/reshape | solution.py:153
  73.5 1.1 %copy.31 = f32[128,512]{1,0:T(8,128)S(1)} copy(f32[128,512]{0,1:T(8,128)} %bitcast.128) | data formatting | bytes 524288 | tf_op jit(solution)/shard_map/reshape | solution.py:152
  74.6 2.5 %collective-permute-done.6 = f32[2,16,512]{2,1,0:T(8,128)} collective-permute-done((f32[2,16,512]{2,1,0:T(8,128)}, f32[2,16,512]{2,1,0:T(8,128)}, u32[]{:S(2)}, u32[]{:S(2)}) %collective-permute-start.6) | collective-permute-done | bytes 65568 | tf_op jit(solution)/shard_map/ppermute | solution.py:85
  77.1 1.0 %fusion.149 = f32[2,16,512]{2,1,0:T(8,128)S(1)} fusion(f32[2,16,512]{2,1,0:T(8,128)} %collective-permute-done.4, f32[1,16,512]{2,1,0:T(8,128)} %get-tuple-element.22, f32[1,16,512]{2,1,0:T(8,128)} %get-tuple-element.23, f32[2,16,512]{2,1,0:T(8,128)} %copy-done.21, f32[1,16,512]{2,1,0:T(8,128)} %get-tuple-element.18, f32[1,16,512]{2,1,0:T(8,128)} %get-tuple-element.19, ...), kind=kLoop, calls=%fused_computation.234 | loop fusion | flops 131072 | bytes 458752 | tf_op jit(solution)/shard_map/add | solution.py:86
  78.2 0.3 broadcast_multiply_fusion
  78.5 1.4 %fusion.3 = bf16[128,512]{1,0:T(8,128)(2,1)S(1)} fusion(f32[128,512]{1,0:T(8,128)S(1)} %copy.34, f32[32,16,512]{2,0,1:T(8,128)S(1)} %get-tuple-element.40, f32[32,16,128]{2,1,0:T(8,128)S(1)} %copy-done.7, f32[32,16]{1,0:T(8,128)S(1)} %copy-done.19), kind=kOutput, calls=%fused_computation.11 | convolution fusion | flops 402849792 | bytes 1705984 | tf_op jit(solution)/shard_map/ks,kc->sc/dot_general | solution.py:159
  80.2 1.4 %fusion.4 = bf16[128,512]{1,0:T(8,128)(2,1)S(1)} fusion(f32[128,512]{1,0:T(8,128)S(1)} %copy.31, f32[32,16,512]{2,0,1:T(8,128)S(1)} %get-tuple-element.41, f32[32,16]{1,0:T(8,128)S(1)} %copy-done.19, f32[32,16,129]{2,1,0:T(8,128)S(1)} %multiply_exponential_fusion.1), kind=kOutput, calls=%fused_computation.12 | convolution fusion | flops 402849792 | bytes 1720320 | tf_op jit(solution)/shard_map/kt,kc->tc/dot_general | solution.py:158
  81.6 0.7 fusion.14
  82.4 6.3 %collective-permute-start.7 = (bf16[3,6,512]{2,1,0:T(8,128)(2,1)S(1)}, bf16[3,6,512]{2,1,0:T(8,128)(2,1)S(1)}, u32[]{:S(2)}, u32[]{:S(2)}) collective-permute-start(bf16[3,6,512]{2,1,0:T(8,128)(2,1)S(1)} %pad_maximum_fusion.8), channel_id=1, source_target_pairs={{8,0},{16,8},{24,16},{32,24},{40,32},{48,40},{56,48},{64,56},{72,6... | collective-permute-start | bytes 55304 | tf_op jit(solution)/shard_map/ppermute | solution.py:19
  88.7 2.0 %collective-permute-done.7 = bf16[3,6,512]{2,1,0:T(8,128)(2,1)S(1)} collective-permute-done((bf16[3,6,512]{2,1,0:T(8,128)(2,1)S(1)}, bf16[3,6,512]{2,1,0:T(8,128)(2,1)S(1)}, u32[]{:S(2)}, u32[]{:S(2)}) %collective-permute-start.7) | collective-permute-done | bytes 18464 | tf_op jit(solution)/shard_map/ppermute | solution.py:19
  90.8 0.9 fusion.40
  91.7 0.9 fusion.23
  92.7 0.9 fusion.57
  (181 shorter events, 1.7 us)
Async XLA Ops:
  0.6 11.3 %copy-start.35 = (f32[3,7,512]{2,1,0:T(8,128)S(1)}, f32[3,7,512]{2,1,0:T(8,128)}, u32[]{:S(2)}) copy-start(f32[3,7,512]{2,1,0:T(8,128)} %param.10) | copy-start | bytes 129028
  2.7 18.3 %collective-permute-start = (bf16[3,6,512]{2,1,0:T(8,128)(2,1)}, bf16[3,6,512]{2,1,0:T(8,128)(2,1)}, u32[]{:S(2)}, u32[]{:S(2)}) collective-permute-start(bf16[3,6,512]{2,1,0:T(8,128)(2,1)} %pad_maximum_fusion.7), channel_id=1, source_target_pairs={{0,8},{8,16},{16,24},{24,32},{32,40},{40,48},{48,56},{56,64},{64,7... | collective-permute-start | bytes 55304 | tf_op jit(solution)/shard_map/ppermute | solution.py:19
  12.0 8.1 %copy-start.18 = (f32[32,16]{1,0:T(8,128)}, f32[32,16]{1,0:T(8,128)S(1)}, u32[]{:S(2)}) copy-start(f32[32,16]{1,0:T(8,128)S(1)} %copy.23) | copy-start | bytes 6148
  13.6 7.3 %copy-start.22 = (bf16[128,512]{1,0:T(8,128)(2,1)S(1)}, bf16[128,512]{1,0:T(8,128)(2,1)}, u32[]{:S(2)}) copy-start(bf16[128,512]{1,0:T(8,128)(2,1)} %param.7) | copy-start | bytes 393220
  14.3 6.6 %copy-start.23 = (bf16[128,512]{1,0:T(8,128)(2,1)S(1)}, bf16[128,512]{1,0:T(8,128)(2,1)}, u32[]{:S(2)}) copy-start(bf16[128,512]{1,0:T(8,128)(2,1)} %param.8) | copy-start | bytes 393220
  14.4 6.6 %copy-start.24 = (bf16[128,512]{1,0:T(8,128)(2,1)S(1)}, bf16[128,512]{1,0:T(8,128)(2,1)}, u32[]{:S(2)}) copy-start(bf16[128,512]{1,0:T(8,128)(2,1)} %param.9) | copy-start | bytes 393220
  14.6 7.2 %copy-start.36 = (f32[1,1,512]{2,1,0:T(1,128)S(1)}, f32[1,1,512]{2,1,0:T(1,128)}, u32[]{:S(2)}) copy-start(f32[1,1,512]{2,1,0:T(1,128)} %get-tuple-element.44) | copy-start | bytes 6148
  14.6 7.2 %copy-start.38 = (f32[1,1,512]{2,1,0:T(1,128)S(1)}, f32[1,1,512]{2,1,0:T(1,128)}, u32[]{:S(2)}) copy-start(f32[1,1,512]{2,1,0:T(1,128)} %get-tuple-element.57) | copy-start | bytes 6148
  14.6 7.2 %copy-start.40 = (f32[1,1,512]{2,1,0:T(1,128)S(1)}, f32[1,1,512]{2,1,0:T(1,128)}, u32[]{:S(2)}) copy-start(f32[1,1,512]{2,1,0:T(1,128)} %get-tuple-element.58) | copy-start | bytes 6148
  14.6 7.2 %copy-start.42 = (f32[1,1,512]{2,1,0:T(1,128)S(1)}, f32[1,1,512]{2,1,0:T(1,128)}, u32[]{:S(2)}) copy-start(f32[1,1,512]{2,1,0:T(1,128)} %get-tuple-element.59) | copy-start | bytes 6148
  14.6 7.2 %copy-start.44 = (f32[1,1,512]{2,1,0:T(1,128)S(1)}, f32[1,1,512]{2,1,0:T(1,128)}, u32[]{:S(2)}) copy-start(f32[1,1,512]{2,1,0:T(1,128)} %get-tuple-element.60) | copy-start | bytes 6148
  14.6 7.2 %copy-start.46 = (f32[1,1,512]{2,1,0:T(1,128)S(1)}, f32[1,1,512]{2,1,0:T(1,128)}, u32[]{:S(2)}) copy-start(f32[1,1,512]{2,1,0:T(1,128)} %get-tuple-element.61) | copy-start | bytes 6148
  14.7 7.2 %copy-start.48 = (f32[1,1,512]{2,1,0:T(1,128)S(1)}, f32[1,1,512]{2,1,0:T(1,128)}, u32[]{:S(2)}) copy-start(f32[1,1,512]{2,1,0:T(1,128)} %get-tuple-element.62) | copy-start | bytes 6148
  14.7 7.4 %copy-start.12 = (bf16[128,512]{1,0:T(8,128)(2,1)S(1)}, bf16[128,512]{1,0:T(8,128)(2,1)}, u32[]{:S(2)}) copy-start(bf16[128,512]{1,0:T(8,128)(2,1)} %param.13) | copy-start | bytes 393220
  14.7 7.5 %copy-start.60 = (f32[1,1,512]{2,1,0:T(1,128)S(1)}, f32[1,1,512]{2,1,0:T(1,128)}, u32[]{:S(2)}) copy-start(f32[1,1,512]{2,1,0:T(1,128)} %get-tuple-element.50) | copy-start | bytes 6148
  14.7 7.5 %copy-start.62 = (f32[1,1,512]{2,1,0:T(1,128)S(1)}, f32[1,1,512]{2,1,0:T(1,128)}, u32[]{:S(2)}) copy-start(f32[1,1,512]{2,1,0:T(1,128)} %get-tuple-element.51) | copy-start | bytes 6148
  14.7 7.5 %copy-start.64 = (f32[1,1,512]{2,1,0:T(1,128)S(1)}, f32[1,1,512]{2,1,0:T(1,128)}, u32[]{:S(2)}) copy-start(f32[1,1,512]{2,1,0:T(1,128)} %get-tuple-element.52) | copy-start | bytes 6148
  14.7 7.5 %copy-start.66 = (f32[1,1,512]{2,1,0:T(1,128)S(1)}, f32[1,1,512]{2,1,0:T(1,128)}, u32[]{:S(2)}) copy-start(f32[1,1,512]{2,1,0:T(1,128)} %get-tuple-element.53) | copy-start | bytes 6148
  14.7 7.5 %copy-start.68 = (f32[1,1,512]{2,1,0:T(1,128)S(1)}, f32[1,1,512]{2,1,0:T(1,128)}, u32[]{:S(2)}) copy-start(f32[1,1,512]{2,1,0:T(1,128)} %get-tuple-element.54) | copy-start | bytes 6148
  14.7 7.5 %copy-start.70 = (f32[1,1,512]{2,1,0:T(1,128)S(1)}, f32[1,1,512]{2,1,0:T(1,128)}, u32[]{:S(2)}) copy-start(f32[1,1,512]{2,1,0:T(1,128)} %get-tuple-element.55) | copy-start | bytes 6148
  14.7 7.5 %copy-start.72 = (f32[1,1,512]{2,1,0:T(1,128)S(1)}, f32[1,1,512]{2,1,0:T(1,128)}, u32[]{:S(2)}) copy-start(f32[1,1,512]{2,1,0:T(1,128)} %get-tuple-element.56) | copy-start | bytes 6148
  27.1 8.6 %collective-permute-start.1 = (f32[2,16,512]{2,1,0:T(8,128)}, f32[2,16,512]{2,1,0:T(8,128)}, u32[]{:S(2)}, u32[]{:S(2)}) collective-permute-start(f32[2,16,512]{2,1,0:T(8,128)} %pad_maximum_fusion.6), channel_id=1, source_target_pairs={{0,8},{8,0},{16,24},{24,16},{32,40},{40,32},{48,56},{56,48},{1,9},... | collective-permute-start | bytes 196616 | tf_op jit(solution)/shard_map/ppermute | solution.py:85
  37.3 5.9 %collective-permute-start.2 = (f32[2,16,512]{2,1,0:T(8,128)}, f32[2,16,512]{2,1,0:T(8,128)}, u32[]{:S(2)}, u32[]{:S(2)}) collective-permute-start(f32[2,16,512]{2,1,0:T(8,128)} %fusion.146), channel_id=1, source_target_pairs={{0,16},{8,24},{16,0},{24,8},{32,48},{40,56},{48,32},{56,40},{1,17}... | collective-permute-start | bytes 196616 | tf_op jit(solution)/shard_map/ppermute | solution.py:85
  40.0 10.8 %copy-start.25 = (f32[1,16,512]{2,1,0:T(8,128)S(1)}, f32[1,16,512]{2,1,0:T(8,128)}, u32[]{:S(2)}) copy-start(f32[1,16,512]{2,1,0:T(8,128)} %get-tuple-element.8) | copy-start | bytes 98308
  40.0 10.8 %copy-start.26 = (f32[1,16,512]{2,1,0:T(8,128)S(1)}, f32[1,16,512]{2,1,0:T(8,128)}, u32[]{:S(2)}) copy-start(f32[1,16,512]{2,1,0:T(8,128)} %get-tuple-element.11) | copy-start | bytes 98308
  40.0 10.8 %copy-start.27 = (f32[1,16,512]{2,1,0:T(8,128)S(1)}, f32[1,16,512]{2,1,0:T(8,128)}, u32[]{:S(2)}) copy-start(f32[1,16,512]{2,1,0:T(8,128)} %get-tuple-element.20) | copy-start | bytes 98308
  40.0 10.8 %copy-start.28 = (f32[1,16,512]{2,1,0:T(8,128)S(1)}, f32[1,16,512]{2,1,0:T(8,128)}, u32[]{:S(2)}) copy-start(f32[1,16,512]{2,1,0:T(8,128)} %get-tuple-element.21) | copy-start | bytes 98308
  40.0 10.8 %copy-start.29 = (f32[1,16,512]{2,1,0:T(8,128)S(1)}, f32[1,16,512]{2,1,0:T(8,128)}, u32[]{:S(2)}) copy-start(f32[1,16,512]{2,1,0:T(8,128)} %get-tuple-element.26) | copy-start | bytes 98308
  40.0 10.8 %copy-start.30 = (f32[1,16,512]{2,1,0:T(8,128)S(1)}, f32[1,16,512]{2,1,0:T(8,128)}, u32[]{:S(2)}) copy-start(f32[1,16,512]{2,1,0:T(8,128)} %get-tuple-element.27) | copy-start | bytes 98308
  40.0 10.8 %copy-start.31 = (f32[1,16,512]{2,1,0:T(8,128)S(1)}, f32[1,16,512]{2,1,0:T(8,128)}, u32[]{:S(2)}) copy-start(f32[1,16,512]{2,1,0:T(8,128)} %get-tuple-element.28) | copy-start | bytes 98308
  40.0 10.8 %copy-start.32 = (f32[1,16,512]{2,1,0:T(8,128)S(1)}, f32[1,16,512]{2,1,0:T(8,128)}, u32[]{:S(2)}) copy-start(f32[1,16,512]{2,1,0:T(8,128)} %get-tuple-element.29) | copy-start | bytes 98308
  40.0 14.3 %copy-start.6 = (bf16[128,512]{0,1:T(8,128)(2,1)S(1)}, bf16[128,512]{0,1:T(8,128)(2,1)}, u32[]{:S(2)}) copy-start(bf16[128,512]{0,1:T(8,128)(2,1)} %copy.32) | copy-start | bytes 393220
  44.2 6.5 %collective-permute-start.3 = (f32[2,16,512]{2,1,0:T(8,128)S(1)}, f32[2,16,512]{2,1,0:T(8,128)S(1)}, u32[]{:S(2)}, u32[]{:S(2)}) collective-permute-start(f32[2,16,512]{2,1,0:T(8,128)S(1)} %fusion.147), channel_id=1, source_target_pairs={{0,32},{8,40},{16,48},{24,56},{32,0},{40,8},{48,16},{56,24},{1,33}... | collective-permute-start | bytes 196616 | tf_op jit(solution)/shard_map/ppermute | solution.py:85
  52.4 5.3 %collective-permute-start.4 = (f32[2,16,512]{2,1,0:T(8,128)}, f32[2,16,512]{2,1,0:T(8,128)}, u32[]{:S(2)}, u32[]{:S(2)}) collective-permute-start(f32[2,16,512]{2,1,0:T(8,128)} %get-tuple-element.43), channel_id=1, source_target_pairs={{0,64},{64,0},{128,192},{192,128},{256,320},{320,256},{384,448},{4... | collective-permute-start | bytes 196616 | tf_op jit(solution)/shard_map/ppermute | solution.py:85
  55.6 10.1 %copy-start.33 = (f32[1,16,512]{2,1,0:T(8,128)S(1)}, f32[1,16,512]{2,1,0:T(8,128)}, u32[]{:S(2)}) copy-start(f32[1,16,512]{2,1,0:T(8,128)} %get-tuple-element.13) | copy-start | bytes 98308
  55.6 10.1 %copy-start.34 = (f32[1,16,512]{2,1,0:T(8,128)S(1)}, f32[1,16,512]{2,1,0:T(8,128)}, u32[]{:S(2)}) copy-start(f32[1,16,512]{2,1,0:T(8,128)} %get-tuple-element.14) | copy-start | bytes 98308
  58.7 6.3 %collective-permute-start.5 = (f32[2,16,512]{2,1,0:T(8,128)S(1)}, f32[2,16,512]{2,1,0:T(8,128)S(1)}, u32[]{:S(2)}, u32[]{:S(2)}) collective-permute-start(f32[2,16,512]{2,1,0:T(8,128)S(1)} %fusion.151), channel_id=1, source_target_pairs={{0,128},{64,192},{128,0},{192,64},{256,384},{320,448},{384,256},{4... | collective-permute-start | bytes 196616 | tf_op jit(solution)/shard_map/ppermute | solution.py:85
  66.3 11.8 %copy-start.20 = (f32[2,16,512]{2,1,0:T(8,128)S(1)}, f32[2,16,512]{2,1,0:T(8,128)}, u32[]{:S(2)}) copy-start(f32[2,16,512]{2,1,0:T(8,128)} %get-tuple-element.42) | copy-start | bytes 196612
  66.3 11.9 %copy-start.9 = (f32[32,512]{1,0:T(8,128)S(1)}, f32[32,512]{1,0:T(8,128)}, u32[]{:S(2)}) copy-start(f32[32,512]{1,0:T(8,128)} %fusion.153) | copy-start | bytes 196612
  66.3 10.8 %collective-permute-start.6 = (f32[2,16,512]{2,1,0:T(8,128)}, f32[2,16,512]{2,1,0:T(8,128)}, u32[]{:S(2)}, u32[]{:S(2)}) collective-permute-start(f32[2,16,512]{2,1,0:T(8,128)} %fusion.152), channel_id=1, source_target_pairs={{0,256},{64,320},{128,384},{192,448},{256,0},{320,64},{384,128},{4... | collective-permute-start | bytes 196616 | tf_op jit(solution)/shard_map/ppermute | solution.py:85
  72.4 6.1 %copy-start.7 = (f32[32,16,128]{2,1,0:T(8,128)S(1)}, f32[32,16,128]{2,1,0:T(8,128)}, u32[]{:S(2)}) copy-start(f32[32,16,128]{2,1,0:T(8,128)} %rev.7) | copy-start | bytes 786436
  72.4 6.1 %copy-start.19 = (f32[32,16]{1,0:T(8,128)S(1)}, f32[32,16]{1,0:T(8,128)}, u32[]{:S(2)}) copy-start(f32[32,16]{1,0:T(8,128)} %copy-done.18) | copy-start | bytes 6148
  79.9 10.9 %copy-start.61 = (f32[1,1,512]{2,1,0:T(1,128)S(1)}, f32[1,1,512]{2,1,0:T(1,128)}, u32[]{:S(2)}) copy-start(f32[1,1,512]{2,1,0:T(1,128)} %get-tuple-element.50) | copy-start | bytes 6148
  79.9 10.9 %copy-start.63 = (f32[1,1,512]{2,1,0:T(1,128)S(1)}, f32[1,1,512]{2,1,0:T(1,128)}, u32[]{:S(2)}) copy-start(f32[1,1,512]{2,1,0:T(1,128)} %get-tuple-element.51) | copy-start | bytes 6148
  79.9 10.9 %copy-start.65 = (f32[1,1,512]{2,1,0:T(1,128)S(1)}, f32[1,1,512]{2,1,0:T(1,128)}, u32[]{:S(2)}) copy-start(f32[1,1,512]{2,1,0:T(1,128)} %get-tuple-element.52) | copy-start | bytes 6148
  79.9 10.9 %copy-start.67 = (f32[1,1,512]{2,1,0:T(1,128)S(1)}, f32[1,1,512]{2,1,0:T(1,128)}, u32[]{:S(2)}) copy-start(f32[1,1,512]{2,1,0:T(1,128)} %get-tuple-element.53) | copy-start | bytes 6148
  79.9 10.9 %copy-start.69 = (f32[1,1,512]{2,1,0:T(1,128)S(1)}, f32[1,1,512]{2,1,0:T(1,128)}, u32[]{:S(2)}) copy-start(f32[1,1,512]{2,1,0:T(1,128)} %get-tuple-element.54) | copy-start | bytes 6148
  79.9 10.9 %copy-start.71 = (f32[1,1,512]{2,1,0:T(1,128)S(1)}, f32[1,1,512]{2,1,0:T(1,128)}, u32[]{:S(2)}) copy-start(f32[1,1,512]{2,1,0:T(1,128)} %get-tuple-element.55) | copy-start | bytes 6148
  79.9 10.9 %copy-start.73 = (f32[1,1,512]{2,1,0:T(1,128)S(1)}, f32[1,1,512]{2,1,0:T(1,128)}, u32[]{:S(2)}) copy-start(f32[1,1,512]{2,1,0:T(1,128)} %get-tuple-element.56) | copy-start | bytes 6148
  80.0 11.7 %copy-start.51 = (f32[1,1,512]{2,1,0:T(1,128)S(1)}, f32[1,1,512]{2,1,0:T(1,128)}, u32[]{:S(2)}) copy-start(f32[1,1,512]{2,1,0:T(1,128)} %get-tuple-element.45) | copy-start | bytes 6148
  80.0 11.7 %copy-start.53 = (f32[1,1,512]{2,1,0:T(1,128)S(1)}, f32[1,1,512]{2,1,0:T(1,128)}, u32[]{:S(2)}) copy-start(f32[1,1,512]{2,1,0:T(1,128)} %get-tuple-element.46) | copy-start | bytes 6148
  80.0 11.7 %copy-start.55 = (f32[1,1,512]{2,1,0:T(1,128)S(1)}, f32[1,1,512]{2,1,0:T(1,128)}, u32[]{:S(2)}) copy-start(f32[1,1,512]{2,1,0:T(1,128)} %get-tuple-element.47) | copy-start | bytes 6148
  80.0 11.7 %copy-start.57 = (f32[1,1,512]{2,1,0:T(1,128)S(1)}, f32[1,1,512]{2,1,0:T(1,128)}, u32[]{:S(2)}) copy-start(f32[1,1,512]{2,1,0:T(1,128)} %get-tuple-element.48) | copy-start | bytes 6148
  80.0 11.7 %copy-start.59 = (f32[1,1,512]{2,1,0:T(1,128)S(1)}, f32[1,1,512]{2,1,0:T(1,128)}, u32[]{:S(2)}) copy-start(f32[1,1,512]{2,1,0:T(1,128)} %get-tuple-element.49) | copy-start | bytes 6148
  80.1 11.7 %copy-start.75 = (f32[1,1,512]{2,1,0:T(1,128)S(1)}, f32[1,1,512]{2,1,0:T(1,128)}, u32[]{:S(2)}) copy-start(f32[1,1,512]{2,1,0:T(1,128)} %copy-done.74) | copy-start | bytes 6148
  80.1 11.7 %copy-start.77 = (f32[1,1,512]{2,1,0:T(1,128)S(1)}, f32[1,1,512]{2,1,0:T(1,128)}, u32[]{:S(2)}) copy-start(f32[1,1,512]{2,1,0:T(1,128)} %copy-done.76) | copy-start | bytes 6148
  80.1 12.5 %copy-start.37 = (f32[1,1,512]{2,1,0:T(1,128)S(1)}, f32[1,1,512]{2,1,0:T(1,128)}, u32[]{:S(2)}) copy-start(f32[1,1,512]{2,1,0:T(1,128)} %get-tuple-element.44) | copy-start | bytes 6148
  80.1 12.5 %copy-start.39 = (f32[1,1,512]{2,1,0:T(1,128)S(1)}, f32[1,1,512]{2,1,0:T(1,128)}, u32[]{:S(2)}) copy-start(f32[1,1,512]{2,1,0:T(1,128)} %get-tuple-element.57) | copy-start | bytes 6148
  80.1 12.5 %copy-start.41 = (f32[1,1,512]{2,1,0:T(1,128)S(1)}, f32[1,1,512]{2,1,0:T(1,128)}, u32[]{:S(2)}) copy-start(f32[1,1,512]{2,1,0:T(1,128)} %get-tuple-element.58) | copy-start | bytes 6148
  80.1 12.5 %copy-start.43 = (f32[1,1,512]{2,1,0:T(1,128)S(1)}, f32[1,1,512]{2,1,0:T(1,128)}, u32[]{:S(2)}) copy-start(f32[1,1,512]{2,1,0:T(1,128)} %get-tuple-element.59) | copy-start | bytes 6148
  80.1 12.5 %copy-start.45 = (f32[1,1,512]{2,1,0:T(1,128)S(1)}, f32[1,1,512]{2,1,0:T(1,128)}, u32[]{:S(2)}) copy-start(f32[1,1,512]{2,1,0:T(1,128)} %get-tuple-element.60) | copy-start | bytes 6148
  80.1 12.5 %copy-start.47 = (f32[1,1,512]{2,1,0:T(1,128)S(1)}, f32[1,1,512]{2,1,0:T(1,128)}, u32[]{:S(2)}) copy-start(f32[1,1,512]{2,1,0:T(1,128)} %get-tuple-element.61) | copy-start | bytes 6148
  80.2 12.5 %copy-start.49 = (f32[1,1,512]{2,1,0:T(1,128)S(1)}, f32[1,1,512]{2,1,0:T(1,128)}, u32[]{:S(2)}) copy-start(f32[1,1,512]{2,1,0:T(1,128)} %get-tuple-element.62) | copy-start | bytes 6148
  82.4 8.4 %collective-permute-start.7 = (bf16[3,6,512]{2,1,0:T(8,128)(2,1)S(1)}, bf16[3,6,512]{2,1,0:T(8,128)(2,1)S(1)}, u32[]{:S(2)}, u32[]{:S(2)}) collective-permute-start(bf16[3,6,512]{2,1,0:T(8,128)(2,1)S(1)} %pad_maximum_fusion.8), channel_id=1, source_target_pairs={{8,0},{16,8},{24,16},{32,24},{40,32},{48,40},{56,48},{64,56},{72,6... | collective-permute-start | bytes 55304 | tf_op jit(solution)/shard_map/ppermute | solution.py:19
  (22 other events, 46.5 us)

commit v6 on v5

--- a/solution.py
+++ b/solution.py
@@ -140,14 +140,15 @@
     place = member.astype(jnp.float32)
     inner_terms = cube_coefficients(inner, member)
     outer_terms = [inner * term for term in cube_coefficients(outer, band)]
-    terms = jnp.stack(inner_terms + outer_terms + [place, inner - 1 - place])
+    unit_terms = [place, inner - 1 - place, jnp.float32(1), jnp.float32(-1)]
+    terms = jnp.stack(inner_terms + outer_terms + unit_terms)
     factors = jnp.exp(-decay_step[None] * terms[:, None, None])
     inner_rounds = cube_weights(factors, inner, member)
     outer_rounds = cube_weights(factors[len(inner_terms) :], outer, band)
     near, group = cube_scan(jnp.stack([end_state, start_state]), inner_rounds, "xc", inner)
     far, _ = cube_scan(group, outer_rounds, "zl", outer)
-    entering = near[0] + factors[-2] * far[0]
-    leaving = near[1] + factors[-1] * far[1]
+    entering = near[0] + factors[-4] * far[0]
+    leaving = near[1] + factors[-3] * far[1]
 
     local_conv = split_dot("gts,sgc->tgc", toeplitz, signal).reshape(block_len, channels)
     local_grad = split_dot("gts,tgc->sgc", toeplitz, cotangent).reshape(block_len, channels)
@@ -160,14 +161,38 @@
     conv_out = rounded(local_conv + carried_conv)
     grad_prod = rounded(local_grad + carried_grad)
 
+    edge = SHORT - 1
+    ahead = jnp.concatenate(
+        [
+            local_conv[:edge],
+            local_grad[:edge],
+            grad_out[:edge].astype(jnp.float32),
+            k_short[:edge].astype(jnp.float32),
+            v_short[:edge].astype(jnp.float32),
+            start_state,
+        ]
+    )
+    ahead = from_behind(ahead, ("zl", "xc"), -1)
+    through = factors[-2] * entering + end_state
+    beyond = (leaving - ahead[5 * edge :]) * factors[-1]
+    next_conv = rounded(
+        ahead[:edge]
+        + jnp.einsum("kt,kc->tc", lead_fwd[:, :edge], spread(through), precision=precise)
+    )
+    next_grad = rounded(
+        ahead[edge : 2 * edge]
+        + jnp.einsum("ks,kc->sc", lead_bwd[:, :edge], spread(beyond), precision=precise)
+    )
+    next_rows = (
+        rounded(ahead[2 * edge : 3 * edge] * next_conv.astype(jnp.float32)),
+        rounded(next_grad.astype(jnp.float32) * ahead[4 * edge : 5 * edge]),
+        rounded(next_grad.astype(jnp.float32) * ahead[3 * edge : 4 * edge]),
+    )
+
     mixer_out = (q_short.astype(jnp.float32) * conv_out.astype(jnp.float32)).astype(jnp.bfloat16)
     grad_qshort = rounded(grad_out.astype(jnp.float32) * conv_out.astype(jnp.float32))
     grad_kshort = rounded(grad_prod.astype(jnp.float32) * v_short.astype(jnp.float32))
     grad_vshort = rounded(grad_prod.astype(jnp.float32) * k_short.astype(jnp.float32))
-    head_rows = jnp.stack(
-        [grad_qshort[: SHORT - 1], grad_kshort[: SHORT - 1], grad_vshort[: SHORT - 1]]
-    )
-    next_rows = from_behind(head_rows, ("zl", "xc"), -1)
     grad_query = short_reverse(grad_qshort, next_rows[0], short_filter[0]).astype(jnp.bfloat16)
     grad_key = short_reverse(grad_kshort, next_rows[1], short_filter[1]).astype(jnp.bfloat16)
     grad_value = short_reverse(grad_vshort, next_rows[2], short_filter[2]).astype(jnp.bfloat16)

time: 94.6 us -> 93.4 us (0.987)
  waiting for transfers between devices: 16.9 us -> 10.1 us
  starting transfers between devices: 29.3 us -> 31.6 us
  local copies, waits for them, and re-layouts: 12.8 us -> 14.9 us
  matrix products: 12.7 us -> 13.8 us
    ppermute x6, waiting for transfers between devices: 14.9 us -> 9.99 us  [cube_scan(): lax.ppermute(window, axis, [(source, source ^ shift) for source in range(...]
    convert_element_type x7 -> x9, other arithmetic: 1.54 us -> 4.7 us  [rounded(): return lax.optimization_barrier(values.astype(jnp.bfloat16))]
    add x4, other arithmetic: 4.22 us -> 1.71 us  [cube_scan(): window = keep * window + take * arrived]
    ppermute x6, starting transfers between devices: 18.5 us -> 20.7 us  [cube_scan(): lax.ppermute(window, axis, [(source, source ^ shift) for source in range(...]
    convert_element_type x0 -> x3, other arithmetic: none -> 2 us  [the longest x1 1.3 us: shards(): grad_out[:edge].astype(jnp.float32)]
    ppermute x2, waiting for transfers between devices: 2 us -> 0.1 us  [from_behind(): lax.ppermute(value, axis, [(source, source + steps) for source in range(l...]
    concatenate x0 -> x1, local copies, waits for them, and re-layouts: none -> 1.75 us  [shards(): jnp.concatenate([local_conv[:edge], local_grad[:edge], grad_out[:edge].as...]
    slice x2, local copies, waits for them, and re-layouts: 1.47 us -> 3.15 us  [short_causal(): filter_taps[offset] * padded[SHORT - 1 - offset:SHORT - 1 - offset + length]]
  transfers between devices with their start and end apart: 8 -> 8, of which waited for: 6 -> 6; matrix products, arithmetic and copies ran while one was open for 25% -> 29% of each run, Pallas kernels for 0% -> 0%
where the time goes in v6:
time: 93.4 us; the launch traced here: 92.1 us
  starting transfers between devices  31.6 us (34%)
  other arithmetic  19.9 us (21%)
  local copies, waits for them, and re-layouts  14.9 us (16%)
  matrix products  13.8 us (15%)
  waiting for transfers between devices  10.1 us (11%)
  between operations  1.89 us (2%)
    ppermute x6, starting transfers between devices, cube_scan(): lax.ppermute(window, axis, [(source, source ^ shift) for source in range(...  20.7 us
    ppermute x2, starting transfers between devices, from_behind(): lax.ppermute(value, axis, [(source, source + steps) for source in range(l...  10.8 us
    ppermute x6, waiting for transfers between devices, cube_scan(): lax.ppermute(window, axis, [(source, source ^ shift) for source in range(...  9.99 us
    convert_element_type x9, other arithmetic, rounded(): return lax.optimization_barrier(values.astype(jnp.bfloat16))  4.7 us
    dot_general x4, matrix products, split_dot(): jnp.einsum(spec, low, values, preferred_element_type=jnp.float32)  3.93 us
    dot_general x1, matrix products, shards(): toeplitz = jnp.einsum('gtm,gms->gts', falling, rising, precision=precise)  3.65 us
    dot_general x4, matrix products, split_dot(): jnp.einsum(spec, high.astype(jnp.bfloat16), values, preferred_element_typ...  3.4 us
    slice x2, local copies, waits for them, and re-layouts, short_causal(): filter_taps[offset] * padded[SHORT - 1 - offset:SHORT - 1 - offset + length]  3.15 us
  transfers between devices with their start and end apart: 8, of which 6 were waited for; matrix products, arithmetic and copies ran while one was open for 29% of the time, Pallas kernels for 0%

profile of v6, /device:TPU:1, one launch (start us, length us, event | category | flops | bytes accessed | tf_op | source)
XLA Modules:
  0.0 92.1 jit_solution(13746357257364435913)
XLA Ops:
  0.6 0.7 slice_bitcast_fusion.6
  1.4 0.7 slice_bitcast_fusion.4
  2.1 4.5 %collective-permute-start = (bf16[3,6,512]{2,1,0:T(8,128)(2,1)S(1)}, bf16[3,6,512]{2,1,0:T(8,128)(2,1)S(1)}, u32[]{:S(2)}, u32[]{:S(2)}) collective-permute-start(bf16[3,6,512]{2,1,0:T(8,128)(2,1)S(1)} %pad_maximum_fusion.7), channel_id=1, source_target_pairs={{0,8},{8,16},{16,24},{24,32},{32,40},{40,48},{48,56},{56,64},{64,7... | collective-permute-start | bytes 55304 | tf_op jit(solution)/shard_map/ppermute | solution.py:19
  6.6 1.8 %fusion.181 = (f32[1,1,512]{2,1,0:T(1,128)}, f32[1,1,512]{2,1,0:T(1,128)S(1)}, f32[1,1,512]{2,1,0:T(1,128)S(1)}, f32[1,1,512]{2,1,0:T(1,128)S(1)}, f32[1,1,512]{...) fusion(f32[3,7,512]{2,1,0:T(8,128)} %param.10), kind=kLoop, calls=%fused_computation.327 | loop fusion | bytes 77824 | tf_op jit(solution)/shard_map/slice | solution.py:32
  8.5 1.4 %fusion.182 = (f32[1,1,512]{2,1,0:T(1,128)}, f32[1,1,512]{2,1,0:T(1,128)}) fusion(f32[3,7,512]{2,1,0:T(8,128)} %param.10), kind=kLoop, calls=%fused_computation.328 | loop fusion | bytes 8192 | tf_op jit(solution)/shard_map/slice | solution.py:32
  9.9 0.7 negate_bitcast_fusion
  10.9 0.2 fusion.180
  11.2 0.7 fusion.20
  12.1 0.7 fusion.19
  12.8 1.3 %slice_convert_fusion.2 = f32[6,512]{1,0:T(8,128)} fusion(bf16[128,512]{1,0:T(8,128)(2,1)} %param.13), kind=kLoop, calls=%fused_computation.305 | loop fusion | flops 3072 | bytes 18432 | tf_op jit(solution)/shard_map/convert_element_type | solution.py:169
  15.0 0.7 slice_select_fusion.6
  15.8 0.8 slice_select_fusion.7
  16.6 3.7 %fusion.133 = f32[32,128,128]{2,1,0:T(8,128)S(1)} fusion(f32[32,16]{1,0:T(8,128)S(1)} %copy.26, f32[128]{0:T(128)S(1)} %get-tuple-element.79, f32[128]{0:T(128)S(1)} %get-tuple-element.80, f32[32,16]{1,0:T(8,128)S(1)} %copy.25), kind=kOutput, calls=%fused_computation.211 | convolution fusion | flops 100859904 | bytes 2102272 | tf_op jit(solution)/shard_map/gtm,gms->gts/dot_general | solution.py:116
  20.3 0.7 convert_element_type.216
  21.1 0.6 fusion.169
  21.7 0.2 fusion.93
  22.0 0.2 fusion.76
  22.3 0.3 copy-done.1
  22.6 0.7 copy-done.3
  23.3 0.8 copy.24
  24.1 1.2 %fusion.183 = f32[512,512]{1,0:T(8,128)S(1)} fusion(bf16[512,128]{1,0:T(8,128)(2,1)} %get-tuple-element.38, bf16[128,512]{1,0:T(8,128)(2,1)S(1)} %fusion.13), kind=kOutput, calls=%fused_computation.329 | convolution fusion | flops 67108864 | bytes 1310720 | tf_op jit(solution)/shard_map/ks,sc->kc/dot_general | solution.py:49
  25.3 2.4 %fusion.110 = bf16[128,512]{1,0:T(8,128)(2,1)S(1)} fusion(f32[6,512]{1,0:T(8,128)} %get-tuple-element.71, f32[128,512]{1,0:T(8,128)} %convert_element_type.216, f32[512]{0:T(512)} %bitcast.142, f32[512]{0:T(512)} %bitcast.144, f32[512]{0:T(512)} %bitcast.146, f32[512]{0:T(512)} %bitcast.148, f32[512]{0:T(512)} %bitcast.150, f32[512]{0:T(512)} %bitcast.152, ...), kind=kLoop, calls=%fused_computation.164 | loop fusion | flops 1310720 | bytes 419840 | tf_op jit(solution)/shard_map/convert_element_type | solution.py:23
  27.7 1.0 %fusion.14 = bf16[128,512]{1,0:T(8,128)(2,1)S(1)} fusion(bf16[128,512]{1,0:T(8,128)(2,1)S(1)} %fusion.110, bf16[128,512]{1,0:T(8,128)(2,1)} %param.13), kind=kLoop, calls=%fused_computation.68 | loop fusion | flops 262144 | bytes 393216 | tf_op jit(solution)/shard_map/convert_element_type | solution.py:23
  28.7 1.2 %convolution_add_fusion.1 = f32[512,512]{1,0:T(8,128)S(1)} fusion(f32[512,512]{1,0:T(8,128)S(1)} %fusion.183, bf16[512,128]{1,0:T(8,128)(2,1)S(1)} %copy-done.17, bf16[128,512]{1,0:T(8,128)(2,1)} %copy-done), kind=kOutput, calls=%fused_computation.4 | convolution fusion | flops 67371008 | bytes 2359296 | tf_op jit(solution)/shard_map/ks,sc->kc/dot_general | solution.py:50
  29.9 0.3 fusion.184
  30.2 0.3 convolution_add_fusion
  30.5 0.3 multiply_reduce_fusion.1
  30.8 5.6 %collective-permute-start.1 = (f32[2,16,512]{2,1,0:T(8,128)S(1)}, f32[2,16,512]{2,1,0:T(8,128)S(1)}, u32[]{:S(2)}, u32[]{:S(2)}) collective-permute-start(f32[2,16,512]{2,1,0:T(8,128)S(1)} %pad_maximum_fusion.6), channel_id=1, source_target_pairs={{0,8},{8,0},{16,24},{24,16},{32,40},{40,32},{48,56},{56,48},{1,9},... | collective-permute-start | bytes 196616 | tf_op jit(solution)/shard_map/ppermute | solution.py:85
  36.4 0.6 fusion.12
  37.1 0.2 collective-permute-done.1
  37.3 0.6 fusion.148
  38.0 1.9 %collective-permute-start.2 = (f32[2,16,512]{2,1,0:T(8,128)}, f32[2,16,512]{2,1,0:T(8,128)}, u32[]{:S(2)}, u32[]{:S(2)}) collective-permute-start(f32[2,16,512]{2,1,0:T(8,128)} %fusion.148), channel_id=1, source_target_pairs={{0,16},{8,24},{16,0},{24,8},{32,48},{40,56},{48,32},{56,40},{1,17}... | collective-permute-start | bytes 196616 | tf_op jit(solution)/shard_map/ppermute | solution.py:85
  39.9 1.4 %convolution_add_fusion.3 = f32[32,16,128]{2,1,0:T(8,128)} fusion(f32[32,16,128]{2,1,0:T(8,128)S(1)} %fusion.12, bf16[128,32,16]{0,2,1:T(8,128)(2,1)S(1)} %bitcast.131, f32[32,128,128]{2,1,0:T(8,128)S(1)} %fusion.133, pred[128,128]{1,0:T(8,128)(4,1)S(1)} %iota_compare_fusion.1), kind=kOutput, calls=%fused_computation.8 | convolution fusion | flops 18939904 | bytes 2768896 | tf_op jit(solution)/shard_map/gts,sgc->tgc/dot_general | solution.py:50
  41.3 0.8 copy.33
  42.1 1.2 %collective-permute-done.2 = f32[2,16,512]{2,1,0:T(8,128)} collective-permute-done((f32[2,16,512]{2,1,0:T(8,128)}, f32[2,16,512]{2,1,0:T(8,128)}, u32[]{:S(2)}, u32[]{:S(2)}) %collective-permute-start.2) | collective-permute-done | bytes 65568 | tf_op jit(solution)/shard_map/ppermute | solution.py:85
  43.3 1.0 %fusion.149 = f32[2,16,512]{2,1,0:T(8,128)S(1)} fusion(f32[1,16,512]{2,1,0:T(8,128)} %get-tuple-element.11, f32[1,16,512]{2,1,0:T(8,128)} %get-tuple-element.26, f32[2,16,512]{2,1,0:T(8,128)} %collective-permute-done.2, f32[2,16,512]{2,1,0:T(8,128)} %copy-done.12, f32[1,16,512]{2,1,0:T(8,128)} %get-tuple-element.27, f32[1,16,512]{2,1,0:T(8,128)} %get-tuple-element.15, ...), kind=kLoop, calls=%fused_computation.234 | loop fusion | flops 180224 | bytes 393216 | tf_op jit(solution)/shard_map/add | solution.py:87
  44.3 1.9 %collective-permute-start.3 = (f32[2,16,512]{2,1,0:T(8,128)S(1)}, f32[2,16,512]{2,1,0:T(8,128)S(1)}, u32[]{:S(2)}, u32[]{:S(2)}) collective-permute-start(f32[2,16,512]{2,1,0:T(8,128)S(1)} %fusion.149), channel_id=1, source_target_pairs={{0,32},{8,40},{16,48},{24,56},{32,0},{40,8},{48,16},{56,24},{1,33}... | collective-permute-start | bytes 196616 | tf_op jit(solution)/shard_map/ppermute | solution.py:85
  46.2 1.3 %fusion.11 = f32[32,16,128]{2,1,0:T(8,128)S(1)} fusion(bf16[128,32,16]{0,2,1:T(8,128)(2,1)} %bitcast.132, f32[32,128,128]{2,1,0:T(8,128)S(1)} %fusion.133, pred[128,128]{1,0:T(8,128)(4,1)S(1)} %iota_compare_fusion.1), kind=kOutput, calls=%fused_computation.65 | convolution fusion | flops 18350080 | bytes 2506752 | tf_op jit(solution)/shard_map/gts,tgc->sgc/dot_general | solution.py:49
  47.6 3.3 %collective-permute-done.3 = f32[2,16,512]{2,1,0:T(8,128)S(1)} collective-permute-done((f32[2,16,512]{2,1,0:T(8,128)S(1)}, f32[2,16,512]{2,1,0:T(8,128)S(1)}, u32[]{:S(2)}, u32[]{:S(2)}) %collective-permute-start.3) | collective-permute-done | bytes 65568 | tf_op jit(solution)/shard_map/ppermute | solution.py:85
  50.9 1.5 %fusion.147 = (f32[2,16,512]{2,1,0:T(8,128)}, f32[2,16,512]{2,1,0:T(8,128)S(1)}) fusion(f32[2,16,512]{2,1,0:T(8,128)S(1)} %copy-done.13, f32[1,16,512]{2,1,0:T(8,128)S(1)} %copy-done.29, f32[1,16,512]{2,1,0:T(8,128)S(1)} %copy-done.30, f32[2,16,512]{2,1,0:T(8,128)} %collective-permute-done.2, f32[1,16,512]{2,1,0:T(8,128)S(1)} %copy-done.27, ...), kind=kLoop, calls=%fused_computation.226 | loop fusion | flops 212992 | bytes 655360 | tf_op jit(solution)/shard_map/add | solution.py:86
  52.4 1.9 %collective-permute-start.4 = (f32[2,16,512]{2,1,0:T(8,128)S(1)}, f32[2,16,512]{2,1,0:T(8,128)S(1)}, u32[]{:S(2)}, u32[]{:S(2)}) collective-permute-start(f32[2,16,512]{2,1,0:T(8,128)S(1)} %get-tuple-element.49), channel_id=1, source_target_pairs={{0,64},{64,0},{128,192},{192,128},{256,320},{320,256},{384,448},{4... | collective-permute-start | bytes 196616 | tf_op jit(solution)/shard_map/ppermute | solution.py:85
  54.3 1.1 %convolution_add_fusion.2 = f32[32,16,128]{2,1,0:T(8,128)} fusion(f32[32,16,128]{2,1,0:T(8,128)S(1)} %fusion.11, bf16[128,32,16]{0,2,1:T(8,128)(2,1)S(1)} %bitcast.133, f32[32,128,128]{2,1,0:T(8,128)S(1)} %fusion.133, pred[128,128]{1,0:T(8,128)(4,1)S(1)} %iota_compare_fusion.1), kind=kOutput, calls=%fused_computation.7 | convolution fusion | flops 18939904 | bytes 2768896 | tf_op jit(solution)/shard_map/gts,tgc->sgc/dot_general | solution.py:50
  55.5 2.0 %collective-permute-done.4 = f32[2,16,512]{2,1,0:T(8,128)S(1)} collective-permute-done((f32[2,16,512]{2,1,0:T(8,128)S(1)}, f32[2,16,512]{2,1,0:T(8,128)S(1)}, u32[]{:S(2)}, u32[]{:S(2)}) %collective-permute-start.4) | collective-permute-done | bytes 65568 | tf_op jit(solution)/shard_map/ppermute | solution.py:85
  57.4 0.6 copy-done.21
  58.1 3.4 %collective-permute-start.5 = (f32[2,16,512]{2,1,0:T(8,128)S(1)}, f32[2,16,512]{2,1,0:T(8,128)S(1)}, u32[]{:S(2)}, u32[]{:S(2)}) collective-permute-start(f32[2,16,512]{2,1,0:T(8,128)S(1)} %fusion.153), channel_id=1, source_target_pairs={{0,128},{64,192},{128,0},{192,64},{256,384},{320,448},{384,256},{4... | collective-permute-start | bytes 196616 | tf_op jit(solution)/shard_map/ppermute | solution.py:85
  61.5 3.3 %collective-permute-done.5 = f32[2,16,512]{2,1,0:T(8,128)S(1)} collective-permute-done((f32[2,16,512]{2,1,0:T(8,128)S(1)}, f32[2,16,512]{2,1,0:T(8,128)S(1)}, u32[]{:S(2)}, u32[]{:S(2)}) %collective-permute-start.5) | collective-permute-done | bytes 65568 | tf_op jit(solution)/shard_map/ppermute | solution.py:85
  64.8 6.1 %collective-permute-start.6 = (f32[2,16,512]{2,1,0:T(8,128)S(1)}, f32[2,16,512]{2,1,0:T(8,128)S(1)}, u32[]{:S(2)}, u32[]{:S(2)}) collective-permute-start(f32[2,16,512]{2,1,0:T(8,128)S(1)} %fusion.154), channel_id=1, source_target_pairs={{0,256},{64,320},{128,384},{192,448},{256,0},{320,64},{384,128},{4... | collective-permute-start | bytes 196616 | tf_op jit(solution)/shard_map/ppermute | solution.py:85
  70.9 0.7 slice_convert_fusion
  71.6 1.1 %copy.35 = f32[6,512]{1,0:T(8,128)S(1)} copy(f32[6,512]{0,1:T(8,128)} %bitcast.126) | data formatting | bytes 24576 | tf_op jit(solution)/shard_map/slice | solution.py:167
  72.7 1.1 %copy.43 = f32[6,512]{1,0:T(8,128)S(1)} copy(f32[6,512]{0,1:T(8,128)} %bitcast.128) | data formatting | bytes 24576 | tf_op jit(solution)/shard_map/slice | solution.py:168
  73.7 1.8 %concatenate.24 = f32[46,512]{1,0:T(8,128)S(1)} concatenate(f32[6,512]{1,0:T(8,128)S(1)} %copy.35, f32[6,512]{1,0:T(8,128)S(1)} %copy.43, f32[6,512]{1,0:T(8,128)} %slice_convert_fusion.2, f32[6,512]{1,0:T(8,128)S(1)} %slice_convert_fusion.1, f32[6,512]{1,0:T(8,128)S(1)} %slice_convert_fusion, f32[16,512]{1,0:T(8,128)} %copy-done.11), dimensions={0} | concatenate | bytes 188416 | tf_op jit(solution)/shard_map/concatenate | solution.py:165
  75.5 6.3 %collective-permute-start.7 = (f32[46,512]{1,0:T(8,128)S(1)}, f32[46,512]{1,0:T(8,128)S(1)}, u32[]{:S(2)}, u32[]{:S(2)}) collective-permute-start(f32[46,512]{1,0:T(8,128)S(1)} %concatenate.24), channel_id=1, source_target_pairs={{8,0},{16,8},{24,16},{32,24},{40,32},{48,40},{56,48},{64,56},{72,6... | collective-permute-start | bytes 282632 | tf_op jit(solution)/shard_map/ppermute | solution.py:19
  81.8 1.1 %copy.38 = f32[128,512]{1,0:T(8,128)S(1)} copy(f32[128,512]{0,1:T(8,128)} %bitcast.129) | data formatting | bytes 524288 | tf_op jit(solution)/shard_map/reshape | solution.py:154
  82.9 1.1 %copy.32 = f32[128,512]{1,0:T(8,128)S(1)} copy(f32[128,512]{0,1:T(8,128)} %bitcast.127) | data formatting | bytes 524288 | tf_op jit(solution)/shard_map/reshape | solution.py:153
  84.0 0.9 fusion.151
  85.0 0.8 fusion.3
  85.9 0.3 broadcast_multiply_fusion
  86.2 0.6 fusion.164
  87.0 0.6 fusion.128
  87.7 0.8 fusion.4
  88.6 0.7 fusion.16
  89.4 0.9 fusion.25
  90.3 0.9 fusion.42
  91.2 0.9 fusion.59
  (183 shorter events, 2.1 us)
Async XLA Ops:
  0.6 11.4 %copy-start.38 = (f32[32,16]{0,1:T(8,128)S(1)}, f32[32,16]{0,1:T(8,128)}, u32[]{:S(2)}) copy-start(f32[32,16]{0,1:T(8,128)} %param.11) | copy-start | bytes 6148
  2.1 19.0 %collective-permute-start = (bf16[3,6,512]{2,1,0:T(8,128)(2,1)S(1)}, bf16[3,6,512]{2,1,0:T(8,128)(2,1)S(1)}, u32[]{:S(2)}, u32[]{:S(2)}) collective-permute-start(bf16[3,6,512]{2,1,0:T(8,128)(2,1)S(1)} %pad_maximum_fusion.7), channel_id=1, source_target_pairs={{0,8},{8,16},{16,24},{24,32},{32,40},{40,48},{48,56},{56,64},{64,7... | collective-permute-start | bytes 55304 | tf_op jit(solution)/shard_map/ppermute | solution.py:19
  8.4 13.3 %copy-start.46 = (f32[1,1,512]{2,1,0:T(1,128)}, f32[1,1,512]{2,1,0:T(1,128)S(1)}, u32[]{:S(2)}) copy-start(f32[1,1,512]{2,1,0:T(1,128)S(1)} %get-tuple-element.56) | copy-start | bytes 6148
  8.4 13.3 %copy-start.48 = (f32[1,1,512]{2,1,0:T(1,128)}, f32[1,1,512]{2,1,0:T(1,128)S(1)}, u32[]{:S(2)}) copy-start(f32[1,1,512]{2,1,0:T(1,128)S(1)} %get-tuple-element.57) | copy-start | bytes 6148
  8.4 13.3 %copy-start.50 = (f32[1,1,512]{2,1,0:T(1,128)}, f32[1,1,512]{2,1,0:T(1,128)S(1)}, u32[]{:S(2)}) copy-start(f32[1,1,512]{2,1,0:T(1,128)S(1)} %get-tuple-element.58) | copy-start | bytes 6148
  8.4 13.3 %copy-start.52 = (f32[1,1,512]{2,1,0:T(1,128)}, f32[1,1,512]{2,1,0:T(1,128)S(1)}, u32[]{:S(2)}) copy-start(f32[1,1,512]{2,1,0:T(1,128)S(1)} %get-tuple-element.59) | copy-start | bytes 6148
  8.4 13.3 %copy-start.54 = (f32[1,1,512]{2,1,0:T(1,128)}, f32[1,1,512]{2,1,0:T(1,128)S(1)}, u32[]{:S(2)}) copy-start(f32[1,1,512]{2,1,0:T(1,128)S(1)} %get-tuple-element.60) | copy-start | bytes 6148
  8.4 13.3 %copy-start.56 = (f32[1,1,512]{2,1,0:T(1,128)}, f32[1,1,512]{2,1,0:T(1,128)S(1)}, u32[]{:S(2)}) copy-start(f32[1,1,512]{2,1,0:T(1,128)S(1)} %get-tuple-element.61) | copy-start | bytes 6148
  8.4 13.3 %copy-start.58 = (f32[1,1,512]{2,1,0:T(1,128)}, f32[1,1,512]{2,1,0:T(1,128)S(1)}, u32[]{:S(2)}) copy-start(f32[1,1,512]{2,1,0:T(1,128)S(1)} %get-tuple-element.62) | copy-start | bytes 6148
  8.4 13.5 %copy-start.60 = (f32[1,1,512]{2,1,0:T(1,128)}, f32[1,1,512]{2,1,0:T(1,128)S(1)}, u32[]{:S(2)}) copy-start(f32[1,1,512]{2,1,0:T(1,128)S(1)} %get-tuple-element.51) | copy-start | bytes 6148
  8.4 13.5 %copy-start.62 = (f32[1,1,512]{2,1,0:T(1,128)}, f32[1,1,512]{2,1,0:T(1,128)S(1)}, u32[]{:S(2)}) copy-start(f32[1,1,512]{2,1,0:T(1,128)S(1)} %get-tuple-element.52) | copy-start | bytes 6148
  8.4 13.5 %copy-start.64 = (f32[1,1,512]{2,1,0:T(1,128)}, f32[1,1,512]{2,1,0:T(1,128)S(1)}, u32[]{:S(2)}) copy-start(f32[1,1,512]{2,1,0:T(1,128)S(1)} %get-tuple-element.53) | copy-start | bytes 6148
  8.5 13.5 %copy-start.66 = (f32[1,1,512]{2,1,0:T(1,128)}, f32[1,1,512]{2,1,0:T(1,128)S(1)}, u32[]{:S(2)}) copy-start(f32[1,1,512]{2,1,0:T(1,128)S(1)} %get-tuple-element.54) | copy-start | bytes 6148
  8.5 13.5 %copy-start.68 = (f32[1,1,512]{2,1,0:T(1,128)}, f32[1,1,512]{2,1,0:T(1,128)S(1)}, u32[]{:S(2)}) copy-start(f32[1,1,512]{2,1,0:T(1,128)S(1)} %get-tuple-element.55) | copy-start | bytes 6148
  14.8 5.4 %copy-start.23 = (bf16[128,512]{1,0:T(8,128)(2,1)S(1)}, bf16[128,512]{1,0:T(8,128)(2,1)}, u32[]{:S(2)}) copy-start(bf16[128,512]{1,0:T(8,128)(2,1)} %param.8) | copy-start | bytes 393220
  15.0 5.3 %copy-start.24 = (bf16[128,512]{1,0:T(8,128)(2,1)S(1)}, bf16[128,512]{1,0:T(8,128)(2,1)}, u32[]{:S(2)}) copy-start(bf16[128,512]{1,0:T(8,128)(2,1)} %param.9) | copy-start | bytes 393220
  15.0 5.3 %copy-start.25 = (bf16[128,512]{1,0:T(8,128)(2,1)S(1)}, bf16[128,512]{1,0:T(8,128)(2,1)}, u32[]{:S(2)}) copy-start(bf16[128,512]{1,0:T(8,128)(2,1)} %param.7) | copy-start | bytes 393220
  16.6 5.5 %copy-start.70 = (f32[1,1,512]{2,1,0:T(1,128)S(1)}, f32[1,1,512]{2,1,0:T(1,128)}, u32[]{:S(2)}) copy-start(f32[1,1,512]{2,1,0:T(1,128)} %get-tuple-element.69) | copy-start | bytes 6148
  16.6 5.5 %copy-start.72 = (f32[1,1,512]{2,1,0:T(1,128)S(1)}, f32[1,1,512]{2,1,0:T(1,128)}, u32[]{:S(2)}) copy-start(f32[1,1,512]{2,1,0:T(1,128)} %get-tuple-element.70) | copy-start | bytes 6148
  24.1 4.7 %copy-start.17 = (bf16[512,128]{1,0:T(8,128)(2,1)S(1)}, bf16[512,128]{1,0:T(8,128)(2,1)}, u32[]{:S(2)}) copy-start(bf16[512,128]{1,0:T(8,128)(2,1)} %get-tuple-element.37) | copy-start | bytes 393220
  24.1 5.9 %copy-start.16 = (bf16[512,128]{1,0:T(8,128)(2,1)S(1)}, bf16[512,128]{1,0:T(8,128)(2,1)}, u32[]{:S(2)}) copy-start(bf16[512,128]{1,0:T(8,128)(2,1)} %get-tuple-element.36) | copy-start | bytes 393220
  30.2 6.2 %copy-start.7 = (bf16[128,512]{0,1:T(8,128)(2,1)S(1)}, bf16[128,512]{0,1:T(8,128)(2,1)}, u32[]{:S(2)}) copy-start(bf16[128,512]{0,1:T(8,128)(2,1)} %copy.24) | copy-start | bytes 393220
  30.5 6.8 %copy-start.18 = (f32[1,16,512]{2,1,0:T(8,128)S(1)}, f32[1,16,512]{2,1,0:T(8,128)}, u32[]{:S(2)}) copy-start(f32[1,16,512]{2,1,0:T(8,128)} %get-tuple-element.27) | copy-start | bytes 98308
  30.5 6.8 %copy-start.19 = (f32[1,16,512]{2,1,0:T(8,128)S(1)}, f32[1,16,512]{2,1,0:T(8,128)}, u32[]{:S(2)}) copy-start(f32[1,16,512]{2,1,0:T(8,128)} %get-tuple-element.15) | copy-start | bytes 98308
  30.8 6.5 %copy-start.9 = (f32[16,512]{1,0:T(8,128)}, f32[16,512]{1,0:T(8,128)S(1)}, u32[]{:S(2)}) copy-start(f32[16,512]{1,0:T(8,128)S(1)} %get-tuple-element.4) | copy-start | bytes 98308
  30.8 7.1 %copy-start.11 = (f32[16,512]{1,0:T(8,128)}, f32[16,512]{1,0:T(8,128)S(1)}, u32[]{:S(2)}) copy-start(f32[16,512]{1,0:T(8,128)S(1)} %get-tuple-element.5) | copy-start | bytes 98308
  30.8 6.5 %collective-permute-start.1 = (f32[2,16,512]{2,1,0:T(8,128)S(1)}, f32[2,16,512]{2,1,0:T(8,128)S(1)}, u32[]{:S(2)}, u32[]{:S(2)}) collective-permute-start(f32[2,16,512]{2,1,0:T(8,128)S(1)} %pad_maximum_fusion.6), channel_id=1, source_target_pairs={{0,8},{8,0},{16,24},{24,16},{32,40},{40,32},{48,56},{56,48},{1,9},... | collective-permute-start | bytes 196616 | tf_op jit(solution)/shard_map/ppermute | solution.py:85
  38.0 5.3 %collective-permute-start.2 = (f32[2,16,512]{2,1,0:T(8,128)}, f32[2,16,512]{2,1,0:T(8,128)}, u32[]{:S(2)}, u32[]{:S(2)}) collective-permute-start(f32[2,16,512]{2,1,0:T(8,128)} %fusion.148), channel_id=1, source_target_pairs={{0,16},{8,24},{16,0},{24,8},{32,48},{40,56},{48,32},{56,40},{1,17}... | collective-permute-start | bytes 196616 | tf_op jit(solution)/shard_map/ppermute | solution.py:85
  42.0 8.8 %copy-start.13 = (f32[2,16,512]{2,1,0:T(8,128)S(1)}, f32[2,16,512]{2,1,0:T(8,128)}, u32[]{:S(2)}) copy-start(f32[2,16,512]{2,1,0:T(8,128)} %copy-done.12) | copy-start | bytes 196612
  42.0 8.8 %copy-start.26 = (f32[1,16,512]{2,1,0:T(8,128)S(1)}, f32[1,16,512]{2,1,0:T(8,128)}, u32[]{:S(2)}) copy-start(f32[1,16,512]{2,1,0:T(8,128)} %get-tuple-element.23) | copy-start | bytes 98308
  42.0 8.8 %copy-start.27 = (f32[1,16,512]{2,1,0:T(8,128)S(1)}, f32[1,16,512]{2,1,0:T(8,128)}, u32[]{:S(2)}) copy-start(f32[1,16,512]{2,1,0:T(8,128)} %get-tuple-element.28) | copy-start | bytes 98308
  42.0 8.8 %copy-start.28 = (f32[1,16,512]{2,1,0:T(8,128)S(1)}, f32[1,16,512]{2,1,0:T(8,128)}, u32[]{:S(2)}) copy-start(f32[1,16,512]{2,1,0:T(8,128)} %get-tuple-element.29) | copy-start | bytes 98308
  42.0 8.8 %copy-start.29 = (f32[1,16,512]{2,1,0:T(8,128)S(1)}, f32[1,16,512]{2,1,0:T(8,128)}, u32[]{:S(2)}) copy-start(f32[1,16,512]{2,1,0:T(8,128)} %get-tuple-element.30) | copy-start | bytes 98308
  42.0 8.8 %copy-start.30 = (f32[1,16,512]{2,1,0:T(8,128)S(1)}, f32[1,16,512]{2,1,0:T(8,128)}, u32[]{:S(2)}) copy-start(f32[1,16,512]{2,1,0:T(8,128)} %get-tuple-element.31) | copy-start | bytes 98308
  42.1 8.8 %copy-start.31 = (f32[1,16,512]{2,1,0:T(8,128)S(1)}, f32[1,16,512]{2,1,0:T(8,128)}, u32[]{:S(2)}) copy-start(f32[1,16,512]{2,1,0:T(8,128)} %get-tuple-element.10) | copy-start | bytes 98308
  42.1 8.8 %copy-start.32 = (f32[1,16,512]{2,1,0:T(8,128)S(1)}, f32[1,16,512]{2,1,0:T(8,128)}, u32[]{:S(2)}) copy-start(f32[1,16,512]{2,1,0:T(8,128)} %get-tuple-element.12) | copy-start | bytes 98308
  42.1 8.8 %copy-start.33 = (f32[1,16,512]{2,1,0:T(8,128)S(1)}, f32[1,16,512]{2,1,0:T(8,128)}, u32[]{:S(2)}) copy-start(f32[1,16,512]{2,1,0:T(8,128)} %get-tuple-element.22) | copy-start | bytes 98308
  42.1 12.2 %copy-start.8 = (bf16[128,512]{0,1:T(8,128)(2,1)S(1)}, bf16[128,512]{0,1:T(8,128)(2,1)}, u32[]{:S(2)}) copy-start(bf16[128,512]{0,1:T(8,128)(2,1)} %copy.33) | copy-start | bytes 393220
  44.3 6.5 %collective-permute-start.3 = (f32[2,16,512]{2,1,0:T(8,128)S(1)}, f32[2,16,512]{2,1,0:T(8,128)S(1)}, u32[]{:S(2)}, u32[]{:S(2)}) collective-permute-start(f32[2,16,512]{2,1,0:T(8,128)S(1)} %fusion.149), channel_id=1, source_target_pairs={{0,32},{8,40},{16,48},{24,56},{32,0},{40,8},{48,16},{56,24},{1,33}... | collective-permute-start | bytes 196616 | tf_op jit(solution)/shard_map/ppermute | solution.py:85
  47.5 10.5 %copy-start.36 = (f32[1,16,512]{2,1,0:T(8,128)S(1)}, f32[1,16,512]{2,1,0:T(8,128)}, u32[]{:S(2)}) copy-start(f32[1,16,512]{2,1,0:T(8,128)} %get-tuple-element.13) | copy-start | bytes 98308
  47.5 10.5 %copy-start.37 = (f32[1,16,512]{2,1,0:T(8,128)S(1)}, f32[1,16,512]{2,1,0:T(8,128)}, u32[]{:S(2)}) copy-start(f32[1,16,512]{2,1,0:T(8,128)} %get-tuple-element.19) | copy-start | bytes 98308
  47.5 13.9 %copy-start.2 = (bf16[128,512]{1,0:T(8,128)(2,1)S(1)}, bf16[128,512]{1,0:T(8,128)(2,1)}, u32[]{:S(2)}) copy-start(bf16[128,512]{1,0:T(8,128)(2,1)} %copy-done.1) | copy-start | bytes 393220
  47.5 17.3 %copy-start.34 = (f32[1,16,512]{2,1,0:T(8,128)S(1)}, f32[1,16,512]{2,1,0:T(8,128)}, u32[]{:S(2)}) copy-start(f32[1,16,512]{2,1,0:T(8,128)} %get-tuple-element.14) | copy-start | bytes 98308
  47.6 17.3 %copy-start.35 = (f32[1,16,512]{2,1,0:T(8,128)S(1)}, f32[1,16,512]{2,1,0:T(8,128)}, u32[]{:S(2)}) copy-start(f32[1,16,512]{2,1,0:T(8,128)} %get-tuple-element.16) | copy-start | bytes 98308
  52.4 5.0 %collective-permute-start.4 = (f32[2,16,512]{2,1,0:T(8,128)S(1)}, f32[2,16,512]{2,1,0:T(8,128)S(1)}, u32[]{:S(2)}, u32[]{:S(2)}) collective-permute-start(f32[2,16,512]{2,1,0:T(8,128)S(1)} %get-tuple-element.49), channel_id=1, source_target_pairs={{0,64},{64,0},{128,192},{192,128},{256,320},{320,256},{384,448},{4... | collective-permute-start | bytes 196616 | tf_op jit(solution)/shard_map/ppermute | solution.py:85
  55.5 29.4 %copy-start.10 = (f32[16,512]{1,0:T(8,128)S(1)}, f32[16,512]{1,0:T(8,128)}, u32[]{:S(2)}) copy-start(f32[16,512]{1,0:T(8,128)} %copy-done.9) | copy-start | bytes 98308
  55.5 29.4 %copy-start.20 = (f32[2,16,512]{2,1,0:T(8,128)S(1)}, f32[2,16,512]{2,1,0:T(8,128)}, u32[]{:S(2)}) copy-start(f32[2,16,512]{2,1,0:T(8,128)} %get-tuple-element.48) | copy-start | bytes 196612
  55.5 30.4 %copy-start.4 = (bf16[128,512]{1,0:T(8,128)(2,1)S(1)}, bf16[128,512]{1,0:T(8,128)(2,1)}, u32[]{:S(2)}) copy-start(bf16[128,512]{1,0:T(8,128)(2,1)} %copy-done.3) | copy-start | bytes 393220
  58.1 25.9 %copy-start.22 = (f32[2,16,512]{2,1,0:T(8,128)S(1)}, f32[2,16,512]{2,1,0:T(8,128)}, u32[]{:S(2)}) copy-start(f32[2,16,512]{2,1,0:T(8,128)} %copy-done.21) | copy-start | bytes 196612
  58.1 6.7 %collective-permute-start.5 = (f32[2,16,512]{2,1,0:T(8,128)S(1)}, f32[2,16,512]{2,1,0:T(8,128)S(1)}, u32[]{:S(2)}, u32[]{:S(2)}) collective-permute-start(f32[2,16,512]{2,1,0:T(8,128)S(1)} %fusion.153), channel_id=1, source_target_pairs={{0,128},{64,192},{128,0},{192,64},{256,384},{320,448},{384,256},{4... | collective-permute-start | bytes 196616 | tf_op jit(solution)/shard_map/ppermute | solution.py:85
  64.8 19.1 %collective-permute-start.6 = (f32[2,16,512]{2,1,0:T(8,128)S(1)}, f32[2,16,512]{2,1,0:T(8,128)S(1)}, u32[]{:S(2)}, u32[]{:S(2)}) collective-permute-start(f32[2,16,512]{2,1,0:T(8,128)S(1)} %fusion.154), channel_id=1, source_target_pairs={{0,256},{64,320},{128,384},{192,448},{256,0},{320,64},{384,128},{4... | collective-permute-start | bytes 196616 | tf_op jit(solution)/shard_map/ppermute | solution.py:85
  75.5 9.5 %collective-permute-start.7 = (f32[46,512]{1,0:T(8,128)S(1)}, f32[46,512]{1,0:T(8,128)S(1)}, u32[]{:S(2)}, u32[]{:S(2)}) collective-permute-start(f32[46,512]{1,0:T(8,128)S(1)} %concatenate.24), channel_id=1, source_target_pairs={{8,0},{16,8},{24,16},{32,24},{40,32},{48,40},{56,48},{64,56},{72,6... | collective-permute-start | bytes 282632 | tf_op jit(solution)/shard_map/ppermute | solution.py:19
  86.9 3.4 %copy-start.47 = (f32[1,1,512]{2,1,0:T(1,128)S(1)}, f32[1,1,512]{2,1,0:T(1,128)}, u32[]{:S(2)}) copy-start(f32[1,1,512]{2,1,0:T(1,128)} %copy-done.46) | copy-start | bytes 6148
  86.9 3.4 %copy-start.49 = (f32[1,1,512]{2,1,0:T(1,128)S(1)}, f32[1,1,512]{2,1,0:T(1,128)}, u32[]{:S(2)}) copy-start(f32[1,1,512]{2,1,0:T(1,128)} %copy-done.48) | copy-start | bytes 6148
  86.9 3.3 %copy-start.51 = (f32[1,1,512]{2,1,0:T(1,128)S(1)}, f32[1,1,512]{2,1,0:T(1,128)}, u32[]{:S(2)}) copy-start(f32[1,1,512]{2,1,0:T(1,128)} %copy-done.50) | copy-start | bytes 6148
  86.9 3.3 %copy-start.53 = (f32[1,1,512]{2,1,0:T(1,128)S(1)}, f32[1,1,512]{2,1,0:T(1,128)}, u32[]{:S(2)}) copy-start(f32[1,1,512]{2,1,0:T(1,128)} %copy-done.52) | copy-start | bytes 6148
  86.9 3.3 %copy-start.55 = (f32[1,1,512]{2,1,0:T(1,128)S(1)}, f32[1,1,512]{2,1,0:T(1,128)}, u32[]{:S(2)}) copy-start(f32[1,1,512]{2,1,0:T(1,128)} %copy-done.54) | copy-start | bytes 6148
  87.0 4.2 %copy-start.39 = (f32[1,1,512]{2,1,0:T(1,128)S(1)}, f32[1,1,512]{2,1,0:T(1,128)}, u32[]{:S(2)}) copy-start(f32[1,1,512]{2,1,0:T(1,128)} %get-tuple-element.50) | copy-start | bytes 6148
  87.0 4.2 %copy-start.40 = (f32[1,1,512]{2,1,0:T(1,128)S(1)}, f32[1,1,512]{2,1,0:T(1,128)}, u32[]{:S(2)}) copy-start(f32[1,1,512]{2,1,0:T(1,128)} %get-tuple-element.63) | copy-start | bytes 6148
  87.0 4.2 %copy-start.41 = (f32[1,1,512]{2,1,0:T(1,128)S(1)}, f32[1,1,512]{2,1,0:T(1,128)}, u32[]{:S(2)}) copy-start(f32[1,1,512]{2,1,0:T(1,128)} %get-tuple-element.64) | copy-start | bytes 6148
  87.0 4.2 %copy-start.42 = (f32[1,1,512]{2,1,0:T(1,128)S(1)}, f32[1,1,512]{2,1,0:T(1,128)}, u32[]{:S(2)}) copy-start(f32[1,1,512]{2,1,0:T(1,128)} %get-tuple-element.65) | copy-start | bytes 6148
  87.0 4.2 %copy-start.43 = (f32[1,1,512]{2,1,0:T(1,128)S(1)}, f32[1,1,512]{2,1,0:T(1,128)}, u32[]{:S(2)}) copy-start(f32[1,1,512]{2,1,0:T(1,128)} %get-tuple-element.66) | copy-start | bytes 6148
  87.0 4.2 %copy-start.44 = (f32[1,1,512]{2,1,0:T(1,128)S(1)}, f32[1,1,512]{2,1,0:T(1,128)}, u32[]{:S(2)}) copy-start(f32[1,1,512]{2,1,0:T(1,128)} %get-tuple-element.67) | copy-start | bytes 6148
  87.0 4.2 %copy-start.45 = (f32[1,1,512]{2,1,0:T(1,128)S(1)}, f32[1,1,512]{2,1,0:T(1,128)}, u32[]{:S(2)}) copy-start(f32[1,1,512]{2,1,0:T(1,128)} %get-tuple-element.68) | copy-start | bytes 6148
  (18 other events, 40.5 us)

commit v7 on v6

--- a/solution.py
+++ b/solution.py
@@ -78,15 +78,17 @@
     return rounds
 
 
-def cube_scan(window, rounds, axis, size):
+def cube_scan(window, rounds, axis, size, held):
     entering = jnp.zeros_like(window)
     shift = 1
     for keep, take, add in rounds:
         arrived = lax.ppermute(window, axis, [(source, source ^ shift) for source in range(size)])
+        if shift == 1:
+            held, arrived = lax.optimization_barrier((held, arrived))
         entering = entering + add * arrived
         window = keep * window + take * arrived
         shift *= 2
-    return entering, window
+    return entering, window, held
 
 
 def shards(inner, u_query, u_key, u_value, short_filter, decay_rate, residue, grad_out):
@@ -110,12 +112,6 @@
     weights = residue * jnp.sqrt(-jnp.expm1(-2.0 * rates))
     lags = jnp.arange(block_len + 1).astype(jnp.float32)
     powers = jnp.exp(-rates[:, :, None] * lags)
-    centred = jnp.arange(block_len).astype(jnp.float32) - block_len // 2
-    falling = weights[:, None, :] * jnp.exp(-centred[None, :, None] * rates[:, None, :])
-    rising = jnp.exp(centred[None, None, :] * rates[:, :, None])
-    toeplitz = jnp.einsum("gtm,gms->gts", falling, rising, precision=precise)
-    lower = jnp.arange(block_len)[:, None] >= jnp.arange(block_len)[None, :]
-    toeplitz = jnp.where(lower[None], toeplitz, 0.0)
 
     signal = product.reshape(block_len, group_count, GROUP)
     cotangent = grad_conv.reshape(block_len, group_count, GROUP)
@@ -145,11 +141,19 @@
     factors = jnp.exp(-decay_step[None] * terms[:, None, None])
     inner_rounds = cube_weights(factors, inner, member)
     outer_rounds = cube_weights(factors[len(inner_terms) :], outer, band)
-    near, group = cube_scan(jnp.stack([end_state, start_state]), inner_rounds, "xc", inner)
-    far, _ = cube_scan(group, outer_rounds, "zl", outer)
+    near, group, (rates, weights) = cube_scan(
+        jnp.stack([end_state, start_state]), inner_rounds, "xc", inner, (rates, weights)
+    )
+    far, _, _ = cube_scan(group, outer_rounds, "zl", outer, ())
     entering = near[0] + factors[-4] * far[0]
     leaving = near[1] + factors[-3] * far[1]
 
+    centred = jnp.arange(block_len).astype(jnp.float32) - block_len // 2
+    falling = weights[:, None, :] * jnp.exp(-centred[None, :, None] * rates[:, None, :])
+    rising = jnp.exp(centred[None, None, :] * rates[:, :, None])
+    toeplitz = jnp.einsum("gtm,gms->gts", falling, rising, precision=precise)
+    lower = jnp.arange(block_len)[:, None] >= jnp.arange(block_len)[None, :]
+    toeplitz = jnp.where(lower[None], toeplitz, 0.0)
     local_conv = split_dot("gts,sgc->tgc", toeplitz, signal).reshape(block_len, channels)
     local_grad = split_dot("gts,tgc->sgc", toeplitz, cotangent).reshape(block_len, channels)
     lead_fwd = (weights[:, :, None] * powers[:, :, 1:]).reshape(group_count * order, block_len)

time: 93.4 us -> 76.9 us (0.82)
  the two profiles are of different devices: /device:TPU:1 before, /device:TPU:15 now
where the time goes in v7:
time: 76.9 us; the launch traced here: 75.7 us
  starting transfers between devices  33.9 us (44%)
  other arithmetic  11.6 us (15%)
  waiting for transfers between devices  9.73 us (13%)
  matrix products  9.61 us (12%)
  local copies, waits for them, and re-layouts  8.91 us (12%)
  between operations  1.96 us (3%)
    ppermute x6, starting transfers between devices, cube_scan(): lax.ppermute(window, axis, [(source, source ^ shift) for source in range(...  24.1 us
    ppermute x2, starting transfers between devices, from_behind(): lax.ppermute(value, axis, [(source, source + steps) for source in range(l...  9.82 us
    ppermute x6, waiting for transfers between devices, cube_scan(): lax.ppermute(window, axis, [(source, source ^ shift) for source in range(...  5.58 us
    ppermute x2, waiting for transfers between devices, from_behind(): lax.ppermute(value, axis, [(source, source + steps) for source in range(l...  4.16 us
    dot_general x1, matrix products, shards(): toeplitz = jnp.einsum('gtm,gms->gts', falling, rising, precision=precise)  3.65 us
    slice x2, local copies, waits for them, and re-layouts, short_causal(): filter_taps[offset] * padded[SHORT - 1 - offset:SHORT - 1 - offset + length]  3.14 us
    concatenate x1, local copies, waits for them, and re-layouts, shards(): jnp.concatenate([local_conv[:edge], local_grad[:edge], grad_out[:edge].as...  2.44 us
    convert_element_type x9, other arithmetic, rounded(): return lax.optimization_barrier(values.astype(jnp.bfloat16))  2.23 us
  transfers between devices with their start and end apart: 8, of which 5 were waited for; matrix products, arithmetic and copies ran while one was open for 24% of the time, Pallas kernels for 0%

profile of v7, /device:TPU:15, one launch (start us, length us, event | category | flops | bytes accessed | tf_op | source)
XLA Modules:
  0.0 75.7 jit_solution(5954883644711840032)
XLA Ops:
  0.6 0.7 slice_bitcast_fusion.6
  1.4 0.7 slice_bitcast_fusion.4
  2.1 4.0 %collective-permute-start = (bf16[3,6,512]{2,1,0:T(8,128)(2,1)S(1)}, bf16[3,6,512]{2,1,0:T(8,128)(2,1)S(1)}, u32[]{:S(2)}, u32[]{:S(2)}) collective-permute-start(bf16[3,6,512]{2,1,0:T(8,128)(2,1)S(1)} %pad_maximum_fusion.7), channel_id=1, source_target_pairs={{0,8},{8,16},{16,24},{24,32},{32,40},{40,48},{48,56},{56,64},{64,7... | collective-permute-start | bytes 55304 | tf_op jit(solution)/shard_map/ppermute | solution.py:19
  6.1 1.8 %fusion.181 = (f32[1,1,512]{2,1,0:T(1,128)}, f32[1,1,512]{2,1,0:T(1,128)S(1)}, f32[1,1,512]{2,1,0:T(1,128)S(1)}, f32[1,1,512]{2,1,0:T(1,128)S(1)}, f32[1,1,512]{...) fusion(f32[3,7,512]{2,1,0:T(8,128)} %param.10), kind=kLoop, calls=%fused_computation.327 | loop fusion | bytes 77824 | tf_op jit(solution)/shard_map/slice | solution.py:32
  8.0 1.4 %fusion.182 = (f32[1,1,512]{2,1,0:T(1,128)}, f32[1,1,512]{2,1,0:T(1,128)}) fusion(f32[3,7,512]{2,1,0:T(8,128)} %param.10), kind=kLoop, calls=%fused_computation.328 | loop fusion | bytes 8192 | tf_op jit(solution)/shard_map/slice | solution.py:32
  9.4 1.3 %negate_bitcast_fusion = (f32[16,32]{1,0:T(8,128)S(1)}, f32[32,16]{0,1:T(8,128)S(1)}, f32[32,16]{0,1:T(8,128)}) fusion(f32[32,16]{0,1:T(8,128)} %param.11, f32[32,16]{0,1:T(8,128)} %param.12), kind=kLoop, calls=%fused_computation.306 | loop fusion | flops 3072 | bytes 10240 | tf_op jit(solution)/shard_map/neg | solution.py:141
  10.7 0.1 copy.25
  10.8 0.1 multiply_exponential_fusion.1
  11.0 0.1 rev.6
  11.3 0.6 slice_convert_fusion.2
  11.9 0.1 broadcast_in_dim.12
  12.1 0.2 neg.35
  12.2 0.1 stack.155
  12.4 0.2 multiply_exponential_fusion
  12.6 0.7 slice_select_fusion.6
  13.3 0.7 slice_select_fusion.7
  14.0 0.5 convert_add_fusion
  14.7 0.2 fusion.93
  15.0 0.9 %fusion.76 = bf16[128,512]{1,0:T(8,128)(2,1)S(1)} fusion(f32[6,512]{1,0:T(8,128)S(1)} %get-tuple-element.77, f32[128,512]{1,0:T(8,128)S(1)} %convert_element_type.226, f32[512]{0:T(512)} %bitcast.180, f32[512]{0:T(512)} %bitcast.178, f32[512]{0:T(512)S(1)} %bitcast.168, f32[512]{0:T(512)S(1)} %bitcast.170, f32[512]{0:T(512)S(1)} %bitcast.172, ...), kind=kLoop, calls=%fused_computation.130 | loop fusion | flops 1310720 | bytes 419840 | tf_op jit(solution)/shard_map/convert_element_type | solution.py:23
  15.9 0.6 slice_convert_fusion.1
  16.6 0.2 fusion.110
  16.9 0.3 fusion.183
  17.2 0.3 convolution_add_fusion.1
  17.5 0.3 fusion.184
  17.8 0.3 convolution_add_fusion
  18.1 0.3 multiply_reduce_fusion.1
  18.4 1.9 %collective-permute-start.1 = (f32[2,16,512]{2,1,0:T(8,128)S(1)}, f32[2,16,512]{2,1,0:T(8,128)S(1)}, u32[]{:S(2)}, u32[]{:S(2)}) collective-permute-start(f32[2,16,512]{2,1,0:T(8,128)S(1)} %pad_maximum_fusion.6), channel_id=1, source_target_pairs={{0,8},{8,0},{16,24},{24,16},{32,40},{40,32},{48,56},{56,48},{1,9},... | collective-permute-start | bytes 196616 | tf_op jit(solution)/shard_map/ppermute | solution.py:85
  20.3 0.6 slice_convert_fusion
  20.9 0.1 copy.33
  21.0 0.1 copy.24
  21.1 0.4 collective-permute-done.1
  21.5 0.1 copy.26
  21.7 1.9 %collective-permute-start.2 = (f32[2,16,512]{2,1,0:T(8,128)S(1)}, f32[2,16,512]{2,1,0:T(8,128)S(1)}, u32[]{:S(2)}, u32[]{:S(2)}) collective-permute-start(f32[2,16,512]{2,1,0:T(8,128)S(1)} %fusion.148), channel_id=1, source_target_pairs={{0,16},{8,24},{16,0},{24,8},{32,48},{40,56},{48,32},{56,40},{1,17}... | collective-permute-start | bytes 196616 | tf_op jit(solution)/shard_map/ppermute | solution.py:85
  23.6 3.7 %fusion.133 = f32[32,128,128]{2,1,0:T(8,128)S(1)} fusion(f32[32,16]{1,0:T(8,128)S(1)} %copy.27, f32[128]{0:T(128)S(1)} %copy-done.60, f32[128]{0:T(128)S(1)} %copy-done.61, f32[32,16]{1,0:T(8,128)S(1)} %copy.26), kind=kOutput, calls=%fused_computation.211 | convolution fusion | flops 100859904 | bytes 2102272 | tf_op jit(solution)/shard_map/gtm,gms->gts/dot_general | solution.py:154
  27.3 0.4 fusion.11
  27.7 0.4 convolution_add_fusion.2
  28.2 3.0 %collective-permute-start.3 = (f32[2,16,512]{2,1,0:T(8,128)S(1)}, f32[2,16,512]{2,1,0:T(8,128)S(1)}, u32[]{:S(2)}, u32[]{:S(2)}) collective-permute-start(f32[2,16,512]{2,1,0:T(8,128)S(1)} %fusion.149), channel_id=1, source_target_pairs={{0,32},{8,40},{16,48},{24,56},{32,0},{40,8},{48,16},{56,24},{1,33}... | collective-permute-start | bytes 196616 | tf_op jit(solution)/shard_map/ppermute | solution.py:85
  31.2 0.6 fusion.12
  31.8 2.9 %collective-permute-done.3 = f32[2,16,512]{2,1,0:T(8,128)S(1)} collective-permute-done((f32[2,16,512]{2,1,0:T(8,128)S(1)}, f32[2,16,512]{2,1,0:T(8,128)S(1)}, u32[]{:S(2)}, u32[]{:S(2)}) %collective-permute-start.3) | collective-permute-done | bytes 65568 | tf_op jit(solution)/shard_map/ppermute | solution.py:85
  34.9 3.7 %collective-permute-start.4 = (f32[2,16,512]{2,1,0:T(8,128)S(1)}, f32[2,16,512]{2,1,0:T(8,128)S(1)}, u32[]{:S(2)}, u32[]{:S(2)}) collective-permute-start(f32[2,16,512]{2,1,0:T(8,128)S(1)} %get-tuple-element.54), channel_id=1, source_target_pairs={{0,64},{64,0},{128,192},{192,128},{256,320},{320,256},{384,448},{4... | collective-permute-start | bytes 196616 | tf_op jit(solution)/shard_map/ppermute | solution.py:85
  38.6 0.7 convolution_add_fusion.3
  39.2 1.0 %collective-permute-done.4 = f32[2,16,512]{2,1,0:T(8,128)S(1)} collective-permute-done((f32[2,16,512]{2,1,0:T(8,128)S(1)}, f32[2,16,512]{2,1,0:T(8,128)S(1)}, u32[]{:S(2)}, u32[]{:S(2)}) %collective-permute-start.4) | collective-permute-done | bytes 65568 | tf_op jit(solution)/shard_map/ppermute | solution.py:85
  40.2 6.5 %collective-permute-start.5 = (f32[2,16,512]{2,1,0:T(8,128)S(1)}, f32[2,16,512]{2,1,0:T(8,128)S(1)}, u32[]{:S(2)}, u32[]{:S(2)}) collective-permute-start(f32[2,16,512]{2,1,0:T(8,128)S(1)} %fusion.153), channel_id=1, source_target_pairs={{0,128},{64,192},{128,0},{192,64},{256,384},{320,448},{384,256},{4... | collective-permute-start | bytes 196616 | tf_op jit(solution)/shard_map/ppermute | solution.py:85
  46.8 0.2 fusion.180
  47.0 0.1 rev.7
  47.1 1.3 %collective-permute-done.5 = f32[2,16,512]{2,1,0:T(8,128)S(1)} collective-permute-done((f32[2,16,512]{2,1,0:T(8,128)S(1)}, f32[2,16,512]{2,1,0:T(8,128)S(1)}, u32[]{:S(2)}, u32[]{:S(2)}) %collective-permute-start.5) | collective-permute-done | bytes 65568 | tf_op jit(solution)/shard_map/ppermute | solution.py:85
  48.4 7.1 %collective-permute-start.6 = (f32[2,16,512]{2,1,0:T(8,128)S(1)}, f32[2,16,512]{2,1,0:T(8,128)S(1)}, u32[]{:S(2)}, u32[]{:S(2)}) collective-permute-start(f32[2,16,512]{2,1,0:T(8,128)S(1)} %fusion.154), channel_id=1, source_target_pairs={{0,256},{64,320},{128,384},{192,448},{256,0},{320,64},{384,128},{4... | collective-permute-start | bytes 196616 | tf_op jit(solution)/shard_map/ppermute | solution.py:85
  55.5 0.1 broadcast_multiply_fusion.2
  55.7 0.1 copy.43
  55.8 0.1 copy.35
  55.9 2.4 %concatenate.24 = f32[46,512]{1,0:T(8,128)S(1)} concatenate(f32[6,512]{1,0:T(8,128)S(1)} %copy.35, f32[6,512]{1,0:T(8,128)S(1)} %copy.43, f32[6,512]{1,0:T(8,128)} %slice_convert_fusion.2, f32[6,512]{1,0:T(8,128)} %slice_convert_fusion.1, f32[6,512]{1,0:T(8,128)} %slice_convert_fusion, f32[16,512]{1,0:T(8,128)S(1)} %get-tuple-element.11), dimensions={0} | concatenate | bytes 188416 | tf_op jit(solution)/shard_map/concatenate | solution.py:169
  58.3 5.8 %collective-permute-start.7 = (f32[46,512]{1,0:T(8,128)S(1)}, f32[46,512]{1,0:T(8,128)S(1)}, u32[]{:S(2)}, u32[]{:S(2)}) collective-permute-start(f32[46,512]{1,0:T(8,128)S(1)} %concatenate.24), channel_id=1, source_target_pairs={{8,0},{16,8},{24,16},{32,24},{40,32},{48,40},{56,48},{64,56},{72,6... | collective-permute-start | bytes 282632 | tf_op jit(solution)/shard_map/ppermute | solution.py:19
  64.2 0.1 copy.38
  64.3 0.1 copy.32
  64.5 4.2 %collective-permute-done.7 = f32[46,512]{1,0:T(8,128)S(1)} collective-permute-done((f32[46,512]{1,0:T(8,128)S(1)}, f32[46,512]{1,0:T(8,128)S(1)}, u32[]{:S(2)}, u32[]{:S(2)}) %collective-permute-start.7) | collective-permute-done | bytes 94240 | tf_op jit(solution)/shard_map/ppermute | solution.py:19
  68.7 0.8 %fusion.3 = bf16[128,512]{1,0:T(8,128)(2,1)S(1)} fusion(f32[128,512]{1,0:T(8,128)S(1)} %copy.38, f32[32,16,128]{2,1,0:T(8,128)S(1)} %broadcast_multiply_fusion.2, f32[16,512]{1,0:T(8,128)S(1)} %get-tuple-element.13, f32[32,512]{1,0:T(8,128)S(1)} %fusion.155), kind=kOutput, calls=%fused_computation.11 | convolution fusion | flops 403046400 | bytes 753664 | tf_op jit(solution)/shard_map/ks,kc->sc/dot_general | solution.py:164
  69.6 0.3 broadcast_multiply_fusion
  69.8 0.6 fusion.164
  70.6 0.6 fusion.128
  71.4 0.8 %fusion.4 = bf16[128,512]{1,0:T(8,128)(2,1)S(1)} fusion(f32[128,512]{1,0:T(8,128)S(1)} %copy.32, f32[32,16,128]{2,1,0:T(8,128)S(1)} %get-tuple-element.39, f32[16,512]{1,0:T(8,128)S(1)} %get-tuple-element.15, f32[32,512]{1,0:T(8,128)S(1)} %fusion.155), kind=kOutput, calls=%fused_computation.12 | convolution fusion | flops 403046400 | bytes 753664 | tf_op jit(solution)/shard_map/kt,kc->tc/dot_general | solution.py:163
  72.1 0.7 fusion.16
  72.9 0.9 %fusion.25 = bf16[128,512]{1,0:T(8,128)(2,1)} fusion(f32[6,512]{1,0:T(8,128)S(1)} %convert_element_type.273, f32[128,512]{1,0:T(8,128)S(1)} %convert_element_type.271, f32[512]{0:T(512)S(1)} %bitcast.181, f32[512]{0:T(512)S(1)} %bitcast.179, f32[512]{0:T(512)S(1)} %bitcast.169, f32[512]{0:T(512)S(1)} %bitcast.171, f32[512]{0:T(512)S(1)} %bitcast.173, ...), kind=kLoop, calls=%fused_computation.79 | loop fusion | flops 1310720 | bytes 419840 | tf_op jit(solution)/shard_map/convert_element_type | solution.py:202
  73.9 0.9 %fusion.42 = bf16[128,512]{1,0:T(8,128)(2,1)} fusion(f32[6,512]{1,0:T(8,128)S(1)} %convert_element_type.268, f32[128,512]{1,0:T(8,128)S(1)} %convert_element_type.264, f32[512]{0:T(512)S(1)} %bitcast.155, f32[512]{0:T(512)S(1)} %bitcast.157, f32[512]{0:T(512)S(1)} %bitcast.159, f32[512]{0:T(512)S(1)} %bitcast.161, f32[512]{0:T(512)S(1)} %bitcast.163, ...), kind=kLoop, calls=%fused_computation.96 | loop fusion | flops 1310720 | bytes 419840 | tf_op jit(solution)/shard_map/convert_element_type | solution.py:201
  74.8 0.9 %fusion.59 = bf16[128,512]{1,0:T(8,128)(2,1)} fusion(f32[6,512]{1,0:T(8,128)S(1)} %convert_element_type.259, f32[128,512]{1,0:T(8,128)S(1)} %convert_element_type.252, f32[512]{0:T(512)S(1)} %bitcast.143, f32[512]{0:T(512)S(1)} %bitcast.145, f32[512]{0:T(512)S(1)} %bitcast.147, f32[512]{0:T(512)S(1)} %bitcast.149, f32[512]{0:T(512)S(1)} %bitcast.151, ...), kind=kLoop, calls=%fused_computation.113 | loop fusion | flops 1310720 | bytes 419840 | tf_op jit(solution)/shard_map/convert_element_type | solution.py:200
  (160 shorter events, 1.0 us)
Async XLA Ops:
  0.6 10.7 %copy-start = (bf16[128,512]{1,0:T(8,128)(2,1)S(1)}, bf16[128,512]{1,0:T(8,128)(2,1)}, u32[]{:S(2)}) copy-start(bf16[128,512]{1,0:T(8,128)(2,1)} %param.13) | copy-start | bytes 393220
  2.1 12.5 %collective-permute-start = (bf16[3,6,512]{2,1,0:T(8,128)(2,1)S(1)}, bf16[3,6,512]{2,1,0:T(8,128)(2,1)S(1)}, u32[]{:S(2)}, u32[]{:S(2)}) collective-permute-start(bf16[3,6,512]{2,1,0:T(8,128)(2,1)S(1)} %pad_maximum_fusion.7), channel_id=1, source_target_pairs={{0,8},{8,16},{16,24},{24,32},{32,40},{40,48},{48,56},{56,64},{64,7... | collective-permute-start | bytes 55304 | tf_op jit(solution)/shard_map/ppermute | solution.py:19
  7.9 6.8 %copy-start.34 = (f32[1,1,512]{2,1,0:T(1,128)}, f32[1,1,512]{2,1,0:T(1,128)S(1)}, u32[]{:S(2)}) copy-start(f32[1,1,512]{2,1,0:T(1,128)S(1)} %get-tuple-element.61) | copy-start | bytes 6148
  7.9 6.8 %copy-start.36 = (f32[1,1,512]{2,1,0:T(1,128)}, f32[1,1,512]{2,1,0:T(1,128)S(1)}, u32[]{:S(2)}) copy-start(f32[1,1,512]{2,1,0:T(1,128)S(1)} %get-tuple-element.62) | copy-start | bytes 6148
  7.9 6.8 %copy-start.38 = (f32[1,1,512]{2,1,0:T(1,128)}, f32[1,1,512]{2,1,0:T(1,128)S(1)}, u32[]{:S(2)}) copy-start(f32[1,1,512]{2,1,0:T(1,128)S(1)} %get-tuple-element.63) | copy-start | bytes 6148
  7.9 6.8 %copy-start.40 = (f32[1,1,512]{2,1,0:T(1,128)}, f32[1,1,512]{2,1,0:T(1,128)S(1)}, u32[]{:S(2)}) copy-start(f32[1,1,512]{2,1,0:T(1,128)S(1)} %get-tuple-element.64) | copy-start | bytes 6148
  7.9 6.8 %copy-start.42 = (f32[1,1,512]{2,1,0:T(1,128)}, f32[1,1,512]{2,1,0:T(1,128)S(1)}, u32[]{:S(2)}) copy-start(f32[1,1,512]{2,1,0:T(1,128)S(1)} %get-tuple-element.65) | copy-start | bytes 6148
  8.0 6.8 %copy-start.44 = (f32[1,1,512]{2,1,0:T(1,128)}, f32[1,1,512]{2,1,0:T(1,128)S(1)}, u32[]{:S(2)}) copy-start(f32[1,1,512]{2,1,0:T(1,128)S(1)} %get-tuple-element.66) | copy-start | bytes 6148
  8.0 6.8 %copy-start.46 = (f32[1,1,512]{2,1,0:T(1,128)}, f32[1,1,512]{2,1,0:T(1,128)S(1)}, u32[]{:S(2)}) copy-start(f32[1,1,512]{2,1,0:T(1,128)S(1)} %get-tuple-element.67) | copy-start | bytes 6148
  8.0 7.0 %copy-start.48 = (f32[1,1,512]{2,1,0:T(1,128)}, f32[1,1,512]{2,1,0:T(1,128)S(1)}, u32[]{:S(2)}) copy-start(f32[1,1,512]{2,1,0:T(1,128)S(1)} %get-tuple-element.56) | copy-start | bytes 6148
  8.0 7.0 %copy-start.50 = (f32[1,1,512]{2,1,0:T(1,128)}, f32[1,1,512]{2,1,0:T(1,128)S(1)}, u32[]{:S(2)}) copy-start(f32[1,1,512]{2,1,0:T(1,128)S(1)} %get-tuple-element.57) | copy-start | bytes 6148
  8.0 7.0 %copy-start.52 = (f32[1,1,512]{2,1,0:T(1,128)}, f32[1,1,512]{2,1,0:T(1,128)S(1)}, u32[]{:S(2)}) copy-start(f32[1,1,512]{2,1,0:T(1,128)S(1)} %get-tuple-element.58) | copy-start | bytes 6148
  8.0 7.0 %copy-start.54 = (f32[1,1,512]{2,1,0:T(1,128)}, f32[1,1,512]{2,1,0:T(1,128)S(1)}, u32[]{:S(2)}) copy-start(f32[1,1,512]{2,1,0:T(1,128)S(1)} %get-tuple-element.59) | copy-start | bytes 6148
  8.0 7.0 %copy-start.56 = (f32[1,1,512]{2,1,0:T(1,128)}, f32[1,1,512]{2,1,0:T(1,128)S(1)}, u32[]{:S(2)}) copy-start(f32[1,1,512]{2,1,0:T(1,128)S(1)} %get-tuple-element.60) | copy-start | bytes 6148
  11.1 3.4 %copy-start.1 = (bf16[128,512]{1,0:T(8,128)(2,1)S(1)}, bf16[128,512]{1,0:T(8,128)(2,1)}, u32[]{:S(2)}) copy-start(bf16[128,512]{1,0:T(8,128)(2,1)} %param.8) | copy-start | bytes 393220
  11.1 3.4 %copy-start.2 = (bf16[128,512]{1,0:T(8,128)(2,1)S(1)}, bf16[128,512]{1,0:T(8,128)(2,1)}, u32[]{:S(2)}) copy-start(bf16[128,512]{1,0:T(8,128)(2,1)} %param.9) | copy-start | bytes 393220
  11.2 3.4 %copy-start.3 = (bf16[128,512]{1,0:T(8,128)(2,1)S(1)}, bf16[128,512]{1,0:T(8,128)(2,1)}, u32[]{:S(2)}) copy-start(bf16[128,512]{1,0:T(8,128)(2,1)} %param.7) | copy-start | bytes 393220
  12.5 4.0 %copy-start.20 = (f32[1,1,512]{2,1,0:T(1,128)S(1)}, f32[1,1,512]{2,1,0:T(1,128)}, u32[]{:S(2)}) copy-start(f32[1,1,512]{2,1,0:T(1,128)} %get-tuple-element.55) | copy-start | bytes 6148
  12.5 4.0 %copy-start.22 = (f32[1,1,512]{2,1,0:T(1,128)S(1)}, f32[1,1,512]{2,1,0:T(1,128)}, u32[]{:S(2)}) copy-start(f32[1,1,512]{2,1,0:T(1,128)} %get-tuple-element.68) | copy-start | bytes 6148
  12.6 4.0 %copy-start.24 = (f32[1,1,512]{2,1,0:T(1,128)S(1)}, f32[1,1,512]{2,1,0:T(1,128)}, u32[]{:S(2)}) copy-start(f32[1,1,512]{2,1,0:T(1,128)} %get-tuple-element.69) | copy-start | bytes 6148
  12.6 4.0 %copy-start.26 = (f32[1,1,512]{2,1,0:T(1,128)S(1)}, f32[1,1,512]{2,1,0:T(1,128)}, u32[]{:S(2)}) copy-start(f32[1,1,512]{2,1,0:T(1,128)} %get-tuple-element.70) | copy-start | bytes 6148
  12.6 4.0 %copy-start.28 = (f32[1,1,512]{2,1,0:T(1,128)S(1)}, f32[1,1,512]{2,1,0:T(1,128)}, u32[]{:S(2)}) copy-start(f32[1,1,512]{2,1,0:T(1,128)} %get-tuple-element.71) | copy-start | bytes 6148
  12.6 4.0 %copy-start.30 = (f32[1,1,512]{2,1,0:T(1,128)S(1)}, f32[1,1,512]{2,1,0:T(1,128)}, u32[]{:S(2)}) copy-start(f32[1,1,512]{2,1,0:T(1,128)} %get-tuple-element.72) | copy-start | bytes 6148
  12.6 4.0 %copy-start.32 = (f32[1,1,512]{2,1,0:T(1,128)S(1)}, f32[1,1,512]{2,1,0:T(1,128)}, u32[]{:S(2)}) copy-start(f32[1,1,512]{2,1,0:T(1,128)} %get-tuple-element.73) | copy-start | bytes 6148
  17.8 3.8 %copy-start.19 = (f32[32,16]{0,1:T(8,128)S(1)}, f32[32,16]{0,1:T(8,128)}, u32[]{:S(2)}) copy-start(f32[32,16]{0,1:T(8,128)} %get-tuple-element.7) | copy-start | bytes 6148
  17.8 3.8 %copy-start.18 = (f32[32,16]{0,1:T(8,128)S(1)}, f32[32,16]{0,1:T(8,128)}, u32[]{:S(2)}) copy-start(f32[32,16]{0,1:T(8,128)} %param.11) | copy-start | bytes 6148
  18.1 5.6 %copy-start.60 = (f32[128]{0:T(128)S(1)}, f32[128]{0:T(128)}, u32[]{:S(2)}) copy-start(f32[128]{0:T(128)} %get-tuple-element.84) | copy-start | bytes 1540
  18.1 5.6 %copy-start.61 = (f32[128]{0:T(128)S(1)}, f32[128]{0:T(128)}, u32[]{:S(2)}) copy-start(f32[128]{0:T(128)} %get-tuple-element.85) | copy-start | bytes 1540
  18.4 3.1 %collective-permute-start.1 = (f32[2,16,512]{2,1,0:T(8,128)S(1)}, f32[2,16,512]{2,1,0:T(8,128)S(1)}, u32[]{:S(2)}, u32[]{:S(2)}) collective-permute-start(f32[2,16,512]{2,1,0:T(8,128)S(1)} %pad_maximum_fusion.6), channel_id=1, source_target_pairs={{0,8},{8,0},{16,24},{24,16},{32,40},{40,32},{48,56},{56,48},{1,9},... | collective-permute-start | bytes 196616 | tf_op jit(solution)/shard_map/ppermute | solution.py:85
  21.7 6.5 %collective-permute-start.2 = (f32[2,16,512]{2,1,0:T(8,128)S(1)}, f32[2,16,512]{2,1,0:T(8,128)S(1)}, u32[]{:S(2)}, u32[]{:S(2)}) collective-permute-start(f32[2,16,512]{2,1,0:T(8,128)S(1)} %fusion.148), channel_id=1, source_target_pairs={{0,16},{8,24},{16,0},{24,8},{32,48},{40,56},{48,32},{56,40},{1,17}... | collective-permute-start | bytes 196616 | tf_op jit(solution)/shard_map/ppermute | solution.py:85
  28.1 6.6 %copy-start.4 = (f32[1,16,512]{2,1,0:T(8,128)S(1)}, f32[1,16,512]{2,1,0:T(8,128)}, u32[]{:S(2)}) copy-start(f32[1,16,512]{2,1,0:T(8,128)} %get-tuple-element.29) | copy-start | bytes 98308
  28.1 6.6 %copy-start.5 = (f32[1,16,512]{2,1,0:T(8,128)S(1)}, f32[1,16,512]{2,1,0:T(8,128)}, u32[]{:S(2)}) copy-start(f32[1,16,512]{2,1,0:T(8,128)} %get-tuple-element.34) | copy-start | bytes 98308
  28.1 6.6 %copy-start.6 = (f32[1,16,512]{2,1,0:T(8,128)S(1)}, f32[1,16,512]{2,1,0:T(8,128)}, u32[]{:S(2)}) copy-start(f32[1,16,512]{2,1,0:T(8,128)} %get-tuple-element.35) | copy-start | bytes 98308
  28.1 6.6 %copy-start.7 = (f32[1,16,512]{2,1,0:T(8,128)S(1)}, f32[1,16,512]{2,1,0:T(8,128)}, u32[]{:S(2)}) copy-start(f32[1,16,512]{2,1,0:T(8,128)} %get-tuple-element.36) | copy-start | bytes 98308
  28.1 6.6 %copy-start.8 = (f32[1,16,512]{2,1,0:T(8,128)S(1)}, f32[1,16,512]{2,1,0:T(8,128)}, u32[]{:S(2)}) copy-start(f32[1,16,512]{2,1,0:T(8,128)} %get-tuple-element.37) | copy-start | bytes 98308
  28.1 6.6 %copy-start.9 = (f32[1,16,512]{2,1,0:T(8,128)S(1)}, f32[1,16,512]{2,1,0:T(8,128)}, u32[]{:S(2)}) copy-start(f32[1,16,512]{2,1,0:T(8,128)} %get-tuple-element.16) | copy-start | bytes 98308
  28.1 6.6 %copy-start.10 = (f32[1,16,512]{2,1,0:T(8,128)S(1)}, f32[1,16,512]{2,1,0:T(8,128)}, u32[]{:S(2)}) copy-start(f32[1,16,512]{2,1,0:T(8,128)} %get-tuple-element.18) | copy-start | bytes 98308
  28.2 6.6 %copy-start.11 = (f32[1,16,512]{2,1,0:T(8,128)S(1)}, f32[1,16,512]{2,1,0:T(8,128)}, u32[]{:S(2)}) copy-start(f32[1,16,512]{2,1,0:T(8,128)} %get-tuple-element.28) | copy-start | bytes 98308
  28.2 6.5 %collective-permute-start.3 = (f32[2,16,512]{2,1,0:T(8,128)S(1)}, f32[2,16,512]{2,1,0:T(8,128)S(1)}, u32[]{:S(2)}, u32[]{:S(2)}) collective-permute-start(f32[2,16,512]{2,1,0:T(8,128)S(1)} %fusion.149), channel_id=1, source_target_pairs={{0,32},{8,40},{16,48},{24,56},{32,0},{40,8},{48,16},{56,24},{1,33}... | collective-permute-start | bytes 196616 | tf_op jit(solution)/shard_map/ppermute | solution.py:85
  31.8 8.4 %copy-start.16 = (f32[1,16,512]{2,1,0:T(8,128)S(1)}, f32[1,16,512]{2,1,0:T(8,128)}, u32[]{:S(2)}) copy-start(f32[1,16,512]{2,1,0:T(8,128)} %get-tuple-element.19) | copy-start | bytes 98308
  31.8 8.4 %copy-start.17 = (f32[1,16,512]{2,1,0:T(8,128)S(1)}, f32[1,16,512]{2,1,0:T(8,128)}, u32[]{:S(2)}) copy-start(f32[1,16,512]{2,1,0:T(8,128)} %get-tuple-element.25) | copy-start | bytes 98308
  34.9 13.6 %copy-start.14 = (f32[1,16,512]{2,1,0:T(8,128)S(1)}, f32[1,16,512]{2,1,0:T(8,128)}, u32[]{:S(2)}) copy-start(f32[1,16,512]{2,1,0:T(8,128)} %get-tuple-element.20) | copy-start | bytes 98308
  34.9 13.6 %copy-start.15 = (f32[1,16,512]{2,1,0:T(8,128)S(1)}, f32[1,16,512]{2,1,0:T(8,128)}, u32[]{:S(2)}) copy-start(f32[1,16,512]{2,1,0:T(8,128)} %get-tuple-element.22) | copy-start | bytes 98308
  34.9 5.3 %collective-permute-start.4 = (f32[2,16,512]{2,1,0:T(8,128)S(1)}, f32[2,16,512]{2,1,0:T(8,128)S(1)}, u32[]{:S(2)}, u32[]{:S(2)}) collective-permute-start(f32[2,16,512]{2,1,0:T(8,128)S(1)} %get-tuple-element.54), channel_id=1, source_target_pairs={{0,64},{64,0},{128,192},{192,128},{256,320},{320,256},{384,448},{4... | collective-permute-start | bytes 196616 | tf_op jit(solution)/shard_map/ppermute | solution.py:85
  40.2 8.2 %collective-permute-start.5 = (f32[2,16,512]{2,1,0:T(8,128)S(1)}, f32[2,16,512]{2,1,0:T(8,128)S(1)}, u32[]{:S(2)}, u32[]{:S(2)}) collective-permute-start(f32[2,16,512]{2,1,0:T(8,128)S(1)} %fusion.153), channel_id=1, source_target_pairs={{0,128},{64,192},{128,0},{192,64},{256,384},{320,448},{384,256},{4... | collective-permute-start | bytes 196616 | tf_op jit(solution)/shard_map/ppermute | solution.py:85
  48.4 16.0 %collective-permute-start.6 = (f32[2,16,512]{2,1,0:T(8,128)S(1)}, f32[2,16,512]{2,1,0:T(8,128)S(1)}, u32[]{:S(2)}, u32[]{:S(2)}) collective-permute-start(f32[2,16,512]{2,1,0:T(8,128)S(1)} %fusion.154), channel_id=1, source_target_pairs={{0,256},{64,320},{128,384},{192,448},{256,0},{320,64},{384,128},{4... | collective-permute-start | bytes 196616 | tf_op jit(solution)/shard_map/ppermute | solution.py:85
  58.3 10.3 %collective-permute-start.7 = (f32[46,512]{1,0:T(8,128)S(1)}, f32[46,512]{1,0:T(8,128)S(1)}, u32[]{:S(2)}, u32[]{:S(2)}) collective-permute-start(f32[46,512]{1,0:T(8,128)S(1)} %concatenate.24), channel_id=1, source_target_pairs={{8,0},{16,8},{24,16},{32,24},{40,32},{48,40},{56,48},{64,56},{72,6... | collective-permute-start | bytes 282632 | tf_op jit(solution)/shard_map/ppermute | solution.py:19
  70.4 2.5 %copy-start.53 = (f32[1,1,512]{2,1,0:T(1,128)S(1)}, f32[1,1,512]{2,1,0:T(1,128)}, u32[]{:S(2)}) copy-start(f32[1,1,512]{2,1,0:T(1,128)} %copy-done.52) | copy-start | bytes 6148
  70.5 2.5 %copy-start.55 = (f32[1,1,512]{2,1,0:T(1,128)S(1)}, f32[1,1,512]{2,1,0:T(1,128)}, u32[]{:S(2)}) copy-start(f32[1,1,512]{2,1,0:T(1,128)} %copy-done.54) | copy-start | bytes 6148
  70.5 2.5 %copy-start.57 = (f32[1,1,512]{2,1,0:T(1,128)S(1)}, f32[1,1,512]{2,1,0:T(1,128)}, u32[]{:S(2)}) copy-start(f32[1,1,512]{2,1,0:T(1,128)} %copy-done.56) | copy-start | bytes 6148
  70.5 3.3 %copy-start.35 = (f32[1,1,512]{2,1,0:T(1,128)S(1)}, f32[1,1,512]{2,1,0:T(1,128)}, u32[]{:S(2)}) copy-start(f32[1,1,512]{2,1,0:T(1,128)} %copy-done.34) | copy-start | bytes 6148
  70.5 3.3 %copy-start.37 = (f32[1,1,512]{2,1,0:T(1,128)S(1)}, f32[1,1,512]{2,1,0:T(1,128)}, u32[]{:S(2)}) copy-start(f32[1,1,512]{2,1,0:T(1,128)} %copy-done.36) | copy-start | bytes 6148
  70.5 3.3 %copy-start.39 = (f32[1,1,512]{2,1,0:T(1,128)S(1)}, f32[1,1,512]{2,1,0:T(1,128)}, u32[]{:S(2)}) copy-start(f32[1,1,512]{2,1,0:T(1,128)} %copy-done.38) | copy-start | bytes 6148
  70.5 3.3 %copy-start.41 = (f32[1,1,512]{2,1,0:T(1,128)S(1)}, f32[1,1,512]{2,1,0:T(1,128)}, u32[]{:S(2)}) copy-start(f32[1,1,512]{2,1,0:T(1,128)} %copy-done.40) | copy-start | bytes 6148
  70.5 3.3 %copy-start.43 = (f32[1,1,512]{2,1,0:T(1,128)S(1)}, f32[1,1,512]{2,1,0:T(1,128)}, u32[]{:S(2)}) copy-start(f32[1,1,512]{2,1,0:T(1,128)} %copy-done.42) | copy-start | bytes 6148
  70.5 3.3 %copy-start.45 = (f32[1,1,512]{2,1,0:T(1,128)S(1)}, f32[1,1,512]{2,1,0:T(1,128)}, u32[]{:S(2)}) copy-start(f32[1,1,512]{2,1,0:T(1,128)} %copy-done.44) | copy-start | bytes 6148
  70.6 3.3 %copy-start.47 = (f32[1,1,512]{2,1,0:T(1,128)S(1)}, f32[1,1,512]{2,1,0:T(1,128)}, u32[]{:S(2)}) copy-start(f32[1,1,512]{2,1,0:T(1,128)} %copy-done.46) | copy-start | bytes 6148
  70.6 4.2 %copy-start.21 = (f32[1,1,512]{2,1,0:T(1,128)S(1)}, f32[1,1,512]{2,1,0:T(1,128)}, u32[]{:S(2)}) copy-start(f32[1,1,512]{2,1,0:T(1,128)} %get-tuple-element.55) | copy-start | bytes 6148
  70.6 4.2 %copy-start.23 = (f32[1,1,512]{2,1,0:T(1,128)S(1)}, f32[1,1,512]{2,1,0:T(1,128)}, u32[]{:S(2)}) copy-start(f32[1,1,512]{2,1,0:T(1,128)} %get-tuple-element.68) | copy-start | bytes 6148
  70.6 4.2 %copy-start.25 = (f32[1,1,512]{2,1,0:T(1,128)S(1)}, f32[1,1,512]{2,1,0:T(1,128)}, u32[]{:S(2)}) copy-start(f32[1,1,512]{2,1,0:T(1,128)} %get-tuple-element.69) | copy-start | bytes 6148
  70.6 4.2 %copy-start.27 = (f32[1,1,512]{2,1,0:T(1,128)S(1)}, f32[1,1,512]{2,1,0:T(1,128)}, u32[]{:S(2)}) copy-start(f32[1,1,512]{2,1,0:T(1,128)} %get-tuple-element.70) | copy-start | bytes 6148
  70.6 4.2 %copy-start.29 = (f32[1,1,512]{2,1,0:T(1,128)S(1)}, f32[1,1,512]{2,1,0:T(1,128)}, u32[]{:S(2)}) copy-start(f32[1,1,512]{2,1,0:T(1,128)} %get-tuple-element.71) | copy-start | bytes 6148
  70.6 4.2 %copy-start.31 = (f32[1,1,512]{2,1,0:T(1,128)S(1)}, f32[1,1,512]{2,1,0:T(1,128)}, u32[]{:S(2)}) copy-start(f32[1,1,512]{2,1,0:T(1,128)} %get-tuple-element.72) | copy-start | bytes 6148
  70.6 4.2 %copy-start.33 = (f32[1,1,512]{2,1,0:T(1,128)S(1)}, f32[1,1,512]{2,1,0:T(1,128)}, u32[]{:S(2)}) copy-start(f32[1,1,512]{2,1,0:T(1,128)} %get-tuple-element.73) | copy-start | bytes 6148
  (6 other events, 11.6 us)

commit v8 on v7

--- a/solution.py
+++ b/solution.py
@@ -102,6 +102,9 @@
         ]
     )
     before = from_behind(rim_rows, ("zl", "xc"), 1)
+    edge = SHORT - 1
+    head_rows = jnp.stack([u_query[:edge], u_key[:edge], u_value[:edge], grad_out[:edge]])
+    after = from_behind(head_rows, ("zl", "xc"), -1)
     q_short = rounded(short_causal(before[0], u_query, short_filter[0]))
     k_short = rounded(short_causal(before[1], u_key, short_filter[1]))
     v_short = rounded(short_causal(before[2], u_value, short_filter[2]))
@@ -136,7 +139,7 @@
     place = member.astype(jnp.float32)
     inner_terms = cube_coefficients(inner, member)
     outer_terms = [inner * term for term in cube_coefficients(outer, band)]
-    unit_terms = [place, inner - 1 - place, jnp.float32(1), jnp.float32(-1)]
+    unit_terms = [place, inner - 1 - place, jnp.float32(1)]
     terms = jnp.stack(inner_terms + outer_terms + unit_terms)
     factors = jnp.exp(-decay_step[None] * terms[:, None, None])
     inner_rounds = cube_weights(factors, inner, member)
@@ -145,8 +148,8 @@
         jnp.stack([end_state, start_state]), inner_rounds, "xc", inner, (rates, weights)
     )
     far, _, _ = cube_scan(group, outer_rounds, "zl", outer, ())
-    entering = near[0] + factors[-4] * far[0]
-    leaving = near[1] + factors[-3] * far[1]
+    entering = near[0] + factors[-3] * far[0]
+    leaving = near[1] + factors[-2] * far[1]
 
     centred = jnp.arange(block_len).astype(jnp.float32) - block_len // 2
     falling = weights[:, None, :] * jnp.exp(-centred[None, :, None] * rates[:, None, :])
@@ -165,32 +168,32 @@
     conv_out = rounded(local_conv + carried_conv)
     grad_prod = rounded(local_grad + carried_grad)
 
-    edge = SHORT - 1
-    ahead = jnp.concatenate(
-        [
-            local_conv[:edge],
-            local_grad[:edge],
-            grad_out[:edge].astype(jnp.float32),
-            k_short[:edge].astype(jnp.float32),
-            v_short[:edge].astype(jnp.float32),
-            start_state,
-        ]
-    )
-    ahead = from_behind(ahead, ("zl", "xc"), -1)
-    through = factors[-2] * entering + end_state
-    beyond = (leaving - ahead[5 * edge :]) * factors[-1]
+    q_next = rounded(short_causal(rim_rows[0], after[0], short_filter[0]))
+    k_next = rounded(short_causal(rim_rows[1], after[1], short_filter[1]))
+    v_next = rounded(short_causal(rim_rows[2], after[2], short_filter[2]))
+    p_next = rounded(k_next.astype(jnp.float32) * v_next.astype(jnp.float32))
+    gc_next = rounded(after[3].astype(jnp.float32) * q_next.astype(jnp.float32))
+    rate_rows = decay_step / block_len
+    weight_rows = jnp.repeat(weights.T, GROUP, axis=1)
+    lag_terms = jnp.concatenate([-jnp.arange(SHORT), jnp.arange(SHORT)]).astype(jnp.float32)
+    lag_powers = jnp.exp(rate_rows[None] * lag_terms[:, None, None])
+    falling_taps = (weight_rows[None] * lag_powers[:SHORT]).sum(1)
+    rising_taps = (weight_rows[None] * lag_powers[SHORT:]).sum(1)
+    rising_taps = jnp.where(jnp.arange(SHORT)[:, None] > 0, rising_taps, 0.0)
+    through = factors[-1] * entering + end_state
+    none_before = jnp.zeros((edge, channels), jnp.float32)
     next_conv = rounded(
-        ahead[:edge]
-        + jnp.einsum("kt,kc->tc", lead_fwd[:, :edge], spread(through), precision=precise)
+        short_causal(none_before, p_next, falling_taps)
+        + ((weight_rows * through)[None] * lag_powers[1:SHORT]).sum(1)
     )
     next_grad = rounded(
-        ahead[edge : 2 * edge]
-        + jnp.einsum("ks,kc->sc", lead_bwd[:, :edge], spread(beyond), precision=precise)
+        ((weight_rows * leaving)[None] * lag_powers[SHORT : SHORT + edge]).sum(1)
+        - short_causal(none_before, gc_next, rising_taps)
     )
     next_rows = (
-        rounded(ahead[2 * edge : 3 * edge] * next_conv.astype(jnp.float32)),
-        rounded(next_grad.astype(jnp.float32) * ahead[4 * edge : 5 * edge]),
-        rounded(next_grad.astype(jnp.float32) * ahead[3 * edge : 4 * edge]),
+        rounded(after[3].astype(jnp.float32) * next_conv.astype(jnp.float32)),
+        rounded(next_grad.astype(jnp.float32) * v_next.astype(jnp.float32)),
+        rounded(next_grad.astype(jnp.float32) * k_next.astype(jnp.float32)),
     )
 
     mixer_out = (q_short.astype(jnp.float32) * conv_out.astype(jnp.float32)).astype(jnp.bfloat16)

time: 76.9 us -> 95.5 us (1.24)
  the two profiles are of different devices: /device:TPU:15 before, /device:TPU:24 now
where the time goes in v8:
time: 95.5 us; the launch traced here: 94.2 us
  starting transfers between devices  38.3 us (40%)
  other arithmetic  28.3 us (30%)
  matrix products  10.5 us (11%)
  waiting for transfers between devices  8.2 us (9%)
  local copies, waits for them, and re-layouts  6.75 us (7%)
  between operations  2.2 us (2%)
    ppermute x6, starting transfers between devices, cube_scan(): lax.ppermute(window, axis, [(source, source ^ shift) for source in range(...  34.7 us
    ppermute x6, waiting for transfers between devices, cube_scan(): lax.ppermute(window, axis, [(source, source ^ shift) for source in range(...  8.2 us
    convert_element_type x15, other arithmetic, rounded(): return lax.optimization_barrier(values.astype(jnp.bfloat16))  5.12 us
    add x4, other arithmetic, cube_scan(): window = keep * window + take * arrived  4.01 us
    dot_general x1, matrix products, shards(): toeplitz = jnp.einsum('gtm,gms->gts', falling, rising, precision=precise)  3.66 us
    ppermute x2, starting transfers between devices, from_behind(): lax.ppermute(value, axis, [(source, source + steps) for source in range(l...  3.61 us
    slice x2, local copies, waits for them, and re-layouts, short_causal(): filter_taps[offset] * padded[SHORT - 1 - offset:SHORT - 1 - offset + length]  3.18 us
    dot_general x4, matrix products, split_dot(): jnp.einsum(spec, low, values, preferred_element_type=jnp.float32)  2.55 us
  transfers between devices with their start and end apart: 8, of which 5 were waited for; matrix products, arithmetic and copies ran while one was open for 27% of the time, Pallas kernels for 0%

profile of v8, /device:TPU:24, one launch (start us, length us, event | category | flops | bytes accessed | tf_op | source)
XLA Modules:
  0.0 94.2 jit_solution(17814281136450046572)
XLA Ops:
  0.6 0.7 slice_convert_fusion.2
  1.4 1.4 %slice_bitcast_fusion.8 = (bf16[1,6,512]{2,1,0:T(8,128)(2,1)S(1)}, f32[6,512]{1,0:T(8,128)}, bf16[1,6,512]{2,1,0:T(8,128)(2,1)S(1)}, bf16[1,6,512]{2,1,0:T(8,128...) fusion(bf16[128,512]{1,0:T(8,128)(2,1)} %param.9, bf16[128,512]{1,0:T(8,128)(2,1)} %param.8), kind=kLoop, calls=%fused_computation.428 | loop fusion | flops 6144 | bytes 73728 | tf_op jit(solution)/shard_map/stack | solution.py:106
  2.7 0.6 pad_maximum_fusion.8
  3.3 2.3 %collective-permute-start = (bf16[3,6,512]{2,1,0:T(8,128)(2,1)}, bf16[3,6,512]{2,1,0:T(8,128)(2,1)}, u32[]{:S(2)}, u32[]{:S(2)}) collective-permute-start(bf16[3,6,512]{2,1,0:T(8,128)(2,1)} %pad_maximum_fusion.8), channel_id=1, source_target_pairs={{0,8},{8,16},{16,24},{24,32},{32,40},{40,48},{48,56},{56,64},{64,7... | collective-permute-start | bytes 55304 | tf_op jit(solution)/shard_map/ppermute | solution.py:19
  5.7 0.7 slice_bitcast_fusion.7
  6.4 0.6 pad_maximum_fusion.7
  7.0 1.3 %collective-permute-start.7 = (bf16[4,6,512]{2,1,0:T(8,128)(2,1)}, bf16[4,6,512]{2,1,0:T(8,128)(2,1)}, u32[]{:S(2)}, u32[]{:S(2)}) collective-permute-start(bf16[4,6,512]{2,1,0:T(8,128)(2,1)} %pad_maximum_fusion.7), channel_id=1, source_target_pairs={{8,0},{16,8},{24,16},{32,24},{40,32},{48,40},{56,48},{64,56},{72,6... | collective-permute-start | bytes 73736 | tf_op jit(solution)/shard_map/ppermute | solution.py:19
  8.3 1.8 %fusion.262 = (f32[1,1,512]{2,1,0:T(1,128)S(1)}, f32[1,1,512]{2,1,0:T(1,128)}, f32[1,1,512]{2,1,0:T(1,128)}, f32[1,1,512]{2,1,0:T(1,128)}, f32[1,1,512]{2,1,0:T(...) fusion(f32[3,7,512]{2,1,0:T(8,128)} %param.10), kind=kLoop, calls=%fused_computation.461 | loop fusion | bytes 77824 | tf_op jit(solution)/shard_map/slice | solution.py:32
  10.1 1.4 %fusion.263 = (f32[1,1,512]{2,1,0:T(1,128)}, f32[1,1,512]{2,1,0:T(1,128)}) fusion(f32[3,7,512]{2,1,0:T(8,128)} %param.10), kind=kLoop, calls=%fused_computation.462 | loop fusion | bytes 8192 | tf_op jit(solution)/shard_map/slice | solution.py:32
  11.5 1.3 %fusion.266 = (f32[32,16]{0,1:T(8,128)S(1)}, f32[32,16]{0,1:T(8,128)}) fusion(f32[32,16]{0,1:T(8,128)} %param.11, f32[32,16]{0,1:T(8,128)} %param.12), kind=kLoop, calls=%fused_computation.465 | loop fusion | flops 2048 | bytes 8192 | tf_op jit(solution)/shard_map/neg | solution.py:117
  13.3 0.7 fusion.20
  14.0 0.6 convert_add_fusion
  14.7 0.7 fusion.19
  15.6 0.2 reshape.203
  16.1 0.2 multiply_exponential_fusion
  16.3 0.7 slice_select_fusion.6
  17.0 0.8 slice_select_fusion.7
  17.8 0.5 iota_compare_fusion.2
  18.5 0.7 fusion.249
  19.3 0.9 fusion.93
  20.2 0.9 fusion.76
  21.2 0.9 fusion.110
  22.2 1.2 %fusion.267 = f32[512,512]{1,0:T(8,128)S(1)} fusion(bf16[512,128]{1,0:T(8,128)(2,1)} %get-tuple-element.47, bf16[128,512]{1,0:T(8,128)(2,1)S(1)} %fusion.13), kind=kOutput, calls=%fused_computation.466 | convolution fusion | flops 67108864 | bytes 1310720 | tf_op jit(solution)/shard_map/ks,sc->kc/dot_general | solution.py:49
  23.4 1.2 %convolution_add_fusion.1 = f32[512,512]{1,0:T(8,128)S(1)} fusion(f32[512,512]{1,0:T(8,128)S(1)} %fusion.267, bf16[512,128]{1,0:T(8,128)(2,1)} %get-tuple-element.46, bf16[128,512]{1,0:T(8,128)(2,1)S(1)} %fusion.13), kind=kOutput, calls=%fused_computation.4 | convolution fusion | flops 67371008 | bytes 2359296 | tf_op jit(solution)/shard_map/ks,sc->kc/dot_general | solution.py:50
  24.6 0.3 fusion.268
  25.0 0.3 convolution_add_fusion
  25.5 0.3 multiply_reduce_fusion.1
  26.0 3.7 %collective-permute-start.1 = (f32[2,16,512]{2,1,0:T(8,128)S(1)}, f32[2,16,512]{2,1,0:T(8,128)S(1)}, u32[]{:S(2)}, u32[]{:S(2)}) collective-permute-start(f32[2,16,512]{2,1,0:T(8,128)S(1)} %pad_maximum_fusion.6), channel_id=1, source_target_pairs={{0,8},{8,0},{16,24},{24,16},{32,40},{40,32},{48,56},{56,48},{1,9},... | collective-permute-start | bytes 196616 | tf_op jit(solution)/shard_map/ppermute | solution.py:85
  29.8 0.7 fusion.244
  30.8 0.6 fusion.175
  31.4 0.6 convert_element_type.327
  32.2 3.7 %fusion.131 = f32[32,128,128]{2,1,0:T(8,128)S(1)} fusion(f32[32,16]{1,0:T(8,128)S(1)} %copy.38, f32[128]{0:T(128)S(1)} %copy-done.73, f32[128]{0:T(128)S(1)} %copy-done.74, f32[32,16]{1,0:T(8,128)S(1)} %copy.37), kind=kOutput, calls=%fused_computation.208 | convolution fusion | flops 100859904 | bytes 2102272 | tf_op jit(solution)/shard_map/gtm,gms->gts/dot_general | solution.py:157
  35.9 0.4 fusion.11
  36.2 0.4 convolution_add_fusion.2
  36.6 0.7 fusion.152
  37.3 3.5 %collective-permute-start.2 = (f32[2,16,512]{2,1,0:T(8,128)}, f32[2,16,512]{2,1,0:T(8,128)}, u32[]{:S(2)}, u32[]{:S(2)}) collective-permute-start(f32[2,16,512]{2,1,0:T(8,128)} %fusion.152), channel_id=1, source_target_pairs={{0,16},{8,24},{16,0},{24,8},{32,48},{40,56},{48,32},{56,40},{1,17}... | collective-permute-start | bytes 196616 | tf_op jit(solution)/shard_map/ppermute | solution.py:85
  40.8 0.6 fusion.12
  41.5 0.7 convolution_add_fusion.3
  42.3 0.8 mul.1066
  43.1 0.8 collective-permute-done.2
  43.9 0.9 fusion.153
  44.8 5.2 %collective-permute-start.3 = (f32[2,16,512]{2,1,0:T(8,128)S(1)}, f32[2,16,512]{2,1,0:T(8,128)S(1)}, u32[]{:S(2)}, u32[]{:S(2)}) collective-permute-start(f32[2,16,512]{2,1,0:T(8,128)S(1)} %fusion.153), channel_id=1, source_target_pairs={{0,32},{8,40},{16,48},{24,56},{32,0},{40,8},{48,16},{56,24},{1,33}... | collective-permute-start | bytes 196616 | tf_op jit(solution)/shard_map/ppermute | solution.py:85
  50.0 0.9 fusion.137
  50.9 1.6 %collective-permute-done.3 = f32[2,16,512]{2,1,0:T(8,128)S(1)} collective-permute-done((f32[2,16,512]{2,1,0:T(8,128)S(1)}, f32[2,16,512]{2,1,0:T(8,128)S(1)}, u32[]{:S(2)}, u32[]{:S(2)}) %collective-permute-start.3) | collective-permute-done | bytes 65568 | tf_op jit(solution)/shard_map/ppermute | solution.py:85
  52.5 1.0 %fusion.151 = (f32[2,16,512]{2,1,0:T(8,128)S(1)}, f32[2,16,512]{2,1,0:T(8,128)S(1)}) fusion(f32[2,16,512]{2,1,0:T(8,128)S(1)} %collective-permute-done.1, f32[1,16,512]{2,1,0:T(8,128)} %get-tuple-element.40, f32[1,16,512]{2,1,0:T(8,128)} %get-tuple-element.41, f32[2,16,512]{2,1,0:T(8,128)} %collective-permute-done.2, f32[1,16,512]{2,1,0:T(8,128)} %get-tuple-element.38, ...), kind=kLoop, calls=%fused_computation.232 | loop fusion | flops 212992 | bytes 655360 | tf_op jit(solution)/shard_map/add | solution.py:88
  53.5 6.2 %collective-permute-start.4 = (f32[2,16,512]{2,1,0:T(8,128)S(1)}, f32[2,16,512]{2,1,0:T(8,128)S(1)}, u32[]{:S(2)}, u32[]{:S(2)}) collective-permute-start(f32[2,16,512]{2,1,0:T(8,128)S(1)} %get-tuple-element.62), channel_id=1, source_target_pairs={{0,64},{64,0},{128,192},{192,128},{256,320},{320,256},{384,448},{4... | collective-permute-start | bytes 196616 | tf_op jit(solution)/shard_map/ppermute | solution.py:85
  59.7 0.7 broadcast_select_fusion
  60.3 1.6 %collective-permute-done.4 = f32[2,16,512]{2,1,0:T(8,128)S(1)} collective-permute-done((f32[2,16,512]{2,1,0:T(8,128)S(1)}, f32[2,16,512]{2,1,0:T(8,128)S(1)}, u32[]{:S(2)}, u32[]{:S(2)}) %collective-permute-start.4) | collective-permute-done | bytes 65568 | tf_op jit(solution)/shard_map/ppermute | solution.py:85
  61.9 0.9 fusion.157
  62.8 5.3 %collective-permute-start.5 = (f32[2,16,512]{2,1,0:T(8,128)S(1)}, f32[2,16,512]{2,1,0:T(8,128)}, u32[]{:S(2)}, u32[]{:S(2)}) collective-permute-start(f32[2,16,512]{2,1,0:T(8,128)S(1)} %fusion.157), channel_id=1, source_target_pairs={{0,128},{64,192},{128,0},{192,64},{256,384},{320,448},{384,256},{4... | collective-permute-start | bytes 196616 | tf_op jit(solution)/shard_map/ppermute | solution.py:85
  68.1 0.6 fusion.265
  68.7 1.7 %collective-permute-done.5 = f32[2,16,512]{2,1,0:T(8,128)} collective-permute-done((f32[2,16,512]{2,1,0:T(8,128)S(1)}, f32[2,16,512]{2,1,0:T(8,128)}, u32[]{:S(2)}, u32[]{:S(2)}) %collective-permute-start.5) | collective-permute-done | bytes 65568 | tf_op jit(solution)/shard_map/ppermute | solution.py:85
  70.4 1.6 %fusion.158 = f32[2,16,512]{2,1,0:T(8,128)} fusion(f32[2,16,512]{2,1,0:T(8,128)S(1)} %fusion.157, f32[1,16,512]{2,1,0:T(8,128)} %get-tuple-element.25, f32[1,16,512]{2,1,0:T(8,128)} %get-tuple-element.26, f32[2,16,512]{2,1,0:T(8,128)} %collective-permute-done.5), kind=kLoop, calls=%fused_computation.253 | loop fusion | flops 81920 | bytes 262144 | tf_op jit(solution)/shard_map/add | solution.py:89
  72.0 10.8 %collective-permute-start.6 = (f32[2,16,512]{2,1,0:T(8,128)}, f32[2,16,512]{2,1,0:T(8,128)}, u32[]{:S(2)}, u32[]{:S(2)}) collective-permute-start(f32[2,16,512]{2,1,0:T(8,128)} %fusion.158), channel_id=1, source_target_pairs={{0,256},{64,320},{128,384},{192,448},{256,0},{320,64},{384,128},{4... | collective-permute-start | bytes 196616 | tf_op jit(solution)/shard_map/ppermute | solution.py:85
  82.8 0.6 fusion.264
  84.0 2.5 %collective-permute-done.6 = f32[2,16,512]{2,1,0:T(8,128)} collective-permute-done((f32[2,16,512]{2,1,0:T(8,128)}, f32[2,16,512]{2,1,0:T(8,128)}, u32[]{:S(2)}, u32[]{:S(2)}) %collective-permute-start.6) | collective-permute-done | bytes 65568 | tf_op jit(solution)/shard_map/ppermute | solution.py:85
  86.5 1.0 %fusion.155 = f32[2,16,512]{2,1,0:T(8,128)S(1)} fusion(f32[2,16,512]{2,1,0:T(8,128)S(1)} %collective-permute-done.4, f32[1,16,512]{2,1,0:T(8,128)} %get-tuple-element.34, f32[1,16,512]{2,1,0:T(8,128)} %get-tuple-element.35, f32[2,16,512]{2,1,0:T(8,128)} %collective-permute-done.5, f32[1,16,512]{2,1,0:T(8,128)} %get-tuple-element.30, ...), kind=kLoop, calls=%fused_computation.243 | loop fusion | flops 131072 | bytes 458752 | tf_op jit(solution)/shard_map/add | solution.py:88
  87.5 0.9 fusion.3
  88.9 0.7 fusion.169
  89.7 0.9 fusion.4
  90.7 0.7 fusion.16
  91.5 0.9 fusion.25
  92.4 0.9 fusion.42
  93.4 0.9 fusion.59
  (199 shorter events, 2.9 us)
Async XLA Ops:
  0.6 14.8 %copy-start.5 = (f32[32,16]{0,1:T(8,128)S(1)}, f32[32,16]{0,1:T(8,128)}, u32[]{:S(2)}) copy-start(f32[32,16]{0,1:T(8,128)} %param.11) | copy-start | bytes 6148
  3.3 15.2 %collective-permute-start = (bf16[3,6,512]{2,1,0:T(8,128)(2,1)}, bf16[3,6,512]{2,1,0:T(8,128)(2,1)}, u32[]{:S(2)}, u32[]{:S(2)}) collective-permute-start(bf16[3,6,512]{2,1,0:T(8,128)(2,1)} %pad_maximum_fusion.8), channel_id=1, source_target_pairs={{0,8},{8,16},{16,24},{24,32},{32,40},{40,48},{48,56},{56,64},{64,7... | collective-permute-start | bytes 55304 | tf_op jit(solution)/shard_map/ppermute | solution.py:19
  7.0 22.8 %collective-permute-start.7 = (bf16[4,6,512]{2,1,0:T(8,128)(2,1)}, bf16[4,6,512]{2,1,0:T(8,128)(2,1)}, u32[]{:S(2)}, u32[]{:S(2)}) collective-permute-start(bf16[4,6,512]{2,1,0:T(8,128)(2,1)} %pad_maximum_fusion.7), channel_id=1, source_target_pairs={{8,0},{16,8},{24,16},{32,24},{40,32},{48,40},{56,48},{64,56},{72,6... | collective-permute-start | bytes 73736 | tf_op jit(solution)/shard_map/ppermute | solution.py:19
  10.0 11.2 %copy-start.12 = (f32[1,1,512]{2,1,0:T(1,128)}, f32[1,1,512]{2,1,0:T(1,128)S(1)}, u32[]{:S(2)}) copy-start(f32[1,1,512]{2,1,0:T(1,128)S(1)} %get-tuple-element.63) | copy-start | bytes 6148
  10.1 11.2 %copy-start.15 = (f32[1,1,512]{2,1,0:T(1,128)}, f32[1,1,512]{2,1,0:T(1,128)S(1)}, u32[]{:S(2)}) copy-start(f32[1,1,512]{2,1,0:T(1,128)S(1)} %get-tuple-element.76) | copy-start | bytes 6148
  10.1 11.2 %copy-start.18 = (f32[1,1,512]{2,1,0:T(1,128)}, f32[1,1,512]{2,1,0:T(1,128)S(1)}, u32[]{:S(2)}) copy-start(f32[1,1,512]{2,1,0:T(1,128)S(1)} %get-tuple-element.77) | copy-start | bytes 6148
  10.1 11.2 %copy-start.21 = (f32[1,1,512]{2,1,0:T(1,128)}, f32[1,1,512]{2,1,0:T(1,128)S(1)}, u32[]{:S(2)}) copy-start(f32[1,1,512]{2,1,0:T(1,128)S(1)} %get-tuple-element.78) | copy-start | bytes 6148
  17.0 5.1 %copy-start = (bf16[128,512]{1,0:T(8,128)(2,1)S(1)}, bf16[128,512]{1,0:T(8,128)(2,1)}, u32[]{:S(2)}) copy-start(bf16[128,512]{1,0:T(8,128)(2,1)} %param.13) | copy-start | bytes 393220
  24.9 5.6 %copy-start.11 = (f32[6,512]{1,0:T(8,128)S(1)}, f32[6,512]{1,0:T(8,128)}, u32[]{:S(2)}) copy-start(f32[6,512]{1,0:T(8,128)} %get-tuple-element.112) | copy-start | bytes 36868
  24.9 5.6 %copy-start.30 = (f32[1,1,512]{2,1,0:T(1,128)S(1)}, f32[1,1,512]{2,1,0:T(1,128)}, u32[]{:S(2)}) copy-start(f32[1,1,512]{2,1,0:T(1,128)} %get-tuple-element.69) | copy-start | bytes 6148
  24.9 5.6 %copy-start.32 = (f32[1,1,512]{2,1,0:T(1,128)S(1)}, f32[1,1,512]{2,1,0:T(1,128)}, u32[]{:S(2)}) copy-start(f32[1,1,512]{2,1,0:T(1,128)} %get-tuple-element.70) | copy-start | bytes 6148
  24.9 5.6 %copy-start.34 = (f32[1,1,512]{2,1,0:T(1,128)S(1)}, f32[1,1,512]{2,1,0:T(1,128)}, u32[]{:S(2)}) copy-start(f32[1,1,512]{2,1,0:T(1,128)} %get-tuple-element.71) | copy-start | bytes 6148
  25.0 5.6 %copy-start.36 = (f32[1,1,512]{2,1,0:T(1,128)S(1)}, f32[1,1,512]{2,1,0:T(1,128)}, u32[]{:S(2)}) copy-start(f32[1,1,512]{2,1,0:T(1,128)} %get-tuple-element.72) | copy-start | bytes 6148
  25.0 5.6 %copy-start.38 = (f32[1,1,512]{2,1,0:T(1,128)S(1)}, f32[1,1,512]{2,1,0:T(1,128)}, u32[]{:S(2)}) copy-start(f32[1,1,512]{2,1,0:T(1,128)} %get-tuple-element.73) | copy-start | bytes 6148
  25.0 5.6 %copy-start.40 = (f32[1,1,512]{2,1,0:T(1,128)S(1)}, f32[1,1,512]{2,1,0:T(1,128)}, u32[]{:S(2)}) copy-start(f32[1,1,512]{2,1,0:T(1,128)} %get-tuple-element.74) | copy-start | bytes 6148
  25.0 5.6 %copy-start.42 = (f32[1,1,512]{2,1,0:T(1,128)S(1)}, f32[1,1,512]{2,1,0:T(1,128)}, u32[]{:S(2)}) copy-start(f32[1,1,512]{2,1,0:T(1,128)} %get-tuple-element.75) | copy-start | bytes 6148
  25.3 5.3 %copy-start.10 = (f32[6,512]{1,0:T(8,128)S(1)}, f32[6,512]{1,0:T(8,128)}, u32[]{:S(2)}) copy-start(f32[6,512]{1,0:T(8,128)} %get-tuple-element.59) | copy-start | bytes 36868
  25.3 5.3 %copy-start.44 = (f32[1,1,512]{2,1,0:T(1,128)S(1)}, f32[1,1,512]{2,1,0:T(1,128)}, u32[]{:S(2)}) copy-start(f32[1,1,512]{2,1,0:T(1,128)} %get-tuple-element.64) | copy-start | bytes 6148
  25.3 5.3 %copy-start.46 = (f32[1,1,512]{2,1,0:T(1,128)S(1)}, f32[1,1,512]{2,1,0:T(1,128)}, u32[]{:S(2)}) copy-start(f32[1,1,512]{2,1,0:T(1,128)} %get-tuple-element.65) | copy-start | bytes 6148
  25.3 5.3 %copy-start.48 = (f32[1,1,512]{2,1,0:T(1,128)S(1)}, f32[1,1,512]{2,1,0:T(1,128)}, u32[]{:S(2)}) copy-start(f32[1,1,512]{2,1,0:T(1,128)} %get-tuple-element.66) | copy-start | bytes 6148
  25.3 5.3 %copy-start.50 = (f32[1,1,512]{2,1,0:T(1,128)S(1)}, f32[1,1,512]{2,1,0:T(1,128)}, u32[]{:S(2)}) copy-start(f32[1,1,512]{2,1,0:T(1,128)} %get-tuple-element.67) | copy-start | bytes 6148
  25.3 5.3 %copy-start.52 = (f32[1,1,512]{2,1,0:T(1,128)S(1)}, f32[1,1,512]{2,1,0:T(1,128)}, u32[]{:S(2)}) copy-start(f32[1,1,512]{2,1,0:T(1,128)} %get-tuple-element.68) | copy-start | bytes 6148
  25.3 5.3 %copy-start.54 = (f32[1,1,512]{2,1,0:T(1,128)S(1)}, f32[1,1,512]{2,1,0:T(1,128)}, u32[]{:S(2)}) copy-start(f32[1,1,512]{2,1,0:T(1,128)} %get-tuple-element.82) | copy-start | bytes 6148
  25.4 5.3 %copy-start.56 = (f32[1,1,512]{2,1,0:T(1,128)S(1)}, f32[1,1,512]{2,1,0:T(1,128)}, u32[]{:S(2)}) copy-start(f32[1,1,512]{2,1,0:T(1,128)} %get-tuple-element.83) | copy-start | bytes 6148
  25.4 5.4 %copy-start.13 = (f32[1,1,512]{2,1,0:T(1,128)S(1)}, f32[1,1,512]{2,1,0:T(1,128)}, u32[]{:S(2)}) copy-start(f32[1,1,512]{2,1,0:T(1,128)} %copy-done.12) | copy-start | bytes 6148
  25.4 5.4 %copy-start.16 = (f32[1,1,512]{2,1,0:T(1,128)S(1)}, f32[1,1,512]{2,1,0:T(1,128)}, u32[]{:S(2)}) copy-start(f32[1,1,512]{2,1,0:T(1,128)} %copy-done.15) | copy-start | bytes 6148
  25.4 5.4 %copy-start.19 = (f32[1,1,512]{2,1,0:T(1,128)S(1)}, f32[1,1,512]{2,1,0:T(1,128)}, u32[]{:S(2)}) copy-start(f32[1,1,512]{2,1,0:T(1,128)} %copy-done.18) | copy-start | bytes 6148
  25.4 5.4 %copy-start.22 = (f32[1,1,512]{2,1,0:T(1,128)S(1)}, f32[1,1,512]{2,1,0:T(1,128)}, u32[]{:S(2)}) copy-start(f32[1,1,512]{2,1,0:T(1,128)} %copy-done.21) | copy-start | bytes 6148
  25.4 5.4 %copy-start.24 = (f32[1,1,512]{2,1,0:T(1,128)S(1)}, f32[1,1,512]{2,1,0:T(1,128)}, u32[]{:S(2)}) copy-start(f32[1,1,512]{2,1,0:T(1,128)} %get-tuple-element.79) | copy-start | bytes 6148
  25.4 5.4 %copy-start.26 = (f32[1,1,512]{2,1,0:T(1,128)S(1)}, f32[1,1,512]{2,1,0:T(1,128)}, u32[]{:S(2)}) copy-start(f32[1,1,512]{2,1,0:T(1,128)} %get-tuple-element.80) | copy-start | bytes 6148
  25.4 5.4 %copy-start.28 = (f32[1,1,512]{2,1,0:T(1,128)S(1)}, f32[1,1,512]{2,1,0:T(1,128)}, u32[]{:S(2)}) copy-start(f32[1,1,512]{2,1,0:T(1,128)} %get-tuple-element.81) | copy-start | bytes 6148
  25.4 6.6 %copy-start.7 = (f32[32,16]{0,1:T(8,128)S(1)}, f32[32,16]{0,1:T(8,128)}, u32[]{:S(2)}) copy-start(f32[32,16]{0,1:T(8,128)} %get-tuple-element.7) | copy-start | bytes 6148
  25.4 6.7 %copy-start.6 = (f32[32,16]{0,1:T(8,128)S(1)}, f32[32,16]{0,1:T(8,128)}, u32[]{:S(2)}) copy-start(f32[32,16]{0,1:T(8,128)} %param.11) | copy-start | bytes 6148
  25.5 6.7 %copy-start.73 = (f32[128]{0:T(128)S(1)}, f32[128]{0:T(128)}, u32[]{:S(2)}) copy-start(f32[128]{0:T(128)} %get-tuple-element.113) | copy-start | bytes 1540
  25.5 6.7 %copy-start.74 = (f32[128]{0:T(128)S(1)}, f32[128]{0:T(128)}, u32[]{:S(2)}) copy-start(f32[128]{0:T(128)} %get-tuple-element.114) | copy-start | bytes 1540
  26.0 6.0 %collective-permute-start.1 = (f32[2,16,512]{2,1,0:T(8,128)S(1)}, f32[2,16,512]{2,1,0:T(8,128)S(1)}, u32[]{:S(2)}, u32[]{:S(2)}) collective-permute-start(f32[2,16,512]{2,1,0:T(8,128)S(1)} %pad_maximum_fusion.6), channel_id=1, source_target_pairs={{0,8},{8,0},{16,24},{24,16},{32,40},{40,32},{48,56},{56,48},{1,9},... | collective-permute-start | bytes 196616 | tf_op jit(solution)/shard_map/ppermute | solution.py:85
  37.3 6.6 %collective-permute-start.2 = (f32[2,16,512]{2,1,0:T(8,128)}, f32[2,16,512]{2,1,0:T(8,128)}, u32[]{:S(2)}, u32[]{:S(2)}) collective-permute-start(f32[2,16,512]{2,1,0:T(8,128)} %fusion.152), channel_id=1, source_target_pairs={{0,16},{8,24},{16,0},{24,8},{32,48},{40,56},{48,32},{56,40},{1,17}... | collective-permute-start | bytes 196616 | tf_op jit(solution)/shard_map/ppermute | solution.py:85
  44.8 7.7 %collective-permute-start.3 = (f32[2,16,512]{2,1,0:T(8,128)S(1)}, f32[2,16,512]{2,1,0:T(8,128)S(1)}, u32[]{:S(2)}, u32[]{:S(2)}) collective-permute-start(f32[2,16,512]{2,1,0:T(8,128)S(1)} %fusion.153), channel_id=1, source_target_pairs={{0,32},{8,40},{16,48},{24,56},{32,0},{40,8},{48,16},{56,24},{1,33}... | collective-permute-start | bytes 196616 | tf_op jit(solution)/shard_map/ppermute | solution.py:85
  53.5 8.4 %collective-permute-start.4 = (f32[2,16,512]{2,1,0:T(8,128)S(1)}, f32[2,16,512]{2,1,0:T(8,128)S(1)}, u32[]{:S(2)}, u32[]{:S(2)}) collective-permute-start(f32[2,16,512]{2,1,0:T(8,128)S(1)} %get-tuple-element.62), channel_id=1, source_target_pairs={{0,64},{64,0},{128,192},{192,128},{256,320},{320,256},{384,448},{4... | collective-permute-start | bytes 196616 | tf_op jit(solution)/shard_map/ppermute | solution.py:85
  62.8 7.6 %collective-permute-start.5 = (f32[2,16,512]{2,1,0:T(8,128)S(1)}, f32[2,16,512]{2,1,0:T(8,128)}, u32[]{:S(2)}, u32[]{:S(2)}) collective-permute-start(f32[2,16,512]{2,1,0:T(8,128)S(1)} %fusion.157), channel_id=1, source_target_pairs={{0,128},{64,192},{128,0},{192,64},{256,384},{320,448},{384,256},{4... | collective-permute-start | bytes 196616 | tf_op jit(solution)/shard_map/ppermute | solution.py:85
  72.0 14.5 %collective-permute-start.6 = (f32[2,16,512]{2,1,0:T(8,128)}, f32[2,16,512]{2,1,0:T(8,128)}, u32[]{:S(2)}, u32[]{:S(2)}) collective-permute-start(f32[2,16,512]{2,1,0:T(8,128)} %fusion.158), channel_id=1, source_target_pairs={{0,256},{64,320},{128,384},{192,448},{256,0},{320,64},{384,128},{4... | collective-permute-start | bytes 196616 | tf_op jit(solution)/shard_map/ppermute | solution.py:85
  83.5 5.2 %copy-start.9 = (f32[6,512]{1,0:T(8,128)S(1)}, f32[6,512]{1,0:T(8,128)}, u32[]{:S(2)}) copy-start(f32[6,512]{1,0:T(8,128)} %convert_element_type.327) | copy-start | bytes 36868
  83.8 4.9 %copy-start.59 = (f32[1,512]{1,0:T(1,128)S(1)}, f32[1,512]{1,0:T(1,128)}, u32[]{:S(2)}) copy-start(f32[1,512]{1,0:T(1,128)} %get-tuple-element.99) | copy-start | bytes 6148
  83.8 4.9 %copy-start.60 = (f32[1,512]{1,0:T(1,128)S(1)}, f32[1,512]{1,0:T(1,128)}, u32[]{:S(2)}) copy-start(f32[1,512]{1,0:T(1,128)} %get-tuple-element.100) | copy-start | bytes 6148
  83.9 4.9 %copy-start.61 = (f32[1,512]{1,0:T(1,128)S(1)}, f32[1,512]{1,0:T(1,128)}, u32[]{:S(2)}) copy-start(f32[1,512]{1,0:T(1,128)} %get-tuple-element.101) | copy-start | bytes 6148
  83.9 4.9 %copy-start.62 = (f32[1,512]{1,0:T(1,128)S(1)}, f32[1,512]{1,0:T(1,128)}, u32[]{:S(2)}) copy-start(f32[1,512]{1,0:T(1,128)} %get-tuple-element.102) | copy-start | bytes 6148
  83.9 4.9 %copy-start.63 = (f32[1,512]{1,0:T(1,128)S(1)}, f32[1,512]{1,0:T(1,128)}, u32[]{:S(2)}) copy-start(f32[1,512]{1,0:T(1,128)} %get-tuple-element.103) | copy-start | bytes 6148
  83.9 4.9 %copy-start.64 = (f32[1,512]{1,0:T(1,128)S(1)}, f32[1,512]{1,0:T(1,128)}, u32[]{:S(2)}) copy-start(f32[1,512]{1,0:T(1,128)} %get-tuple-element.104) | copy-start | bytes 6148
  83.9 4.9 %copy-start.65 = (f32[1,512]{1,0:T(1,128)S(1)}, f32[1,512]{1,0:T(1,128)}, u32[]{:S(2)}) copy-start(f32[1,512]{1,0:T(1,128)} %get-tuple-element.105) | copy-start | bytes 6148
  83.9 4.9 %copy-start.58 = (bf16[6,512]{1,0:T(8,128)(2,1)S(1)}, bf16[6,512]{1,0:T(8,128)(2,1)}, u32[]{:S(2)}) copy-start(bf16[6,512]{1,0:T(8,128)(2,1)} %fusion.175) | copy-start | bytes 18436
  83.9 5.7 %copy-start.66 = (f32[1,512]{1,0:T(1,128)S(1)}, f32[1,512]{1,0:T(1,128)}, u32[]{:S(2)}) copy-start(f32[1,512]{1,0:T(1,128)} %get-tuple-element.92) | copy-start | bytes 6148
  83.9 5.7 %copy-start.67 = (f32[1,512]{1,0:T(1,128)S(1)}, f32[1,512]{1,0:T(1,128)}, u32[]{:S(2)}) copy-start(f32[1,512]{1,0:T(1,128)} %get-tuple-element.93) | copy-start | bytes 6148
  83.9 5.7 %copy-start.68 = (f32[1,512]{1,0:T(1,128)S(1)}, f32[1,512]{1,0:T(1,128)}, u32[]{:S(2)}) copy-start(f32[1,512]{1,0:T(1,128)} %get-tuple-element.94) | copy-start | bytes 6148
  83.9 5.7 %copy-start.69 = (f32[1,512]{1,0:T(1,128)S(1)}, f32[1,512]{1,0:T(1,128)}, u32[]{:S(2)}) copy-start(f32[1,512]{1,0:T(1,128)} %get-tuple-element.95) | copy-start | bytes 6148
  84.0 5.7 %copy-start.70 = (f32[1,512]{1,0:T(1,128)S(1)}, f32[1,512]{1,0:T(1,128)}, u32[]{:S(2)}) copy-start(f32[1,512]{1,0:T(1,128)} %get-tuple-element.96) | copy-start | bytes 6148
  84.0 5.7 %copy-start.71 = (f32[1,512]{1,0:T(1,128)S(1)}, f32[1,512]{1,0:T(1,128)}, u32[]{:S(2)}) copy-start(f32[1,512]{1,0:T(1,128)} %get-tuple-element.97) | copy-start | bytes 6148
  84.0 5.7 %copy-start.72 = (f32[1,512]{1,0:T(1,128)S(1)}, f32[1,512]{1,0:T(1,128)}, u32[]{:S(2)}) copy-start(f32[1,512]{1,0:T(1,128)} %get-tuple-element.98) | copy-start | bytes 6148
  88.5 4.8 %copy-start.14 = (f32[1,1,512]{2,1,0:T(1,128)S(1)}, f32[1,1,512]{2,1,0:T(1,128)}, u32[]{:S(2)}) copy-start(f32[1,1,512]{2,1,0:T(1,128)} %copy-done.12) | copy-start | bytes 6148
  88.6 4.8 %copy-start.17 = (f32[1,1,512]{2,1,0:T(1,128)S(1)}, f32[1,1,512]{2,1,0:T(1,128)}, u32[]{:S(2)}) copy-start(f32[1,1,512]{2,1,0:T(1,128)} %copy-done.15) | copy-start | bytes 6148
  88.6 4.8 %copy-start.20 = (f32[1,1,512]{2,1,0:T(1,128)S(1)}, f32[1,1,512]{2,1,0:T(1,128)}, u32[]{:S(2)}) copy-start(f32[1,1,512]{2,1,0:T(1,128)} %copy-done.18) | copy-start | bytes 6148
  88.6 4.8 %copy-start.23 = (f32[1,1,512]{2,1,0:T(1,128)S(1)}, f32[1,1,512]{2,1,0:T(1,128)}, u32[]{:S(2)}) copy-start(f32[1,1,512]{2,1,0:T(1,128)} %copy-done.21) | copy-start | bytes 6148
  88.6 4.7 %copy-start.25 = (f32[1,1,512]{2,1,0:T(1,128)S(1)}, f32[1,1,512]{2,1,0:T(1,128)}, u32[]{:S(2)}) copy-start(f32[1,1,512]{2,1,0:T(1,128)} %get-tuple-element.79) | copy-start | bytes 6148
  88.6 4.7 %copy-start.27 = (f32[1,1,512]{2,1,0:T(1,128)S(1)}, f32[1,1,512]{2,1,0:T(1,128)}, u32[]{:S(2)}) copy-start(f32[1,1,512]{2,1,0:T(1,128)} %get-tuple-element.80) | copy-start | bytes 6148
  88.6 4.7 %copy-start.29 = (f32[1,1,512]{2,1,0:T(1,128)S(1)}, f32[1,1,512]{2,1,0:T(1,128)}, u32[]{:S(2)}) copy-start(f32[1,1,512]{2,1,0:T(1,128)} %get-tuple-element.81) | copy-start | bytes 6148
  (19 other events, 63.5 us)

commit v9 on v7

--- a/solution.py
+++ b/solution.py
@@ -144,9 +144,6 @@
     near, group, (rates, weights) = cube_scan(
         jnp.stack([end_state, start_state]), inner_rounds, "xc", inner, (rates, weights)
     )
-    far, _, _ = cube_scan(group, outer_rounds, "zl", outer, ())
-    entering = near[0] + factors[-4] * far[0]
-    leaving = near[1] + factors[-3] * far[1]
 
     centred = jnp.arange(block_len).astype(jnp.float32) - block_len // 2
     falling = weights[:, None, :] * jnp.exp(-centred[None, :, None] * rates[:, None, :])
@@ -156,6 +153,20 @@
     toeplitz = jnp.where(lower[None], toeplitz, 0.0)
     local_conv = split_dot("gts,sgc->tgc", toeplitz, signal).reshape(block_len, channels)
     local_grad = split_dot("gts,tgc->sgc", toeplitz, cotangent).reshape(block_len, channels)
+    edge = SHORT - 1
+    slab = 8
+    pieces = [local_conv, local_grad, grad_out, k_short, v_short]
+    ahead = jnp.concatenate(
+        [piece[:slab].astype(jnp.float32) for piece in pieces] + [start_state]
+    )
+    ahead = from_behind(ahead, ("zl", "xc"), -1)
+    far, _, ahead = cube_scan(group, outer_rounds, "zl", outer, ahead)
+    entering = near[0] + factors[-4] * far[0]
+    leaving = near[1] + factors[-3] * far[1]
+    next_local_conv, next_local_grad, next_grad_out, next_k, next_v = (
+        ahead[slab * piece : slab * piece + edge] for piece in range(len(pieces))
+    )
+    next_start = ahead[slab * len(pieces) :]
     lead_fwd = (weights[:, :, None] * powers[:, :, 1:]).reshape(group_count * order, block_len)
     lead_bwd = (weights[:, :, None] * powers[:, :, block_len:0:-1]).reshape(
         group_count * order, block_len
@@ -165,32 +176,20 @@
     conv_out = rounded(local_conv + carried_conv)
     grad_prod = rounded(local_grad + carried_grad)
 
-    edge = SHORT - 1
-    ahead = jnp.concatenate(
-        [
-            local_conv[:edge],
-            local_grad[:edge],
-            grad_out[:edge].astype(jnp.float32),
-            k_short[:edge].astype(jnp.float32),
-            v_short[:edge].astype(jnp.float32),
-            start_state,
-        ]
-    )
-    ahead = from_behind(ahead, ("zl", "xc"), -1)
     through = factors[-2] * entering + end_state
-    beyond = (leaving - ahead[5 * edge :]) * factors[-1]
+    beyond = (leaving - next_start) * factors[-1]
     next_conv = rounded(
-        ahead[:edge]
+        next_local_conv
         + jnp.einsum("kt,kc->tc", lead_fwd[:, :edge], spread(through), precision=precise)
     )
     next_grad = rounded(
-        ahead[edge : 2 * edge]
+        next_local_grad
         + jnp.einsum("ks,kc->sc", lead_bwd[:, :edge], spread(beyond), precision=precise)
     )
     next_rows = (
-        rounded(ahead[2 * edge : 3 * edge] * next_conv.astype(jnp.float32)),
-        rounded(next_grad.astype(jnp.float32) * ahead[4 * edge : 5 * edge]),
-        rounded(next_grad.astype(jnp.float32) * ahead[3 * edge : 4 * edge]),
+        rounded(next_grad_out.astype(jnp.float32) * next_conv.astype(jnp.float32)),
+        rounded(next_grad.astype(jnp.float32) * next_v.astype(jnp.float32)),
+        rounded(next_grad.astype(jnp.float32) * next_k.astype(jnp.float32)),
     )
 
     mixer_out = (q_short.astype(jnp.float32) * conv_out.astype(jnp.float32)).astype(jnp.bfloat16)

time: 76.9 us -> 85.9 us (1.12)
  the two profiles are of different devices: /device:TPU:15 before, /device:TPU:24 now
where the time goes in v9:
time: 85.9 us; the launch traced here: 84.7 us
  starting transfers between devices  33.5 us (39%)
  other arithmetic  16.4 us (19%)
  waiting for transfers between devices  12.4 us (14%)
  matrix products  11.2 us (13%)
  local copies, waits for them, and re-layouts  9.18 us (11%)
  between operations  2.09 us (2%)
    ppermute x6, starting transfers between devices, cube_scan(): lax.ppermute(window, axis, [(source, source ^ shift) for source in range(...  30.5 us
    ppermute x6, waiting for transfers between devices, cube_scan(): lax.ppermute(window, axis, [(source, source ^ shift) for source in range(...  12.4 us
    dot_general x1, matrix products, shards(): toeplitz = jnp.einsum('gtm,gms->gts', falling, rising, precision=precise)  4.31 us
    unnamed x3, other arithmetic  3.22 us
    ppermute x2, starting transfers between devices, from_behind(): lax.ppermute(value, axis, [(source, source + steps) for source in range(l...  3.02 us
    unnamed x140, local copies, waits for them, and re-layouts  2.85 us
    add x4, other arithmetic, cube_scan(): window = keep * window + take * arrived  2.85 us
    dot_general x4, matrix products, split_dot(): jnp.einsum(spec, low, values, preferred_element_type=jnp.float32)  2.54 us
  transfers between devices with their start and end apart: 8, of which 5 were waited for; matrix products, arithmetic and copies ran while one was open for 12% of the time, Pallas kernels for 0%

profile of v9, /device:TPU:24, one launch (start us, length us, event | category | flops | bytes accessed | tf_op | source)
XLA Modules:
  0.0 84.7 jit_solution(4635631461018139282)
XLA Ops:
  0.6 0.7 slice_bitcast_fusion.6
  1.3 0.7 slice_bitcast_fusion.4
  2.1 1.7 %collective-permute-start = (bf16[3,6,512]{2,1,0:T(8,128)(2,1)S(1)}, bf16[3,6,512]{2,1,0:T(8,128)(2,1)S(1)}, u32[]{:S(2)}, u32[]{:S(2)}) collective-permute-start(bf16[3,6,512]{2,1,0:T(8,128)(2,1)S(1)} %pad_maximum_fusion.7), channel_id=1, source_target_pairs={{0,8},{8,16},{16,24},{24,32},{32,40},{40,48},{48,56},{56,64},{64,7... | collective-permute-start | bytes 55304 | tf_op jit(solution)/shard_map/ppermute | solution.py:19
  3.8 0.8 fusion.179
  4.6 1.2 %fusion.178 = (f32[1,1,512]{2,1,0:T(1,128)S(1)}, f32[1,1,512]{2,1,0:T(1,128)S(1)}, f32[1,1,512]{2,1,0:T(1,128)S(1)}, f32[1,1,512]{2,1,0:T(1,128)S(1)}, f32[1,1,5...) fusion(f32[3,7,512]{2,1,0:T(8,128)} %param.10), kind=kLoop, calls=%fused_computation.326 | loop fusion | bytes 77824 | tf_op jit(solution)/shard_map/slice | solution.py:32
  6.0 0.7 negate_bitcast_fusion
  6.8 0.1 multiply_exponential_fusion.1
  7.0 0.8 copy-done
  7.8 0.1 rev.6
  8.3 0.2 neg.35
  8.6 0.2 multiply_exponential_fusion
  8.8 0.7 slice_select_fusion.6
  9.5 0.8 slice_select_fusion.7
  10.6 0.2 fusion.76
  10.9 0.2 fusion.93
  11.2 0.2 fusion.110
  11.5 0.3 fusion.180
  11.8 0.3 convolution_add_fusion.1
  12.1 0.3 fusion.181
  12.4 0.3 convolution_add_fusion
  12.7 0.3 multiply_reduce_fusion.1
  13.0 3.7 %collective-permute-start.1 = (f32[2,16,512]{2,1,0:T(8,128)S(1)}, f32[2,16,512]{2,1,0:T(8,128)S(1)}, u32[]{:S(2)}, u32[]{:S(2)}) collective-permute-start(f32[2,16,512]{2,1,0:T(8,128)S(1)} %pad_maximum_fusion.6), channel_id=1, source_target_pairs={{0,8},{8,0},{16,24},{24,16},{32,40},{40,32},{48,56},{56,48},{1,9},... | collective-permute-start | bytes 196616 | tf_op jit(solution)/shard_map/ppermute | solution.py:85
  16.7 0.6 convert_add_fusion
  17.7 0.5 copy-done.10
  18.2 4.3 %fusion.133 = f32[32,128,128]{2,1,0:T(8,128)S(1)} fusion(f32[32,16]{1,0:T(8,128)S(1)} %copy.27, f32[128]{0:T(128)} %get-tuple-element.88, f32[128]{0:T(128)} %get-tuple-element.89, f32[32,16]{1,0:T(8,128)S(1)} %copy.26), kind=kOutput, calls=%fused_computation.211 | convolution fusion | flops 100859904 | bytes 2102272 | tf_op jit(solution)/shard_map/gtm,gms->gts/dot_general | solution.py:151
  22.5 0.6 fusion.12
  23.2 0.7 convolution_add_fusion.3
  24.0 0.6 constant_dynamic-update-slice_fusion.2
  24.6 0.4 fusion.11
  24.9 1.3 %convolution_add_fusion.2 = f32[32,16,128]{2,1,0:T(8,128)S(1)} fusion(f32[32,16,128]{2,1,0:T(8,128)S(1)} %fusion.11, bf16[128,32,16]{0,2,1:T(8,128)(2,1)} %bitcast.131, f32[32,128,128]{2,1,0:T(8,128)S(1)} %fusion.133, pred[128,128]{1,0:T(8,128)(4,1)S(1)} %iota_compare_fusion.1), kind=kOutput, calls=%fused_computation.7 | convolution fusion | flops 18939904 | bytes 2768896 | tf_op jit(solution)/shard_map/gts,tgc->sgc/dot_general | solution.py:50
  26.4 0.6 constant_dynamic-update-slice_fusion.1
  27.0 1.3 %convert_dynamic-update-slice_fusion.2 = f32[56,512]{1,0:T(8,128)} fusion(f32[56,512]{1,0:T(8,128)} %constant_dynamic-update-slice_fusion.1, bf16[128,512]{1,0:T(8,128)(2,1)} %param.13), kind=kLoop, calls=%fused_computation.295 | loop fusion | flops 4096 | bytes 24576
  28.3 1.3 %convert_dynamic-update-slice_fusion.1 = f32[56,512]{1,0:T(8,128)} fusion(f32[56,512]{1,0:T(8,128)} %convert_dynamic-update-slice_fusion.2, bf16[128,512]{1,0:T(8,128)(2,1)} %copy-done.2), kind=kLoop, calls=%fused_computation.294 | loop fusion | flops 4096 | bytes 24576
  29.6 1.0 %fusion.148 = f32[2,16,512]{2,1,0:T(8,128)S(1)} fusion(f32[1,16,512]{2,1,0:T(8,128)} %get-tuple-element.25, f32[1,16,512]{2,1,0:T(8,128)} %get-tuple-element.37, f32[2,16,512]{2,1,0:T(8,128)} %copy-done.10, f32[1,16,512]{2,1,0:T(8,128)} %bitcast.138, f32[1,16,512]{2,1,0:T(8,128)} %bitcast.135), kind=kLoop, calls=%fused_computation.230 | loop fusion | flops 98304 | bytes 262144 | tf_op jit(solution)/shard_map/add | solution.py:89
  30.6 3.4 %collective-permute-start.2 = (f32[2,16,512]{2,1,0:T(8,128)S(1)}, f32[2,16,512]{2,1,0:T(8,128)S(1)}, u32[]{:S(2)}, u32[]{:S(2)}) collective-permute-start(f32[2,16,512]{2,1,0:T(8,128)S(1)} %fusion.148), channel_id=1, source_target_pairs={{0,16},{8,24},{16,0},{24,8},{32,48},{40,56},{48,32},{56,40},{1,17}... | collective-permute-start | bytes 196616 | tf_op jit(solution)/shard_map/ppermute | solution.py:85
  34.0 0.6 convert_dynamic-update-slice_fusion
  34.6 2.2 %collective-permute-done.2 = f32[2,16,512]{2,1,0:T(8,128)S(1)} collective-permute-done((f32[2,16,512]{2,1,0:T(8,128)S(1)}, f32[2,16,512]{2,1,0:T(8,128)S(1)}, u32[]{:S(2)}, u32[]{:S(2)}) %collective-permute-start.2) | collective-permute-done | bytes 65568 | tf_op jit(solution)/shard_map/ppermute | solution.py:85
  36.8 1.0 %fusion.149 = f32[2,16,512]{2,1,0:T(8,128)S(1)} fusion(f32[1,16,512]{2,1,0:T(8,128)} %get-tuple-element.21, f32[1,16,512]{2,1,0:T(8,128)} %get-tuple-element.36, f32[2,16,512]{2,1,0:T(8,128)S(1)} %collective-permute-done.2, f32[2,16,512]{2,1,0:T(8,128)} %copy-done.10, f32[1,16,512]{2,1,0:T(8,128)} %get-tuple-element.37, ...), kind=kLoop, calls=%fused_computation.234 | loop fusion | flops 180224 | bytes 393216 | tf_op jit(solution)/shard_map/add | solution.py:89
  37.9 4.9 %collective-permute-start.3 = (f32[2,16,512]{2,1,0:T(8,128)S(1)}, f32[2,16,512]{2,1,0:T(8,128)S(1)}, u32[]{:S(2)}, u32[]{:S(2)}) collective-permute-start(f32[2,16,512]{2,1,0:T(8,128)S(1)} %fusion.149), channel_id=1, source_target_pairs={{0,32},{8,40},{16,48},{24,56},{32,0},{40,8},{48,16},{56,24},{1,33}... | collective-permute-start | bytes 196616 | tf_op jit(solution)/shard_map/ppermute | solution.py:85
  42.8 1.4 %constant_dynamic-update-slice_fusion = f32[56,512]{1,0:T(8,128)} fusion(f32[56,512]{1,0:T(8,128)} %convert_dynamic-update-slice_fusion, f32[16,512]{1,0:T(8,128)} %copy-done.9), kind=kLoop, calls=%fused_computation.296 | loop fusion | bytes 65536 | tf_op jit(solution)/shard_map/concatenate | solution.py:159
  44.1 1.3 %collective-permute-start.4 = (f32[56,512]{1,0:T(8,128)}, f32[56,512]{1,0:T(8,128)S(1)}, u32[]{:S(2)}, u32[]{:S(2)}) collective-permute-start(f32[56,512]{1,0:T(8,128)} %constant_dynamic-update-slice_fusion), channel_id=1, source_target_pairs={{8,0},{16,8},{24,16},{32,24},{40,32},{48,40},{56,48},{64,56},{72,6... | collective-permute-start | bytes 344072 | tf_op jit(solution)/shard_map/ppermute | solution.py:19
  45.4 0.2 collective-permute-done.3
  45.7 1.0 %fusion.147 = (f32[2,16,512]{2,1,0:T(8,128)S(1)}, f32[2,16,512]{2,1,0:T(8,128)S(1)}) fusion(f32[2,16,512]{2,1,0:T(8,128)} %copy-done.10, f32[1,16,512]{2,1,0:T(8,128)} %get-tuple-element.40, f32[1,16,512]{2,1,0:T(8,128)} %get-tuple-element.41, f32[2,16,512]{2,1,0:T(8,128)S(1)} %collective-permute-done.2, f32[1,16,512]{2,1,0:T(8,128)} %get-tuple-element.38, ...), kind=kLoop, calls=%fused_computation.227 | loop fusion | flops 212992 | bytes 655360 | tf_op jit(solution)/shard_map/add | solution.py:88
  46.7 4.2 %collective-permute-start.5 = (f32[2,16,512]{2,1,0:T(8,128)S(1)}, f32[2,16,512]{2,1,0:T(8,128)S(1)}, u32[]{:S(2)}, u32[]{:S(2)}) collective-permute-start(f32[2,16,512]{2,1,0:T(8,128)S(1)} %get-tuple-element.58), channel_id=1, source_target_pairs={{0,64},{64,0},{128,192},{192,128},{256,320},{320,256},{384,448},{4... | collective-permute-start | bytes 196616 | tf_op jit(solution)/shard_map/ppermute | solution.py:85
  50.9 2.7 %collective-permute-done.5 = f32[2,16,512]{2,1,0:T(8,128)S(1)} collective-permute-done((f32[2,16,512]{2,1,0:T(8,128)S(1)}, f32[2,16,512]{2,1,0:T(8,128)S(1)}, u32[]{:S(2)}, u32[]{:S(2)}) %collective-permute-start.5) | collective-permute-done | bytes 65568 | tf_op jit(solution)/shard_map/ppermute | solution.py:85
  53.6 0.9 %fusion.153 = f32[2,16,512]{2,1,0:T(8,128)S(1)} fusion(f32[2,16,512]{2,1,0:T(8,128)S(1)} %get-tuple-element.58, f32[1,16,512]{2,1,0:T(8,128)} %get-tuple-element.23, f32[1,16,512]{2,1,0:T(8,128)} %get-tuple-element.29, f32[2,16,512]{2,1,0:T(8,128)S(1)} %collective-permute-done.5), kind=kLoop, calls=%fused_computation.244 | loop fusion | flops 81920 | bytes 262144 | tf_op jit(solution)/shard_map/add | solution.py:89
  54.5 6.4 %collective-permute-start.6 = (f32[2,16,512]{2,1,0:T(8,128)S(1)}, f32[2,16,512]{2,1,0:T(8,128)S(1)}, u32[]{:S(2)}, u32[]{:S(2)}) collective-permute-start(f32[2,16,512]{2,1,0:T(8,128)S(1)} %fusion.153), channel_id=1, source_target_pairs={{0,128},{64,192},{128,0},{192,64},{256,384},{320,448},{384,256},{4... | collective-permute-start | bytes 196616 | tf_op jit(solution)/shard_map/ppermute | solution.py:85
  60.9 0.9 %fusion.177 = (f32[32,16,128]{2,1,0:T(8,128)S(1)}, f32[32,16,128]{2,1,0:T(8,128)S(1)}) fusion(f32[32,16,129]{2,1,0:T(8,128)S(1)} %copy-done.1, f32[32,16]{1,0:T(8,128)} %copy-done.13), kind=kLoop, calls=%fused_computation.325 | loop fusion | flops 65536 | bytes 788480 | tf_op jit(solution)/shard_map/slice | solution.py:170
  61.8 0.1 rev.7
  62.0 2.5 %collective-permute-done.6 = f32[2,16,512]{2,1,0:T(8,128)S(1)} collective-permute-done((f32[2,16,512]{2,1,0:T(8,128)S(1)}, f32[2,16,512]{2,1,0:T(8,128)S(1)}, u32[]{:S(2)}, u32[]{:S(2)}) %collective-permute-start.6) | collective-permute-done | bytes 65568 | tf_op jit(solution)/shard_map/ppermute | solution.py:85
  64.5 8.0 %collective-permute-start.7 = (f32[2,16,512]{2,1,0:T(8,128)S(1)}, f32[2,16,512]{2,1,0:T(8,128)S(1)}, u32[]{:S(2)}, u32[]{:S(2)}) collective-permute-start(f32[2,16,512]{2,1,0:T(8,128)S(1)} %fusion.154), channel_id=1, source_target_pairs={{0,256},{64,320},{128,384},{192,448},{256,0},{320,64},{384,128},{4... | collective-permute-start | bytes 196616 | tf_op jit(solution)/shard_map/ppermute | solution.py:85
  72.5 0.1 broadcast_multiply_fusion.2
  72.7 0.1 copy.35
  72.8 0.1 copy.38
  72.9 4.6 %collective-permute-done.7 = f32[2,16,512]{2,1,0:T(8,128)S(1)} collective-permute-done((f32[2,16,512]{2,1,0:T(8,128)S(1)}, f32[2,16,512]{2,1,0:T(8,128)S(1)}, u32[]{:S(2)}, u32[]{:S(2)}) %collective-permute-start.7) | collective-permute-done | bytes 65568 | tf_op jit(solution)/shard_map/ppermute | solution.py:85
  77.7 0.8 fusion.4
  78.5 0.7 fusion.16
  79.2 0.3 broadcast_multiply_fusion
  79.5 0.6 add_convert_fusion
  80.2 0.6 fusion.128
  81.0 0.8 fusion.3
  82.0 0.9 %fusion.59 = bf16[128,512]{1,0:T(8,128)(2,1)} fusion(f32[6,512]{1,0:T(8,128)S(1)} %convert_element_type.259, f32[128,512]{1,0:T(8,128)S(1)} %convert_element_type.255, f32[512]{0:T(512)S(1)} %bitcast.167, f32[512]{0:T(512)S(1)} %bitcast.169, f32[512]{0:T(512)S(1)} %bitcast.171, f32[512]{0:T(512)S(1)} %bitcast.173, f32[512]{0:T(512)S(1)} %bitcast.175, ...), kind=kLoop, calls=%fused_computation.113 | loop fusion | flops 1310720 | bytes 419840 | tf_op jit(solution)/shard_map/convert_element_type | solution.py:199
  82.9 0.9 %fusion.42 = bf16[128,512]{1,0:T(8,128)(2,1)} fusion(f32[6,512]{1,0:T(8,128)S(1)} %convert_element_type.268, f32[128,512]{1,0:T(8,128)S(1)} %convert_element_type.264, f32[512]{0:T(512)S(1)} %bitcast.151, f32[512]{0:T(512)S(1)} %bitcast.153, f32[512]{0:T(512)S(1)} %bitcast.155, f32[512]{0:T(512)S(1)} %bitcast.157, f32[512]{0:T(512)S(1)} %bitcast.159, ...), kind=kLoop, calls=%fused_computation.96 | loop fusion | flops 1310720 | bytes 419840 | tf_op jit(solution)/shard_map/convert_element_type | solution.py:200
  83.8 0.9 %fusion.25 = bf16[128,512]{1,0:T(8,128)(2,1)} fusion(f32[6,512]{1,0:T(8,128)S(1)} %convert_element_type.273, f32[128,512]{1,0:T(8,128)S(1)} %convert_element_type.271, f32[512]{0:T(512)S(1)} %bitcast.181, f32[512]{0:T(512)S(1)} %bitcast.179, f32[512]{0:T(512)S(1)} %bitcast.141, f32[512]{0:T(512)S(1)} %bitcast.143, f32[512]{0:T(512)S(1)} %bitcast.145, ...), kind=kLoop, calls=%fused_computation.79 | loop fusion | flops 1310720 | bytes 419840 | tf_op jit(solution)/shard_map/convert_element_type | solution.py:201
  (176 shorter events, 1.7 us)
Async XLA Ops:
  2.1 8.4 %collective-permute-start = (bf16[3,6,512]{2,1,0:T(8,128)(2,1)S(1)}, bf16[3,6,512]{2,1,0:T(8,128)(2,1)S(1)}, u32[]{:S(2)}, u32[]{:S(2)}) collective-permute-start(bf16[3,6,512]{2,1,0:T(8,128)(2,1)S(1)} %pad_maximum_fusion.7), channel_id=1, source_target_pairs={{0,8},{8,16},{16,24},{24,32},{32,40},{40,48},{48,56},{56,64},{64,7... | collective-permute-start | bytes 55304 | tf_op jit(solution)/shard_map/ppermute | solution.py:19
  4.6 5.9 %copy-start.65 = (f32[1,1,512]{2,1,0:T(1,128)}, f32[1,1,512]{2,1,0:T(1,128)S(1)}, u32[]{:S(2)}) copy-start(f32[1,1,512]{2,1,0:T(1,128)S(1)} %get-tuple-element.78) | copy-start | bytes 6148
  4.6 5.9 %copy-start.67 = (f32[1,1,512]{2,1,0:T(1,128)}, f32[1,1,512]{2,1,0:T(1,128)S(1)}, u32[]{:S(2)}) copy-start(f32[1,1,512]{2,1,0:T(1,128)S(1)} %get-tuple-element.79) | copy-start | bytes 6148
  5.8 4.7 %copy-start.27 = (f32[1,1,512]{2,1,0:T(1,128)}, f32[1,1,512]{2,1,0:T(1,128)S(1)}, u32[]{:S(2)}) copy-start(f32[1,1,512]{2,1,0:T(1,128)S(1)} %get-tuple-element.60) | copy-start | bytes 6148
  5.8 4.7 %copy-start.29 = (f32[1,1,512]{2,1,0:T(1,128)}, f32[1,1,512]{2,1,0:T(1,128)S(1)}, u32[]{:S(2)}) copy-start(f32[1,1,512]{2,1,0:T(1,128)S(1)} %get-tuple-element.61) | copy-start | bytes 6148
  5.8 4.7 %copy-start.31 = (f32[1,1,512]{2,1,0:T(1,128)}, f32[1,1,512]{2,1,0:T(1,128)S(1)}, u32[]{:S(2)}) copy-start(f32[1,1,512]{2,1,0:T(1,128)S(1)} %get-tuple-element.62) | copy-start | bytes 6148
  5.8 4.7 %copy-start.33 = (f32[1,1,512]{2,1,0:T(1,128)}, f32[1,1,512]{2,1,0:T(1,128)S(1)}, u32[]{:S(2)}) copy-start(f32[1,1,512]{2,1,0:T(1,128)S(1)} %get-tuple-element.63) | copy-start | bytes 6148
  5.8 4.7 %copy-start.35 = (f32[1,1,512]{2,1,0:T(1,128)}, f32[1,1,512]{2,1,0:T(1,128)S(1)}, u32[]{:S(2)}) copy-start(f32[1,1,512]{2,1,0:T(1,128)S(1)} %get-tuple-element.64) | copy-start | bytes 6148
  5.8 5.0 %copy-start.37 = (f32[1,1,512]{2,1,0:T(1,128)}, f32[1,1,512]{2,1,0:T(1,128)S(1)}, u32[]{:S(2)}) copy-start(f32[1,1,512]{2,1,0:T(1,128)S(1)} %get-tuple-element.65) | copy-start | bytes 6148
  5.9 5.0 %copy-start.39 = (f32[1,1,512]{2,1,0:T(1,128)}, f32[1,1,512]{2,1,0:T(1,128)S(1)}, u32[]{:S(2)}) copy-start(f32[1,1,512]{2,1,0:T(1,128)S(1)} %get-tuple-element.66) | copy-start | bytes 6148
  5.9 5.0 %copy-start.41 = (f32[1,1,512]{2,1,0:T(1,128)}, f32[1,1,512]{2,1,0:T(1,128)S(1)}, u32[]{:S(2)}) copy-start(f32[1,1,512]{2,1,0:T(1,128)S(1)} %get-tuple-element.67) | copy-start | bytes 6148
  5.9 5.0 %copy-start.43 = (f32[1,1,512]{2,1,0:T(1,128)}, f32[1,1,512]{2,1,0:T(1,128)S(1)}, u32[]{:S(2)}) copy-start(f32[1,1,512]{2,1,0:T(1,128)S(1)} %get-tuple-element.68) | copy-start | bytes 6148
  5.9 5.0 %copy-start.45 = (f32[1,1,512]{2,1,0:T(1,128)}, f32[1,1,512]{2,1,0:T(1,128)S(1)}, u32[]{:S(2)}) copy-start(f32[1,1,512]{2,1,0:T(1,128)S(1)} %get-tuple-element.69) | copy-start | bytes 6148
  5.9 5.0 %copy-start.47 = (f32[1,1,512]{2,1,0:T(1,128)}, f32[1,1,512]{2,1,0:T(1,128)S(1)}, u32[]{:S(2)}) copy-start(f32[1,1,512]{2,1,0:T(1,128)S(1)} %get-tuple-element.70) | copy-start | bytes 6148
  5.9 5.0 %copy-start.49 = (f32[1,1,512]{2,1,0:T(1,128)}, f32[1,1,512]{2,1,0:T(1,128)S(1)}, u32[]{:S(2)}) copy-start(f32[1,1,512]{2,1,0:T(1,128)S(1)} %get-tuple-element.71) | copy-start | bytes 6148
  5.9 5.2 %copy-start.51 = (f32[1,1,512]{2,1,0:T(1,128)}, f32[1,1,512]{2,1,0:T(1,128)S(1)}, u32[]{:S(2)}) copy-start(f32[1,1,512]{2,1,0:T(1,128)S(1)} %get-tuple-element.59) | copy-start | bytes 6148
  5.9 5.2 %copy-start.53 = (f32[1,1,512]{2,1,0:T(1,128)}, f32[1,1,512]{2,1,0:T(1,128)S(1)}, u32[]{:S(2)}) copy-start(f32[1,1,512]{2,1,0:T(1,128)S(1)} %get-tuple-element.72) | copy-start | bytes 6148
  5.9 5.2 %copy-start.55 = (f32[1,1,512]{2,1,0:T(1,128)}, f32[1,1,512]{2,1,0:T(1,128)S(1)}, u32[]{:S(2)}) copy-start(f32[1,1,512]{2,1,0:T(1,128)S(1)} %get-tuple-element.73) | copy-start | bytes 6148
  5.9 5.2 %copy-start.57 = (f32[1,1,512]{2,1,0:T(1,128)}, f32[1,1,512]{2,1,0:T(1,128)S(1)}, u32[]{:S(2)}) copy-start(f32[1,1,512]{2,1,0:T(1,128)S(1)} %get-tuple-element.74) | copy-start | bytes 6148
  6.0 5.2 %copy-start.59 = (f32[1,1,512]{2,1,0:T(1,128)}, f32[1,1,512]{2,1,0:T(1,128)S(1)}, u32[]{:S(2)}) copy-start(f32[1,1,512]{2,1,0:T(1,128)S(1)} %get-tuple-element.75) | copy-start | bytes 6148
  6.0 5.2 %copy-start.61 = (f32[1,1,512]{2,1,0:T(1,128)}, f32[1,1,512]{2,1,0:T(1,128)S(1)}, u32[]{:S(2)}) copy-start(f32[1,1,512]{2,1,0:T(1,128)S(1)} %get-tuple-element.76) | copy-start | bytes 6148
  6.0 5.2 %copy-start.63 = (f32[1,1,512]{2,1,0:T(1,128)}, f32[1,1,512]{2,1,0:T(1,128)S(1)}, u32[]{:S(2)}) copy-start(f32[1,1,512]{2,1,0:T(1,128)S(1)} %get-tuple-element.77) | copy-start | bytes 6148
  7.9 2.4 %copy-start.15 = (bf16[128,512]{1,0:T(8,128)(2,1)S(1)}, bf16[128,512]{1,0:T(8,128)(2,1)}, u32[]{:S(2)}) copy-start(bf16[128,512]{1,0:T(8,128)(2,1)} %param.9) | copy-start | bytes 393220
  8.0 2.4 %copy-start.16 = (bf16[128,512]{1,0:T(8,128)(2,1)S(1)}, bf16[128,512]{1,0:T(8,128)(2,1)}, u32[]{:S(2)}) copy-start(bf16[128,512]{1,0:T(8,128)(2,1)} %param.8) | copy-start | bytes 393220
  8.8 2.7 %copy-start.11 = (bf16[128,512]{1,0:T(8,128)(2,1)S(1)}, bf16[128,512]{1,0:T(8,128)(2,1)}, u32[]{:S(2)}) copy-start(bf16[128,512]{1,0:T(8,128)(2,1)} %param.13) | copy-start | bytes 393220
  12.4 5.2 %copy-start.26 = (f32[32,16]{0,1:T(8,128)S(1)}, f32[32,16]{0,1:T(8,128)}, u32[]{:S(2)}) copy-start(f32[32,16]{0,1:T(8,128)} %param.11) | copy-start | bytes 6148
  12.9 3.7 %copy-start.7 = (f32[16,512]{1,0:T(8,128)}, f32[16,512]{1,0:T(8,128)S(1)}, u32[]{:S(2)}) copy-start(f32[16,512]{1,0:T(8,128)S(1)} %get-tuple-element.14) | copy-start | bytes 98308
  13.0 3.7 %copy-start.9 = (f32[16,512]{1,0:T(8,128)}, f32[16,512]{1,0:T(8,128)S(1)}, u32[]{:S(2)}) copy-start(f32[16,512]{1,0:T(8,128)S(1)} %get-tuple-element.15) | copy-start | bytes 98308
  13.0 4.6 %collective-permute-start.1 = (f32[2,16,512]{2,1,0:T(8,128)S(1)}, f32[2,16,512]{2,1,0:T(8,128)S(1)}, u32[]{:S(2)}, u32[]{:S(2)}) collective-permute-start(f32[2,16,512]{2,1,0:T(8,128)S(1)} %pad_maximum_fusion.6), channel_id=1, source_target_pairs={{0,8},{8,0},{16,24},{24,16},{32,40},{40,32},{48,56},{56,48},{1,9},... | collective-permute-start | bytes 196616 | tf_op jit(solution)/shard_map/ppermute | solution.py:85
  17.5 7.1 %copy-start.6 = (bf16[128,512]{0,1:T(8,128)(2,1)}, bf16[128,512]{0,1:T(8,128)(2,1)S(1)}, u32[]{:S(2)}) copy-start(bf16[128,512]{0,1:T(8,128)(2,1)S(1)} %copy.30) | copy-start | bytes 393220
  17.7 4.8 %copy-start.13 = (f32[32,16]{1,0:T(8,128)}, f32[32,16]{1,0:T(8,128)S(1)}, u32[]{:S(2)}) copy-start(f32[32,16]{1,0:T(8,128)S(1)} %copy.26) | copy-start | bytes 6148
  26.3 34.6 %copy-start.1 = (f32[32,16,129]{2,1,0:T(8,128)S(1)}, f32[32,16,129]{2,1,0:T(8,128)}, u32[]{:S(2)}) copy-start(f32[32,16,129]{2,1,0:T(8,128)} %copy-done) | copy-start | bytes 792580
  26.3 38.3 %copy-start.24 = (f32[1,16,512]{2,1,0:T(8,128)S(1)}, f32[1,16,512]{2,1,0:T(8,128)}, u32[]{:S(2)}) copy-start(f32[1,16,512]{2,1,0:T(8,128)} %get-tuple-element.24) | copy-start | bytes 98308
  26.3 38.3 %copy-start.25 = (f32[1,16,512]{2,1,0:T(8,128)S(1)}, f32[1,16,512]{2,1,0:T(8,128)}, u32[]{:S(2)}) copy-start(f32[1,16,512]{2,1,0:T(8,128)} %get-tuple-element.26) | copy-start | bytes 98308
  26.3 46.3 %copy-start.14 = (f32[32,16]{1,0:T(8,128)S(1)}, f32[32,16]{1,0:T(8,128)}, u32[]{:S(2)}) copy-start(f32[32,16]{1,0:T(8,128)} %copy-done.13) | copy-start | bytes 6148
  30.6 6.2 %collective-permute-start.2 = (f32[2,16,512]{2,1,0:T(8,128)S(1)}, f32[2,16,512]{2,1,0:T(8,128)S(1)}, u32[]{:S(2)}, u32[]{:S(2)}) collective-permute-start(f32[2,16,512]{2,1,0:T(8,128)S(1)} %fusion.148), channel_id=1, source_target_pairs={{0,16},{8,24},{16,0},{24,8},{32,48},{40,56},{48,32},{56,40},{1,17}... | collective-permute-start | bytes 196616 | tf_op jit(solution)/shard_map/ppermute | solution.py:85
  37.8 39.8 %copy-start.18 = (f32[1,16,512]{2,1,0:T(8,128)S(1)}, f32[1,16,512]{2,1,0:T(8,128)}, u32[]{:S(2)}) copy-start(f32[1,16,512]{2,1,0:T(8,128)} %get-tuple-element.34) | copy-start | bytes 98308
  37.8 39.7 %copy-start.19 = (f32[1,16,512]{2,1,0:T(8,128)S(1)}, f32[1,16,512]{2,1,0:T(8,128)}, u32[]{:S(2)}) copy-start(f32[1,16,512]{2,1,0:T(8,128)} %get-tuple-element.35) | copy-start | bytes 98308
  37.8 39.7 %copy-start.20 = (f32[1,16,512]{2,1,0:T(8,128)S(1)}, f32[1,16,512]{2,1,0:T(8,128)}, u32[]{:S(2)}) copy-start(f32[1,16,512]{2,1,0:T(8,128)} %get-tuple-element.27) | copy-start | bytes 98308
  37.8 39.7 %copy-start.21 = (f32[1,16,512]{2,1,0:T(8,128)S(1)}, f32[1,16,512]{2,1,0:T(8,128)}, u32[]{:S(2)}) copy-start(f32[1,16,512]{2,1,0:T(8,128)} %get-tuple-element.28) | copy-start | bytes 98308
  37.9 39.7 %copy-start.22 = (f32[1,16,512]{2,1,0:T(8,128)S(1)}, f32[1,16,512]{2,1,0:T(8,128)}, u32[]{:S(2)}) copy-start(f32[1,16,512]{2,1,0:T(8,128)} %get-tuple-element.30) | copy-start | bytes 98308
  37.9 39.7 %copy-start.23 = (f32[1,16,512]{2,1,0:T(8,128)S(1)}, f32[1,16,512]{2,1,0:T(8,128)}, u32[]{:S(2)}) copy-start(f32[1,16,512]{2,1,0:T(8,128)} %get-tuple-element.31) | copy-start | bytes 98308
  37.9 7.8 %collective-permute-start.3 = (f32[2,16,512]{2,1,0:T(8,128)S(1)}, f32[2,16,512]{2,1,0:T(8,128)S(1)}, u32[]{:S(2)}, u32[]{:S(2)}) collective-permute-start(f32[2,16,512]{2,1,0:T(8,128)S(1)} %fusion.149), channel_id=1, source_target_pairs={{0,32},{8,40},{16,48},{24,56},{32,0},{40,8},{48,16},{56,24},{1,33}... | collective-permute-start | bytes 196616 | tf_op jit(solution)/shard_map/ppermute | solution.py:85
  44.1 6.8 %collective-permute-start.4 = (f32[56,512]{1,0:T(8,128)}, f32[56,512]{1,0:T(8,128)S(1)}, u32[]{:S(2)}, u32[]{:S(2)}) collective-permute-start(f32[56,512]{1,0:T(8,128)} %constant_dynamic-update-slice_fusion), channel_id=1, source_target_pairs={{8,0},{16,8},{24,16},{32,24},{40,32},{48,40},{56,48},{64,56},{72,6... | collective-permute-start | bytes 344072 | tf_op jit(solution)/shard_map/ppermute | solution.py:19
  46.7 31.0 %copy-start.8 = (f32[16,512]{1,0:T(8,128)S(1)}, f32[16,512]{1,0:T(8,128)}, u32[]{:S(2)}) copy-start(f32[16,512]{1,0:T(8,128)} %copy-done.7) | copy-start | bytes 98308
  46.7 7.0 %collective-permute-start.5 = (f32[2,16,512]{2,1,0:T(8,128)S(1)}, f32[2,16,512]{2,1,0:T(8,128)S(1)}, u32[]{:S(2)}, u32[]{:S(2)}) collective-permute-start(f32[2,16,512]{2,1,0:T(8,128)S(1)} %get-tuple-element.58), channel_id=1, source_target_pairs={{0,64},{64,0},{128,192},{192,128},{256,320},{320,256},{384,448},{4... | collective-permute-start | bytes 196616 | tf_op jit(solution)/shard_map/ppermute | solution.py:85
  54.5 10.0 %collective-permute-start.6 = (f32[2,16,512]{2,1,0:T(8,128)S(1)}, f32[2,16,512]{2,1,0:T(8,128)S(1)}, u32[]{:S(2)}, u32[]{:S(2)}) collective-permute-start(f32[2,16,512]{2,1,0:T(8,128)S(1)} %fusion.153), channel_id=1, source_target_pairs={{0,128},{64,192},{128,0},{192,64},{256,384},{320,448},{384,256},{4... | collective-permute-start | bytes 196616 | tf_op jit(solution)/shard_map/ppermute | solution.py:85
  61.8 16.6 %copy-start.5 = (bf16[128,512]{1,0:T(8,128)(2,1)S(1)}, bf16[128,512]{1,0:T(8,128)(2,1)}, u32[]{:S(2)}) copy-start(bf16[128,512]{1,0:T(8,128)(2,1)} %copy-done.4) | copy-start | bytes 393220
  61.8 16.6 %copy-start.12 = (bf16[128,512]{1,0:T(8,128)(2,1)S(1)}, bf16[128,512]{1,0:T(8,128)(2,1)}, u32[]{:S(2)}) copy-start(bf16[128,512]{1,0:T(8,128)(2,1)} %param.13) | copy-start | bytes 393220
  64.5 13.0 %collective-permute-start.7 = (f32[2,16,512]{2,1,0:T(8,128)S(1)}, f32[2,16,512]{2,1,0:T(8,128)S(1)}, u32[]{:S(2)}, u32[]{:S(2)}) collective-permute-start(f32[2,16,512]{2,1,0:T(8,128)S(1)} %fusion.154), channel_id=1, source_target_pairs={{0,256},{64,320},{128,384},{192,448},{256,0},{320,64},{384,128},{4... | collective-permute-start | bytes 196616 | tf_op jit(solution)/shard_map/ppermute | solution.py:85
  80.2 2.7 %copy-start.38 = (f32[1,1,512]{2,1,0:T(1,128)S(1)}, f32[1,1,512]{2,1,0:T(1,128)}, u32[]{:S(2)}) copy-start(f32[1,1,512]{2,1,0:T(1,128)} %copy-done.37) | copy-start | bytes 6148
  80.2 2.7 %copy-start.40 = (f32[1,1,512]{2,1,0:T(1,128)S(1)}, f32[1,1,512]{2,1,0:T(1,128)}, u32[]{:S(2)}) copy-start(f32[1,1,512]{2,1,0:T(1,128)} %copy-done.39) | copy-start | bytes 6148
  80.2 2.7 %copy-start.42 = (f32[1,1,512]{2,1,0:T(1,128)S(1)}, f32[1,1,512]{2,1,0:T(1,128)}, u32[]{:S(2)}) copy-start(f32[1,1,512]{2,1,0:T(1,128)} %copy-done.41) | copy-start | bytes 6148
  80.2 2.7 %copy-start.44 = (f32[1,1,512]{2,1,0:T(1,128)S(1)}, f32[1,1,512]{2,1,0:T(1,128)}, u32[]{:S(2)}) copy-start(f32[1,1,512]{2,1,0:T(1,128)} %copy-done.43) | copy-start | bytes 6148
  80.2 2.7 %copy-start.46 = (f32[1,1,512]{2,1,0:T(1,128)S(1)}, f32[1,1,512]{2,1,0:T(1,128)}, u32[]{:S(2)}) copy-start(f32[1,1,512]{2,1,0:T(1,128)} %copy-done.45) | copy-start | bytes 6148
  80.2 2.7 %copy-start.48 = (f32[1,1,512]{2,1,0:T(1,128)S(1)}, f32[1,1,512]{2,1,0:T(1,128)}, u32[]{:S(2)}) copy-start(f32[1,1,512]{2,1,0:T(1,128)} %copy-done.47) | copy-start | bytes 6148
  80.2 2.7 %copy-start.50 = (f32[1,1,512]{2,1,0:T(1,128)S(1)}, f32[1,1,512]{2,1,0:T(1,128)}, u32[]{:S(2)}) copy-start(f32[1,1,512]{2,1,0:T(1,128)} %copy-done.49) | copy-start | bytes 6148
  80.8 3.0 %copy-start.28 = (f32[1,1,512]{2,1,0:T(1,128)S(1)}, f32[1,1,512]{2,1,0:T(1,128)}, u32[]{:S(2)}) copy-start(f32[1,1,512]{2,1,0:T(1,128)} %copy-done.27) | copy-start | bytes 6148
  80.8 3.0 %copy-start.30 = (f32[1,1,512]{2,1,0:T(1,128)S(1)}, f32[1,1,512]{2,1,0:T(1,128)}, u32[]{:S(2)}) copy-start(f32[1,1,512]{2,1,0:T(1,128)} %copy-done.29) | copy-start | bytes 6148
  80.8 3.0 %copy-start.32 = (f32[1,1,512]{2,1,0:T(1,128)S(1)}, f32[1,1,512]{2,1,0:T(1,128)}, u32[]{:S(2)}) copy-start(f32[1,1,512]{2,1,0:T(1,128)} %copy-done.31) | copy-start | bytes 6148
  80.8 3.0 %copy-start.34 = (f32[1,1,512]{2,1,0:T(1,128)S(1)}, f32[1,1,512]{2,1,0:T(1,128)}, u32[]{:S(2)}) copy-start(f32[1,1,512]{2,1,0:T(1,128)} %copy-done.33) | copy-start | bytes 6148
  80.9 3.0 %copy-start.36 = (f32[1,1,512]{2,1,0:T(1,128)S(1)}, f32[1,1,512]{2,1,0:T(1,128)}, u32[]{:S(2)}) copy-start(f32[1,1,512]{2,1,0:T(1,128)} %copy-done.35) | copy-start | bytes 6148
  80.9 3.0 %copy-start.66 = (f32[1,1,512]{2,1,0:T(1,128)S(1)}, f32[1,1,512]{2,1,0:T(1,128)}, u32[]{:S(2)}) copy-start(f32[1,1,512]{2,1,0:T(1,128)} %copy-done.65) | copy-start | bytes 6148
  80.9 3.0 %copy-start.68 = (f32[1,1,512]{2,1,0:T(1,128)S(1)}, f32[1,1,512]{2,1,0:T(1,128)}, u32[]{:S(2)}) copy-start(f32[1,1,512]{2,1,0:T(1,128)} %copy-done.67) | copy-start | bytes 6148
  (13 other events, 20.8 us)

commit v10 on v7

--- a/solution.py
+++ b/solution.py
@@ -166,31 +166,26 @@
     grad_prod = rounded(local_grad + carried_grad)
 
     edge = SHORT - 1
+    slab = 8
+    pieces = [local_conv, local_grad, grad_out, k_short, v_short]
     ahead = jnp.concatenate(
-        [
-            local_conv[:edge],
-            local_grad[:edge],
-            grad_out[:edge].astype(jnp.float32),
-            k_short[:edge].astype(jnp.float32),
-            v_short[:edge].astype(jnp.float32),
-            start_state,
-        ]
+        [piece[:slab].astype(jnp.float32) for piece in pieces] + [start_state]
     )
     ahead = from_behind(ahead, ("zl", "xc"), -1)
     through = factors[-2] * entering + end_state
-    beyond = (leaving - ahead[5 * edge :]) * factors[-1]
+    beyond = (leaving - ahead[slab * len(pieces) :]) * factors[-1]
     next_conv = rounded(
         ahead[:edge]
         + jnp.einsum("kt,kc->tc", lead_fwd[:, :edge], spread(through), precision=precise)
     )
     next_grad = rounded(
-        ahead[edge : 2 * edge]
+        ahead[slab : slab + edge]
         + jnp.einsum("ks,kc->sc", lead_bwd[:, :edge], spread(beyond), precision=precise)
     )
     next_rows = (
-        rounded(ahead[2 * edge : 3 * edge] * next_conv.astype(jnp.float32)),
-        rounded(next_grad.astype(jnp.float32) * ahead[4 * edge : 5 * edge]),
-        rounded(next_grad.astype(jnp.float32) * ahead[3 * edge : 4 * edge]),
+        rounded(ahead[2 * slab : 2 * slab + edge] * next_conv.astype(jnp.float32)),
+        rounded(next_grad.astype(jnp.float32) * ahead[4 * slab : 4 * slab + edge]),
+        rounded(next_grad.astype(jnp.float32) * ahead[3 * slab : 3 * slab + edge]),
     )
 
     mixer_out = (q_short.astype(jnp.float32) * conv_out.astype(jnp.float32)).astype(jnp.bfloat16)

time: 76.9 us -> 89.6 us (1.17)
  the two profiles are of different devices: /device:TPU:15 before, /device:TPU:1 now
where the time goes in v10:
time: 89.6 us; the launch traced here: 88.4 us
  starting transfers between devices  29.9 us (33%)
  waiting for transfers between devices  16.5 us (18%)
  other arithmetic  14.6 us (16%)
  matrix products  13.7 us (15%)
  local copies, waits for them, and re-layouts  11.5 us (13%)
  between operations  2.09 us (2%)
    ppermute x6, starting transfers between devices, cube_scan(): lax.ppermute(window, axis, [(source, source ^ shift) for source in range(...  18.4 us
    ppermute x6, waiting for transfers between devices, cube_scan(): lax.ppermute(window, axis, [(source, source ^ shift) for source in range(...  13.5 us
    ppermute x2, starting transfers between devices, from_behind(): lax.ppermute(value, axis, [(source, source + steps) for source in range(l...  11.5 us
    dot_general x1, matrix products, shards(): toeplitz = jnp.einsum('gtm,gms->gts', falling, rising, precision=precise)  4.45 us
    add x4, other arithmetic, cube_scan(): window = keep * window + take * arrived  3.68 us
    dot_general x4, matrix products, split_dot(): jnp.einsum(spec, high.astype(jnp.bfloat16), values, preferred_element_typ...  3.44 us
    dot_general x4, matrix products, split_dot(): jnp.einsum(spec, low, values, preferred_element_type=jnp.float32)  3.06 us
    ppermute x2, waiting for transfers between devices, from_behind(): lax.ppermute(value, axis, [(source, source + steps) for source in range(l...  2.95 us
  transfers between devices with their start and end apart: 8, of which 5 were waited for; matrix products, arithmetic and copies ran while one was open for 11% of the time, Pallas kernels for 0%

profile of v10, /device:TPU:1, one launch (start us, length us, event | category | flops | bytes accessed | tf_op | source)
XLA Modules:
  0.0 88.4 jit_solution(3139634129014018315)
XLA Ops:
  0.6 0.7 slice_bitcast_fusion.6
  1.3 0.7 slice_bitcast_fusion.4
  2.1 4.5 %collective-permute-start = (bf16[3,6,512]{2,1,0:T(8,128)(2,1)S(1)}, bf16[3,6,512]{2,1,0:T(8,128)(2,1)S(1)}, u32[]{:S(2)}, u32[]{:S(2)}) collective-permute-start(bf16[3,6,512]{2,1,0:T(8,128)(2,1)S(1)} %pad_maximum_fusion.7), channel_id=1, source_target_pairs={{0,8},{8,16},{16,24},{24,32},{32,40},{40,48},{48,56},{56,64},{64,7... | collective-permute-start | bytes 55304 | tf_op jit(solution)/shard_map/ppermute | solution.py:19
  6.6 1.2 %fusion.181 = (f32[1,1,512]{2,1,0:T(1,128)S(1)}, f32[1,1,512]{2,1,0:T(1,128)S(1)}, f32[1,1,512]{2,1,0:T(1,128)S(1)}, f32[1,1,512]{2,1,0:T(1,128)S(1)}, f32[1,1,5...) fusion(f32[3,7,512]{2,1,0:T(8,128)} %param.10), kind=kLoop, calls=%fused_computation.330 | loop fusion | bytes 77824 | tf_op jit(solution)/shard_map/slice | solution.py:32
  7.9 0.8 fusion.182
  8.8 0.7 negate_bitcast_fusion
  9.6 0.1 multiply_exponential_fusion.1
  10.3 0.2 neg.35
  10.5 0.2 multiply_exponential_fusion
  10.7 0.7 slice_select_fusion.6
  11.5 0.8 slice_select_fusion.7
  12.5 0.2 fusion.93
  12.8 0.2 fusion.76
  13.2 0.5 copy-done.2
  13.7 0.2 fusion.110
  14.0 0.3 fusion.183
  14.3 0.3 convolution_add_fusion.1
  14.5 0.3 fusion.184
  14.8 0.3 convolution_add_fusion
  15.1 0.3 multiply_reduce_fusion.1
  15.4 5.6 %collective-permute-start.1 = (f32[2,16,512]{2,1,0:T(8,128)S(1)}, f32[2,16,512]{2,1,0:T(8,128)S(1)}, u32[]{:S(2)}, u32[]{:S(2)}) collective-permute-start(f32[2,16,512]{2,1,0:T(8,128)S(1)} %pad_maximum_fusion.6), channel_id=1, source_target_pairs={{0,8},{8,0},{16,24},{24,16},{32,40},{40,32},{48,56},{56,48},{1,9},... | collective-permute-start | bytes 196616 | tf_op jit(solution)/shard_map/ppermute | solution.py:85
  21.0 0.6 convert_add_fusion
  21.6 0.8 copy.33
  22.3 0.8 copy.24
  23.1 0.6 copy-done.12
  23.8 0.2 fusion.180
  24.1 0.1 broadcast_multiply_fusion.2
  24.3 0.7 copy.27
  25.0 4.4 %fusion.133 = f32[32,128,128]{2,1,0:T(8,128)S(1)} fusion(f32[32,16]{1,0:T(8,128)} %copy.27, f32[128]{0:T(128)} %get-tuple-element.84, f32[128]{0:T(128)} %get-tuple-element.85, f32[32,16]{1,0:T(8,128)} %copy-done.15), kind=kOutput, calls=%fused_computation.211 | convolution fusion | flops 100859904 | bytes 2102272 | tf_op jit(solution)/shard_map/gtm,gms->gts/dot_general | solution.py:154
  29.4 1.3 %fusion.11 = f32[32,16,128]{2,1,0:T(8,128)S(1)} fusion(bf16[128,32,16]{0,2,1:T(8,128)(2,1)} %bitcast.132, f32[32,128,128]{2,1,0:T(8,128)S(1)} %fusion.133, pred[128,128]{1,0:T(8,128)(4,1)S(1)} %iota_compare_fusion.1), kind=kOutput, calls=%fused_computation.65 | convolution fusion | flops 18350080 | bytes 2506752 | tf_op jit(solution)/shard_map/gts,tgc->sgc/dot_general | solution.py:49
  30.7 1.1 %convolution_add_fusion.2 = f32[32,16,128]{2,1,0:T(8,128)} fusion(f32[32,16,128]{2,1,0:T(8,128)S(1)} %fusion.11, bf16[128,32,16]{0,2,1:T(8,128)(2,1)S(1)} %bitcast.133, f32[32,128,128]{2,1,0:T(8,128)S(1)} %fusion.133, pred[128,128]{1,0:T(8,128)(4,1)S(1)} %iota_compare_fusion.1), kind=kOutput, calls=%fused_computation.7 | convolution fusion | flops 18939904 | bytes 2768896 | tf_op jit(solution)/shard_map/gts,tgc->sgc/dot_general | solution.py:50
  31.8 1.7 %copy.43 = f32[8,512]{1,0:T(8,128)} copy(f32[8,512]{0,1:T(8,128)} %bitcast.126) | data formatting | bytes 32768 | tf_op jit(solution)/shard_map/slice | solution.py:172
  33.5 1.6 %fusion.12 = f32[32,16,128]{2,1,0:T(8,128)S(1)} fusion(bf16[128,32,16]{0,2,1:T(8,128)(2,1)} %bitcast.130, f32[32,128,128]{2,1,0:T(8,128)S(1)} %fusion.133, pred[128,128]{1,0:T(8,128)(4,1)S(1)} %iota_compare_fusion.1), kind=kOutput, calls=%fused_computation.66 | convolution fusion | flops 18350080 | bytes 2506752 | tf_op jit(solution)/shard_map/gts,sgc->tgc/dot_general | solution.py:49
  35.1 1.4 %convolution_add_fusion.3 = f32[32,16,128]{2,1,0:T(8,128)} fusion(f32[32,16,128]{2,1,0:T(8,128)S(1)} %fusion.12, bf16[128,32,16]{0,2,1:T(8,128)(2,1)S(1)} %bitcast.131, f32[32,128,128]{2,1,0:T(8,128)S(1)} %fusion.133, pred[128,128]{1,0:T(8,128)(4,1)S(1)} %iota_compare_fusion.1), kind=kOutput, calls=%fused_computation.8 | convolution fusion | flops 18939904 | bytes 2768896 | tf_op jit(solution)/shard_map/gts,sgc->tgc/dot_general | solution.py:50
  36.5 1.1 %copy.35 = f32[8,512]{1,0:T(8,128)S(1)} copy(f32[8,512]{0,1:T(8,128)} %bitcast.128) | data formatting | bytes 32768 | tf_op jit(solution)/shard_map/slice | solution.py:172
  37.6 1.0 %fusion.148 = f32[2,16,512]{2,1,0:T(8,128)S(1)} fusion(f32[1,16,512]{2,1,0:T(8,128)} %get-tuple-element.21, f32[1,16,512]{2,1,0:T(8,128)} %get-tuple-element.33, f32[2,16,512]{2,1,0:T(8,128)} %copy-done.12, f32[1,16,512]{2,1,0:T(8,128)} %bitcast.138, f32[1,16,512]{2,1,0:T(8,128)} %bitcast.135), kind=kLoop, calls=%fused_computation.230 | loop fusion | flops 98304 | bytes 262144 | tf_op jit(solution)/shard_map/add | solution.py:89
  38.6 1.9 %collective-permute-start.2 = (f32[2,16,512]{2,1,0:T(8,128)S(1)}, f32[2,16,512]{2,1,0:T(8,128)S(1)}, u32[]{:S(2)}, u32[]{:S(2)}) collective-permute-start(f32[2,16,512]{2,1,0:T(8,128)S(1)} %fusion.148), channel_id=1, source_target_pairs={{0,16},{8,24},{16,0},{24,8},{32,48},{40,56},{48,32},{56,40},{1,17}... | collective-permute-start | bytes 196616 | tf_op jit(solution)/shard_map/ppermute | solution.py:85
  40.5 0.7 constant_dynamic-update-slice_fusion.1
  41.3 3.0 %collective-permute-done.2 = f32[2,16,512]{2,1,0:T(8,128)S(1)} collective-permute-done((f32[2,16,512]{2,1,0:T(8,128)S(1)}, f32[2,16,512]{2,1,0:T(8,128)S(1)}, u32[]{:S(2)}, u32[]{:S(2)}) %collective-permute-start.2) | collective-permute-done | bytes 65568 | tf_op jit(solution)/shard_map/ppermute | solution.py:85
  44.2 1.0 %fusion.149 = f32[2,16,512]{2,1,0:T(8,128)S(1)} fusion(f32[1,16,512]{2,1,0:T(8,128)} %get-tuple-element.17, f32[1,16,512]{2,1,0:T(8,128)} %get-tuple-element.32, f32[2,16,512]{2,1,0:T(8,128)S(1)} %collective-permute-done.2, f32[2,16,512]{2,1,0:T(8,128)} %copy-done.12, f32[1,16,512]{2,1,0:T(8,128)} %get-tuple-element.33, ...), kind=kLoop, calls=%fused_computation.234 | loop fusion | flops 180224 | bytes 393216 | tf_op jit(solution)/shard_map/add | solution.py:89
  45.2 2.1 %collective-permute-start.3 = (f32[2,16,512]{2,1,0:T(8,128)S(1)}, f32[2,16,512]{2,1,0:T(8,128)S(1)}, u32[]{:S(2)}, u32[]{:S(2)}) collective-permute-start(f32[2,16,512]{2,1,0:T(8,128)S(1)} %fusion.149), channel_id=1, source_target_pairs={{0,32},{8,40},{16,48},{24,56},{32,0},{40,8},{48,16},{56,24},{1,33}... | collective-permute-start | bytes 196616 | tf_op jit(solution)/shard_map/ppermute | solution.py:85
  47.3 0.7 convert_dynamic-update-slice_fusion.2
  48.0 3.9 %collective-permute-done.3 = f32[2,16,512]{2,1,0:T(8,128)S(1)} collective-permute-done((f32[2,16,512]{2,1,0:T(8,128)S(1)}, f32[2,16,512]{2,1,0:T(8,128)S(1)}, u32[]{:S(2)}, u32[]{:S(2)}) %collective-permute-start.3) | collective-permute-done | bytes 65568 | tf_op jit(solution)/shard_map/ppermute | solution.py:85
  51.9 1.0 %fusion.147 = (f32[2,16,512]{2,1,0:T(8,128)S(1)}, f32[2,16,512]{2,1,0:T(8,128)S(1)}) fusion(f32[2,16,512]{2,1,0:T(8,128)} %copy-done.12, f32[1,16,512]{2,1,0:T(8,128)} %get-tuple-element.36, f32[1,16,512]{2,1,0:T(8,128)} %get-tuple-element.37, f32[2,16,512]{2,1,0:T(8,128)S(1)} %collective-permute-done.2, f32[1,16,512]{2,1,0:T(8,128)} %get-tuple-element.34, ...), kind=kLoop, calls=%fused_computation.227 | loop fusion | flops 212992 | bytes 655360 | tf_op jit(solution)/shard_map/add | solution.py:88
  52.9 1.9 %collective-permute-start.4 = (f32[2,16,512]{2,1,0:T(8,128)S(1)}, f32[2,16,512]{2,1,0:T(8,128)S(1)}, u32[]{:S(2)}, u32[]{:S(2)}) collective-permute-start(f32[2,16,512]{2,1,0:T(8,128)S(1)} %get-tuple-element.54), channel_id=1, source_target_pairs={{0,64},{64,0},{128,192},{192,128},{256,320},{320,256},{384,448},{4... | collective-permute-start | bytes 196616 | tf_op jit(solution)/shard_map/ppermute | solution.py:85
  54.8 3.1 %collective-permute-done.4 = f32[2,16,512]{2,1,0:T(8,128)S(1)} collective-permute-done((f32[2,16,512]{2,1,0:T(8,128)S(1)}, f32[2,16,512]{2,1,0:T(8,128)S(1)}, u32[]{:S(2)}, u32[]{:S(2)}) %collective-permute-start.4) | collective-permute-done | bytes 65568 | tf_op jit(solution)/shard_map/ppermute | solution.py:85
  57.9 0.9 fusion.153
  58.7 2.0 %collective-permute-start.5 = (f32[2,16,512]{2,1,0:T(8,128)S(1)}, f32[2,16,512]{2,1,0:T(8,128)S(1)}, u32[]{:S(2)}, u32[]{:S(2)}) collective-permute-start(f32[2,16,512]{2,1,0:T(8,128)S(1)} %fusion.153), channel_id=1, source_target_pairs={{0,128},{64,192},{128,0},{192,64},{256,384},{320,448},{384,256},{4... | collective-permute-start | bytes 196616 | tf_op jit(solution)/shard_map/ppermute | solution.py:85
  60.8 0.7 convert_dynamic-update-slice_fusion
  61.5 3.6 %collective-permute-done.5 = f32[2,16,512]{2,1,0:T(8,128)S(1)} collective-permute-done((f32[2,16,512]{2,1,0:T(8,128)S(1)}, f32[2,16,512]{2,1,0:T(8,128)S(1)}, u32[]{:S(2)}, u32[]{:S(2)}) %collective-permute-start.5) | collective-permute-done | bytes 65568 | tf_op jit(solution)/shard_map/ppermute | solution.py:85
  65.1 0.9 fusion.154
  65.9 5.0 %collective-permute-start.6 = (f32[2,16,512]{2,1,0:T(8,128)S(1)}, f32[2,16,512]{2,1,0:T(8,128)S(1)}, u32[]{:S(2)}, u32[]{:S(2)}) collective-permute-start(f32[2,16,512]{2,1,0:T(8,128)S(1)} %fusion.154), channel_id=1, source_target_pairs={{0,256},{64,320},{128,384},{192,448},{256,0},{320,64},{384,128},{4... | collective-permute-start | bytes 196616 | tf_op jit(solution)/shard_map/ppermute | solution.py:85
  70.9 7.0 %collective-permute-start.7 = (f32[56,512]{1,0:T(8,128)S(1)}, f32[56,512]{1,0:T(8,128)S(1)}, u32[]{:S(2)}, u32[]{:S(2)}) collective-permute-start(f32[56,512]{1,0:T(8,128)S(1)} %constant_dynamic-update-slice_fusion), channel_id=1, source_target_pairs={{8,0},{16,8},{24,16},{32,24},{40,32},{48,40},{56,48},{64,56},{72,6... | collective-permute-start | bytes 344072 | tf_op jit(solution)/shard_map/ppermute | solution.py:19
  78.0 0.1 copy.38
  78.4 2.9 %collective-permute-done.7 = f32[56,512]{1,0:T(8,128)S(1)} collective-permute-done((f32[56,512]{1,0:T(8,128)S(1)}, f32[56,512]{1,0:T(8,128)S(1)}, u32[]{:S(2)}, u32[]{:S(2)}) %collective-permute-start.7) | collective-permute-done | bytes 114720 | tf_op jit(solution)/shard_map/ppermute | solution.py:19
  81.3 0.8 fusion.3
  82.2 0.3 broadcast_multiply_fusion
  82.5 0.6 fusion.164
  83.3 0.6 fusion.128
  84.0 0.8 fusion.4
  84.9 0.7 fusion.16
  85.7 0.9 %fusion.25 = bf16[128,512]{1,0:T(8,128)(2,1)} fusion(f32[6,512]{1,0:T(8,128)S(1)} %convert_element_type.273, f32[128,512]{1,0:T(8,128)S(1)} %convert_element_type.271, f32[512]{0:T(512)S(1)} %bitcast.181, f32[512]{0:T(512)S(1)} %bitcast.179, f32[512]{0:T(512)S(1)} %bitcast.169, f32[512]{0:T(512)S(1)} %bitcast.171, f32[512]{0:T(512)S(1)} %bitcast.173, ...), kind=kLoop, calls=%fused_computation.79 | loop fusion | flops 1310720 | bytes 419840 | tf_op jit(solution)/shard_map/convert_element_type | solution.py:197
  86.6 0.9 %fusion.42 = bf16[128,512]{1,0:T(8,128)(2,1)} fusion(f32[6,512]{1,0:T(8,128)S(1)} %convert_element_type.268, f32[128,512]{1,0:T(8,128)S(1)} %convert_element_type.264, f32[512]{0:T(512)S(1)} %bitcast.155, f32[512]{0:T(512)S(1)} %bitcast.157, f32[512]{0:T(512)S(1)} %bitcast.159, f32[512]{0:T(512)S(1)} %bitcast.161, f32[512]{0:T(512)S(1)} %bitcast.163, ...), kind=kLoop, calls=%fused_computation.96 | loop fusion | flops 1310720 | bytes 419840 | tf_op jit(solution)/shard_map/convert_element_type | solution.py:196
  87.5 0.9 %fusion.59 = bf16[128,512]{1,0:T(8,128)(2,1)} fusion(f32[6,512]{1,0:T(8,128)S(1)} %convert_element_type.259, f32[128,512]{1,0:T(8,128)S(1)} %convert_element_type.252, f32[512]{0:T(512)S(1)} %bitcast.143, f32[512]{0:T(512)S(1)} %bitcast.145, f32[512]{0:T(512)S(1)} %bitcast.147, f32[512]{0:T(512)S(1)} %bitcast.149, f32[512]{0:T(512)S(1)} %bitcast.151, ...), kind=kLoop, calls=%fused_computation.113 | loop fusion | flops 1310720 | bytes 419840 | tf_op jit(solution)/shard_map/convert_element_type | solution.py:195
  (174 shorter events, 1.6 us)
Async XLA Ops:
  2.1 10.3 %collective-permute-start = (bf16[3,6,512]{2,1,0:T(8,128)(2,1)S(1)}, bf16[3,6,512]{2,1,0:T(8,128)(2,1)S(1)}, u32[]{:S(2)}, u32[]{:S(2)}) collective-permute-start(bf16[3,6,512]{2,1,0:T(8,128)(2,1)S(1)} %pad_maximum_fusion.7), channel_id=1, source_target_pairs={{0,8},{8,16},{16,24},{24,32},{32,40},{40,48},{48,56},{56,64},{64,7... | collective-permute-start | bytes 55304 | tf_op jit(solution)/shard_map/ppermute | solution.py:19
  7.8 4.7 %copy-start.40 = (f32[1,1,512]{2,1,0:T(1,128)}, f32[1,1,512]{2,1,0:T(1,128)S(1)}, u32[]{:S(2)}) copy-start(f32[1,1,512]{2,1,0:T(1,128)S(1)} %get-tuple-element.61) | copy-start | bytes 6148
  7.8 4.7 %copy-start.42 = (f32[1,1,512]{2,1,0:T(1,128)}, f32[1,1,512]{2,1,0:T(1,128)S(1)}, u32[]{:S(2)}) copy-start(f32[1,1,512]{2,1,0:T(1,128)S(1)} %get-tuple-element.62) | copy-start | bytes 6148
  7.8 4.7 %copy-start.44 = (f32[1,1,512]{2,1,0:T(1,128)}, f32[1,1,512]{2,1,0:T(1,128)S(1)}, u32[]{:S(2)}) copy-start(f32[1,1,512]{2,1,0:T(1,128)S(1)} %get-tuple-element.63) | copy-start | bytes 6148
  7.8 4.7 %copy-start.46 = (f32[1,1,512]{2,1,0:T(1,128)}, f32[1,1,512]{2,1,0:T(1,128)S(1)}, u32[]{:S(2)}) copy-start(f32[1,1,512]{2,1,0:T(1,128)S(1)} %get-tuple-element.64) | copy-start | bytes 6148
  7.8 4.7 %copy-start.48 = (f32[1,1,512]{2,1,0:T(1,128)}, f32[1,1,512]{2,1,0:T(1,128)S(1)}, u32[]{:S(2)}) copy-start(f32[1,1,512]{2,1,0:T(1,128)S(1)} %get-tuple-element.65) | copy-start | bytes 6148
  7.8 4.7 %copy-start.50 = (f32[1,1,512]{2,1,0:T(1,128)}, f32[1,1,512]{2,1,0:T(1,128)S(1)}, u32[]{:S(2)}) copy-start(f32[1,1,512]{2,1,0:T(1,128)S(1)} %get-tuple-element.66) | copy-start | bytes 6148
  7.8 4.7 %copy-start.52 = (f32[1,1,512]{2,1,0:T(1,128)}, f32[1,1,512]{2,1,0:T(1,128)S(1)}, u32[]{:S(2)}) copy-start(f32[1,1,512]{2,1,0:T(1,128)S(1)} %get-tuple-element.67) | copy-start | bytes 6148
  7.8 4.9 %copy-start.54 = (f32[1,1,512]{2,1,0:T(1,128)}, f32[1,1,512]{2,1,0:T(1,128)S(1)}, u32[]{:S(2)}) copy-start(f32[1,1,512]{2,1,0:T(1,128)S(1)} %get-tuple-element.56) | copy-start | bytes 6148
  7.8 4.9 %copy-start.56 = (f32[1,1,512]{2,1,0:T(1,128)}, f32[1,1,512]{2,1,0:T(1,128)S(1)}, u32[]{:S(2)}) copy-start(f32[1,1,512]{2,1,0:T(1,128)S(1)} %get-tuple-element.57) | copy-start | bytes 6148
  7.8 4.9 %copy-start.58 = (f32[1,1,512]{2,1,0:T(1,128)}, f32[1,1,512]{2,1,0:T(1,128)S(1)}, u32[]{:S(2)}) copy-start(f32[1,1,512]{2,1,0:T(1,128)S(1)} %get-tuple-element.58) | copy-start | bytes 6148
  7.9 4.9 %copy-start.60 = (f32[1,1,512]{2,1,0:T(1,128)}, f32[1,1,512]{2,1,0:T(1,128)S(1)}, u32[]{:S(2)}) copy-start(f32[1,1,512]{2,1,0:T(1,128)S(1)} %get-tuple-element.59) | copy-start | bytes 6148
  7.9 4.9 %copy-start.62 = (f32[1,1,512]{2,1,0:T(1,128)}, f32[1,1,512]{2,1,0:T(1,128)S(1)}, u32[]{:S(2)}) copy-start(f32[1,1,512]{2,1,0:T(1,128)S(1)} %get-tuple-element.60) | copy-start | bytes 6148
  7.9 5.2 %copy-start.26 = (f32[1,1,512]{2,1,0:T(1,128)}, f32[1,1,512]{2,1,0:T(1,128)S(1)}, u32[]{:S(2)}) copy-start(f32[1,1,512]{2,1,0:T(1,128)S(1)} %get-tuple-element.55) | copy-start | bytes 6148
  7.9 5.2 %copy-start.28 = (f32[1,1,512]{2,1,0:T(1,128)}, f32[1,1,512]{2,1,0:T(1,128)S(1)}, u32[]{:S(2)}) copy-start(f32[1,1,512]{2,1,0:T(1,128)S(1)} %get-tuple-element.68) | copy-start | bytes 6148
  7.9 5.2 %copy-start.30 = (f32[1,1,512]{2,1,0:T(1,128)}, f32[1,1,512]{2,1,0:T(1,128)S(1)}, u32[]{:S(2)}) copy-start(f32[1,1,512]{2,1,0:T(1,128)S(1)} %get-tuple-element.69) | copy-start | bytes 6148
  7.9 5.2 %copy-start.32 = (f32[1,1,512]{2,1,0:T(1,128)}, f32[1,1,512]{2,1,0:T(1,128)S(1)}, u32[]{:S(2)}) copy-start(f32[1,1,512]{2,1,0:T(1,128)S(1)} %get-tuple-element.70) | copy-start | bytes 6148
  7.9 5.2 %copy-start.34 = (f32[1,1,512]{2,1,0:T(1,128)}, f32[1,1,512]{2,1,0:T(1,128)S(1)}, u32[]{:S(2)}) copy-start(f32[1,1,512]{2,1,0:T(1,128)S(1)} %get-tuple-element.71) | copy-start | bytes 6148
  7.9 5.2 %copy-start.36 = (f32[1,1,512]{2,1,0:T(1,128)}, f32[1,1,512]{2,1,0:T(1,128)S(1)}, u32[]{:S(2)}) copy-start(f32[1,1,512]{2,1,0:T(1,128)S(1)} %get-tuple-element.72) | copy-start | bytes 6148
  7.9 5.2 %copy-start.38 = (f32[1,1,512]{2,1,0:T(1,128)}, f32[1,1,512]{2,1,0:T(1,128)S(1)}, u32[]{:S(2)}) copy-start(f32[1,1,512]{2,1,0:T(1,128)S(1)} %get-tuple-element.73) | copy-start | bytes 6148
  8.7 4.0 %copy-start.64 = (f32[1,1,512]{2,1,0:T(1,128)}, f32[1,1,512]{2,1,0:T(1,128)S(1)}, u32[]{:S(2)}) copy-start(f32[1,1,512]{2,1,0:T(1,128)S(1)} %get-tuple-element.74) | copy-start | bytes 6148
  8.7 4.0 %copy-start.66 = (f32[1,1,512]{2,1,0:T(1,128)}, f32[1,1,512]{2,1,0:T(1,128)S(1)}, u32[]{:S(2)}) copy-start(f32[1,1,512]{2,1,0:T(1,128)S(1)} %get-tuple-element.75) | copy-start | bytes 6148
  10.7 3.2 %copy-start.13 = (bf16[128,512]{1,0:T(8,128)(2,1)S(1)}, bf16[128,512]{1,0:T(8,128)(2,1)}, u32[]{:S(2)}) copy-start(bf16[128,512]{1,0:T(8,128)(2,1)} %param.13) | copy-start | bytes 393220
  15.1 9.2 %copy-start.25 = (f32[32,16]{0,1:T(8,128)S(1)}, f32[32,16]{0,1:T(8,128)}, u32[]{:S(2)}) copy-start(f32[32,16]{0,1:T(8,128)} %param.11) | copy-start | bytes 6148
  15.4 7.7 %copy-start.8 = (f32[16,512]{1,0:T(8,128)}, f32[16,512]{1,0:T(8,128)S(1)}, u32[]{:S(2)}) copy-start(f32[16,512]{1,0:T(8,128)S(1)} %get-tuple-element.10) | copy-start | bytes 98308
  15.4 7.7 %copy-start.10 = (f32[16,512]{1,0:T(8,128)}, f32[16,512]{1,0:T(8,128)S(1)}, u32[]{:S(2)}) copy-start(f32[16,512]{1,0:T(8,128)S(1)} %get-tuple-element.11) | copy-start | bytes 98308
  15.4 7.7 %collective-permute-start.1 = (f32[2,16,512]{2,1,0:T(8,128)S(1)}, f32[2,16,512]{2,1,0:T(8,128)S(1)}, u32[]{:S(2)}, u32[]{:S(2)}) collective-permute-start(f32[2,16,512]{2,1,0:T(8,128)S(1)} %pad_maximum_fusion.6), channel_id=1, source_target_pairs={{0,8},{8,0},{16,24},{24,16},{32,40},{40,32},{48,56},{56,48},{1,9},... | collective-permute-start | bytes 196616 | tf_op jit(solution)/shard_map/ppermute | solution.py:85
  25.0 5.7 %copy-start.7 = (bf16[128,512]{0,1:T(8,128)(2,1)S(1)}, bf16[128,512]{0,1:T(8,128)(2,1)}, u32[]{:S(2)}) copy-start(bf16[128,512]{0,1:T(8,128)(2,1)} %copy.33) | copy-start | bytes 393220
  36.5 34.5 %copy-start.11 = (f32[16,512]{1,0:T(8,128)S(1)}, f32[16,512]{1,0:T(8,128)}, u32[]{:S(2)}) copy-start(f32[16,512]{1,0:T(8,128)} %copy-done.10) | copy-start | bytes 98308
  36.5 41.5 %copy-start = (f32[32,16,128]{2,1,0:T(8,128)S(1)}, f32[32,16,128]{2,1,0:T(8,128)}, u32[]{:S(2)}) copy-start(f32[32,16,128]{2,1,0:T(8,128)} %convolution_add_fusion.2) | copy-start | bytes 786436
  36.5 41.6 %copy-start.1 = (f32[32,16,128]{2,1,0:T(8,128)S(1)}, f32[32,16,128]{2,1,0:T(8,128)}, u32[]{:S(2)}) copy-start(f32[32,16,128]{2,1,0:T(8,128)} %convolution_add_fusion.3) | copy-start | bytes 786436
  36.5 41.8 %copy-start.19 = (f32[1,16,512]{2,1,0:T(8,128)S(1)}, f32[1,16,512]{2,1,0:T(8,128)}, u32[]{:S(2)}) copy-start(f32[1,16,512]{2,1,0:T(8,128)} %get-tuple-element.30) | copy-start | bytes 98308
  36.5 41.8 %copy-start.20 = (f32[1,16,512]{2,1,0:T(8,128)S(1)}, f32[1,16,512]{2,1,0:T(8,128)}, u32[]{:S(2)}) copy-start(f32[1,16,512]{2,1,0:T(8,128)} %get-tuple-element.31) | copy-start | bytes 98308
  36.5 41.8 %copy-start.21 = (f32[1,16,512]{2,1,0:T(8,128)S(1)}, f32[1,16,512]{2,1,0:T(8,128)}, u32[]{:S(2)}) copy-start(f32[1,16,512]{2,1,0:T(8,128)} %get-tuple-element.23) | copy-start | bytes 98308
  36.5 41.8 %copy-start.22 = (f32[1,16,512]{2,1,0:T(8,128)S(1)}, f32[1,16,512]{2,1,0:T(8,128)}, u32[]{:S(2)}) copy-start(f32[1,16,512]{2,1,0:T(8,128)} %get-tuple-element.24) | copy-start | bytes 98308
  36.5 41.8 %copy-start.23 = (f32[1,16,512]{2,1,0:T(8,128)S(1)}, f32[1,16,512]{2,1,0:T(8,128)}, u32[]{:S(2)}) copy-start(f32[1,16,512]{2,1,0:T(8,128)} %get-tuple-element.26) | copy-start | bytes 98308
  36.5 41.8 %copy-start.24 = (f32[1,16,512]{2,1,0:T(8,128)S(1)}, f32[1,16,512]{2,1,0:T(8,128)}, u32[]{:S(2)}) copy-start(f32[1,16,512]{2,1,0:T(8,128)} %get-tuple-element.27) | copy-start | bytes 98308
  36.5 41.8 %copy-start.9 = (f32[16,512]{1,0:T(8,128)S(1)}, f32[16,512]{1,0:T(8,128)}, u32[]{:S(2)}) copy-start(f32[16,512]{1,0:T(8,128)} %copy-done.8) | copy-start | bytes 98308
  38.6 5.6 %collective-permute-start.2 = (f32[2,16,512]{2,1,0:T(8,128)S(1)}, f32[2,16,512]{2,1,0:T(8,128)S(1)}, u32[]{:S(2)}, u32[]{:S(2)}) collective-permute-start(f32[2,16,512]{2,1,0:T(8,128)S(1)} %fusion.148), channel_id=1, source_target_pairs={{0,16},{8,24},{16,0},{24,8},{32,48},{40,56},{48,32},{56,40},{1,17}... | collective-permute-start | bytes 196616 | tf_op jit(solution)/shard_map/ppermute | solution.py:85
  45.2 36.9 %copy-start.3 = (bf16[128,512]{1,0:T(8,128)(2,1)S(1)}, bf16[128,512]{1,0:T(8,128)(2,1)}, u32[]{:S(2)}) copy-start(bf16[128,512]{1,0:T(8,128)(2,1)} %copy-done.2) | copy-start | bytes 393220
  45.2 6.6 %collective-permute-start.3 = (f32[2,16,512]{2,1,0:T(8,128)S(1)}, f32[2,16,512]{2,1,0:T(8,128)S(1)}, u32[]{:S(2)}, u32[]{:S(2)}) collective-permute-start(f32[2,16,512]{2,1,0:T(8,128)S(1)} %fusion.149), channel_id=1, source_target_pairs={{0,32},{8,40},{16,48},{24,56},{32,0},{40,8},{48,16},{56,24},{1,33}... | collective-permute-start | bytes 196616 | tf_op jit(solution)/shard_map/ppermute | solution.py:85
  52.9 5.0 %collective-permute-start.4 = (f32[2,16,512]{2,1,0:T(8,128)S(1)}, f32[2,16,512]{2,1,0:T(8,128)S(1)}, u32[]{:S(2)}, u32[]{:S(2)}) collective-permute-start(f32[2,16,512]{2,1,0:T(8,128)S(1)} %get-tuple-element.54), channel_id=1, source_target_pairs={{0,64},{64,0},{128,192},{192,128},{256,320},{320,256},{384,448},{4... | collective-permute-start | bytes 196616 | tf_op jit(solution)/shard_map/ppermute | solution.py:85
  58.7 6.3 %collective-permute-start.5 = (f32[2,16,512]{2,1,0:T(8,128)S(1)}, f32[2,16,512]{2,1,0:T(8,128)S(1)}, u32[]{:S(2)}, u32[]{:S(2)}) collective-permute-start(f32[2,16,512]{2,1,0:T(8,128)S(1)} %fusion.153), channel_id=1, source_target_pairs={{0,128},{64,192},{128,0},{192,64},{256,384},{320,448},{384,256},{4... | collective-permute-start | bytes 196616 | tf_op jit(solution)/shard_map/ppermute | solution.py:85
  65.9 12.3 %collective-permute-start.6 = (f32[2,16,512]{2,1,0:T(8,128)S(1)}, f32[2,16,512]{2,1,0:T(8,128)S(1)}, u32[]{:S(2)}, u32[]{:S(2)}) collective-permute-start(f32[2,16,512]{2,1,0:T(8,128)S(1)} %fusion.154), channel_id=1, source_target_pairs={{0,256},{64,320},{128,384},{192,448},{256,0},{320,64},{384,128},{4... | collective-permute-start | bytes 196616 | tf_op jit(solution)/shard_map/ppermute | solution.py:85
  70.9 10.4 %collective-permute-start.7 = (f32[56,512]{1,0:T(8,128)S(1)}, f32[56,512]{1,0:T(8,128)S(1)}, u32[]{:S(2)}, u32[]{:S(2)}) collective-permute-start(f32[56,512]{1,0:T(8,128)S(1)} %constant_dynamic-update-slice_fusion), channel_id=1, source_target_pairs={{8,0},{16,8},{24,16},{32,24},{40,32},{48,40},{56,48},{64,56},{72,6... | collective-permute-start | bytes 344072 | tf_op jit(solution)/shard_map/ppermute | solution.py:19
  83.1 2.5 %copy-start.59 = (f32[1,1,512]{2,1,0:T(1,128)S(1)}, f32[1,1,512]{2,1,0:T(1,128)}, u32[]{:S(2)}) copy-start(f32[1,1,512]{2,1,0:T(1,128)} %copy-done.58) | copy-start | bytes 6148
  83.2 2.5 %copy-start.61 = (f32[1,1,512]{2,1,0:T(1,128)S(1)}, f32[1,1,512]{2,1,0:T(1,128)}, u32[]{:S(2)}) copy-start(f32[1,1,512]{2,1,0:T(1,128)} %copy-done.60) | copy-start | bytes 6148
  83.2 2.5 %copy-start.63 = (f32[1,1,512]{2,1,0:T(1,128)S(1)}, f32[1,1,512]{2,1,0:T(1,128)}, u32[]{:S(2)}) copy-start(f32[1,1,512]{2,1,0:T(1,128)} %copy-done.62) | copy-start | bytes 6148
  83.2 2.5 %copy-start.65 = (f32[1,1,512]{2,1,0:T(1,128)S(1)}, f32[1,1,512]{2,1,0:T(1,128)}, u32[]{:S(2)}) copy-start(f32[1,1,512]{2,1,0:T(1,128)} %copy-done.64) | copy-start | bytes 6148
  83.2 2.5 %copy-start.67 = (f32[1,1,512]{2,1,0:T(1,128)S(1)}, f32[1,1,512]{2,1,0:T(1,128)}, u32[]{:S(2)}) copy-start(f32[1,1,512]{2,1,0:T(1,128)} %copy-done.66) | copy-start | bytes 6148
  83.2 3.4 %copy-start.41 = (f32[1,1,512]{2,1,0:T(1,128)S(1)}, f32[1,1,512]{2,1,0:T(1,128)}, u32[]{:S(2)}) copy-start(f32[1,1,512]{2,1,0:T(1,128)} %copy-done.40) | copy-start | bytes 6148
  83.2 3.4 %copy-start.43 = (f32[1,1,512]{2,1,0:T(1,128)S(1)}, f32[1,1,512]{2,1,0:T(1,128)}, u32[]{:S(2)}) copy-start(f32[1,1,512]{2,1,0:T(1,128)} %copy-done.42) | copy-start | bytes 6148
  83.2 3.3 %copy-start.45 = (f32[1,1,512]{2,1,0:T(1,128)S(1)}, f32[1,1,512]{2,1,0:T(1,128)}, u32[]{:S(2)}) copy-start(f32[1,1,512]{2,1,0:T(1,128)} %copy-done.44) | copy-start | bytes 6148
  83.2 3.3 %copy-start.47 = (f32[1,1,512]{2,1,0:T(1,128)S(1)}, f32[1,1,512]{2,1,0:T(1,128)}, u32[]{:S(2)}) copy-start(f32[1,1,512]{2,1,0:T(1,128)} %copy-done.46) | copy-start | bytes 6148
  83.2 3.3 %copy-start.49 = (f32[1,1,512]{2,1,0:T(1,128)S(1)}, f32[1,1,512]{2,1,0:T(1,128)}, u32[]{:S(2)}) copy-start(f32[1,1,512]{2,1,0:T(1,128)} %copy-done.48) | copy-start | bytes 6148
  83.2 3.3 %copy-start.51 = (f32[1,1,512]{2,1,0:T(1,128)S(1)}, f32[1,1,512]{2,1,0:T(1,128)}, u32[]{:S(2)}) copy-start(f32[1,1,512]{2,1,0:T(1,128)} %copy-done.50) | copy-start | bytes 6148
  83.3 3.3 %copy-start.53 = (f32[1,1,512]{2,1,0:T(1,128)S(1)}, f32[1,1,512]{2,1,0:T(1,128)}, u32[]{:S(2)}) copy-start(f32[1,1,512]{2,1,0:T(1,128)} %copy-done.52) | copy-start | bytes 6148
  83.3 4.2 %copy-start.27 = (f32[1,1,512]{2,1,0:T(1,128)S(1)}, f32[1,1,512]{2,1,0:T(1,128)}, u32[]{:S(2)}) copy-start(f32[1,1,512]{2,1,0:T(1,128)} %copy-done.26) | copy-start | bytes 6148
  83.3 4.2 %copy-start.29 = (f32[1,1,512]{2,1,0:T(1,128)S(1)}, f32[1,1,512]{2,1,0:T(1,128)}, u32[]{:S(2)}) copy-start(f32[1,1,512]{2,1,0:T(1,128)} %copy-done.28) | copy-start | bytes 6148
  83.3 4.2 %copy-start.31 = (f32[1,1,512]{2,1,0:T(1,128)S(1)}, f32[1,1,512]{2,1,0:T(1,128)}, u32[]{:S(2)}) copy-start(f32[1,1,512]{2,1,0:T(1,128)} %copy-done.30) | copy-start | bytes 6148
  83.3 4.2 %copy-start.33 = (f32[1,1,512]{2,1,0:T(1,128)S(1)}, f32[1,1,512]{2,1,0:T(1,128)}, u32[]{:S(2)}) copy-start(f32[1,1,512]{2,1,0:T(1,128)} %copy-done.32) | copy-start | bytes 6148
  83.3 4.2 %copy-start.35 = (f32[1,1,512]{2,1,0:T(1,128)S(1)}, f32[1,1,512]{2,1,0:T(1,128)}, u32[]{:S(2)}) copy-start(f32[1,1,512]{2,1,0:T(1,128)} %copy-done.34) | copy-start | bytes 6148
  83.3 4.2 %copy-start.37 = (f32[1,1,512]{2,1,0:T(1,128)S(1)}, f32[1,1,512]{2,1,0:T(1,128)}, u32[]{:S(2)}) copy-start(f32[1,1,512]{2,1,0:T(1,128)} %copy-done.36) | copy-start | bytes 6148
  83.3 4.2 %copy-start.39 = (f32[1,1,512]{2,1,0:T(1,128)S(1)}, f32[1,1,512]{2,1,0:T(1,128)}, u32[]{:S(2)}) copy-start(f32[1,1,512]{2,1,0:T(1,128)} %copy-done.38) | copy-start | bytes 6148
  (12 other events, 21.7 us)

commit v11 on v8

--- a/solution.py
+++ b/solution.py
@@ -102,9 +102,6 @@
         ]
     )
     before = from_behind(rim_rows, ("zl", "xc"), 1)
-    edge = SHORT - 1
-    head_rows = jnp.stack([u_query[:edge], u_key[:edge], u_value[:edge], grad_out[:edge]])
-    after = from_behind(head_rows, ("zl", "xc"), -1)
     q_short = rounded(short_causal(before[0], u_query, short_filter[0]))
     k_short = rounded(short_causal(before[1], u_key, short_filter[1]))
     v_short = rounded(short_causal(before[2], u_value, short_filter[2]))
@@ -147,7 +144,10 @@
     near, group, (rates, weights) = cube_scan(
         jnp.stack([end_state, start_state]), inner_rounds, "xc", inner, (rates, weights)
     )
-    far, _, _ = cube_scan(group, outer_rounds, "zl", outer, ())
+    edge = SHORT - 1
+    head_rows = jnp.stack([q_short[:edge], k_short[:edge], v_short[:edge], grad_out[:edge]])
+    after = from_behind(head_rows, ("zl", "xc"), -1)
+    far, _, after = cube_scan(group, outer_rounds, "zl", outer, after)
     entering = near[0] + factors[-3] * far[0]
     leaving = near[1] + factors[-2] * far[1]
 
@@ -168,11 +168,9 @@
     conv_out = rounded(local_conv + carried_conv)
     grad_prod = rounded(local_grad + carried_grad)
 
-    q_next = rounded(short_causal(rim_rows[0], after[0], short_filter[0]))
-    k_next = rounded(short_causal(rim_rows[1], after[1], short_filter[1]))
-    v_next = rounded(short_causal(rim_rows[2], after[2], short_filter[2]))
-    p_next = rounded(k_next.astype(jnp.float32) * v_next.astype(jnp.float32))
-    gc_next = rounded(after[3].astype(jnp.float32) * q_next.astype(jnp.float32))
+    q_next, k_next, v_next, go_next = (after[row].astype(jnp.float32) for row in range(4))
+    p_next = rounded(k_next * v_next)
+    gc_next = rounded(go_next * q_next)
     rate_rows = decay_step / block_len
     weight_rows = jnp.repeat(weights.T, GROUP, axis=1)
     lag_terms = jnp.concatenate([-jnp.arange(SHORT), jnp.arange(SHORT)]).astype(jnp.float32)
@@ -191,9 +189,9 @@
         - short_causal(none_before, gc_next, rising_taps)
     )
     next_rows = (
-        rounded(after[3].astype(jnp.float32) * next_conv.astype(jnp.float32)),
-        rounded(next_grad.astype(jnp.float32) * v_next.astype(jnp.float32)),
-        rounded(next_grad.astype(jnp.float32) * k_next.astype(jnp.float32)),
+        rounded(go_next * next_conv.astype(jnp.float32)),
+        rounded(next_grad.astype(jnp.float32) * v_next),
+        rounded(next_grad.astype(jnp.float32) * k_next),
     )
 
     mixer_out = (q_short.astype(jnp.float32) * conv_out.astype(jnp.float32)).astype(jnp.bfloat16)

time: 95.5 us -> 87.9 us (0.920)
  the two profiles are of different devices: /device:TPU:24 before, /device:TPU:18 now
where the time goes in v11:
time: 87.9 us; the launch traced here: 86.9 us
  starting transfers between devices  36.8 us (42%)
  other arithmetic  16.5 us (19%)
  matrix products  11.8 us (13%)
  local copies, waits for them, and re-layouts  9.78 us (11%)
  waiting for transfers between devices  9.56 us (11%)
  between operations  2.46 us (3%)
    ppermute x6, starting transfers between devices, cube_scan(): lax.ppermute(window, axis, [(source, source ^ shift) for source in range(...  32.7 us
    ppermute x6, waiting for transfers between devices, cube_scan(): lax.ppermute(window, axis, [(source, source ^ shift) for source in range(...  9.56 us
    dot_general x1, matrix products, shards(): toeplitz = jnp.einsum('gtm,gms->gts', falling, rising, precision=precise)  4.45 us
    ppermute x2, starting transfers between devices, from_behind(): lax.ppermute(value, axis, [(source, source + steps) for source in range(l...  4.09 us
    convert_element_type x12, other arithmetic, rounded(): return lax.optimization_barrier(values.astype(jnp.bfloat16))  3.74 us
    dot_general x4, matrix products, split_dot(): jnp.einsum(spec, low, values, preferred_element_type=jnp.float32)  3.07 us
    dot_general x4, matrix products, split_dot(): jnp.einsum(spec, high.astype(jnp.bfloat16), values, preferred_element_typ...  2.52 us
    slice x2, local copies, waits for them, and re-layouts, short_causal(): filter_taps[offset] * padded[SHORT - 1 - offset:SHORT - 1 - offset + length]  1.97 us
  transfers between devices with their start and end apart: 8, of which 5 were waited for; matrix products, arithmetic and copies ran while one was open for 28% of the time, Pallas kernels for 0%

profile of v11, /device:TPU:18, one launch (start us, length us, event | category | flops | bytes accessed | tf_op | source)
XLA Modules:
  0.0 86.9 jit_solution(6513297337224617545)
XLA Ops:
  0.6 0.7 slice_bitcast_fusion.9
  1.4 0.7 slice_bitcast_fusion.7
  2.1 2.1 %collective-permute-start = (bf16[3,6,512]{2,1,0:T(8,128)(2,1)S(1)}, bf16[3,6,512]{2,1,0:T(8,128)(2,1)S(1)}, u32[]{:S(2)}, u32[]{:S(2)}) collective-permute-start(bf16[3,6,512]{2,1,0:T(8,128)(2,1)S(1)} %pad_maximum_fusion.8), channel_id=1, source_target_pairs={{0,8},{8,16},{16,24},{24,32},{32,40},{40,48},{48,56},{56,64},{64,7... | collective-permute-start | bytes 55304 | tf_op jit(solution)/shard_map/ppermute | solution.py:19
  4.2 1.2 %fusion.211 = (f32[1,1,512]{2,1,0:T(1,128)S(1)}, f32[1,1,512]{2,1,0:T(1,128)S(1)}, f32[1,1,512]{2,1,0:T(1,128)S(1)}, f32[1,1,512]{2,1,0:T(1,128)S(1)}, f32[1,1,5...) fusion(f32[3,7,512]{2,1,0:T(8,128)} %param.10), kind=kLoop, calls=%fused_computation.376 | loop fusion | bytes 77824 | tf_op jit(solution)/shard_map/slice | solution.py:32
  5.5 0.8 fusion.212
  6.3 0.7 fusion.215
  7.2 0.1 multiply_exponential_fusion.1
  7.3 0.1 fusion.210
  7.6 0.8 fusion.20
  8.4 0.6 convert_add_fusion
  9.0 0.7 fusion.19
  9.9 0.2 reshape.203
  10.2 0.1 multiply_exponential_fusion.2
  10.5 0.2 multiply_exponential_fusion
  10.6 0.8 slice_select_fusion.6
  11.4 0.2 copy-done
  11.6 0.8 slice_select_fusion.7
  12.4 0.5 iota_compare_fusion.2
  13.0 0.8 rev.7
  14.0 0.2 fusion.110
  14.3 0.2 fusion.93
  14.7 0.2 fusion.76
  15.0 0.8 copy.35
  15.7 0.3 fusion.216
  16.0 0.8 copy.42
  16.8 0.3 fusion.217
  17.1 0.3 convolution_add_fusion.1
  17.4 0.3 convolution_add_fusion
  17.7 0.3 multiply_reduce_fusion.1
  18.0 3.5 %collective-permute-start.1 = (f32[2,16,512]{2,1,0:T(8,128)S(1)}, f32[2,16,512]{2,1,0:T(8,128)S(1)}, u32[]{:S(2)}, u32[]{:S(2)}) collective-permute-start(f32[2,16,512]{2,1,0:T(8,128)S(1)} %pad_maximum_fusion.6), channel_id=1, source_target_pairs={{0,8},{8,0},{16,24},{24,16},{32,40},{40,32},{48,56},{56,48},{1,9},... | collective-permute-start | bytes 196616 | tf_op jit(solution)/shard_map/ppermute | solution.py:85
  21.5 0.6 pad_maximum_fusion.7
  22.1 2.0 %collective-permute-start.4 = (bf16[4,6,512]{2,1,0:T(8,128)(2,1)}, bf16[4,6,512]{2,1,0:T(8,128)(2,1)}, u32[]{:S(2)}, u32[]{:S(2)}) collective-permute-start(bf16[4,6,512]{2,1,0:T(8,128)(2,1)} %pad_maximum_fusion.7), channel_id=1, source_target_pairs={{8,0},{16,8},{24,16},{32,24},{40,32},{48,40},{56,48},{64,56},{72,6... | collective-permute-start | bytes 73736 | tf_op jit(solution)/shard_map/ppermute | solution.py:19
  24.2 0.7 copy.37
  24.9 0.7 copy.38
  25.6 4.4 %fusion.131 = f32[32,128,128]{2,1,0:T(8,128)S(1)} fusion(f32[32,16]{1,0:T(8,128)} %copy.38, f32[128]{0:T(128)} %get-tuple-element.103, f32[128]{0:T(128)} %get-tuple-element.104, f32[32,16]{1,0:T(8,128)} %copy.37), kind=kOutput, calls=%fused_computation.208 | convolution fusion | flops 100859904 | bytes 2102272 | tf_op jit(solution)/shard_map/gtm,gms->gts/dot_general | solution.py:157
  30.0 0.4 fusion.11
  30.4 1.1 %convolution_add_fusion.2 = f32[32,16,128]{2,1,0:T(8,128)} fusion(f32[32,16,128]{2,1,0:T(8,128)S(1)} %fusion.11, bf16[128,32,16]{0,2,1:T(8,128)(2,1)S(1)} %bitcast.147, f32[32,128,128]{2,1,0:T(8,128)S(1)} %fusion.131, pred[128,128]{1,0:T(8,128)(4,1)S(1)} %iota_compare_fusion.1), kind=kOutput, calls=%fused_computation.7 | convolution fusion | flops 18939904 | bytes 2768896 | tf_op jit(solution)/shard_map/gts,tgc->sgc/dot_general | solution.py:50
  31.6 0.6 fusion.152
  32.2 1.9 %collective-permute-start.2 = (f32[2,16,512]{2,1,0:T(8,128)}, f32[2,16,512]{2,1,0:T(8,128)}, u32[]{:S(2)}, u32[]{:S(2)}) collective-permute-start(f32[2,16,512]{2,1,0:T(8,128)} %fusion.152), channel_id=1, source_target_pairs={{0,16},{8,24},{16,0},{24,8},{32,48},{40,56},{48,32},{56,40},{1,17}... | collective-permute-start | bytes 196616 | tf_op jit(solution)/shard_map/ppermute | solution.py:85
  34.3 0.8 mul.898
  35.0 1.6 %fusion.12 = f32[32,16,128]{2,1,0:T(8,128)S(1)} fusion(bf16[128,32,16]{0,2,1:T(8,128)(2,1)} %bitcast.144, f32[32,128,128]{2,1,0:T(8,128)S(1)} %fusion.131, pred[128,128]{1,0:T(8,128)(4,1)S(1)} %iota_compare_fusion.1), kind=kOutput, calls=%fused_computation.65 | convolution fusion | flops 18350080 | bytes 2506752 | tf_op jit(solution)/shard_map/gts,sgc->tgc/dot_general | solution.py:49
  36.8 1.4 %convolution_add_fusion.3 = f32[32,16,128]{2,1,0:T(8,128)} fusion(f32[32,16,128]{2,1,0:T(8,128)S(1)} %fusion.12, bf16[128,32,16]{0,2,1:T(8,128)(2,1)S(1)} %bitcast.145, f32[32,128,128]{2,1,0:T(8,128)S(1)} %fusion.131, pred[128,128]{1,0:T(8,128)(4,1)S(1)} %iota_compare_fusion.1), kind=kOutput, calls=%fused_computation.8 | convolution fusion | flops 18939904 | bytes 2768896 | tf_op jit(solution)/shard_map/gts,sgc->tgc/dot_general | solution.py:50
  38.4 0.3 collective-permute-done.2
  38.8 0.9 fusion.153
  39.7 4.6 %collective-permute-start.3 = (f32[2,16,512]{2,1,0:T(8,128)S(1)}, f32[2,16,512]{2,1,0:T(8,128)S(1)}, u32[]{:S(2)}, u32[]{:S(2)}) collective-permute-start(f32[2,16,512]{2,1,0:T(8,128)S(1)} %fusion.153), channel_id=1, source_target_pairs={{0,32},{8,40},{16,48},{24,56},{32,0},{40,8},{48,16},{56,24},{1,33}... | collective-permute-start | bytes 196616 | tf_op jit(solution)/shard_map/ppermute | solution.py:85
  44.4 3.0 %collective-permute-done.3 = f32[2,16,512]{2,1,0:T(8,128)S(1)} collective-permute-done((f32[2,16,512]{2,1,0:T(8,128)S(1)}, f32[2,16,512]{2,1,0:T(8,128)S(1)}, u32[]{:S(2)}, u32[]{:S(2)}) %collective-permute-start.3) | collective-permute-done | bytes 65568 | tf_op jit(solution)/shard_map/ppermute | solution.py:85
  47.5 0.9 %fusion.151 = (f32[2,16,512]{2,1,0:T(8,128)S(1)}, f32[2,16,512]{2,1,0:T(8,128)S(1)}) fusion(f32[2,16,512]{2,1,0:T(8,128)S(1)} %copy-done.14, f32[1,16,512]{2,1,0:T(8,128)S(1)} %copy-done.39, f32[1,16,512]{2,1,0:T(8,128)S(1)} %copy-done.40, f32[2,16,512]{2,1,0:T(8,128)} %collective-permute-done.2, f32[1,16,512]{2,1,0:T(8,128)S(1)} %copy-done.37, ...), kind=kLoop, calls=%fused_computation.232 | loop fusion | flops 212992 | bytes 655360 | tf_op jit(solution)/shard_map/add | solution.py:88
  48.5 6.1 %collective-permute-start.5 = (f32[2,16,512]{2,1,0:T(8,128)S(1)}, f32[2,16,512]{2,1,0:T(8,128)S(1)}, u32[]{:S(2)}, u32[]{:S(2)}) collective-permute-start(f32[2,16,512]{2,1,0:T(8,128)S(1)} %get-tuple-element.57), channel_id=1, source_target_pairs={{0,64},{64,0},{128,192},{192,128},{256,320},{320,256},{384,448},{4... | collective-permute-start | bytes 196616 | tf_op jit(solution)/shard_map/ppermute | solution.py:85
  54.6 2.2 %collective-permute-done.5 = f32[2,16,512]{2,1,0:T(8,128)S(1)} collective-permute-done((f32[2,16,512]{2,1,0:T(8,128)S(1)}, f32[2,16,512]{2,1,0:T(8,128)S(1)}, u32[]{:S(2)}, u32[]{:S(2)}) %collective-permute-start.5) | collective-permute-done | bytes 65568 | tf_op jit(solution)/shard_map/ppermute | solution.py:85
  56.9 5.3 %collective-permute-start.6 = (f32[2,16,512]{2,1,0:T(8,128)S(1)}, f32[2,16,512]{2,1,0:T(8,128)S(1)}, u32[]{:S(2)}, u32[]{:S(2)}) collective-permute-start(f32[2,16,512]{2,1,0:T(8,128)S(1)} %fusion.157), channel_id=1, source_target_pairs={{0,128},{64,192},{128,0},{192,64},{256,384},{320,448},{384,256},{4... | collective-permute-start | bytes 196616 | tf_op jit(solution)/shard_map/ppermute | solution.py:85
  62.2 0.2 reshape.204
  62.6 1.8 %collective-permute-done.6 = f32[2,16,512]{2,1,0:T(8,128)S(1)} collective-permute-done((f32[2,16,512]{2,1,0:T(8,128)S(1)}, f32[2,16,512]{2,1,0:T(8,128)S(1)}, u32[]{:S(2)}, u32[]{:S(2)}) %collective-permute-start.6) | collective-permute-done | bytes 65568 | tf_op jit(solution)/shard_map/ppermute | solution.py:85
  64.4 11.2 %collective-permute-start.7 = (f32[2,16,512]{2,1,0:T(8,128)S(1)}, f32[2,16,512]{2,1,0:T(8,128)S(1)}, u32[]{:S(2)}, u32[]{:S(2)}) collective-permute-start(f32[2,16,512]{2,1,0:T(8,128)S(1)} %fusion.158), channel_id=1, source_target_pairs={{0,256},{64,320},{128,384},{192,448},{256,0},{320,64},{384,128},{4... | collective-permute-start | bytes 196616 | tf_op jit(solution)/shard_map/ppermute | solution.py:85
  75.6 0.7 fusion.166
  76.4 2.2 %collective-permute-done.7 = f32[2,16,512]{2,1,0:T(8,128)S(1)} collective-permute-done((f32[2,16,512]{2,1,0:T(8,128)S(1)}, f32[2,16,512]{2,1,0:T(8,128)S(1)}, u32[]{:S(2)}, u32[]{:S(2)}) %collective-permute-start.7) | collective-permute-done | bytes 65568 | tf_op jit(solution)/shard_map/ppermute | solution.py:85
  78.7 0.9 fusion.163
  79.6 0.9 fusion.3
  80.9 0.7 fusion.169
  81.7 0.7 fusion.165
  82.4 0.9 %fusion.4 = bf16[128,512]{1,0:T(8,128)(2,1)S(1)} fusion(f32[128,512]{1,0:T(8,128)S(1)} %copy.41, f32[16,512]{1,0:T(8,128)S(1)} %get-tuple-element.23, f32[32,512]{1,0:T(8,128)S(1)} %fusion.159, f32[32,16]{1,0:T(8,128)S(1)} %copy-done.26, f32[32,16,129]{2,1,0:T(8,128)S(1)} %multiply_exponential_fusion.1), kind=kOutput, calls=%fused_computation.12 | convolution fusion | flops 403111936 | bytes 770048 | tf_op jit(solution)/shard_map/kt,kc->tc/dot_general | solution.py:166
  83.3 0.7 fusion.16
  84.1 0.9 %fusion.25 = bf16[128,512]{1,0:T(8,128)(2,1)} fusion(f32[6,512]{1,0:T(8,128)S(1)} %convert_element_type.313, f32[128,512]{1,0:T(8,128)S(1)} %convert_element_type.311, f32[512]{0:T(512)S(1)} %bitcast.199, f32[512]{0:T(512)S(1)} %bitcast.197, f32[512]{0:T(512)S(1)} %bitcast.187, f32[512]{0:T(512)S(1)} %bitcast.189, f32[512]{0:T(512)S(1)} %bitcast.191, ...), kind=kLoop, calls=%fused_computation.78 | loop fusion | flops 1310720 | bytes 419840 | tf_op jit(solution)/shard_map/convert_element_type | solution.py:203
  85.1 0.9 %fusion.42 = bf16[128,512]{1,0:T(8,128)(2,1)} fusion(f32[6,512]{1,0:T(8,128)S(1)} %convert_element_type.308, f32[128,512]{1,0:T(8,128)S(1)} %convert_element_type.300, f32[512]{0:T(512)S(1)} %bitcast.173, f32[512]{0:T(512)S(1)} %bitcast.175, f32[512]{0:T(512)S(1)} %bitcast.177, f32[512]{0:T(512)S(1)} %bitcast.179, f32[512]{0:T(512)S(1)} %bitcast.181, ...), kind=kLoop, calls=%fused_computation.95 | loop fusion | flops 1310720 | bytes 419840 | tf_op jit(solution)/shard_map/convert_element_type | solution.py:202
  86.0 0.9 %fusion.59 = bf16[128,512]{1,0:T(8,128)(2,1)} fusion(f32[6,512]{1,0:T(8,128)S(1)} %convert_element_type.295, f32[128,512]{1,0:T(8,128)S(1)} %convert_element_type.282, f32[512]{0:T(512)S(1)} %bitcast.161, f32[512]{0:T(512)S(1)} %bitcast.163, f32[512]{0:T(512)S(1)} %bitcast.165, f32[512]{0:T(512)S(1)} %bitcast.167, f32[512]{0:T(512)S(1)} %bitcast.169, ...), kind=kLoop, calls=%fused_computation.112 | loop fusion | flops 1310720 | bytes 419840 | tf_op jit(solution)/shard_map/convert_element_type | solution.py:201
  (242 shorter events, 2.0 us)
Async XLA Ops:
  0.6 9.1 %copy-start.51 = (f32[32,16]{0,1:T(8,128)S(1)}, f32[32,16]{0,1:T(8,128)}, u32[]{:S(2)}) copy-start(f32[32,16]{0,1:T(8,128)} %param.11) | copy-start | bytes 6148
  2.1 8.0 %copy-start.15 = (bf16[128,512]{1,0:T(8,128)(2,1)S(1)}, bf16[128,512]{1,0:T(8,128)(2,1)}, u32[]{:S(2)}) copy-start(bf16[128,512]{1,0:T(8,128)(2,1)} %param.13) | copy-start | bytes 393220
  2.1 11.8 %collective-permute-start = (bf16[3,6,512]{2,1,0:T(8,128)(2,1)S(1)}, bf16[3,6,512]{2,1,0:T(8,128)(2,1)S(1)}, u32[]{:S(2)}, u32[]{:S(2)}) collective-permute-start(bf16[3,6,512]{2,1,0:T(8,128)(2,1)S(1)} %pad_maximum_fusion.8), channel_id=1, source_target_pairs={{0,8},{8,16},{16,24},{24,32},{32,40},{40,48},{48,56},{56,64},{64,7... | collective-permute-start | bytes 55304 | tf_op jit(solution)/shard_map/ppermute | solution.py:19
  5.3 8.6 %copy-start.54 = (f32[1,1,512]{2,1,0:T(1,128)}, f32[1,1,512]{2,1,0:T(1,128)S(1)}, u32[]{:S(2)}) copy-start(f32[1,1,512]{2,1,0:T(1,128)S(1)} %get-tuple-element.58) | copy-start | bytes 6148
  5.3 8.6 %copy-start.56 = (f32[1,1,512]{2,1,0:T(1,128)}, f32[1,1,512]{2,1,0:T(1,128)S(1)}, u32[]{:S(2)}) copy-start(f32[1,1,512]{2,1,0:T(1,128)S(1)} %get-tuple-element.71) | copy-start | bytes 6148
  5.4 8.6 %copy-start.58 = (f32[1,1,512]{2,1,0:T(1,128)}, f32[1,1,512]{2,1,0:T(1,128)S(1)}, u32[]{:S(2)}) copy-start(f32[1,1,512]{2,1,0:T(1,128)S(1)} %get-tuple-element.72) | copy-start | bytes 6148
  5.4 8.6 %copy-start.60 = (f32[1,1,512]{2,1,0:T(1,128)}, f32[1,1,512]{2,1,0:T(1,128)S(1)}, u32[]{:S(2)}) copy-start(f32[1,1,512]{2,1,0:T(1,128)S(1)} %get-tuple-element.73) | copy-start | bytes 6148
  5.4 8.6 %copy-start.62 = (f32[1,1,512]{2,1,0:T(1,128)}, f32[1,1,512]{2,1,0:T(1,128)S(1)}, u32[]{:S(2)}) copy-start(f32[1,1,512]{2,1,0:T(1,128)S(1)} %get-tuple-element.74) | copy-start | bytes 6148
  5.4 8.6 %copy-start.64 = (f32[1,1,512]{2,1,0:T(1,128)}, f32[1,1,512]{2,1,0:T(1,128)S(1)}, u32[]{:S(2)}) copy-start(f32[1,1,512]{2,1,0:T(1,128)S(1)} %get-tuple-element.75) | copy-start | bytes 6148
  5.4 8.6 %copy-start.66 = (f32[1,1,512]{2,1,0:T(1,128)}, f32[1,1,512]{2,1,0:T(1,128)S(1)}, u32[]{:S(2)}) copy-start(f32[1,1,512]{2,1,0:T(1,128)S(1)} %get-tuple-element.76) | copy-start | bytes 6148
  5.4 8.8 %copy-start.68 = (f32[1,1,512]{2,1,0:T(1,128)}, f32[1,1,512]{2,1,0:T(1,128)S(1)}, u32[]{:S(2)}) copy-start(f32[1,1,512]{2,1,0:T(1,128)S(1)} %get-tuple-element.64) | copy-start | bytes 6148
  5.4 8.8 %copy-start.70 = (f32[1,1,512]{2,1,0:T(1,128)}, f32[1,1,512]{2,1,0:T(1,128)S(1)}, u32[]{:S(2)}) copy-start(f32[1,1,512]{2,1,0:T(1,128)S(1)} %get-tuple-element.65) | copy-start | bytes 6148
  5.4 8.8 %copy-start.72 = (f32[1,1,512]{2,1,0:T(1,128)}, f32[1,1,512]{2,1,0:T(1,128)S(1)}, u32[]{:S(2)}) copy-start(f32[1,1,512]{2,1,0:T(1,128)S(1)} %get-tuple-element.66) | copy-start | bytes 6148
  5.4 8.8 %copy-start.74 = (f32[1,1,512]{2,1,0:T(1,128)}, f32[1,1,512]{2,1,0:T(1,128)S(1)}, u32[]{:S(2)}) copy-start(f32[1,1,512]{2,1,0:T(1,128)S(1)} %get-tuple-element.67) | copy-start | bytes 6148
  5.4 8.8 %copy-start.76 = (f32[1,1,512]{2,1,0:T(1,128)}, f32[1,1,512]{2,1,0:T(1,128)S(1)}, u32[]{:S(2)}) copy-start(f32[1,1,512]{2,1,0:T(1,128)S(1)} %get-tuple-element.68) | copy-start | bytes 6148
  5.5 8.8 %copy-start.78 = (f32[1,1,512]{2,1,0:T(1,128)}, f32[1,1,512]{2,1,0:T(1,128)S(1)}, u32[]{:S(2)}) copy-start(f32[1,1,512]{2,1,0:T(1,128)S(1)} %get-tuple-element.69) | copy-start | bytes 6148
  5.5 8.8 %copy-start.80 = (f32[1,1,512]{2,1,0:T(1,128)}, f32[1,1,512]{2,1,0:T(1,128)S(1)}, u32[]{:S(2)}) copy-start(f32[1,1,512]{2,1,0:T(1,128)S(1)} %get-tuple-element.70) | copy-start | bytes 6148
  5.5 9.1 %copy-start.82 = (f32[1,1,512]{2,1,0:T(1,128)}, f32[1,1,512]{2,1,0:T(1,128)S(1)}, u32[]{:S(2)}) copy-start(f32[1,1,512]{2,1,0:T(1,128)S(1)} %get-tuple-element.59) | copy-start | bytes 6148
  5.5 9.1 %copy-start.84 = (f32[1,1,512]{2,1,0:T(1,128)}, f32[1,1,512]{2,1,0:T(1,128)S(1)}, u32[]{:S(2)}) copy-start(f32[1,1,512]{2,1,0:T(1,128)S(1)} %get-tuple-element.60) | copy-start | bytes 6148
  5.5 9.1 %copy-start.86 = (f32[1,1,512]{2,1,0:T(1,128)}, f32[1,1,512]{2,1,0:T(1,128)S(1)}, u32[]{:S(2)}) copy-start(f32[1,1,512]{2,1,0:T(1,128)S(1)} %get-tuple-element.61) | copy-start | bytes 6148
  5.5 9.1 %copy-start.88 = (f32[1,1,512]{2,1,0:T(1,128)}, f32[1,1,512]{2,1,0:T(1,128)S(1)}, u32[]{:S(2)}) copy-start(f32[1,1,512]{2,1,0:T(1,128)S(1)} %get-tuple-element.62) | copy-start | bytes 6148
  5.5 9.1 %copy-start.90 = (f32[1,1,512]{2,1,0:T(1,128)}, f32[1,1,512]{2,1,0:T(1,128)S(1)}, u32[]{:S(2)}) copy-start(f32[1,1,512]{2,1,0:T(1,128)S(1)} %get-tuple-element.63) | copy-start | bytes 6148
  6.3 8.3 %copy-start.92 = (f32[1,1,512]{2,1,0:T(1,128)}, f32[1,1,512]{2,1,0:T(1,128)S(1)}, u32[]{:S(2)}) copy-start(f32[1,1,512]{2,1,0:T(1,128)S(1)} %get-tuple-element.77) | copy-start | bytes 6148
  6.3 8.3 %copy-start.94 = (f32[1,1,512]{2,1,0:T(1,128)}, f32[1,1,512]{2,1,0:T(1,128)S(1)}, u32[]{:S(2)}) copy-start(f32[1,1,512]{2,1,0:T(1,128)S(1)} %get-tuple-element.78) | copy-start | bytes 6148
  7.1 17.1 %copy-start.52 = (f32[32,16]{0,1:T(8,128)}, f32[32,16]{0,1:T(8,128)S(1)}, u32[]{:S(2)}) copy-start(f32[32,16]{0,1:T(8,128)S(1)} %get-tuple-element.9) | copy-start | bytes 6148
  17.7 12.3 %copy-start.6 = (bf16[128,512]{0,1:T(8,128)(2,1)S(1)}, bf16[128,512]{0,1:T(8,128)(2,1)}, u32[]{:S(2)}) copy-start(bf16[128,512]{0,1:T(8,128)(2,1)} %copy.42) | copy-start | bytes 393220
  17.9 13.6 %copy-start.10 = (f32[16,512]{1,0:T(8,128)}, f32[16,512]{1,0:T(8,128)S(1)}, u32[]{:S(2)}) copy-start(f32[16,512]{1,0:T(8,128)S(1)} %get-tuple-element.18) | copy-start | bytes 98308
  18.0 13.6 %copy-start.17 = (f32[16,512]{1,0:T(8,128)}, f32[16,512]{1,0:T(8,128)S(1)}, u32[]{:S(2)}) copy-start(f32[16,512]{1,0:T(8,128)S(1)} %get-tuple-element.19) | copy-start | bytes 98308
  18.0 6.2 %collective-permute-start.1 = (f32[2,16,512]{2,1,0:T(8,128)S(1)}, f32[2,16,512]{2,1,0:T(8,128)S(1)}, u32[]{:S(2)}, u32[]{:S(2)}) collective-permute-start(f32[2,16,512]{2,1,0:T(8,128)S(1)} %pad_maximum_fusion.6), channel_id=1, source_target_pairs={{0,8},{8,0},{16,24},{24,16},{32,40},{40,32},{48,56},{56,48},{1,9},... | collective-permute-start | bytes 196616 | tf_op jit(solution)/shard_map/ppermute | solution.py:85
  22.1 32.5 %collective-permute-start.4 = (bf16[4,6,512]{2,1,0:T(8,128)(2,1)}, bf16[4,6,512]{2,1,0:T(8,128)(2,1)}, u32[]{:S(2)}, u32[]{:S(2)}) collective-permute-start(bf16[4,6,512]{2,1,0:T(8,128)(2,1)} %pad_maximum_fusion.7), channel_id=1, source_target_pairs={{8,0},{16,8},{24,16},{32,24},{40,32},{48,40},{56,48},{64,56},{72,6... | collective-permute-start | bytes 73736 | tf_op jit(solution)/shard_map/ppermute | solution.py:19
  24.2 7.4 %copy-start.13 = (f32[2,16,512]{2,1,0:T(8,128)}, f32[2,16,512]{2,1,0:T(8,128)S(1)}, u32[]{:S(2)}) copy-start(f32[2,16,512]{2,1,0:T(8,128)S(1)} %collective-permute-done.1) | copy-start | bytes 196612
  32.2 6.6 %collective-permute-start.2 = (f32[2,16,512]{2,1,0:T(8,128)}, f32[2,16,512]{2,1,0:T(8,128)}, u32[]{:S(2)}, u32[]{:S(2)}) collective-permute-start(f32[2,16,512]{2,1,0:T(8,128)} %fusion.152), channel_id=1, source_target_pairs={{0,16},{8,24},{16,0},{24,8},{32,48},{40,56},{48,32},{56,40},{1,17}... | collective-permute-start | bytes 196616 | tf_op jit(solution)/shard_map/ppermute | solution.py:85
  36.7 7.6 %copy-start.96 = (pred[7]{0:T(512)(128)(4,1)S(1)}, pred[7]{0:T(512)(128)(4,1)}, u32[]{:S(2)}) copy-start(pred[7]{0:T(512)(128)(4,1)} %iota_compare_fusion.2) | copy-start | bytes 25
  36.7 10.7 %copy-start.36 = (f32[1,16,512]{2,1,0:T(8,128)S(1)}, f32[1,16,512]{2,1,0:T(8,128)}, u32[]{:S(2)}) copy-start(f32[1,16,512]{2,1,0:T(8,128)} %get-tuple-element.37) | copy-start | bytes 98308
  36.7 10.7 %copy-start.37 = (f32[1,16,512]{2,1,0:T(8,128)S(1)}, f32[1,16,512]{2,1,0:T(8,128)}, u32[]{:S(2)}) copy-start(f32[1,16,512]{2,1,0:T(8,128)} %get-tuple-element.42) | copy-start | bytes 98308
  36.7 10.7 %copy-start.38 = (f32[1,16,512]{2,1,0:T(8,128)S(1)}, f32[1,16,512]{2,1,0:T(8,128)}, u32[]{:S(2)}) copy-start(f32[1,16,512]{2,1,0:T(8,128)} %get-tuple-element.43) | copy-start | bytes 98308
  36.8 10.7 %copy-start.39 = (f32[1,16,512]{2,1,0:T(8,128)S(1)}, f32[1,16,512]{2,1,0:T(8,128)}, u32[]{:S(2)}) copy-start(f32[1,16,512]{2,1,0:T(8,128)} %get-tuple-element.44) | copy-start | bytes 98308
  36.8 10.7 %copy-start.40 = (f32[1,16,512]{2,1,0:T(8,128)S(1)}, f32[1,16,512]{2,1,0:T(8,128)}, u32[]{:S(2)}) copy-start(f32[1,16,512]{2,1,0:T(8,128)} %get-tuple-element.45) | copy-start | bytes 98308
  36.8 10.7 %copy-start.41 = (f32[1,16,512]{2,1,0:T(8,128)S(1)}, f32[1,16,512]{2,1,0:T(8,128)}, u32[]{:S(2)}) copy-start(f32[1,16,512]{2,1,0:T(8,128)} %get-tuple-element.24) | copy-start | bytes 98308
  36.8 10.7 %copy-start.42 = (f32[1,16,512]{2,1,0:T(8,128)S(1)}, f32[1,16,512]{2,1,0:T(8,128)}, u32[]{:S(2)}) copy-start(f32[1,16,512]{2,1,0:T(8,128)} %get-tuple-element.27) | copy-start | bytes 98308
  36.8 10.7 %copy-start.43 = (f32[1,16,512]{2,1,0:T(8,128)S(1)}, f32[1,16,512]{2,1,0:T(8,128)}, u32[]{:S(2)}) copy-start(f32[1,16,512]{2,1,0:T(8,128)} %get-tuple-element.36) | copy-start | bytes 98308
  36.8 20.0 %copy-start.49 = (f32[1,16,512]{2,1,0:T(8,128)S(1)}, f32[1,16,512]{2,1,0:T(8,128)}, u32[]{:S(2)}) copy-start(f32[1,16,512]{2,1,0:T(8,128)} %get-tuple-element.28) | copy-start | bytes 98308
  36.8 20.0 %copy-start.50 = (f32[1,16,512]{2,1,0:T(8,128)S(1)}, f32[1,16,512]{2,1,0:T(8,128)}, u32[]{:S(2)}) copy-start(f32[1,16,512]{2,1,0:T(8,128)} %get-tuple-element.33) | copy-start | bytes 98308
  38.2 24.1 %copy-start.8 = (f32[32,16,128]{2,1,0:T(8,128)S(1)}, f32[32,16,128]{2,1,0:T(8,128)}, u32[]{:S(2)}) copy-start(f32[32,16,128]{2,1,0:T(8,128)} %convolution_add_fusion.2) | copy-start | bytes 786436
  38.2 24.2 %copy-start.9 = (f32[32,16,128]{2,1,0:T(8,128)S(1)}, f32[32,16,128]{2,1,0:T(8,128)}, u32[]{:S(2)}) copy-start(f32[32,16,128]{2,1,0:T(8,128)} %convolution_add_fusion.3) | copy-start | bytes 786436
  38.2 26.1 %copy-start.47 = (f32[1,16,512]{2,1,0:T(8,128)S(1)}, f32[1,16,512]{2,1,0:T(8,128)}, u32[]{:S(2)}) copy-start(f32[1,16,512]{2,1,0:T(8,128)} %get-tuple-element.29) | copy-start | bytes 98308
  38.2 26.1 %copy-start.48 = (f32[1,16,512]{2,1,0:T(8,128)S(1)}, f32[1,16,512]{2,1,0:T(8,128)}, u32[]{:S(2)}) copy-start(f32[1,16,512]{2,1,0:T(8,128)} %get-tuple-element.30) | copy-start | bytes 98308
  38.2 40.3 %copy-start.30 = (f32[1,16,512]{2,1,0:T(8,128)S(1)}, f32[1,16,512]{2,1,0:T(8,128)}, u32[]{:S(2)}) copy-start(f32[1,16,512]{2,1,0:T(8,128)} %get-tuple-element.38) | copy-start | bytes 98308
  38.3 40.3 %copy-start.31 = (f32[1,16,512]{2,1,0:T(8,128)S(1)}, f32[1,16,512]{2,1,0:T(8,128)}, u32[]{:S(2)}) copy-start(f32[1,16,512]{2,1,0:T(8,128)} %get-tuple-element.39) | copy-start | bytes 98308
  38.3 40.3 %copy-start.32 = (f32[1,16,512]{2,1,0:T(8,128)S(1)}, f32[1,16,512]{2,1,0:T(8,128)}, u32[]{:S(2)}) copy-start(f32[1,16,512]{2,1,0:T(8,128)} %get-tuple-element.31) | copy-start | bytes 98308
  38.3 40.3 %copy-start.33 = (f32[1,16,512]{2,1,0:T(8,128)S(1)}, f32[1,16,512]{2,1,0:T(8,128)}, u32[]{:S(2)}) copy-start(f32[1,16,512]{2,1,0:T(8,128)} %get-tuple-element.32) | copy-start | bytes 98308
  38.3 40.3 %copy-start.34 = (f32[1,16,512]{2,1,0:T(8,128)S(1)}, f32[1,16,512]{2,1,0:T(8,128)}, u32[]{:S(2)}) copy-start(f32[1,16,512]{2,1,0:T(8,128)} %get-tuple-element.34) | copy-start | bytes 98308
  38.3 40.3 %copy-start.35 = (f32[1,16,512]{2,1,0:T(8,128)S(1)}, f32[1,16,512]{2,1,0:T(8,128)}, u32[]{:S(2)}) copy-start(f32[1,16,512]{2,1,0:T(8,128)} %get-tuple-element.35) | copy-start | bytes 98308
  38.3 40.4 %copy-start.12 = (f32[16,512]{1,0:T(8,128)S(1)}, f32[16,512]{1,0:T(8,128)}, u32[]{:S(2)}) copy-start(f32[16,512]{1,0:T(8,128)} %copy-done.10) | copy-start | bytes 98308
  38.4 41.1 %copy-start.7 = (f32[32,16,128]{2,1,0:T(8,128)S(1)}, f32[32,16,128]{2,1,0:T(8,128)}, u32[]{:S(2)}) copy-start(f32[32,16,128]{2,1,0:T(8,128)} %rev.7) | copy-start | bytes 786436
  38.4 41.1 %copy-start.26 = (f32[32,16]{1,0:T(8,128)S(1)}, f32[32,16]{1,0:T(8,128)}, u32[]{:S(2)}) copy-start(f32[32,16]{1,0:T(8,128)} %copy.37) | copy-start | bytes 6148
  39.7 7.8 %collective-permute-start.3 = (f32[2,16,512]{2,1,0:T(8,128)S(1)}, f32[2,16,512]{2,1,0:T(8,128)S(1)}, u32[]{:S(2)}, u32[]{:S(2)}) collective-permute-start(f32[2,16,512]{2,1,0:T(8,128)S(1)} %fusion.153), channel_id=1, source_target_pairs={{0,32},{8,40},{16,48},{24,56},{32,0},{40,8},{48,16},{56,24},{1,33}... | collective-permute-start | bytes 196616 | tf_op jit(solution)/shard_map/ppermute | solution.py:85
  47.5 32.9 %copy-start.2 = (bf16[128,512]{1,0:T(8,128)(2,1)S(1)}, bf16[128,512]{1,0:T(8,128)(2,1)}, u32[]{:S(2)}) copy-start(bf16[128,512]{1,0:T(8,128)(2,1)} %copy-done.1) | copy-start | bytes 393220
  47.5 32.9 %copy-start.4 = (bf16[128,512]{1,0:T(8,128)(2,1)S(1)}, bf16[128,512]{1,0:T(8,128)(2,1)}, u32[]{:S(2)}) copy-start(bf16[128,512]{1,0:T(8,128)(2,1)} %copy-done.3) | copy-start | bytes 393220
  48.5 8.4 %collective-permute-start.5 = (f32[2,16,512]{2,1,0:T(8,128)S(1)}, f32[2,16,512]{2,1,0:T(8,128)S(1)}, u32[]{:S(2)}, u32[]{:S(2)}) collective-permute-start(f32[2,16,512]{2,1,0:T(8,128)S(1)} %get-tuple-element.57), channel_id=1, source_target_pairs={{0,64},{64,0},{128,192},{192,128},{256,320},{320,256},{384,448},{4... | collective-permute-start | bytes 196616 | tf_op jit(solution)/shard_map/ppermute | solution.py:85
  56.9 7.5 %collective-permute-start.6 = (f32[2,16,512]{2,1,0:T(8,128)S(1)}, f32[2,16,512]{2,1,0:T(8,128)S(1)}, u32[]{:S(2)}, u32[]{:S(2)}) collective-permute-start(f32[2,16,512]{2,1,0:T(8,128)S(1)} %fusion.157), channel_id=1, source_target_pairs={{0,128},{64,192},{128,0},{192,64},{256,384},{320,448},{384,256},{4... | collective-permute-start | bytes 196616 | tf_op jit(solution)/shard_map/ppermute | solution.py:85
  64.4 14.2 %collective-permute-start.7 = (f32[2,16,512]{2,1,0:T(8,128)S(1)}, f32[2,16,512]{2,1,0:T(8,128)S(1)}, u32[]{:S(2)}, u32[]{:S(2)}) collective-permute-start(f32[2,16,512]{2,1,0:T(8,128)S(1)} %fusion.158), channel_id=1, source_target_pairs={{0,256},{64,320},{128,384},{192,448},{256,0},{320,64},{384,128},{4... | collective-permute-start | bytes 196616 | tf_op jit(solution)/shard_map/ppermute | solution.py:85
  80.7 5.3 %copy-start.55 = (f32[1,1,512]{2,1,0:T(1,128)S(1)}, f32[1,1,512]{2,1,0:T(1,128)}, u32[]{:S(2)}) copy-start(f32[1,1,512]{2,1,0:T(1,128)} %copy-done.54) | copy-start | bytes 6148
  80.7 5.3 %copy-start.57 = (f32[1,1,512]{2,1,0:T(1,128)S(1)}, f32[1,1,512]{2,1,0:T(1,128)}, u32[]{:S(2)}) copy-start(f32[1,1,512]{2,1,0:T(1,128)} %copy-done.56) | copy-start | bytes 6148
  (41 other events, 138.7 us)

commit v12 on v11

--- a/solution.py
+++ b/solution.py
@@ -78,12 +78,12 @@
     return rounds
 
 
-def cube_scan(window, rounds, axis, size, held):
+def cube_scan(window, rounds, axis, size, held, hold_at=1):
     entering = jnp.zeros_like(window)
     shift = 1
     for keep, take, add in rounds:
         arrived = lax.ppermute(window, axis, [(source, source ^ shift) for source in range(size)])
-        if shift == 1:
+        if shift == hold_at:
             held, arrived = lax.optimization_barrier((held, arrived))
         entering = entering + add * arrived
         window = keep * window + take * arrived
@@ -142,7 +142,7 @@
     inner_rounds = cube_weights(factors, inner, member)
     outer_rounds = cube_weights(factors[len(inner_terms) :], outer, band)
     near, group, (rates, weights) = cube_scan(
-        jnp.stack([end_state, start_state]), inner_rounds, "xc", inner, (rates, weights)
+        jnp.stack([end_state, start_state]), inner_rounds, "xc", inner, (rates, weights), 2
     )
     edge = SHORT - 1
     head_rows = jnp.stack([q_short[:edge], k_short[:edge], v_short[:edge], grad_out[:edge]])

time: 87.9 us -> 80.5 us (0.916)
  the two profiles are of different devices: /device:TPU:18 before, /device:TPU:24 now
where the time goes in v12:
time: 80.5 us; the launch traced here: 79.5 us
  starting transfers between devices  33.3 us (41%)
  other arithmetic  14.3 us (18%)
  matrix products  11.7 us (15%)
  local copies, waits for them, and re-layouts  9.48 us (12%)
  waiting for transfers between devices  8.3 us (10%)
  between operations  2.46 us (3%)
    ppermute x6, starting transfers between devices, cube_scan(): lax.ppermute(window, axis, [(source, source ^ shift) for source in range(...  30.1 us
    ppermute x6, waiting for transfers between devices, cube_scan(): lax.ppermute(window, axis, [(source, source ^ shift) for source in range(...  8.29 us
    dot_general x1, matrix products, shards(): toeplitz = jnp.einsum('gtm,gms->gts', falling, rising, precision=precise)  4.28 us
    convert_element_type x12, other arithmetic, rounded(): return lax.optimization_barrier(values.astype(jnp.bfloat16))  3.74 us
    ppermute x2, starting transfers between devices, from_behind(): lax.ppermute(value, axis, [(source, source + steps) for source in range(l...  3.15 us
    dot_general x4, matrix products, split_dot(): jnp.einsum(spec, low, values, preferred_element_type=jnp.float32)  3.07 us
    dot_general x4, matrix products, split_dot(): jnp.einsum(spec, high.astype(jnp.bfloat16), values, preferred_element_typ...  2.52 us
    slice x2, local copies, waits for them, and re-layouts, short_causal(): filter_taps[offset] * padded[SHORT - 1 - offset:SHORT - 1 - offset + length]  1.97 us
  transfers between devices with their start and end apart: 8, of which 4 were waited for; matrix products, arithmetic and copies ran while one was open for 29% of the time, Pallas kernels for 0%

profile of v12, /device:TPU:24, one launch (start us, length us, event | category | flops | bytes accessed | tf_op | source)
XLA Modules:
  0.0 79.5 jit_solution(7253032976873577634)
XLA Ops:
  0.6 0.7 slice_bitcast_fusion.9
  1.4 0.7 slice_bitcast_fusion.7
  2.1 1.9 %collective-permute-start = (bf16[3,6,512]{2,1,0:T(8,128)(2,1)S(1)}, bf16[3,6,512]{2,1,0:T(8,128)(2,1)S(1)}, u32[]{:S(2)}, u32[]{:S(2)}) collective-permute-start(bf16[3,6,512]{2,1,0:T(8,128)(2,1)S(1)} %pad_maximum_fusion.8), channel_id=1, source_target_pairs={{0,8},{8,16},{16,24},{24,32},{32,40},{40,48},{48,56},{56,64},{64,7... | collective-permute-start | bytes 55304 | tf_op jit(solution)/shard_map/ppermute | solution.py:19
  4.0 1.2 %fusion.211 = (f32[1,1,512]{2,1,0:T(1,128)S(1)}, f32[1,1,512]{2,1,0:T(1,128)S(1)}, f32[1,1,512]{2,1,0:T(1,128)S(1)}, f32[1,1,512]{2,1,0:T(1,128)S(1)}, f32[1,1,5...) fusion(f32[3,7,512]{2,1,0:T(8,128)} %param.10), kind=kLoop, calls=%fused_computation.376 | loop fusion | bytes 77824 | tf_op jit(solution)/shard_map/slice | solution.py:32
  5.3 0.8 %fusion.212 = (f32[1,1,512]{2,1,0:T(1,128)S(1)}, f32[1,1,512]{2,1,0:T(1,128)S(1)}) fusion(f32[3,7,512]{2,1,0:T(8,128)} %param.10), kind=kLoop, calls=%fused_computation.377 | loop fusion | bytes 8192 | tf_op jit(solution)/shard_map/slice | solution.py:32
  6.2 0.7 fusion.215
  7.0 0.1 multiply_exponential_fusion.1
  7.1 0.1 fusion.210
  7.3 0.1 rev.6
  7.5 0.5 convert_add_fusion
  8.2 0.1 broadcast_in_dim.27
  8.4 0.2 reshape.198
  8.7 0.1 multiply_exponential_fusion.2
  8.9 0.2 multiply_exponential_fusion
  9.1 0.8 slice_select_fusion.6
  9.8 0.2 copy-done
  10.0 0.8 slice_select_fusion.7
  10.8 0.6 iota_compare_fusion.2
  11.5 0.8 %rev.7 = f32[32,16,128]{2,1,0:T(8,128)} reverse(f32[32,16,128]{2,1,0:T(8,128)S(1)} %get-tuple-element.46), dimensions={2} | reverse | bytes 524288 | tf_op jit(solution)/shard_map/rev | solution.py:163
  12.5 0.2 fusion.110
  12.8 0.2 fusion.93
  13.2 0.2 fusion.76
  13.5 0.3 fusion.216
  13.7 0.3 convolution_add_fusion.1
  14.0 0.3 fusion.217
  14.3 0.3 convolution_add_fusion
  14.6 0.3 multiply_reduce_fusion.1
  14.9 3.7 %collective-permute-start.1 = (f32[2,16,512]{2,1,0:T(8,128)S(1)}, f32[2,16,512]{2,1,0:T(8,128)S(1)}, u32[]{:S(2)}, u32[]{:S(2)}) collective-permute-start(f32[2,16,512]{2,1,0:T(8,128)S(1)} %pad_maximum_fusion.6), channel_id=1, source_target_pairs={{0,8},{8,0},{16,24},{24,16},{32,40},{40,32},{48,56},{56,48},{1,9},... | collective-permute-start | bytes 196616 | tf_op jit(solution)/shard_map/ppermute | solution.py:85
  18.6 0.1 copy.42
  18.7 0.8 copy.35
  19.5 3.4 %collective-permute-start.2 = (f32[2,16,512]{2,1,0:T(8,128)S(1)}, f32[2,16,512]{2,1,0:T(8,128)S(1)}, u32[]{:S(2)}, u32[]{:S(2)}) collective-permute-start(f32[2,16,512]{2,1,0:T(8,128)S(1)} %fusion.150), channel_id=1, source_target_pairs={{0,16},{8,24},{16,0},{24,8},{32,48},{40,56},{48,32},{56,40},{1,17}... | collective-permute-start | bytes 196616 | tf_op jit(solution)/shard_map/ppermute | solution.py:85
  22.9 0.6 pad_maximum_fusion.7
  23.6 1.3 %collective-permute-start.4 = (bf16[4,6,512]{2,1,0:T(8,128)(2,1)}, bf16[4,6,512]{2,1,0:T(8,128)(2,1)}, u32[]{:S(2)}, u32[]{:S(2)}) collective-permute-start(bf16[4,6,512]{2,1,0:T(8,128)(2,1)} %pad_maximum_fusion.7), channel_id=1, source_target_pairs={{8,0},{16,8},{24,16},{32,24},{40,32},{48,40},{56,48},{64,56},{72,6... | collective-permute-start | bytes 73736 | tf_op jit(solution)/shard_map/ppermute | solution.py:19
  24.9 0.9 %collective-permute-done.2 = f32[2,16,512]{2,1,0:T(8,128)S(1)} collective-permute-done((f32[2,16,512]{2,1,0:T(8,128)S(1)}, f32[2,16,512]{2,1,0:T(8,128)S(1)}, u32[]{:S(2)}, u32[]{:S(2)}) %collective-permute-start.2) | collective-permute-done | bytes 65568 | tf_op jit(solution)/shard_map/ppermute | solution.py:85
  25.8 0.6 copy-done.24
  26.5 4.3 %fusion.131 = f32[32,128,128]{2,1,0:T(8,128)S(1)} fusion(f32[32,16]{1,0:T(8,128)S(1)} %copy.38, f32[128]{0:T(128)} %get-tuple-element.103, f32[128]{0:T(128)} %get-tuple-element.104, f32[32,16]{1,0:T(8,128)S(1)} %copy.37), kind=kOutput, calls=%fused_computation.208 | convolution fusion | flops 100859904 | bytes 2102272 | tf_op jit(solution)/shard_map/gtm,gms->gts/dot_general | solution.py:157
  30.9 0.4 fusion.11
  31.3 1.1 %convolution_add_fusion.2 = f32[32,16,128]{2,1,0:T(8,128)} fusion(f32[32,16,128]{2,1,0:T(8,128)S(1)} %fusion.11, bf16[128,32,16]{0,2,1:T(8,128)(2,1)S(1)} %bitcast.147, f32[32,128,128]{2,1,0:T(8,128)S(1)} %fusion.131, pred[128,128]{1,0:T(8,128)(4,1)S(1)} %iota_compare_fusion.1), kind=kOutput, calls=%fused_computation.7 | convolution fusion | flops 18939904 | bytes 2768896 | tf_op jit(solution)/shard_map/gts,tgc->sgc/dot_general | solution.py:50
  32.5 0.6 fusion.153
  33.1 4.7 %collective-permute-start.3 = (f32[2,16,512]{2,1,0:T(8,128)}, f32[2,16,512]{2,1,0:T(8,128)}, u32[]{:S(2)}, u32[]{:S(2)}) collective-permute-start(f32[2,16,512]{2,1,0:T(8,128)} %fusion.153), channel_id=1, source_target_pairs={{0,32},{8,40},{16,48},{24,56},{32,0},{40,8},{48,16},{56,24},{1,33}... | collective-permute-start | bytes 196616 | tf_op jit(solution)/shard_map/ppermute | solution.py:85
  37.8 0.1 broadcast_in_dim.29
  38.0 0.8 mul.898
  38.7 1.6 %fusion.12 = f32[32,16,128]{2,1,0:T(8,128)S(1)} fusion(bf16[128,32,16]{0,2,1:T(8,128)(2,1)} %bitcast.144, f32[32,128,128]{2,1,0:T(8,128)S(1)} %fusion.131, pred[128,128]{1,0:T(8,128)(4,1)S(1)} %iota_compare_fusion.1), kind=kOutput, calls=%fused_computation.65 | convolution fusion | flops 18350080 | bytes 2506752 | tf_op jit(solution)/shard_map/gts,sgc->tgc/dot_general | solution.py:49
  40.5 1.4 %convolution_add_fusion.3 = f32[32,16,128]{2,1,0:T(8,128)} fusion(f32[32,16,128]{2,1,0:T(8,128)S(1)} %fusion.12, bf16[128,32,16]{0,2,1:T(8,128)(2,1)S(1)} %bitcast.145, f32[32,128,128]{2,1,0:T(8,128)S(1)} %fusion.131, pred[128,128]{1,0:T(8,128)(4,1)S(1)} %iota_compare_fusion.1), kind=kOutput, calls=%fused_computation.8 | convolution fusion | flops 18939904 | bytes 2768896 | tf_op jit(solution)/shard_map/gts,sgc->tgc/dot_general | solution.py:50
  42.3 1.0 %fusion.152 = (f32[2,16,512]{2,1,0:T(8,128)S(1)}, f32[2,16,512]{2,1,0:T(8,128)S(1)}) fusion(f32[2,16,512]{2,1,0:T(8,128)S(1)} %copy-done.13, f32[1,16,512]{2,1,0:T(8,128)S(1)} %copy-done.39, f32[1,16,512]{2,1,0:T(8,128)S(1)} %copy-done.40, f32[2,16,512]{2,1,0:T(8,128)S(1)} %copy-done.26, f32[1,16,512]{2,1,0:T(8,128)S(1)} %copy-done.37, ...), kind=kLoop, calls=%fused_computation.235 | loop fusion | flops 212992 | bytes 655360 | tf_op jit(solution)/shard_map/add | solution.py:88
  43.2 3.8 %collective-permute-start.5 = (f32[2,16,512]{2,1,0:T(8,128)S(1)}, f32[2,16,512]{2,1,0:T(8,128)S(1)}, u32[]{:S(2)}, u32[]{:S(2)}) collective-permute-start(f32[2,16,512]{2,1,0:T(8,128)S(1)} %get-tuple-element.57), channel_id=1, source_target_pairs={{0,64},{64,0},{128,192},{192,128},{256,320},{320,256},{384,448},{4... | collective-permute-start | bytes 196616 | tf_op jit(solution)/shard_map/ppermute | solution.py:85
  47.1 2.4 %collective-permute-done.5 = f32[2,16,512]{2,1,0:T(8,128)S(1)} collective-permute-done((f32[2,16,512]{2,1,0:T(8,128)S(1)}, f32[2,16,512]{2,1,0:T(8,128)S(1)}, u32[]{:S(2)}, u32[]{:S(2)}) %collective-permute-start.5) | collective-permute-done | bytes 65568 | tf_op jit(solution)/shard_map/ppermute | solution.py:85
  49.6 6.4 %collective-permute-start.6 = (f32[2,16,512]{2,1,0:T(8,128)S(1)}, f32[2,16,512]{2,1,0:T(8,128)S(1)}, u32[]{:S(2)}, u32[]{:S(2)}) collective-permute-start(f32[2,16,512]{2,1,0:T(8,128)S(1)} %fusion.157), channel_id=1, source_target_pairs={{0,128},{64,192},{128,0},{192,64},{256,384},{320,448},{384,256},{4... | collective-permute-start | bytes 196616 | tf_op jit(solution)/shard_map/ppermute | solution.py:85
  56.0 0.2 reshape.204
  56.1 1.1 %copy.43 = f32[128,512]{1,0:T(8,128)S(1)} copy(f32[128,512]{0,1:T(8,128)} %bitcast.148) | data formatting | bytes 524288 | tf_op jit(solution)/shard_map/reshape | solution.py:161
  57.2 0.1 copy.41
  57.4 1.2 %collective-permute-done.6 = f32[2,16,512]{2,1,0:T(8,128)S(1)} collective-permute-done((f32[2,16,512]{2,1,0:T(8,128)S(1)}, f32[2,16,512]{2,1,0:T(8,128)S(1)}, u32[]{:S(2)}, u32[]{:S(2)}) %collective-permute-start.6) | collective-permute-done | bytes 65568 | tf_op jit(solution)/shard_map/ppermute | solution.py:85
  58.6 8.1 %collective-permute-start.7 = (f32[2,16,512]{2,1,0:T(8,128)S(1)}, f32[2,16,512]{2,1,0:T(8,128)S(1)}, u32[]{:S(2)}, u32[]{:S(2)}) collective-permute-start(f32[2,16,512]{2,1,0:T(8,128)S(1)} %fusion.158), channel_id=1, source_target_pairs={{0,256},{64,320},{128,384},{192,448},{256,0},{320,64},{384,128},{4... | collective-permute-start | bytes 196616 | tf_op jit(solution)/shard_map/ppermute | solution.py:85
  66.7 0.7 fusion.166
  67.5 3.7 %collective-permute-done.7 = f32[2,16,512]{2,1,0:T(8,128)S(1)} collective-permute-done((f32[2,16,512]{2,1,0:T(8,128)S(1)}, f32[2,16,512]{2,1,0:T(8,128)S(1)}, u32[]{:S(2)}, u32[]{:S(2)}) %collective-permute-start.7) | collective-permute-done | bytes 65568 | tf_op jit(solution)/shard_map/ppermute | solution.py:85
  71.3 0.9 %fusion.163 = (f32[16,512]{1,0:T(8,128)S(1)}, f32[16,512]{1,0:T(8,128)S(1)}, f32[16,512]{1,0:T(8,128)S(1)}, f32[16,512]{1,0:T(8,128)S(1)}) fusion(f32[1,16,512]{2,1,0:T(8,128)S(1)} %reshape.204, f32[21,16,512]{2,1,0:T(8,128)} %copy-done, f32[16,512]{1,0:T(8,128)S(1)} %copy-done.10, f32[2,16,512]{2,1,0:T(8,128)S(1)} %fusion.155, ...), kind=kLoop, calls=%fused_computation.273 | loop fusion | flops 65536 | bytes 425984 | tf_op jit(solution)/shard_map/mul | solution.py:185
  72.2 0.9 %fusion.3 = bf16[128,512]{1,0:T(8,128)(2,1)S(1)} fusion(f32[128,512]{1,0:T(8,128)S(1)} %copy.43, f32[16,512]{1,0:T(8,128)S(1)} %get-tuple-element.22, f32[32,512]{1,0:T(8,128)S(1)} %fusion.159, f32[32,16,128]{2,1,0:T(8,128)S(1)} %copy-done.6, f32[32,16]{1,0:T(8,128)S(1)} %copy-done.23), kind=kOutput, calls=%fused_computation.11 | convolution fusion | flops 403111936 | bytes 755712 | tf_op jit(solution)/shard_map/ks,kc->sc/dot_general | solution.py:167
  73.5 0.7 fusion.169
  74.3 0.7 fusion.165
  75.0 0.9 %fusion.4 = bf16[128,512]{1,0:T(8,128)(2,1)S(1)} fusion(f32[128,512]{1,0:T(8,128)S(1)} %copy.41, f32[16,512]{1,0:T(8,128)S(1)} %get-tuple-element.23, f32[32,512]{1,0:T(8,128)S(1)} %fusion.159, f32[32,16]{1,0:T(8,128)S(1)} %copy-done.23, f32[32,16,129]{2,1,0:T(8,128)S(1)} %multiply_exponential_fusion.1), kind=kOutput, calls=%fused_computation.12 | convolution fusion | flops 403111936 | bytes 770048 | tf_op jit(solution)/shard_map/kt,kc->tc/dot_general | solution.py:166
  75.9 0.7 fusion.16
  76.7 0.9 %fusion.25 = bf16[128,512]{1,0:T(8,128)(2,1)} fusion(f32[6,512]{1,0:T(8,128)S(1)} %convert_element_type.313, f32[128,512]{1,0:T(8,128)S(1)} %convert_element_type.311, f32[512]{0:T(512)S(1)} %bitcast.199, f32[512]{0:T(512)S(1)} %bitcast.197, f32[512]{0:T(512)S(1)} %bitcast.187, f32[512]{0:T(512)S(1)} %bitcast.189, f32[512]{0:T(512)S(1)} %bitcast.191, ...), kind=kLoop, calls=%fused_computation.78 | loop fusion | flops 1310720 | bytes 419840 | tf_op jit(solution)/shard_map/convert_element_type | solution.py:203
  77.7 0.9 %fusion.42 = bf16[128,512]{1,0:T(8,128)(2,1)} fusion(f32[6,512]{1,0:T(8,128)S(1)} %convert_element_type.308, f32[128,512]{1,0:T(8,128)S(1)} %convert_element_type.300, f32[512]{0:T(512)S(1)} %bitcast.173, f32[512]{0:T(512)S(1)} %bitcast.175, f32[512]{0:T(512)S(1)} %bitcast.177, f32[512]{0:T(512)S(1)} %bitcast.179, f32[512]{0:T(512)S(1)} %bitcast.181, ...), kind=kLoop, calls=%fused_computation.95 | loop fusion | flops 1310720 | bytes 419840 | tf_op jit(solution)/shard_map/convert_element_type | solution.py:202
  78.6 0.9 %fusion.59 = bf16[128,512]{1,0:T(8,128)(2,1)} fusion(f32[6,512]{1,0:T(8,128)S(1)} %convert_element_type.295, f32[128,512]{1,0:T(8,128)S(1)} %convert_element_type.282, f32[512]{0:T(512)S(1)} %bitcast.161, f32[512]{0:T(512)S(1)} %bitcast.163, f32[512]{0:T(512)S(1)} %bitcast.165, f32[512]{0:T(512)S(1)} %bitcast.167, f32[512]{0:T(512)S(1)} %bitcast.169, ...), kind=kLoop, calls=%fused_computation.112 | loop fusion | flops 1310720 | bytes 419840 | tf_op jit(solution)/shard_map/convert_element_type | solution.py:201
  (242 shorter events, 1.7 us)
Async XLA Ops:
  0.6 7.6 %copy-start.51 = (f32[32,16]{0,1:T(8,128)S(1)}, f32[32,16]{0,1:T(8,128)}, u32[]{:S(2)}) copy-start(f32[32,16]{0,1:T(8,128)} %param.11) | copy-start | bytes 6148
  2.1 6.5 %copy-start.14 = (bf16[128,512]{1,0:T(8,128)(2,1)S(1)}, bf16[128,512]{1,0:T(8,128)(2,1)}, u32[]{:S(2)}) copy-start(bf16[128,512]{1,0:T(8,128)(2,1)} %param.13) | copy-start | bytes 393220
  2.1 10.3 %collective-permute-start = (bf16[3,6,512]{2,1,0:T(8,128)(2,1)S(1)}, bf16[3,6,512]{2,1,0:T(8,128)(2,1)S(1)}, u32[]{:S(2)}, u32[]{:S(2)}) collective-permute-start(bf16[3,6,512]{2,1,0:T(8,128)(2,1)S(1)} %pad_maximum_fusion.8), channel_id=1, source_target_pairs={{0,8},{8,16},{16,24},{24,32},{32,40},{40,48},{48,56},{56,64},{64,7... | collective-permute-start | bytes 55304 | tf_op jit(solution)/shard_map/ppermute | solution.py:19
  5.2 7.2 %copy-start.54 = (f32[1,1,512]{2,1,0:T(1,128)}, f32[1,1,512]{2,1,0:T(1,128)S(1)}, u32[]{:S(2)}) copy-start(f32[1,1,512]{2,1,0:T(1,128)S(1)} %get-tuple-element.58) | copy-start | bytes 6148
  5.2 7.2 %copy-start.56 = (f32[1,1,512]{2,1,0:T(1,128)}, f32[1,1,512]{2,1,0:T(1,128)S(1)}, u32[]{:S(2)}) copy-start(f32[1,1,512]{2,1,0:T(1,128)S(1)} %get-tuple-element.71) | copy-start | bytes 6148
  5.2 7.2 %copy-start.58 = (f32[1,1,512]{2,1,0:T(1,128)}, f32[1,1,512]{2,1,0:T(1,128)S(1)}, u32[]{:S(2)}) copy-start(f32[1,1,512]{2,1,0:T(1,128)S(1)} %get-tuple-element.72) | copy-start | bytes 6148
  5.2 7.2 %copy-start.60 = (f32[1,1,512]{2,1,0:T(1,128)}, f32[1,1,512]{2,1,0:T(1,128)S(1)}, u32[]{:S(2)}) copy-start(f32[1,1,512]{2,1,0:T(1,128)S(1)} %get-tuple-element.73) | copy-start | bytes 6148
  5.2 7.2 %copy-start.62 = (f32[1,1,512]{2,1,0:T(1,128)}, f32[1,1,512]{2,1,0:T(1,128)S(1)}, u32[]{:S(2)}) copy-start(f32[1,1,512]{2,1,0:T(1,128)S(1)} %get-tuple-element.74) | copy-start | bytes 6148
  5.2 7.2 %copy-start.64 = (f32[1,1,512]{2,1,0:T(1,128)}, f32[1,1,512]{2,1,0:T(1,128)S(1)}, u32[]{:S(2)}) copy-start(f32[1,1,512]{2,1,0:T(1,128)S(1)} %get-tuple-element.75) | copy-start | bytes 6148
  5.2 7.2 %copy-start.66 = (f32[1,1,512]{2,1,0:T(1,128)}, f32[1,1,512]{2,1,0:T(1,128)S(1)}, u32[]{:S(2)}) copy-start(f32[1,1,512]{2,1,0:T(1,128)S(1)} %get-tuple-element.76) | copy-start | bytes 6148
  5.2 7.5 %copy-start.68 = (f32[1,1,512]{2,1,0:T(1,128)}, f32[1,1,512]{2,1,0:T(1,128)S(1)}, u32[]{:S(2)}) copy-start(f32[1,1,512]{2,1,0:T(1,128)S(1)} %get-tuple-element.64) | copy-start | bytes 6148
  5.2 7.5 %copy-start.70 = (f32[1,1,512]{2,1,0:T(1,128)}, f32[1,1,512]{2,1,0:T(1,128)S(1)}, u32[]{:S(2)}) copy-start(f32[1,1,512]{2,1,0:T(1,128)S(1)} %get-tuple-element.65) | copy-start | bytes 6148
  5.2 7.5 %copy-start.72 = (f32[1,1,512]{2,1,0:T(1,128)}, f32[1,1,512]{2,1,0:T(1,128)S(1)}, u32[]{:S(2)}) copy-start(f32[1,1,512]{2,1,0:T(1,128)S(1)} %get-tuple-element.66) | copy-start | bytes 6148
  5.3 7.5 %copy-start.74 = (f32[1,1,512]{2,1,0:T(1,128)}, f32[1,1,512]{2,1,0:T(1,128)S(1)}, u32[]{:S(2)}) copy-start(f32[1,1,512]{2,1,0:T(1,128)S(1)} %get-tuple-element.67) | copy-start | bytes 6148
  5.3 7.5 %copy-start.76 = (f32[1,1,512]{2,1,0:T(1,128)}, f32[1,1,512]{2,1,0:T(1,128)S(1)}, u32[]{:S(2)}) copy-start(f32[1,1,512]{2,1,0:T(1,128)S(1)} %get-tuple-element.68) | copy-start | bytes 6148
  5.3 7.5 %copy-start.78 = (f32[1,1,512]{2,1,0:T(1,128)}, f32[1,1,512]{2,1,0:T(1,128)S(1)}, u32[]{:S(2)}) copy-start(f32[1,1,512]{2,1,0:T(1,128)S(1)} %get-tuple-element.69) | copy-start | bytes 6148
  5.3 7.5 %copy-start.80 = (f32[1,1,512]{2,1,0:T(1,128)}, f32[1,1,512]{2,1,0:T(1,128)S(1)}, u32[]{:S(2)}) copy-start(f32[1,1,512]{2,1,0:T(1,128)S(1)} %get-tuple-element.70) | copy-start | bytes 6148
  5.3 7.8 %copy-start.82 = (f32[1,1,512]{2,1,0:T(1,128)}, f32[1,1,512]{2,1,0:T(1,128)S(1)}, u32[]{:S(2)}) copy-start(f32[1,1,512]{2,1,0:T(1,128)S(1)} %get-tuple-element.59) | copy-start | bytes 6148
  5.3 7.8 %copy-start.84 = (f32[1,1,512]{2,1,0:T(1,128)}, f32[1,1,512]{2,1,0:T(1,128)S(1)}, u32[]{:S(2)}) copy-start(f32[1,1,512]{2,1,0:T(1,128)S(1)} %get-tuple-element.60) | copy-start | bytes 6148
  5.3 7.8 %copy-start.86 = (f32[1,1,512]{2,1,0:T(1,128)}, f32[1,1,512]{2,1,0:T(1,128)S(1)}, u32[]{:S(2)}) copy-start(f32[1,1,512]{2,1,0:T(1,128)S(1)} %get-tuple-element.61) | copy-start | bytes 6148
  5.3 7.8 %copy-start.88 = (f32[1,1,512]{2,1,0:T(1,128)}, f32[1,1,512]{2,1,0:T(1,128)S(1)}, u32[]{:S(2)}) copy-start(f32[1,1,512]{2,1,0:T(1,128)S(1)} %get-tuple-element.62) | copy-start | bytes 6148
  5.3 7.8 %copy-start.90 = (f32[1,1,512]{2,1,0:T(1,128)}, f32[1,1,512]{2,1,0:T(1,128)S(1)}, u32[]{:S(2)}) copy-start(f32[1,1,512]{2,1,0:T(1,128)S(1)} %get-tuple-element.63) | copy-start | bytes 6148
  6.1 7.0 %copy-start.92 = (f32[1,1,512]{2,1,0:T(1,128)}, f32[1,1,512]{2,1,0:T(1,128)S(1)}, u32[]{:S(2)}) copy-start(f32[1,1,512]{2,1,0:T(1,128)S(1)} %get-tuple-element.77) | copy-start | bytes 6148
  6.1 7.0 %copy-start.94 = (f32[1,1,512]{2,1,0:T(1,128)}, f32[1,1,512]{2,1,0:T(1,128)S(1)}, u32[]{:S(2)}) copy-start(f32[1,1,512]{2,1,0:T(1,128)S(1)} %get-tuple-element.78) | copy-start | bytes 6148
  6.9 19.5 %copy-start.52 = (f32[32,16]{0,1:T(8,128)}, f32[32,16]{0,1:T(8,128)S(1)}, u32[]{:S(2)}) copy-start(f32[32,16]{0,1:T(8,128)S(1)} %get-tuple-element.9) | copy-start | bytes 6148
  10.0 9.5 %copy-start.18 = (f32[1,16,512]{2,1,0:T(8,128)}, f32[1,16,512]{2,1,0:T(8,128)S(1)}, u32[]{:S(2)}) copy-start(f32[1,16,512]{2,1,0:T(8,128)S(1)} %get-tuple-element.45) | copy-start | bytes 98308
  10.8 8.7 %copy-start.20 = (f32[1,16,512]{2,1,0:T(8,128)}, f32[1,16,512]{2,1,0:T(8,128)S(1)}, u32[]{:S(2)}) copy-start(f32[1,16,512]{2,1,0:T(8,128)S(1)} %get-tuple-element.25) | copy-start | bytes 98308
  13.4 5.2 %copy-start.3 = (bf16[128,512]{1,0:T(8,128)(2,1)}, bf16[128,512]{1,0:T(8,128)(2,1)S(1)}, u32[]{:S(2)}) copy-start(bf16[128,512]{1,0:T(8,128)(2,1)S(1)} %fusion.76) | copy-start | bytes 393220
  14.9 11.7 %copy-start.8 = (f32[16,512]{1,0:T(8,128)}, f32[16,512]{1,0:T(8,128)S(1)}, u32[]{:S(2)}) copy-start(f32[16,512]{1,0:T(8,128)S(1)} %get-tuple-element.18) | copy-start | bytes 98308
  14.9 11.7 %copy-start.16 = (f32[16,512]{1,0:T(8,128)}, f32[16,512]{1,0:T(8,128)S(1)}, u32[]{:S(2)}) copy-start(f32[16,512]{1,0:T(8,128)S(1)} %get-tuple-element.19) | copy-start | bytes 98308
  14.9 4.6 %collective-permute-start.1 = (f32[2,16,512]{2,1,0:T(8,128)S(1)}, f32[2,16,512]{2,1,0:T(8,128)S(1)}, u32[]{:S(2)}, u32[]{:S(2)}) collective-permute-start(f32[2,16,512]{2,1,0:T(8,128)S(1)} %pad_maximum_fusion.6), channel_id=1, source_target_pairs={{0,8},{8,0},{16,24},{24,16},{32,40},{40,32},{48,56},{56,48},{1,9},... | collective-permute-start | bytes 196616 | tf_op jit(solution)/shard_map/ppermute | solution.py:85
  19.5 7.0 %copy-start.11 = (f32[2,16,512]{2,1,0:T(8,128)}, f32[2,16,512]{2,1,0:T(8,128)S(1)}, u32[]{:S(2)}) copy-start(f32[2,16,512]{2,1,0:T(8,128)S(1)} %collective-permute-done.1) | copy-start | bytes 196612
  19.5 6.2 %collective-permute-start.2 = (f32[2,16,512]{2,1,0:T(8,128)S(1)}, f32[2,16,512]{2,1,0:T(8,128)S(1)}, u32[]{:S(2)}, u32[]{:S(2)}) collective-permute-start(f32[2,16,512]{2,1,0:T(8,128)S(1)} %fusion.150), channel_id=1, source_target_pairs={{0,16},{8,24},{16,0},{24,8},{32,48},{40,56},{48,32},{56,40},{1,17}... | collective-permute-start | bytes 196616 | tf_op jit(solution)/shard_map/ppermute | solution.py:85
  23.6 23.5 %collective-permute-start.4 = (bf16[4,6,512]{2,1,0:T(8,128)(2,1)}, bf16[4,6,512]{2,1,0:T(8,128)(2,1)}, u32[]{:S(2)}, u32[]{:S(2)}) collective-permute-start(bf16[4,6,512]{2,1,0:T(8,128)(2,1)} %pad_maximum_fusion.7), channel_id=1, source_target_pairs={{8,0},{16,8},{24,16},{32,24},{40,32},{48,40},{56,48},{64,56},{72,6... | collective-permute-start | bytes 73736 | tf_op jit(solution)/shard_map/ppermute | solution.py:19
  31.3 6.5 %copy-start.53 = (f32[32,16]{0,1:T(8,128)S(1)}, f32[32,16]{0,1:T(8,128)}, u32[]{:S(2)}) copy-start(f32[32,16]{0,1:T(8,128)} %copy-done.52) | copy-start | bytes 6148
  33.1 9.1 %collective-permute-start.3 = (f32[2,16,512]{2,1,0:T(8,128)}, f32[2,16,512]{2,1,0:T(8,128)}, u32[]{:S(2)}, u32[]{:S(2)}) collective-permute-start(f32[2,16,512]{2,1,0:T(8,128)} %fusion.153), channel_id=1, source_target_pairs={{0,32},{8,40},{16,48},{24,56},{32,0},{40,8},{48,16},{56,24},{1,33}... | collective-permute-start | bytes 196616 | tf_op jit(solution)/shard_map/ppermute | solution.py:85
  40.5 9.1 %copy-start.49 = (f32[1,16,512]{2,1,0:T(8,128)S(1)}, f32[1,16,512]{2,1,0:T(8,128)}, u32[]{:S(2)}) copy-start(f32[1,16,512]{2,1,0:T(8,128)} %get-tuple-element.28) | copy-start | bytes 98308
  40.5 9.1 %copy-start.50 = (f32[1,16,512]{2,1,0:T(8,128)S(1)}, f32[1,16,512]{2,1,0:T(8,128)}, u32[]{:S(2)}) copy-start(f32[1,16,512]{2,1,0:T(8,128)} %get-tuple-element.33) | copy-start | bytes 98308
  41.9 15.3 %copy-start.7 = (f32[32,16,128]{2,1,0:T(8,128)S(1)}, f32[32,16,128]{2,1,0:T(8,128)}, u32[]{:S(2)}) copy-start(f32[32,16,128]{2,1,0:T(8,128)} %convolution_add_fusion.3) | copy-start | bytes 786436
  41.9 16.7 %copy-start.47 = (f32[1,16,512]{2,1,0:T(8,128)S(1)}, f32[1,16,512]{2,1,0:T(8,128)}, u32[]{:S(2)}) copy-start(f32[1,16,512]{2,1,0:T(8,128)} %get-tuple-element.29) | copy-start | bytes 98308
  41.9 16.7 %copy-start.48 = (f32[1,16,512]{2,1,0:T(8,128)S(1)}, f32[1,16,512]{2,1,0:T(8,128)}, u32[]{:S(2)}) copy-start(f32[1,16,512]{2,1,0:T(8,128)} %get-tuple-element.30) | copy-start | bytes 98308
  41.9 29.3 %copy-start.30 = (f32[1,16,512]{2,1,0:T(8,128)S(1)}, f32[1,16,512]{2,1,0:T(8,128)}, u32[]{:S(2)}) copy-start(f32[1,16,512]{2,1,0:T(8,128)} %get-tuple-element.38) | copy-start | bytes 98308
  41.9 29.3 %copy-start.31 = (f32[1,16,512]{2,1,0:T(8,128)S(1)}, f32[1,16,512]{2,1,0:T(8,128)}, u32[]{:S(2)}) copy-start(f32[1,16,512]{2,1,0:T(8,128)} %get-tuple-element.39) | copy-start | bytes 98308
  41.9 29.3 %copy-start.32 = (f32[1,16,512]{2,1,0:T(8,128)S(1)}, f32[1,16,512]{2,1,0:T(8,128)}, u32[]{:S(2)}) copy-start(f32[1,16,512]{2,1,0:T(8,128)} %get-tuple-element.31) | copy-start | bytes 98308
  41.9 29.3 %copy-start.33 = (f32[1,16,512]{2,1,0:T(8,128)S(1)}, f32[1,16,512]{2,1,0:T(8,128)}, u32[]{:S(2)}) copy-start(f32[1,16,512]{2,1,0:T(8,128)} %get-tuple-element.32) | copy-start | bytes 98308
  41.9 29.3 %copy-start.34 = (f32[1,16,512]{2,1,0:T(8,128)S(1)}, f32[1,16,512]{2,1,0:T(8,128)}, u32[]{:S(2)}) copy-start(f32[1,16,512]{2,1,0:T(8,128)} %get-tuple-element.34) | copy-start | bytes 98308
  41.9 29.3 %copy-start.35 = (f32[1,16,512]{2,1,0:T(8,128)S(1)}, f32[1,16,512]{2,1,0:T(8,128)}, u32[]{:S(2)}) copy-start(f32[1,16,512]{2,1,0:T(8,128)} %get-tuple-element.35) | copy-start | bytes 98308
  42.0 29.3 %copy-start.10 = (f32[16,512]{1,0:T(8,128)S(1)}, f32[16,512]{1,0:T(8,128)}, u32[]{:S(2)}) copy-start(f32[16,512]{1,0:T(8,128)} %copy-done.8) | copy-start | bytes 98308
  42.0 30.2 %copy-start.6 = (f32[32,16,128]{2,1,0:T(8,128)S(1)}, f32[32,16,128]{2,1,0:T(8,128)}, u32[]{:S(2)}) copy-start(f32[32,16,128]{2,1,0:T(8,128)} %rev.7) | copy-start | bytes 786436
  42.0 30.2 %copy-start.23 = (f32[32,16]{1,0:T(8,128)S(1)}, f32[32,16]{1,0:T(8,128)}, u32[]{:S(2)}) copy-start(f32[32,16]{1,0:T(8,128)} %copy-done.22) | copy-start | bytes 6148
  42.3 30.8 %copy-start.2 = (bf16[128,512]{1,0:T(8,128)(2,1)S(1)}, bf16[128,512]{1,0:T(8,128)(2,1)}, u32[]{:S(2)}) copy-start(bf16[128,512]{1,0:T(8,128)(2,1)} %copy-done.1) | copy-start | bytes 393220
  42.3 30.8 %copy-start.4 = (bf16[128,512]{1,0:T(8,128)(2,1)S(1)}, bf16[128,512]{1,0:T(8,128)(2,1)}, u32[]{:S(2)}) copy-start(bf16[128,512]{1,0:T(8,128)(2,1)} %copy-done.3) | copy-start | bytes 393220
  43.2 6.3 %collective-permute-start.5 = (f32[2,16,512]{2,1,0:T(8,128)S(1)}, f32[2,16,512]{2,1,0:T(8,128)S(1)}, u32[]{:S(2)}, u32[]{:S(2)}) collective-permute-start(f32[2,16,512]{2,1,0:T(8,128)S(1)} %get-tuple-element.57), channel_id=1, source_target_pairs={{0,64},{64,0},{128,192},{192,128},{256,320},{320,256},{384,448},{4... | collective-permute-start | bytes 196616 | tf_op jit(solution)/shard_map/ppermute | solution.py:85
  49.6 9.0 %collective-permute-start.6 = (f32[2,16,512]{2,1,0:T(8,128)S(1)}, f32[2,16,512]{2,1,0:T(8,128)S(1)}, u32[]{:S(2)}, u32[]{:S(2)}) collective-permute-start(f32[2,16,512]{2,1,0:T(8,128)S(1)} %fusion.157), channel_id=1, source_target_pairs={{0,128},{64,192},{128,0},{192,64},{256,384},{320,448},{384,256},{4... | collective-permute-start | bytes 196616 | tf_op jit(solution)/shard_map/ppermute | solution.py:85
  58.6 12.6 %collective-permute-start.7 = (f32[2,16,512]{2,1,0:T(8,128)S(1)}, f32[2,16,512]{2,1,0:T(8,128)S(1)}, u32[]{:S(2)}, u32[]{:S(2)}) collective-permute-start(f32[2,16,512]{2,1,0:T(8,128)S(1)} %fusion.158), channel_id=1, source_target_pairs={{0,256},{64,320},{128,384},{192,448},{256,0},{320,64},{384,128},{4... | collective-permute-start | bytes 196616 | tf_op jit(solution)/shard_map/ppermute | solution.py:85
  71.3 4.7 %copy-start.15 = (bf16[128,512]{1,0:T(8,128)(2,1)S(1)}, bf16[128,512]{1,0:T(8,128)(2,1)}, u32[]{:S(2)}) copy-start(bf16[128,512]{1,0:T(8,128)(2,1)} %param.13) | copy-start | bytes 393220
  73.2 4.5 %copy-start.69 = (f32[1,1,512]{2,1,0:T(1,128)S(1)}, f32[1,1,512]{2,1,0:T(1,128)}, u32[]{:S(2)}) copy-start(f32[1,1,512]{2,1,0:T(1,128)} %copy-done.68) | copy-start | bytes 6148
  73.3 5.3 %copy-start.55 = (f32[1,1,512]{2,1,0:T(1,128)S(1)}, f32[1,1,512]{2,1,0:T(1,128)}, u32[]{:S(2)}) copy-start(f32[1,1,512]{2,1,0:T(1,128)} %copy-done.54) | copy-start | bytes 6148
  73.3 5.3 %copy-start.57 = (f32[1,1,512]{2,1,0:T(1,128)S(1)}, f32[1,1,512]{2,1,0:T(1,128)}, u32[]{:S(2)}) copy-start(f32[1,1,512]{2,1,0:T(1,128)} %copy-done.56) | copy-start | bytes 6148
  73.3 5.3 %copy-start.59 = (f32[1,1,512]{2,1,0:T(1,128)S(1)}, f32[1,1,512]{2,1,0:T(1,128)}, u32[]{:S(2)}) copy-start(f32[1,1,512]{2,1,0:T(1,128)} %copy-done.58) | copy-start | bytes 6148
  73.3 5.3 %copy-start.61 = (f32[1,1,512]{2,1,0:T(1,128)S(1)}, f32[1,1,512]{2,1,0:T(1,128)}, u32[]{:S(2)}) copy-start(f32[1,1,512]{2,1,0:T(1,128)} %copy-done.60) | copy-start | bytes 6148
  73.3 5.3 %copy-start.63 = (f32[1,1,512]{2,1,0:T(1,128)S(1)}, f32[1,1,512]{2,1,0:T(1,128)}, u32[]{:S(2)}) copy-start(f32[1,1,512]{2,1,0:T(1,128)} %copy-done.62) | copy-start | bytes 6148
  73.3 5.3 %copy-start.65 = (f32[1,1,512]{2,1,0:T(1,128)S(1)}, f32[1,1,512]{2,1,0:T(1,128)}, u32[]{:S(2)}) copy-start(f32[1,1,512]{2,1,0:T(1,128)} %copy-done.64) | copy-start | bytes 6148
  73.3 5.3 %copy-start.67 = (f32[1,1,512]{2,1,0:T(1,128)S(1)}, f32[1,1,512]{2,1,0:T(1,128)}, u32[]{:S(2)}) copy-start(f32[1,1,512]{2,1,0:T(1,128)} %copy-done.66) | copy-start | bytes 6148
  (41 other events, 106.5 us)

commit v13 on v7

--- a/solution.py
+++ b/solution.py
@@ -78,12 +78,12 @@
     return rounds
 
 
-def cube_scan(window, rounds, axis, size, held):
+def cube_scan(window, rounds, axis, size, held, hold_at=1):
     entering = jnp.zeros_like(window)
     shift = 1
     for keep, take, add in rounds:
         arrived = lax.ppermute(window, axis, [(source, source ^ shift) for source in range(size)])
-        if shift == 1:
+        if shift == hold_at:
             held, arrived = lax.optimization_barrier((held, arrived))
         entering = entering + add * arrived
         window = keep * window + take * arrived
@@ -142,7 +142,7 @@
     inner_rounds = cube_weights(factors, inner, member)
     outer_rounds = cube_weights(factors[len(inner_terms) :], outer, band)
     near, group, (rates, weights) = cube_scan(
-        jnp.stack([end_state, start_state]), inner_rounds, "xc", inner, (rates, weights)
+        jnp.stack([end_state, start_state]), inner_rounds, "xc", inner, (rates, weights), 2
     )
     far, _, _ = cube_scan(group, outer_rounds, "zl", outer, ())
     entering = near[0] + factors[-4] * far[0]

time: 76.9 us -> 78 us (1.014)
  the two profiles are of different devices: /device:TPU:15 before, /device:TPU:1 now
where the time goes in v13:
time: 78 us; the launch traced here: 76.7 us
  starting transfers between devices  35.8 us (46%)
  other arithmetic  12.4 us (16%)
  matrix products  9.63 us (12%)
  local copies, waits for them, and re-layouts  8.93 us (11%)
  waiting for transfers between devices  8.02 us (10%)
  between operations  1.95 us (2%)
    ppermute x6, starting transfers between devices, cube_scan(): lax.ppermute(window, axis, [(source, source ^ shift) for source in range(...  25.8 us
    ppermute x2, starting transfers between devices, from_behind(): lax.ppermute(value, axis, [(source, source + steps) for source in range(l...  10 us
    ppermute x6, waiting for transfers between devices, cube_scan(): lax.ppermute(window, axis, [(source, source ^ shift) for source in range(...  5.38 us
    dot_general x1, matrix products, shards(): toeplitz = jnp.einsum('gtm,gms->gts', falling, rising, precision=precise)  3.65 us
    slice x2, local copies, waits for them, and re-layouts, short_causal(): filter_taps[offset] * padded[SHORT - 1 - offset:SHORT - 1 - offset + length]  3.18 us
    ppermute x2, waiting for transfers between devices, from_behind(): lax.ppermute(value, axis, [(source, source + steps) for source in range(l...  2.63 us
    concatenate x1, local copies, waits for them, and re-layouts, shards(): jnp.concatenate([local_conv[:edge], local_grad[:edge], grad_out[:edge].as...  2.44 us
    convert_element_type x9, other arithmetic, rounded(): return lax.optimization_barrier(values.astype(jnp.bfloat16))  2.27 us
  transfers between devices with their start and end apart: 8, of which 5 were waited for; matrix products, arithmetic and copies ran while one was open for 24% of the time, Pallas kernels for 0%

profile of v13, /device:TPU:1, one launch (start us, length us, event | category | flops | bytes accessed | tf_op | source)
XLA Modules:
  0.0 76.7 jit_solution(15625798286517908545)
XLA Ops:
  0.6 0.7 slice_bitcast_fusion.6
  1.4 0.7 slice_bitcast_fusion.4
  2.1 4.5 %collective-permute-start = (bf16[3,6,512]{2,1,0:T(8,128)(2,1)S(1)}, bf16[3,6,512]{2,1,0:T(8,128)(2,1)}, u32[]{:S(2)}, u32[]{:S(2)}) collective-permute-start(bf16[3,6,512]{2,1,0:T(8,128)(2,1)S(1)} %pad_maximum_fusion.7), channel_id=1, source_target_pairs={{0,8},{8,16},{16,24},{24,32},{32,40},{40,48},{48,56},{56,64},{64,7... | collective-permute-start | bytes 55304 | tf_op jit(solution)/shard_map/ppermute | solution.py:19
  6.7 1.4 %fusion.182 = (f32[1,1,512]{2,1,0:T(1,128)}, f32[1,1,512]{2,1,0:T(1,128)}) fusion(f32[3,7,512]{2,1,0:T(8,128)} %param.10), kind=kLoop, calls=%fused_computation.328 | loop fusion | bytes 8192 | tf_op jit(solution)/shard_map/slice | solution.py:32
  8.1 1.8 %fusion.181 = (f32[1,1,512]{2,1,0:T(1,128)S(1)}, f32[1,1,512]{2,1,0:T(1,128)}, f32[1,1,512]{2,1,0:T(1,128)}, f32[1,1,512]{2,1,0:T(1,128)}, f32[1,1,512]{2,1,0:T(...) fusion(f32[3,7,512]{2,1,0:T(8,128)} %param.10), kind=kLoop, calls=%fused_computation.327 | loop fusion | bytes 77824 | tf_op jit(solution)/shard_map/slice | solution.py:32
  9.9 1.3 %fusion.183 = (f32[32,16]{0,1:T(8,128)S(1)}, f32[16,32]{1,0:T(8,128)S(1)}, f32[32,16]{0,1:T(8,128)}) fusion(f32[32,16]{0,1:T(8,128)} %param.11, f32[32,16]{0,1:T(8,128)} %param.12), kind=kLoop, calls=%fused_computation.329 | loop fusion | flops 3072 | bytes 10240 | tf_op jit(solution)/shard_map/neg | solution.py:114
  11.3 0.1 multiply_exponential_fusion.1
  11.5 0.1 rev.6
  11.8 0.6 slice_convert_fusion.2
  12.4 0.1 broadcast_in_dim.11
  12.5 0.2 neg.33
  12.7 0.1 stack.152
  12.9 0.2 multiply_exponential_fusion
  13.2 0.7 slice_select_fusion.6
  13.8 0.7 slice_select_fusion.7
  14.6 0.6 convert_add_fusion
  15.2 0.7 fusion.169
  16.0 0.9 %fusion.110 = bf16[128,512]{1,0:T(8,128)(2,1)S(1)} fusion(f32[6,512]{1,0:T(8,128)S(1)} %get-tuple-element.76, f32[128,512]{1,0:T(8,128)S(1)} %convert_element_type.216, f32[512]{0:T(512)S(1)} %bitcast.142, f32[512]{0:T(512)} %bitcast.144, f32[512]{0:T(512)} %bitcast.146, f32[512]{0:T(512)} %bitcast.148, f32[512]{0:T(512)} %bitcast.150, f32[512]{0:T(512)} %bitcast.152, ...), kind=kLoop, calls=%fused_computation.164 | loop fusion | flops 1310720 | bytes 419840 | tf_op jit(solution)/shard_map/convert_element_type | solution.py:23
  17.0 0.2 fusion.93
  17.4 0.2 fusion.76
  17.6 0.3 fusion.184
  17.9 0.3 convolution_add_fusion.1
  18.2 0.3 fusion.185
  18.5 0.3 convolution_add_fusion
  18.8 0.3 multiply_reduce_fusion.1
  19.1 6.1 %collective-permute-start.1 = (f32[2,16,512]{2,1,0:T(8,128)S(1)}, f32[2,16,512]{2,1,0:T(8,128)S(1)}, u32[]{:S(2)}, u32[]{:S(2)}) collective-permute-start(f32[2,16,512]{2,1,0:T(8,128)S(1)} %pad_maximum_fusion.6), channel_id=1, source_target_pairs={{0,8},{8,0},{16,24},{24,16},{32,40},{40,32},{48,56},{56,48},{1,9},... | collective-permute-start | bytes 196616 | tf_op jit(solution)/shard_map/ppermute | solution.py:85
  25.2 0.6 slice_convert_fusion.1
  25.8 0.3 collective-permute-done.1
  26.1 1.9 %collective-permute-start.2 = (f32[2,16,512]{2,1,0:T(8,128)S(1)}, f32[2,16,512]{2,1,0:T(8,128)S(1)}, u32[]{:S(2)}, u32[]{:S(2)}) collective-permute-start(f32[2,16,512]{2,1,0:T(8,128)S(1)} %fusion.146), channel_id=1, source_target_pairs={{0,16},{8,24},{16,0},{24,8},{32,48},{40,56},{48,32},{56,40},{1,17}... | collective-permute-start | bytes 196616 | tf_op jit(solution)/shard_map/ppermute | solution.py:85
  28.1 0.6 slice_convert_fusion
  28.7 0.1 copy.33
  28.8 0.1 copy.24
  28.9 2.2 %collective-permute-done.2 = f32[2,16,512]{2,1,0:T(8,128)S(1)} collective-permute-done((f32[2,16,512]{2,1,0:T(8,128)S(1)}, f32[2,16,512]{2,1,0:T(8,128)S(1)}, u32[]{:S(2)}, u32[]{:S(2)}) %collective-permute-start.2) | collective-permute-done | bytes 65568 | tf_op jit(solution)/shard_map/ppermute | solution.py:85
  31.2 0.1 copy.26
  31.3 1.9 %collective-permute-start.3 = (f32[2,16,512]{2,1,0:T(8,128)S(1)}, f32[2,16,512]{2,1,0:T(8,128)S(1)}, u32[]{:S(2)}, u32[]{:S(2)}) collective-permute-start(f32[2,16,512]{2,1,0:T(8,128)S(1)} %fusion.149), channel_id=1, source_target_pairs={{0,32},{8,40},{16,48},{24,56},{32,0},{40,8},{48,16},{56,24},{1,33}... | collective-permute-start | bytes 196616 | tf_op jit(solution)/shard_map/ppermute | solution.py:85
  33.3 3.7 %fusion.133 = f32[32,128,128]{2,1,0:T(8,128)S(1)} fusion(f32[32,16]{1,0:T(8,128)S(1)} %copy.27, f32[128]{0:T(128)S(1)} %copy-done.55, f32[128]{0:T(128)S(1)} %copy-done.56, f32[32,16]{1,0:T(8,128)S(1)} %copy.26), kind=kOutput, calls=%fused_computation.211 | convolution fusion | flops 100859904 | bytes 2102272 | tf_op jit(solution)/shard_map/gtm,gms->gts/dot_general | solution.py:154
  37.0 0.4 fusion.11
  37.4 0.4 convolution_add_fusion.2
  37.8 0.6 fusion.12
  38.6 2.9 %collective-permute-start.4 = (f32[2,16,512]{2,1,0:T(8,128)S(1)}, f32[2,16,512]{2,1,0:T(8,128)S(1)}, u32[]{:S(2)}, u32[]{:S(2)}) collective-permute-start(f32[2,16,512]{2,1,0:T(8,128)S(1)} %get-tuple-element.54), channel_id=1, source_target_pairs={{0,64},{64,0},{128,192},{192,128},{256,320},{320,256},{384,448},{4... | collective-permute-start | bytes 196616 | tf_op jit(solution)/shard_map/ppermute | solution.py:85
  41.5 0.7 convolution_add_fusion.3
  42.1 1.6 %collective-permute-done.4 = f32[2,16,512]{2,1,0:T(8,128)S(1)} collective-permute-done((f32[2,16,512]{2,1,0:T(8,128)S(1)}, f32[2,16,512]{2,1,0:T(8,128)S(1)}, u32[]{:S(2)}, u32[]{:S(2)}) %collective-permute-start.4) | collective-permute-done | bytes 65568 | tf_op jit(solution)/shard_map/ppermute | solution.py:85
  43.7 5.6 %collective-permute-start.5 = (f32[2,16,512]{2,1,0:T(8,128)S(1)}, f32[2,16,512]{2,1,0:T(8,128)S(1)}, u32[]{:S(2)}, u32[]{:S(2)}) collective-permute-start(f32[2,16,512]{2,1,0:T(8,128)S(1)} %fusion.153), channel_id=1, source_target_pairs={{0,128},{64,192},{128,0},{192,64},{256,384},{320,448},{384,256},{4... | collective-permute-start | bytes 196616 | tf_op jit(solution)/shard_map/ppermute | solution.py:85
  49.4 0.2 fusion.180
  49.6 0.1 rev.7
  49.7 1.3 %collective-permute-done.5 = f32[2,16,512]{2,1,0:T(8,128)S(1)} collective-permute-done((f32[2,16,512]{2,1,0:T(8,128)S(1)}, f32[2,16,512]{2,1,0:T(8,128)S(1)}, u32[]{:S(2)}, u32[]{:S(2)}) %collective-permute-start.5) | collective-permute-done | bytes 65568 | tf_op jit(solution)/shard_map/ppermute | solution.py:85
  51.0 7.3 %collective-permute-start.6 = (f32[2,16,512]{2,1,0:T(8,128)S(1)}, f32[2,16,512]{2,1,0:T(8,128)S(1)}, u32[]{:S(2)}, u32[]{:S(2)}) collective-permute-start(f32[2,16,512]{2,1,0:T(8,128)S(1)} %fusion.154), channel_id=1, source_target_pairs={{0,256},{64,320},{128,384},{192,448},{256,0},{320,64},{384,128},{4... | collective-permute-start | bytes 196616 | tf_op jit(solution)/shard_map/ppermute | solution.py:85
  58.4 0.1 broadcast_multiply_fusion.2
  58.5 0.1 copy.43
  58.6 0.1 copy.38
  58.7 0.1 copy.35
  58.9 2.4 %concatenate.24 = f32[46,512]{1,0:T(8,128)S(1)} concatenate(f32[6,512]{1,0:T(8,128)S(1)} %copy.35, f32[6,512]{1,0:T(8,128)S(1)} %copy.43, f32[6,512]{1,0:T(8,128)} %slice_convert_fusion.2, f32[6,512]{1,0:T(8,128)} %slice_convert_fusion.1, f32[6,512]{1,0:T(8,128)} %slice_convert_fusion, f32[16,512]{1,0:T(8,128)S(1)} %get-tuple-element.11), dimensions={0} | concatenate | bytes 188416 | tf_op jit(solution)/shard_map/concatenate | solution.py:169
  61.3 5.5 %collective-permute-start.7 = (f32[46,512]{1,0:T(8,128)S(1)}, f32[46,512]{1,0:T(8,128)S(1)}, u32[]{:S(2)}, u32[]{:S(2)}) collective-permute-start(f32[46,512]{1,0:T(8,128)S(1)} %concatenate.24), channel_id=1, source_target_pairs={{8,0},{16,8},{24,16},{32,24},{40,32},{48,40},{56,48},{64,56},{72,6... | collective-permute-start | bytes 282632 | tf_op jit(solution)/shard_map/ppermute | solution.py:19
  66.8 0.1 copy.32
  67.0 2.6 %collective-permute-done.7 = f32[46,512]{1,0:T(8,128)S(1)} collective-permute-done((f32[46,512]{1,0:T(8,128)S(1)}, f32[46,512]{1,0:T(8,128)S(1)}, u32[]{:S(2)}, u32[]{:S(2)}) %collective-permute-start.7) | collective-permute-done | bytes 94240 | tf_op jit(solution)/shard_map/ppermute | solution.py:19
  69.7 0.8 %fusion.3 = bf16[128,512]{1,0:T(8,128)(2,1)S(1)} fusion(f32[128,512]{1,0:T(8,128)S(1)} %copy.38, f32[32,16,128]{2,1,0:T(8,128)S(1)} %broadcast_multiply_fusion.2, f32[16,512]{1,0:T(8,128)S(1)} %get-tuple-element.13, f32[32,512]{1,0:T(8,128)S(1)} %fusion.155), kind=kOutput, calls=%fused_computation.11 | convolution fusion | flops 403046400 | bytes 753664 | tf_op jit(solution)/shard_map/ks,kc->sc/dot_general | solution.py:164
  70.6 0.8 %fusion.4 = bf16[128,512]{1,0:T(8,128)(2,1)S(1)} fusion(f32[128,512]{1,0:T(8,128)S(1)} %copy.32, f32[32,16,128]{2,1,0:T(8,128)S(1)} %get-tuple-element.39, f32[16,512]{1,0:T(8,128)S(1)} %get-tuple-element.15, f32[32,512]{1,0:T(8,128)S(1)} %fusion.155), kind=kOutput, calls=%fused_computation.12 | convolution fusion | flops 403046400 | bytes 753664 | tf_op jit(solution)/shard_map/kt,kc->tc/dot_general | solution.py:163
  71.4 0.7 fusion.16
  72.2 0.3 broadcast_multiply_fusion
  72.6 0.6 fusion.164
  73.2 0.6 fusion.128
  74.0 0.9 %fusion.42 = bf16[128,512]{1,0:T(8,128)(2,1)} fusion(f32[6,512]{1,0:T(8,128)S(1)} %convert_element_type.268, f32[128,512]{1,0:T(8,128)S(1)} %convert_element_type.264, f32[512]{0:T(512)S(1)} %bitcast.165, f32[512]{0:T(512)S(1)} %bitcast.167, f32[512]{0:T(512)S(1)} %bitcast.169, f32[512]{0:T(512)S(1)} %bitcast.171, f32[512]{0:T(512)S(1)} %bitcast.173, ...), kind=kLoop, calls=%fused_computation.96 | loop fusion | flops 1310720 | bytes 419840 | tf_op jit(solution)/shard_map/convert_element_type | solution.py:201
  74.9 0.9 %fusion.25 = bf16[128,512]{1,0:T(8,128)(2,1)} fusion(f32[6,512]{1,0:T(8,128)S(1)} %convert_element_type.273, f32[128,512]{1,0:T(8,128)S(1)} %convert_element_type.271, f32[512]{0:T(512)S(1)} %bitcast.181, f32[512]{0:T(512)S(1)} %bitcast.179, f32[512]{0:T(512)S(1)} %bitcast.155, f32[512]{0:T(512)S(1)} %bitcast.157, f32[512]{0:T(512)S(1)} %bitcast.159, ...), kind=kLoop, calls=%fused_computation.79 | loop fusion | flops 1310720 | bytes 419840 | tf_op jit(solution)/shard_map/convert_element_type | solution.py:202
  75.8 0.9 %fusion.59 = bf16[128,512]{1,0:T(8,128)(2,1)} fusion(f32[6,512]{1,0:T(8,128)S(1)} %convert_element_type.259, f32[128,512]{1,0:T(8,128)S(1)} %convert_element_type.252, f32[512]{0:T(512)S(1)} %bitcast.143, f32[512]{0:T(512)S(1)} %bitcast.145, f32[512]{0:T(512)S(1)} %bitcast.147, f32[512]{0:T(512)S(1)} %bitcast.149, f32[512]{0:T(512)S(1)} %bitcast.151, ...), kind=kLoop, calls=%fused_computation.113 | loop fusion | flops 1310720 | bytes 419840 | tf_op jit(solution)/shard_map/convert_element_type | solution.py:200
  (150 shorter events, 1.0 us)
Async XLA Ops:
  0.6 11.1 %copy-start = (bf16[128,512]{1,0:T(8,128)(2,1)S(1)}, bf16[128,512]{1,0:T(8,128)(2,1)}, u32[]{:S(2)}) copy-start(bf16[128,512]{1,0:T(8,128)(2,1)} %param.13) | copy-start | bytes 393220
  2.1 13.1 %collective-permute-start = (bf16[3,6,512]{2,1,0:T(8,128)(2,1)S(1)}, bf16[3,6,512]{2,1,0:T(8,128)(2,1)}, u32[]{:S(2)}, u32[]{:S(2)}) collective-permute-start(bf16[3,6,512]{2,1,0:T(8,128)(2,1)S(1)} %pad_maximum_fusion.7), channel_id=1, source_target_pairs={{0,8},{8,16},{16,24},{24,32},{32,40},{40,48},{48,56},{56,64},{64,7... | collective-permute-start | bytes 55304 | tf_op jit(solution)/shard_map/ppermute | solution.py:19
  9.9 6.1 %copy-start.18 = (f32[1,1,512]{2,1,0:T(1,128)}, f32[1,1,512]{2,1,0:T(1,128)S(1)}, u32[]{:S(2)}) copy-start(f32[1,1,512]{2,1,0:T(1,128)S(1)} %get-tuple-element.55) | copy-start | bytes 6148
  9.9 6.1 %copy-start.20 = (f32[1,1,512]{2,1,0:T(1,128)}, f32[1,1,512]{2,1,0:T(1,128)S(1)}, u32[]{:S(2)}) copy-start(f32[1,1,512]{2,1,0:T(1,128)S(1)} %get-tuple-element.68) | copy-start | bytes 6148
  11.5 3.6 %copy-start.1 = (bf16[128,512]{1,0:T(8,128)(2,1)S(1)}, bf16[128,512]{1,0:T(8,128)(2,1)}, u32[]{:S(2)}) copy-start(bf16[128,512]{1,0:T(8,128)(2,1)} %param.7) | copy-start | bytes 393220
  11.6 3.5 %copy-start.2 = (bf16[128,512]{1,0:T(8,128)(2,1)S(1)}, bf16[128,512]{1,0:T(8,128)(2,1)}, u32[]{:S(2)}) copy-start(bf16[128,512]{1,0:T(8,128)(2,1)} %param.8) | copy-start | bytes 393220
  11.7 3.5 %copy-start.3 = (bf16[128,512]{1,0:T(8,128)(2,1)S(1)}, bf16[128,512]{1,0:T(8,128)(2,1)}, u32[]{:S(2)}) copy-start(bf16[128,512]{1,0:T(8,128)(2,1)} %param.9) | copy-start | bytes 393220
  12.8 4.1 %copy-start.37 = (f32[1,1,512]{2,1,0:T(1,128)S(1)}, f32[1,1,512]{2,1,0:T(1,128)}, u32[]{:S(2)}) copy-start(f32[1,1,512]{2,1,0:T(1,128)} %get-tuple-element.61) | copy-start | bytes 6148
  12.9 4.1 %copy-start.39 = (f32[1,1,512]{2,1,0:T(1,128)S(1)}, f32[1,1,512]{2,1,0:T(1,128)}, u32[]{:S(2)}) copy-start(f32[1,1,512]{2,1,0:T(1,128)} %get-tuple-element.62) | copy-start | bytes 6148
  12.9 4.1 %copy-start.41 = (f32[1,1,512]{2,1,0:T(1,128)S(1)}, f32[1,1,512]{2,1,0:T(1,128)}, u32[]{:S(2)}) copy-start(f32[1,1,512]{2,1,0:T(1,128)} %get-tuple-element.63) | copy-start | bytes 6148
  12.9 4.1 %copy-start.43 = (f32[1,1,512]{2,1,0:T(1,128)S(1)}, f32[1,1,512]{2,1,0:T(1,128)}, u32[]{:S(2)}) copy-start(f32[1,1,512]{2,1,0:T(1,128)} %get-tuple-element.64) | copy-start | bytes 6148
  12.9 4.1 %copy-start.45 = (f32[1,1,512]{2,1,0:T(1,128)S(1)}, f32[1,1,512]{2,1,0:T(1,128)}, u32[]{:S(2)}) copy-start(f32[1,1,512]{2,1,0:T(1,128)} %get-tuple-element.65) | copy-start | bytes 6148
  12.9 4.1 %copy-start.47 = (f32[1,1,512]{2,1,0:T(1,128)S(1)}, f32[1,1,512]{2,1,0:T(1,128)}, u32[]{:S(2)}) copy-start(f32[1,1,512]{2,1,0:T(1,128)} %get-tuple-element.66) | copy-start | bytes 6148
  12.9 4.1 %copy-start.49 = (f32[1,1,512]{2,1,0:T(1,128)S(1)}, f32[1,1,512]{2,1,0:T(1,128)}, u32[]{:S(2)}) copy-start(f32[1,1,512]{2,1,0:T(1,128)} %get-tuple-element.67) | copy-start | bytes 6148
  13.1 4.2 %copy-start.27 = (f32[1,1,512]{2,1,0:T(1,128)S(1)}, f32[1,1,512]{2,1,0:T(1,128)}, u32[]{:S(2)}) copy-start(f32[1,1,512]{2,1,0:T(1,128)} %get-tuple-element.56) | copy-start | bytes 6148
  13.1 4.2 %copy-start.29 = (f32[1,1,512]{2,1,0:T(1,128)S(1)}, f32[1,1,512]{2,1,0:T(1,128)}, u32[]{:S(2)}) copy-start(f32[1,1,512]{2,1,0:T(1,128)} %get-tuple-element.57) | copy-start | bytes 6148
  13.1 4.2 %copy-start.31 = (f32[1,1,512]{2,1,0:T(1,128)S(1)}, f32[1,1,512]{2,1,0:T(1,128)}, u32[]{:S(2)}) copy-start(f32[1,1,512]{2,1,0:T(1,128)} %get-tuple-element.58) | copy-start | bytes 6148
  13.1 4.2 %copy-start.33 = (f32[1,1,512]{2,1,0:T(1,128)S(1)}, f32[1,1,512]{2,1,0:T(1,128)}, u32[]{:S(2)}) copy-start(f32[1,1,512]{2,1,0:T(1,128)} %get-tuple-element.59) | copy-start | bytes 6148
  13.1 4.2 %copy-start.35 = (f32[1,1,512]{2,1,0:T(1,128)S(1)}, f32[1,1,512]{2,1,0:T(1,128)}, u32[]{:S(2)}) copy-start(f32[1,1,512]{2,1,0:T(1,128)} %get-tuple-element.60) | copy-start | bytes 6148
  13.1 4.2 %copy-start.51 = (f32[1,1,512]{2,1,0:T(1,128)S(1)}, f32[1,1,512]{2,1,0:T(1,128)}, u32[]{:S(2)}) copy-start(f32[1,1,512]{2,1,0:T(1,128)} %get-tuple-element.74) | copy-start | bytes 6148
  13.2 4.2 %copy-start.53 = (f32[1,1,512]{2,1,0:T(1,128)S(1)}, f32[1,1,512]{2,1,0:T(1,128)}, u32[]{:S(2)}) copy-start(f32[1,1,512]{2,1,0:T(1,128)} %get-tuple-element.75) | copy-start | bytes 6148
  18.8 12.4 %copy-start.17 = (f32[32,16]{0,1:T(8,128)S(1)}, f32[32,16]{0,1:T(8,128)}, u32[]{:S(2)}) copy-start(f32[32,16]{0,1:T(8,128)} %get-tuple-element.7) | copy-start | bytes 6148
  18.8 12.4 %copy-start.16 = (f32[32,16]{0,1:T(8,128)S(1)}, f32[32,16]{0,1:T(8,128)}, u32[]{:S(2)}) copy-start(f32[32,16]{0,1:T(8,128)} %param.11) | copy-start | bytes 6148
  18.8 12.5 %copy-start.10 = (f32[1,16,512]{2,1,0:T(8,128)S(1)}, f32[1,16,512]{2,1,0:T(8,128)}, u32[]{:S(2)}) copy-start(f32[1,16,512]{2,1,0:T(8,128)} %get-tuple-element.32) | copy-start | bytes 98308
  18.8 12.5 %copy-start.11 = (f32[1,16,512]{2,1,0:T(8,128)S(1)}, f32[1,16,512]{2,1,0:T(8,128)}, u32[]{:S(2)}) copy-start(f32[1,16,512]{2,1,0:T(8,128)} %get-tuple-element.17) | copy-start | bytes 98308
  18.8 14.5 %copy-start.55 = (f32[128]{0:T(128)S(1)}, f32[128]{0:T(128)}, u32[]{:S(2)}) copy-start(f32[128]{0:T(128)} %get-tuple-element.84) | copy-start | bytes 1540
  18.8 14.5 %copy-start.56 = (f32[128]{0:T(128)S(1)}, f32[128]{0:T(128)}, u32[]{:S(2)}) copy-start(f32[128]{0:T(128)} %get-tuple-element.85) | copy-start | bytes 1540
  19.1 7.0 %collective-permute-start.1 = (f32[2,16,512]{2,1,0:T(8,128)S(1)}, f32[2,16,512]{2,1,0:T(8,128)S(1)}, u32[]{:S(2)}, u32[]{:S(2)}) collective-permute-start(f32[2,16,512]{2,1,0:T(8,128)S(1)} %pad_maximum_fusion.6), channel_id=1, source_target_pairs={{0,8},{8,0},{16,24},{24,16},{32,40},{40,32},{48,56},{56,48},{1,9},... | collective-permute-start | bytes 196616 | tf_op jit(solution)/shard_map/ppermute | solution.py:85
  26.1 5.0 %collective-permute-start.2 = (f32[2,16,512]{2,1,0:T(8,128)S(1)}, f32[2,16,512]{2,1,0:T(8,128)S(1)}, u32[]{:S(2)}, u32[]{:S(2)}) collective-permute-start(f32[2,16,512]{2,1,0:T(8,128)S(1)} %fusion.146), channel_id=1, source_target_pairs={{0,16},{8,24},{16,0},{24,8},{32,48},{40,56},{48,32},{56,40},{1,17}... | collective-permute-start | bytes 196616 | tf_op jit(solution)/shard_map/ppermute | solution.py:85
  31.3 7.1 %collective-permute-start.3 = (f32[2,16,512]{2,1,0:T(8,128)S(1)}, f32[2,16,512]{2,1,0:T(8,128)S(1)}, u32[]{:S(2)}, u32[]{:S(2)}) collective-permute-start(f32[2,16,512]{2,1,0:T(8,128)S(1)} %fusion.149), channel_id=1, source_target_pairs={{0,32},{8,40},{16,48},{24,56},{32,0},{40,8},{48,16},{56,24},{1,33}... | collective-permute-start | bytes 196616 | tf_op jit(solution)/shard_map/ppermute | solution.py:85
  37.3 1.1 %copy-start.5 = (f32[1,16,512]{2,1,0:T(8,128)S(1)}, f32[1,16,512]{2,1,0:T(8,128)}, u32[]{:S(2)}) copy-start(f32[1,16,512]{2,1,0:T(8,128)} %get-tuple-element.35) | copy-start | bytes 98308
  37.3 1.1 %copy-start.6 = (f32[1,16,512]{2,1,0:T(8,128)S(1)}, f32[1,16,512]{2,1,0:T(8,128)}, u32[]{:S(2)}) copy-start(f32[1,16,512]{2,1,0:T(8,128)} %get-tuple-element.36) | copy-start | bytes 98308
  37.3 1.1 %copy-start.7 = (f32[1,16,512]{2,1,0:T(8,128)S(1)}, f32[1,16,512]{2,1,0:T(8,128)}, u32[]{:S(2)}) copy-start(f32[1,16,512]{2,1,0:T(8,128)} %get-tuple-element.16) | copy-start | bytes 98308
  37.4 1.1 %copy-start.8 = (f32[1,16,512]{2,1,0:T(8,128)S(1)}, f32[1,16,512]{2,1,0:T(8,128)}, u32[]{:S(2)}) copy-start(f32[1,16,512]{2,1,0:T(8,128)} %get-tuple-element.18) | copy-start | bytes 98308
  37.4 1.1 %copy-start.9 = (f32[1,16,512]{2,1,0:T(8,128)S(1)}, f32[1,16,512]{2,1,0:T(8,128)}, u32[]{:S(2)}) copy-start(f32[1,16,512]{2,1,0:T(8,128)} %get-tuple-element.28) | copy-start | bytes 98308
  38.4 5.3 %copy-start.14 = (f32[1,16,512]{2,1,0:T(8,128)S(1)}, f32[1,16,512]{2,1,0:T(8,128)}, u32[]{:S(2)}) copy-start(f32[1,16,512]{2,1,0:T(8,128)} %get-tuple-element.19) | copy-start | bytes 98308
  38.4 5.3 %copy-start.15 = (f32[1,16,512]{2,1,0:T(8,128)S(1)}, f32[1,16,512]{2,1,0:T(8,128)}, u32[]{:S(2)}) copy-start(f32[1,16,512]{2,1,0:T(8,128)} %get-tuple-element.25) | copy-start | bytes 98308
  38.5 12.5 %copy-start.12 = (f32[1,16,512]{2,1,0:T(8,128)S(1)}, f32[1,16,512]{2,1,0:T(8,128)}, u32[]{:S(2)}) copy-start(f32[1,16,512]{2,1,0:T(8,128)} %get-tuple-element.20) | copy-start | bytes 98308
  38.6 12.5 %copy-start.13 = (f32[1,16,512]{2,1,0:T(8,128)S(1)}, f32[1,16,512]{2,1,0:T(8,128)}, u32[]{:S(2)}) copy-start(f32[1,16,512]{2,1,0:T(8,128)} %get-tuple-element.22) | copy-start | bytes 98308
  38.6 5.1 %collective-permute-start.4 = (f32[2,16,512]{2,1,0:T(8,128)S(1)}, f32[2,16,512]{2,1,0:T(8,128)S(1)}, u32[]{:S(2)}, u32[]{:S(2)}) collective-permute-start(f32[2,16,512]{2,1,0:T(8,128)S(1)} %get-tuple-element.54), channel_id=1, source_target_pairs={{0,64},{64,0},{128,192},{192,128},{256,320},{320,256},{384,448},{4... | collective-permute-start | bytes 196616 | tf_op jit(solution)/shard_map/ppermute | solution.py:85
  43.7 7.3 %collective-permute-start.5 = (f32[2,16,512]{2,1,0:T(8,128)S(1)}, f32[2,16,512]{2,1,0:T(8,128)S(1)}, u32[]{:S(2)}, u32[]{:S(2)}) collective-permute-start(f32[2,16,512]{2,1,0:T(8,128)S(1)} %fusion.153), channel_id=1, source_target_pairs={{0,128},{64,192},{128,0},{192,64},{256,384},{320,448},{384,256},{4... | collective-permute-start | bytes 196616 | tf_op jit(solution)/shard_map/ppermute | solution.py:85
  51.0 15.9 %collective-permute-start.6 = (f32[2,16,512]{2,1,0:T(8,128)S(1)}, f32[2,16,512]{2,1,0:T(8,128)S(1)}, u32[]{:S(2)}, u32[]{:S(2)}) collective-permute-start(f32[2,16,512]{2,1,0:T(8,128)S(1)} %fusion.154), channel_id=1, source_target_pairs={{0,256},{64,320},{128,384},{192,448},{256,0},{320,64},{384,128},{4... | collective-permute-start | bytes 196616 | tf_op jit(solution)/shard_map/ppermute | solution.py:85
  61.3 8.4 %collective-permute-start.7 = (f32[46,512]{1,0:T(8,128)S(1)}, f32[46,512]{1,0:T(8,128)S(1)}, u32[]{:S(2)}, u32[]{:S(2)}) collective-permute-start(f32[46,512]{1,0:T(8,128)S(1)} %concatenate.24), channel_id=1, source_target_pairs={{8,0},{16,8},{24,16},{32,24},{40,32},{48,40},{56,48},{64,56},{72,6... | collective-permute-start | bytes 282632 | tf_op jit(solution)/shard_map/ppermute | solution.py:19
  72.1 1.8 %copy-start.38 = (f32[1,1,512]{2,1,0:T(1,128)S(1)}, f32[1,1,512]{2,1,0:T(1,128)}, u32[]{:S(2)}) copy-start(f32[1,1,512]{2,1,0:T(1,128)} %get-tuple-element.61) | copy-start | bytes 6148
  72.1 1.8 %copy-start.40 = (f32[1,1,512]{2,1,0:T(1,128)S(1)}, f32[1,1,512]{2,1,0:T(1,128)}, u32[]{:S(2)}) copy-start(f32[1,1,512]{2,1,0:T(1,128)} %get-tuple-element.62) | copy-start | bytes 6148
  72.1 1.8 %copy-start.42 = (f32[1,1,512]{2,1,0:T(1,128)S(1)}, f32[1,1,512]{2,1,0:T(1,128)}, u32[]{:S(2)}) copy-start(f32[1,1,512]{2,1,0:T(1,128)} %get-tuple-element.63) | copy-start | bytes 6148
  72.2 1.8 %copy-start.44 = (f32[1,1,512]{2,1,0:T(1,128)S(1)}, f32[1,1,512]{2,1,0:T(1,128)}, u32[]{:S(2)}) copy-start(f32[1,1,512]{2,1,0:T(1,128)} %get-tuple-element.64) | copy-start | bytes 6148
  72.2 1.8 %copy-start.46 = (f32[1,1,512]{2,1,0:T(1,128)S(1)}, f32[1,1,512]{2,1,0:T(1,128)}, u32[]{:S(2)}) copy-start(f32[1,1,512]{2,1,0:T(1,128)} %get-tuple-element.65) | copy-start | bytes 6148
  72.2 1.8 %copy-start.48 = (f32[1,1,512]{2,1,0:T(1,128)S(1)}, f32[1,1,512]{2,1,0:T(1,128)}, u32[]{:S(2)}) copy-start(f32[1,1,512]{2,1,0:T(1,128)} %get-tuple-element.66) | copy-start | bytes 6148
  72.2 1.8 %copy-start.50 = (f32[1,1,512]{2,1,0:T(1,128)S(1)}, f32[1,1,512]{2,1,0:T(1,128)}, u32[]{:S(2)}) copy-start(f32[1,1,512]{2,1,0:T(1,128)} %get-tuple-element.67) | copy-start | bytes 6148
  72.5 2.4 %copy-start.28 = (f32[1,1,512]{2,1,0:T(1,128)S(1)}, f32[1,1,512]{2,1,0:T(1,128)}, u32[]{:S(2)}) copy-start(f32[1,1,512]{2,1,0:T(1,128)} %get-tuple-element.56) | copy-start | bytes 6148
  72.5 2.4 %copy-start.30 = (f32[1,1,512]{2,1,0:T(1,128)S(1)}, f32[1,1,512]{2,1,0:T(1,128)}, u32[]{:S(2)}) copy-start(f32[1,1,512]{2,1,0:T(1,128)} %get-tuple-element.57) | copy-start | bytes 6148
  72.5 2.4 %copy-start.32 = (f32[1,1,512]{2,1,0:T(1,128)S(1)}, f32[1,1,512]{2,1,0:T(1,128)}, u32[]{:S(2)}) copy-start(f32[1,1,512]{2,1,0:T(1,128)} %get-tuple-element.58) | copy-start | bytes 6148
  72.5 2.4 %copy-start.34 = (f32[1,1,512]{2,1,0:T(1,128)S(1)}, f32[1,1,512]{2,1,0:T(1,128)}, u32[]{:S(2)}) copy-start(f32[1,1,512]{2,1,0:T(1,128)} %get-tuple-element.59) | copy-start | bytes 6148
  72.5 2.4 %copy-start.36 = (f32[1,1,512]{2,1,0:T(1,128)S(1)}, f32[1,1,512]{2,1,0:T(1,128)}, u32[]{:S(2)}) copy-start(f32[1,1,512]{2,1,0:T(1,128)} %get-tuple-element.60) | copy-start | bytes 6148
  72.5 2.4 %copy-start.52 = (f32[1,1,512]{2,1,0:T(1,128)S(1)}, f32[1,1,512]{2,1,0:T(1,128)}, u32[]{:S(2)}) copy-start(f32[1,1,512]{2,1,0:T(1,128)} %get-tuple-element.74) | copy-start | bytes 6148
  72.5 2.4 %copy-start.54 = (f32[1,1,512]{2,1,0:T(1,128)S(1)}, f32[1,1,512]{2,1,0:T(1,128)}, u32[]{:S(2)}) copy-start(f32[1,1,512]{2,1,0:T(1,128)} %get-tuple-element.75) | copy-start | bytes 6148
  72.5 3.3 %copy-start.19 = (f32[1,1,512]{2,1,0:T(1,128)S(1)}, f32[1,1,512]{2,1,0:T(1,128)}, u32[]{:S(2)}) copy-start(f32[1,1,512]{2,1,0:T(1,128)} %copy-done.18) | copy-start | bytes 6148
  72.5 3.3 %copy-start.21 = (f32[1,1,512]{2,1,0:T(1,128)S(1)}, f32[1,1,512]{2,1,0:T(1,128)}, u32[]{:S(2)}) copy-start(f32[1,1,512]{2,1,0:T(1,128)} %copy-done.20) | copy-start | bytes 6148
  72.6 3.3 %copy-start.22 = (f32[1,1,512]{2,1,0:T(1,128)S(1)}, f32[1,1,512]{2,1,0:T(1,128)}, u32[]{:S(2)}) copy-start(f32[1,1,512]{2,1,0:T(1,128)} %get-tuple-element.69) | copy-start | bytes 6148
  72.6 3.3 %copy-start.23 = (f32[1,1,512]{2,1,0:T(1,128)S(1)}, f32[1,1,512]{2,1,0:T(1,128)}, u32[]{:S(2)}) copy-start(f32[1,1,512]{2,1,0:T(1,128)} %get-tuple-element.70) | copy-start | bytes 6148
  72.6 3.2 %copy-start.24 = (f32[1,1,512]{2,1,0:T(1,128)S(1)}, f32[1,1,512]{2,1,0:T(1,128)}, u32[]{:S(2)}) copy-start(f32[1,1,512]{2,1,0:T(1,128)} %get-tuple-element.71) | copy-start | bytes 6148
  72.6 3.2 %copy-start.25 = (f32[1,1,512]{2,1,0:T(1,128)S(1)}, f32[1,1,512]{2,1,0:T(1,128)}, u32[]{:S(2)}) copy-start(f32[1,1,512]{2,1,0:T(1,128)} %get-tuple-element.72) | copy-start | bytes 6148
  72.6 3.2 %copy-start.26 = (f32[1,1,512]{2,1,0:T(1,128)S(1)}, f32[1,1,512]{2,1,0:T(1,128)}, u32[]{:S(2)}) copy-start(f32[1,1,512]{2,1,0:T(1,128)} %get-tuple-element.73) | copy-start | bytes 6148
  (1 other events, 1.1 us)

commit v14 on v7

--- a/solution.py
+++ b/solution.py
@@ -102,9 +102,9 @@
         ]
     )
     before = from_behind(rim_rows, ("zl", "xc"), 1)
-    q_short = rounded(short_causal(before[0], u_query, short_filter[0]))
-    k_short = rounded(short_causal(before[1], u_key, short_filter[1]))
-    v_short = rounded(short_causal(before[2], u_value, short_filter[2]))
+    q_short = short_causal(before[0], u_query, short_filter[0]).astype(jnp.bfloat16)
+    k_short = short_causal(before[1], u_key, short_filter[1]).astype(jnp.bfloat16)
+    v_short = short_causal(before[2], u_value, short_filter[2]).astype(jnp.bfloat16)
     product = rounded(k_short.astype(jnp.float32) * v_short.astype(jnp.float32))
     grad_conv = rounded(grad_out.astype(jnp.float32) * q_short.astype(jnp.float32))
 

time: 76.9 us -> 71 us (0.923)
  the two profiles are of different devices: /device:TPU:15 before, /device:TPU:1 now
where the time goes in v14:
time: 71 us; the launch traced here: 69.7 us
  starting transfers between devices  34.2 us (48%)
  other arithmetic  10.1 us (14%)
  matrix products  9.64 us (14%)
  waiting for transfers between devices  8.06 us (11%)
  local copies, waits for them, and re-layouts  5.65 us (8%)
  between operations  2.05 us (3%)
    ppermute x6, starting transfers between devices, cube_scan(): lax.ppermute(window, axis, [(source, source ^ shift) for source in range(...  23.9 us
    ppermute x2, starting transfers between devices, from_behind(): lax.ppermute(value, axis, [(source, source + steps) for source in range(l...  10.3 us
    ppermute x6, waiting for transfers between devices, cube_scan(): lax.ppermute(window, axis, [(source, source ^ shift) for source in range(...  7.04 us
    dot_general x1, matrix products, shards(): toeplitz = jnp.einsum('gtm,gms->gts', falling, rising, precision=precise)  3.65 us
    slice x2, local copies, waits for them, and re-layouts, short_causal(): filter_taps[offset] * padded[SHORT - 1 - offset:SHORT - 1 - offset + length]  1.97 us
    dot_general x4, matrix products, split_dot(): jnp.einsum(spec, low, values, preferred_element_type=jnp.float32)  1.63 us
    dot_general x4, matrix products, split_dot(): jnp.einsum(spec, high.astype(jnp.bfloat16), values, preferred_element_typ...  1.56 us
    convert_element_type x6, other arithmetic, rounded(): return lax.optimization_barrier(values.astype(jnp.bfloat16))  1.53 us
  transfers between devices with their start and end apart: 8, of which 4 were waited for; matrix products, arithmetic and copies ran while one was open for 20% of the time, Pallas kernels for 0%

profile of v14, /device:TPU:1, one launch (start us, length us, event | category | flops | bytes accessed | tf_op | source)
XLA Modules:
  0.0 69.7 jit_solution(9199334807040478284)
XLA Ops:
  0.6 0.7 %slice_bitcast_fusion.6 = bf16[1,6,512]{2,1,0:T(8,128)(2,1)S(1)} fusion(bf16[128,512]{1,0:T(8,128)(2,1)} %param.7), kind=kLoop, calls=%fused_computation.310 | loop fusion | bytes 12288 | tf_op jit(solution)/shard_map/stack | solution.py:97
  1.4 0.7 %slice_bitcast_fusion.4 = (bf16[1,6,512]{2,1,0:T(8,128)(2,1)S(1)}, bf16[1,6,512]{2,1,0:T(8,128)(2,1)S(1)}) fusion(bf16[128,512]{1,0:T(8,128)(2,1)} %param.9, bf16[128,512]{1,0:T(8,128)(2,1)} %param.8), kind=kLoop, calls=%fused_computation.308 | loop fusion | bytes 24576 | tf_op jit(solution)/shard_map/stack | solution.py:97
  2.1 4.5 %collective-permute-start = (bf16[3,6,512]{2,1,0:T(8,128)(2,1)S(1)}, bf16[3,6,512]{2,1,0:T(8,128)(2,1)S(1)}, u32[]{:S(2)}, u32[]{:S(2)}) collective-permute-start(bf16[3,6,512]{2,1,0:T(8,128)(2,1)S(1)} %pad_maximum_fusion.7), channel_id=1, source_target_pairs={{0,8},{8,16},{16,24},{24,32},{32,40},{40,48},{48,56},{56,64},{64,7... | collective-permute-start | bytes 55304 | tf_op jit(solution)/shard_map/ppermute | solution.py:19
  6.6 1.2 %fusion.184 = (f32[1,1,512]{2,1,0:T(1,128)S(1)}, f32[1,1,512]{2,1,0:T(1,128)S(1)}, f32[1,1,512]{2,1,0:T(1,128)S(1)}, f32[1,1,512]{2,1,0:T(1,128)S(1)}, f32[1,1,5...) fusion(f32[3,7,512]{2,1,0:T(8,128)} %param.10), kind=kLoop, calls=%fused_computation.327 | loop fusion | bytes 77824 | tf_op jit(solution)/shard_map/slice | solution.py:32
  8.0 0.8 %fusion.185 = (f32[1,1,512]{2,1,0:T(1,128)S(1)}, f32[1,1,512]{2,1,0:T(1,128)S(1)}) fusion(f32[3,7,512]{2,1,0:T(8,128)} %param.10), kind=kLoop, calls=%fused_computation.328 | loop fusion | bytes 8192 | tf_op jit(solution)/shard_map/slice | solution.py:32
  8.8 0.7 %negate_bitcast_fusion = (f32[16,32]{1,0:T(8,128)S(1)}, f32[32,16]{0,1:T(8,128)S(1)}, f32[32,16]{0,1:T(8,128)S(1)}) fusion(f32[32,16]{0,1:T(8,128)} %param.11, f32[32,16]{0,1:T(8,128)} %param.12), kind=kLoop, calls=%fused_computation.306 | loop fusion | flops 3072 | bytes 10240 | tf_op jit(solution)/shard_map/neg | solution.py:141
  9.6 0.1 copy.25
  9.6 0.1 multiply_exponential_fusion.1
  9.8 0.1 rev.6
  10.2 0.1 broadcast_in_dim.12
  10.4 0.2 neg.35
  10.5 0.1 stack.155
  10.6 0.2 multiply_exponential_fusion
  10.8 0.7 %slice_select_fusion.6 = (f32[1,16,512]{2,1,0:T(8,128)}, f32[1,16,512]{2,1,0:T(8,128)}, f32[1,16,512]{2,1,0:T(8,128)}, f32[1,16,512]{2,1,0:T(8,128)}, f32[1,16,5...) fusion(f32[22,16,512]{2,1,0:T(8,128)S(1)} %multiply_exponential, ...), kind=kLoop, calls=%fused_computation.270 | loop fusion | flops 73728 | bytes 589828 | tf_op jit(solution)/shard_map/jit(_where)/select_n | solution.py:74
  11.5 0.7 %slice_select_fusion.7 = (f32[1,16,512]{2,1,0:T(8,128)}, f32[1,16,512]{2,1,0:T(8,128)}, f32[1,16,512]{2,1,0:T(8,128)}, f32[1,16,512]{2,1,0:T(8,128)S(1)}, f32[1,...) fusion(f32[22,16,512]{2,1,0:T(8,128)S(1)} %multiply_exponential, ...), kind=kLoop, calls=%fused_computation.271 | loop fusion | flops 106496 | bytes 753670 | tf_op jit(solution)/shard_map/jit(_where)/select_n | solution.py:74
  12.5 0.5 fusion.13
  13.1 0.3 fusion.14
  13.4 0.3 fusion.186
  13.6 0.3 convolution_add_fusion.1
  13.9 0.3 fusion.187
  14.2 0.3 convolution_add_fusion
  14.5 0.3 multiply_reduce_fusion.1
  14.8 5.6 %collective-permute-start.1 = (f32[2,16,512]{2,1,0:T(8,128)S(1)}, f32[2,16,512]{2,1,0:T(8,128)S(1)}, u32[]{:S(2)}, u32[]{:S(2)}) collective-permute-start(f32[2,16,512]{2,1,0:T(8,128)S(1)} %pad_maximum_fusion.6), channel_id=1, source_target_pairs={{0,8},{8,0},{16,24},{24,16},{32,40},{40,32},{48,56},{56,48},{1,9},... | collective-permute-start | bytes 196616 | tf_op jit(solution)/shard_map/ppermute | solution.py:85
  20.4 0.6 slice_convert_fusion.1
  21.0 0.1 copy.33
  21.1 0.1 copy.24
  21.2 0.0 collective-permute-done.1
  21.2 0.1 copy.26
  21.3 0.1 copy.27
  21.4 1.9 %collective-permute-start.2 = (f32[2,16,512]{2,1,0:T(8,128)S(1)}, f32[2,16,512]{2,1,0:T(8,128)S(1)}, u32[]{:S(2)}, u32[]{:S(2)}) collective-permute-start(f32[2,16,512]{2,1,0:T(8,128)S(1)} %fusion.148), channel_id=1, source_target_pairs={{0,16},{8,24},{16,0},{24,8},{32,48},{40,56},{48,32},{56,40},{1,17}... | collective-permute-start | bytes 196616 | tf_op jit(solution)/shard_map/ppermute | solution.py:85
  23.3 3.7 %fusion.133 = f32[32,128,128]{2,1,0:T(8,128)S(1)} fusion(f32[32,16]{1,0:T(8,128)S(1)} %copy.27, f32[128]{0:T(128)S(1)} %get-tuple-element.89, f32[128]{0:T(128)S(1)} %get-tuple-element.90, f32[32,16]{1,0:T(8,128)S(1)} %copy.26), kind=kOutput, calls=%fused_computation.211 | convolution fusion | flops 100859904 | bytes 2102272 | tf_op jit(solution)/shard_map/gtm,gms->gts/dot_general | solution.py:154
  27.0 0.4 fusion.11
  27.4 0.4 convolution_add_fusion.2
  27.9 2.6 %collective-permute-start.3 = (f32[2,16,512]{2,1,0:T(8,128)S(1)}, f32[2,16,512]{2,1,0:T(8,128)S(1)}, u32[]{:S(2)}, u32[]{:S(2)}) collective-permute-start(f32[2,16,512]{2,1,0:T(8,128)S(1)} %fusion.149), channel_id=1, source_target_pairs={{0,32},{8,40},{16,48},{24,56},{32,0},{40,8},{48,16},{56,24},{1,33}... | collective-permute-start | bytes 196616 | tf_op jit(solution)/shard_map/ppermute | solution.py:85
  30.5 0.6 fusion.12
  31.2 3.3 %collective-permute-done.3 = f32[2,16,512]{2,1,0:T(8,128)S(1)} collective-permute-done((f32[2,16,512]{2,1,0:T(8,128)S(1)}, f32[2,16,512]{2,1,0:T(8,128)S(1)}, u32[]{:S(2)}, u32[]{:S(2)}) %collective-permute-start.3) | collective-permute-done | bytes 65568 | tf_op jit(solution)/shard_map/ppermute | solution.py:85
  34.6 1.9 %collective-permute-start.4 = (f32[2,16,512]{2,1,0:T(8,128)S(1)}, f32[2,16,512]{2,1,0:T(8,128)S(1)}, u32[]{:S(2)}, u32[]{:S(2)}) collective-permute-start(f32[2,16,512]{2,1,0:T(8,128)S(1)} %get-tuple-element.59), channel_id=1, source_target_pairs={{0,64},{64,0},{128,192},{192,128},{256,320},{320,256},{384,448},{4... | collective-permute-start | bytes 196616 | tf_op jit(solution)/shard_map/ppermute | solution.py:85
  36.5 0.7 convolution_add_fusion.3
  37.1 2.4 %collective-permute-done.4 = f32[2,16,512]{2,1,0:T(8,128)S(1)} collective-permute-done((f32[2,16,512]{2,1,0:T(8,128)S(1)}, f32[2,16,512]{2,1,0:T(8,128)S(1)}, u32[]{:S(2)}, u32[]{:S(2)}) %collective-permute-start.4) | collective-permute-done | bytes 65568 | tf_op jit(solution)/shard_map/ppermute | solution.py:85
  39.6 4.6 %collective-permute-start.5 = (f32[2,16,512]{2,1,0:T(8,128)S(1)}, f32[2,16,512]{2,1,0:T(8,128)S(1)}, u32[]{:S(2)}, u32[]{:S(2)}) collective-permute-start(f32[2,16,512]{2,1,0:T(8,128)S(1)} %fusion.153), channel_id=1, source_target_pairs={{0,128},{64,192},{128,0},{192,64},{256,384},{320,448},{384,256},{4... | collective-permute-start | bytes 196616 | tf_op jit(solution)/shard_map/ppermute | solution.py:85
  44.2 0.2 fusion.183
  44.4 0.1 rev.7
  44.5 1.3 %collective-permute-done.5 = f32[2,16,512]{2,1,0:T(8,128)S(1)} collective-permute-done((f32[2,16,512]{2,1,0:T(8,128)S(1)}, f32[2,16,512]{2,1,0:T(8,128)S(1)}, u32[]{:S(2)}, u32[]{:S(2)}) %collective-permute-start.5) | collective-permute-done | bytes 65568 | tf_op jit(solution)/shard_map/ppermute | solution.py:85
  45.9 0.6 fusion.154
  46.5 7.3 %collective-permute-start.6 = (f32[2,16,512]{2,1,0:T(8,128)}, f32[2,16,512]{2,1,0:T(8,128)}, u32[]{:S(2)}, u32[]{:S(2)}) collective-permute-start(f32[2,16,512]{2,1,0:T(8,128)} %fusion.154), channel_id=1, source_target_pairs={{0,256},{64,320},{128,384},{192,448},{256,0},{320,64},{384,128},{4... | collective-permute-start | bytes 196616 | tf_op jit(solution)/shard_map/ppermute | solution.py:85
  53.9 0.1 broadcast_multiply_fusion.2
  54.0 0.1 copy.43
  54.1 0.1 copy.35
  54.2 0.3 concatenate.24
  54.6 5.8 %collective-permute-start.7 = (f32[46,512]{1,0:T(8,128)S(1)}, f32[46,512]{1,0:T(8,128)S(1)}, u32[]{:S(2)}, u32[]{:S(2)}) collective-permute-start(f32[46,512]{1,0:T(8,128)S(1)} %concatenate.24), channel_id=1, source_target_pairs={{8,0},{16,8},{24,16},{32,24},{40,32},{48,40},{56,48},{64,56},{72,6... | collective-permute-start | bytes 282632 | tf_op jit(solution)/shard_map/ppermute | solution.py:19
  60.4 0.1 copy.38
  60.5 0.1 copy.32
  60.7 0.9 %fusion.151 = f32[2,16,512]{2,1,0:T(8,128)S(1)} fusion(f32[2,16,512]{2,1,0:T(8,128)S(1)} %collective-permute-done.4, f32[1,16,512]{2,1,0:T(8,128)S(1)} %copy-done.4, f32[1,16,512]{2,1,0:T(8,128)S(1)} %copy-done.5, f32[2,16,512]{2,1,0:T(8,128)S(1)} %collective-permute-done.5, f32[1,16,512]{2,1,0:T(8,128)S(1)} %copy-done.8, f32[1,16,512]{2,1,0:T(8,128)S(1)} %copy-done.9, ...), kind=kLoop, calls=%fused_computation.238 | loop fusion | flops 131072 | bytes 458752 | tf_op jit(solution)/shard_map/add | solution.py:88
  61.6 1.0 %collective-permute-done.7 = f32[46,512]{1,0:T(8,128)S(1)} collective-permute-done((f32[46,512]{1,0:T(8,128)S(1)}, f32[46,512]{1,0:T(8,128)S(1)}, u32[]{:S(2)}, u32[]{:S(2)}) %collective-permute-start.7) | collective-permute-done | bytes 94240 | tf_op jit(solution)/shard_map/ppermute | solution.py:19
  62.6 0.8 %fusion.3 = bf16[128,512]{1,0:T(8,128)(2,1)S(1)} fusion(f32[128,512]{1,0:T(8,128)S(1)} %copy.38, f32[32,16,128]{2,1,0:T(8,128)S(1)} %broadcast_multiply_fusion.2, f32[16,512]{1,0:T(8,128)S(1)} %get-tuple-element.13, f32[32,512]{1,0:T(8,128)S(1)} %fusion.155), kind=kOutput, calls=%fused_computation.11 | convolution fusion | flops 403046400 | bytes 753664 | tf_op jit(solution)/shard_map/ks,kc->sc/dot_general | solution.py:164
  63.4 0.1 fusion.18
  63.5 0.3 broadcast_multiply_fusion
  63.8 0.6 fusion.164
  64.6 0.6 fusion.128
  65.3 0.8 %fusion.4 = bf16[128,512]{1,0:T(8,128)(2,1)S(1)} fusion(f32[128,512]{1,0:T(8,128)S(1)} %copy.32, f32[32,16,128]{2,1,0:T(8,128)S(1)} %get-tuple-element.44, f32[16,512]{1,0:T(8,128)S(1)} %get-tuple-element.20, f32[32,512]{1,0:T(8,128)S(1)} %fusion.155), kind=kOutput, calls=%fused_computation.12 | convolution fusion | flops 403046400 | bytes 753664 | tf_op jit(solution)/shard_map/kt,kc->tc/dot_general | solution.py:163
  66.1 0.7 %fusion.16 = (bf16[128,512]{1,0:T(8,128)(2,1)S(1)}, bf16[128,512]{1,0:T(8,128)(2,1)}) fusion(bf16[128,512]{1,0:T(8,128)(2,1)S(1)} %fusion.4, bf16[128,512]{1,0:T(8,128)(2,1)S(1)} %copy-done, bf16[128,512]{1,0:T(8,128)(2,1)S(1)} %get-tuple-element.15), kind=kLoop, calls=%fused_computation.70 | loop fusion | flops 458752 | bytes 655360 | tf_op jit(solution)/shard_map/convert_element_type | solution.py:23
  66.9 0.9 %fusion.25 = bf16[128,512]{1,0:T(8,128)(2,1)} fusion(f32[6,512]{1,0:T(8,128)S(1)} %convert_element_type.273, f32[128,512]{1,0:T(8,128)S(1)} %convert_element_type.271, f32[512]{0:T(512)S(1)} %bitcast.181, f32[512]{0:T(512)S(1)} %bitcast.179, f32[512]{0:T(512)S(1)} %bitcast.169, f32[512]{0:T(512)S(1)} %bitcast.171, f32[512]{0:T(512)S(1)} %bitcast.173, ...), kind=kLoop, calls=%fused_computation.79 | loop fusion | flops 1310720 | bytes 419840 | tf_op jit(solution)/shard_map/convert_element_type | solution.py:202
  67.8 0.9 %fusion.42 = bf16[128,512]{1,0:T(8,128)(2,1)} fusion(f32[6,512]{1,0:T(8,128)S(1)} %convert_element_type.268, f32[128,512]{1,0:T(8,128)S(1)} %convert_element_type.264, f32[512]{0:T(512)S(1)} %bitcast.155, f32[512]{0:T(512)S(1)} %bitcast.157, f32[512]{0:T(512)S(1)} %bitcast.159, f32[512]{0:T(512)S(1)} %bitcast.161, f32[512]{0:T(512)S(1)} %bitcast.163, ...), kind=kLoop, calls=%fused_computation.96 | loop fusion | flops 1310720 | bytes 419840 | tf_op jit(solution)/shard_map/convert_element_type | solution.py:201
  68.8 0.9 %fusion.59 = bf16[128,512]{1,0:T(8,128)(2,1)} fusion(f32[6,512]{1,0:T(8,128)S(1)} %convert_element_type.259, f32[128,512]{1,0:T(8,128)S(1)} %convert_element_type.252, f32[512]{0:T(512)S(1)} %bitcast.143, f32[512]{0:T(512)S(1)} %bitcast.145, f32[512]{0:T(512)S(1)} %bitcast.147, f32[512]{0:T(512)S(1)} %bitcast.149, f32[512]{0:T(512)S(1)} %bitcast.151, ...), kind=kLoop, calls=%fused_computation.113 | loop fusion | flops 1310720 | bytes 419840 | tf_op jit(solution)/shard_map/convert_element_type | solution.py:200
  (163 shorter events, 0.8 us)
Async XLA Ops:
  0.6 9.5 %copy-start = (bf16[128,512]{1,0:T(8,128)(2,1)S(1)}, bf16[128,512]{1,0:T(8,128)(2,1)}, u32[]{:S(2)}) copy-start(bf16[128,512]{1,0:T(8,128)(2,1)} %param.13) | copy-start | bytes 393220
  2.1 10.3 %collective-permute-start = (bf16[3,6,512]{2,1,0:T(8,128)(2,1)S(1)}, bf16[3,6,512]{2,1,0:T(8,128)(2,1)S(1)}, u32[]{:S(2)}, u32[]{:S(2)}) collective-permute-start(bf16[3,6,512]{2,1,0:T(8,128)(2,1)S(1)} %pad_maximum_fusion.7), channel_id=1, source_target_pairs={{0,8},{8,16},{16,24},{24,32},{32,40},{40,48},{48,56},{56,64},{64,7... | collective-permute-start | bytes 55304 | tf_op jit(solution)/shard_map/ppermute | solution.py:19
  7.8 4.6 %copy-start.37 = (f32[1,1,512]{2,1,0:T(1,128)}, f32[1,1,512]{2,1,0:T(1,128)S(1)}, u32[]{:S(2)}) copy-start(f32[1,1,512]{2,1,0:T(1,128)S(1)} %get-tuple-element.66) | copy-start | bytes 6148
  7.8 4.6 %copy-start.39 = (f32[1,1,512]{2,1,0:T(1,128)}, f32[1,1,512]{2,1,0:T(1,128)S(1)}, u32[]{:S(2)}) copy-start(f32[1,1,512]{2,1,0:T(1,128)S(1)} %get-tuple-element.67) | copy-start | bytes 6148
  7.8 4.6 %copy-start.41 = (f32[1,1,512]{2,1,0:T(1,128)}, f32[1,1,512]{2,1,0:T(1,128)S(1)}, u32[]{:S(2)}) copy-start(f32[1,1,512]{2,1,0:T(1,128)S(1)} %get-tuple-element.68) | copy-start | bytes 6148
  7.8 4.6 %copy-start.43 = (f32[1,1,512]{2,1,0:T(1,128)}, f32[1,1,512]{2,1,0:T(1,128)S(1)}, u32[]{:S(2)}) copy-start(f32[1,1,512]{2,1,0:T(1,128)S(1)} %get-tuple-element.69) | copy-start | bytes 6148
  7.8 4.6 %copy-start.45 = (f32[1,1,512]{2,1,0:T(1,128)}, f32[1,1,512]{2,1,0:T(1,128)S(1)}, u32[]{:S(2)}) copy-start(f32[1,1,512]{2,1,0:T(1,128)S(1)} %get-tuple-element.70) | copy-start | bytes 6148
  7.9 4.6 %copy-start.47 = (f32[1,1,512]{2,1,0:T(1,128)}, f32[1,1,512]{2,1,0:T(1,128)S(1)}, u32[]{:S(2)}) copy-start(f32[1,1,512]{2,1,0:T(1,128)S(1)} %get-tuple-element.71) | copy-start | bytes 6148
  7.9 4.6 %copy-start.49 = (f32[1,1,512]{2,1,0:T(1,128)}, f32[1,1,512]{2,1,0:T(1,128)S(1)}, u32[]{:S(2)}) copy-start(f32[1,1,512]{2,1,0:T(1,128)S(1)} %get-tuple-element.72) | copy-start | bytes 6148
  7.9 4.6 %copy-start.51 = (f32[1,1,512]{2,1,0:T(1,128)}, f32[1,1,512]{2,1,0:T(1,128)S(1)}, u32[]{:S(2)}) copy-start(f32[1,1,512]{2,1,0:T(1,128)S(1)} %get-tuple-element.61) | copy-start | bytes 6148
  7.9 4.6 %copy-start.53 = (f32[1,1,512]{2,1,0:T(1,128)}, f32[1,1,512]{2,1,0:T(1,128)S(1)}, u32[]{:S(2)}) copy-start(f32[1,1,512]{2,1,0:T(1,128)S(1)} %get-tuple-element.62) | copy-start | bytes 6148
  7.9 4.6 %copy-start.55 = (f32[1,1,512]{2,1,0:T(1,128)}, f32[1,1,512]{2,1,0:T(1,128)S(1)}, u32[]{:S(2)}) copy-start(f32[1,1,512]{2,1,0:T(1,128)S(1)} %get-tuple-element.63) | copy-start | bytes 6148
  7.9 4.6 %copy-start.57 = (f32[1,1,512]{2,1,0:T(1,128)}, f32[1,1,512]{2,1,0:T(1,128)S(1)}, u32[]{:S(2)}) copy-start(f32[1,1,512]{2,1,0:T(1,128)S(1)} %get-tuple-element.64) | copy-start | bytes 6148
  7.9 4.6 %copy-start.59 = (f32[1,1,512]{2,1,0:T(1,128)}, f32[1,1,512]{2,1,0:T(1,128)S(1)}, u32[]{:S(2)}) copy-start(f32[1,1,512]{2,1,0:T(1,128)S(1)} %get-tuple-element.65) | copy-start | bytes 6148
  7.9 5.1 %copy-start.23 = (f32[1,1,512]{2,1,0:T(1,128)}, f32[1,1,512]{2,1,0:T(1,128)S(1)}, u32[]{:S(2)}) copy-start(f32[1,1,512]{2,1,0:T(1,128)S(1)} %get-tuple-element.60) | copy-start | bytes 6148
  7.9 5.1 %copy-start.25 = (f32[1,1,512]{2,1,0:T(1,128)}, f32[1,1,512]{2,1,0:T(1,128)S(1)}, u32[]{:S(2)}) copy-start(f32[1,1,512]{2,1,0:T(1,128)S(1)} %get-tuple-element.73) | copy-start | bytes 6148
  7.9 5.1 %copy-start.27 = (f32[1,1,512]{2,1,0:T(1,128)}, f32[1,1,512]{2,1,0:T(1,128)S(1)}, u32[]{:S(2)}) copy-start(f32[1,1,512]{2,1,0:T(1,128)S(1)} %get-tuple-element.74) | copy-start | bytes 6148
  8.0 5.1 %copy-start.29 = (f32[1,1,512]{2,1,0:T(1,128)}, f32[1,1,512]{2,1,0:T(1,128)S(1)}, u32[]{:S(2)}) copy-start(f32[1,1,512]{2,1,0:T(1,128)S(1)} %get-tuple-element.75) | copy-start | bytes 6148
  8.0 5.1 %copy-start.31 = (f32[1,1,512]{2,1,0:T(1,128)}, f32[1,1,512]{2,1,0:T(1,128)S(1)}, u32[]{:S(2)}) copy-start(f32[1,1,512]{2,1,0:T(1,128)S(1)} %get-tuple-element.76) | copy-start | bytes 6148
  8.0 5.1 %copy-start.33 = (f32[1,1,512]{2,1,0:T(1,128)}, f32[1,1,512]{2,1,0:T(1,128)S(1)}, u32[]{:S(2)}) copy-start(f32[1,1,512]{2,1,0:T(1,128)S(1)} %get-tuple-element.77) | copy-start | bytes 6148
  8.0 5.1 %copy-start.35 = (f32[1,1,512]{2,1,0:T(1,128)}, f32[1,1,512]{2,1,0:T(1,128)S(1)}, u32[]{:S(2)}) copy-start(f32[1,1,512]{2,1,0:T(1,128)S(1)} %get-tuple-element.78) | copy-start | bytes 6148
  8.8 3.7 %copy-start.61 = (f32[1,1,512]{2,1,0:T(1,128)}, f32[1,1,512]{2,1,0:T(1,128)S(1)}, u32[]{:S(2)}) copy-start(f32[1,1,512]{2,1,0:T(1,128)S(1)} %get-tuple-element.79) | copy-start | bytes 6148
  8.8 3.7 %copy-start.63 = (f32[1,1,512]{2,1,0:T(1,128)}, f32[1,1,512]{2,1,0:T(1,128)S(1)}, u32[]{:S(2)}) copy-start(f32[1,1,512]{2,1,0:T(1,128)S(1)} %get-tuple-element.80) | copy-start | bytes 6148
  14.2 7.1 %copy-start.22 = (f32[32,16]{0,1:T(8,128)S(1)}, f32[32,16]{0,1:T(8,128)}, u32[]{:S(2)}) copy-start(f32[32,16]{0,1:T(8,128)} %param.11) | copy-start | bytes 6148
  14.8 6.4 %collective-permute-start.1 = (f32[2,16,512]{2,1,0:T(8,128)S(1)}, f32[2,16,512]{2,1,0:T(8,128)S(1)}, u32[]{:S(2)}, u32[]{:S(2)}) collective-permute-start(f32[2,16,512]{2,1,0:T(8,128)S(1)} %pad_maximum_fusion.6), channel_id=1, source_target_pairs={{0,8},{8,0},{16,24},{24,16},{32,40},{40,32},{48,56},{56,48},{1,9},... | collective-permute-start | bytes 196616 | tf_op jit(solution)/shard_map/ppermute | solution.py:85
  21.4 6.5 %collective-permute-start.2 = (f32[2,16,512]{2,1,0:T(8,128)S(1)}, f32[2,16,512]{2,1,0:T(8,128)S(1)}, u32[]{:S(2)}, u32[]{:S(2)}) collective-permute-start(f32[2,16,512]{2,1,0:T(8,128)S(1)} %fusion.148), channel_id=1, source_target_pairs={{0,16},{8,24},{16,0},{24,8},{32,48},{40,56},{48,32},{56,40},{1,17}... | collective-permute-start | bytes 196616 | tf_op jit(solution)/shard_map/ppermute | solution.py:85
  27.8 6.6 %copy-start.10 = (f32[1,16,512]{2,1,0:T(8,128)S(1)}, f32[1,16,512]{2,1,0:T(8,128)}, u32[]{:S(2)}) copy-start(f32[1,16,512]{2,1,0:T(8,128)} %get-tuple-element.34) | copy-start | bytes 98308
  27.8 6.6 %copy-start.11 = (f32[1,16,512]{2,1,0:T(8,128)S(1)}, f32[1,16,512]{2,1,0:T(8,128)}, u32[]{:S(2)}) copy-start(f32[1,16,512]{2,1,0:T(8,128)} %get-tuple-element.39) | copy-start | bytes 98308
  27.8 6.6 %copy-start.12 = (f32[1,16,512]{2,1,0:T(8,128)S(1)}, f32[1,16,512]{2,1,0:T(8,128)}, u32[]{:S(2)}) copy-start(f32[1,16,512]{2,1,0:T(8,128)} %get-tuple-element.40) | copy-start | bytes 98308
  27.8 6.6 %copy-start.13 = (f32[1,16,512]{2,1,0:T(8,128)S(1)}, f32[1,16,512]{2,1,0:T(8,128)}, u32[]{:S(2)}) copy-start(f32[1,16,512]{2,1,0:T(8,128)} %get-tuple-element.41) | copy-start | bytes 98308
  27.8 6.6 %copy-start.14 = (f32[1,16,512]{2,1,0:T(8,128)S(1)}, f32[1,16,512]{2,1,0:T(8,128)}, u32[]{:S(2)}) copy-start(f32[1,16,512]{2,1,0:T(8,128)} %get-tuple-element.42) | copy-start | bytes 98308
  27.8 6.6 %copy-start.15 = (f32[1,16,512]{2,1,0:T(8,128)S(1)}, f32[1,16,512]{2,1,0:T(8,128)}, u32[]{:S(2)}) copy-start(f32[1,16,512]{2,1,0:T(8,128)} %get-tuple-element.21) | copy-start | bytes 98308
  27.8 6.6 %copy-start.16 = (f32[1,16,512]{2,1,0:T(8,128)S(1)}, f32[1,16,512]{2,1,0:T(8,128)}, u32[]{:S(2)}) copy-start(f32[1,16,512]{2,1,0:T(8,128)} %get-tuple-element.23) | copy-start | bytes 98308
  27.9 6.6 %copy-start.17 = (f32[1,16,512]{2,1,0:T(8,128)S(1)}, f32[1,16,512]{2,1,0:T(8,128)}, u32[]{:S(2)}) copy-start(f32[1,16,512]{2,1,0:T(8,128)} %get-tuple-element.33) | copy-start | bytes 98308
  27.9 6.5 %collective-permute-start.3 = (f32[2,16,512]{2,1,0:T(8,128)S(1)}, f32[2,16,512]{2,1,0:T(8,128)S(1)}, u32[]{:S(2)}, u32[]{:S(2)}) collective-permute-start(f32[2,16,512]{2,1,0:T(8,128)S(1)} %fusion.149), channel_id=1, source_target_pairs={{0,32},{8,40},{16,48},{24,56},{32,0},{40,8},{48,16},{56,24},{1,33}... | collective-permute-start | bytes 196616 | tf_op jit(solution)/shard_map/ppermute | solution.py:85
  34.6 11.3 %copy-start.20 = (f32[1,16,512]{2,1,0:T(8,128)S(1)}, f32[1,16,512]{2,1,0:T(8,128)}, u32[]{:S(2)}) copy-start(f32[1,16,512]{2,1,0:T(8,128)} %get-tuple-element.25) | copy-start | bytes 98308
  34.6 5.0 %collective-permute-start.4 = (f32[2,16,512]{2,1,0:T(8,128)S(1)}, f32[2,16,512]{2,1,0:T(8,128)S(1)}, u32[]{:S(2)}, u32[]{:S(2)}) collective-permute-start(f32[2,16,512]{2,1,0:T(8,128)S(1)} %get-tuple-element.59), channel_id=1, source_target_pairs={{0,64},{64,0},{128,192},{192,128},{256,320},{320,256},{384,448},{4... | collective-permute-start | bytes 196616 | tf_op jit(solution)/shard_map/ppermute | solution.py:85
  37.1 17.1 %copy-start.21 = (f32[6,512]{1,0:T(8,128)S(1)}, f32[6,512]{1,0:T(8,128)}, u32[]{:S(2)}) copy-start(f32[6,512]{1,0:T(8,128)} %slice_convert_fusion.1) | copy-start | bytes 36868
  39.6 21.1 %copy-start.4 = (f32[1,16,512]{2,1,0:T(8,128)S(1)}, f32[1,16,512]{2,1,0:T(8,128)}, u32[]{:S(2)}) copy-start(f32[1,16,512]{2,1,0:T(8,128)} %get-tuple-element.35) | copy-start | bytes 98308
  39.6 21.1 %copy-start.5 = (f32[1,16,512]{2,1,0:T(8,128)S(1)}, f32[1,16,512]{2,1,0:T(8,128)}, u32[]{:S(2)}) copy-start(f32[1,16,512]{2,1,0:T(8,128)} %get-tuple-element.36) | copy-start | bytes 98308
  39.6 21.1 %copy-start.6 = (f32[1,16,512]{2,1,0:T(8,128)S(1)}, f32[1,16,512]{2,1,0:T(8,128)}, u32[]{:S(2)}) copy-start(f32[1,16,512]{2,1,0:T(8,128)} %get-tuple-element.28) | copy-start | bytes 98308
  39.6 21.1 %copy-start.7 = (f32[1,16,512]{2,1,0:T(8,128)S(1)}, f32[1,16,512]{2,1,0:T(8,128)}, u32[]{:S(2)}) copy-start(f32[1,16,512]{2,1,0:T(8,128)} %get-tuple-element.29) | copy-start | bytes 98308
  39.6 21.1 %copy-start.8 = (f32[1,16,512]{2,1,0:T(8,128)S(1)}, f32[1,16,512]{2,1,0:T(8,128)}, u32[]{:S(2)}) copy-start(f32[1,16,512]{2,1,0:T(8,128)} %get-tuple-element.31) | copy-start | bytes 98308
  39.6 21.1 %copy-start.9 = (f32[1,16,512]{2,1,0:T(8,128)S(1)}, f32[1,16,512]{2,1,0:T(8,128)}, u32[]{:S(2)}) copy-start(f32[1,16,512]{2,1,0:T(8,128)} %get-tuple-element.32) | copy-start | bytes 98308
  39.6 6.2 %collective-permute-start.5 = (f32[2,16,512]{2,1,0:T(8,128)S(1)}, f32[2,16,512]{2,1,0:T(8,128)S(1)}, u32[]{:S(2)}, u32[]{:S(2)}) collective-permute-start(f32[2,16,512]{2,1,0:T(8,128)S(1)} %fusion.153), channel_id=1, source_target_pairs={{0,128},{64,192},{128,0},{192,64},{256,384},{320,448},{384,256},{4... | collective-permute-start | bytes 196616 | tf_op jit(solution)/shard_map/ppermute | solution.py:85
  46.5 14.1 %collective-permute-start.6 = (f32[2,16,512]{2,1,0:T(8,128)}, f32[2,16,512]{2,1,0:T(8,128)}, u32[]{:S(2)}, u32[]{:S(2)}) collective-permute-start(f32[2,16,512]{2,1,0:T(8,128)} %fusion.154), channel_id=1, source_target_pairs={{0,256},{64,320},{128,384},{192,448},{256,0},{320,64},{384,128},{4... | collective-permute-start | bytes 196616 | tf_op jit(solution)/shard_map/ppermute | solution.py:85
  54.6 8.0 %collective-permute-start.7 = (f32[46,512]{1,0:T(8,128)S(1)}, f32[46,512]{1,0:T(8,128)S(1)}, u32[]{:S(2)}, u32[]{:S(2)}) collective-permute-start(f32[46,512]{1,0:T(8,128)S(1)} %concatenate.24), channel_id=1, source_target_pairs={{8,0},{16,8},{24,16},{32,24},{40,32},{48,40},{56,48},{64,56},{72,6... | collective-permute-start | bytes 282632 | tf_op jit(solution)/shard_map/ppermute | solution.py:19
  64.4 2.5 %copy-start.56 = (f32[1,1,512]{2,1,0:T(1,128)S(1)}, f32[1,1,512]{2,1,0:T(1,128)}, u32[]{:S(2)}) copy-start(f32[1,1,512]{2,1,0:T(1,128)} %copy-done.55) | copy-start | bytes 6148
  64.4 2.5 %copy-start.58 = (f32[1,1,512]{2,1,0:T(1,128)S(1)}, f32[1,1,512]{2,1,0:T(1,128)}, u32[]{:S(2)}) copy-start(f32[1,1,512]{2,1,0:T(1,128)} %copy-done.57) | copy-start | bytes 6148
  64.4 2.5 %copy-start.60 = (f32[1,1,512]{2,1,0:T(1,128)S(1)}, f32[1,1,512]{2,1,0:T(1,128)}, u32[]{:S(2)}) copy-start(f32[1,1,512]{2,1,0:T(1,128)} %copy-done.59) | copy-start | bytes 6148
  64.5 3.3 %copy-start.38 = (f32[1,1,512]{2,1,0:T(1,128)S(1)}, f32[1,1,512]{2,1,0:T(1,128)}, u32[]{:S(2)}) copy-start(f32[1,1,512]{2,1,0:T(1,128)} %copy-done.37) | copy-start | bytes 6148
  64.5 3.3 %copy-start.40 = (f32[1,1,512]{2,1,0:T(1,128)S(1)}, f32[1,1,512]{2,1,0:T(1,128)}, u32[]{:S(2)}) copy-start(f32[1,1,512]{2,1,0:T(1,128)} %copy-done.39) | copy-start | bytes 6148
  64.5 3.3 %copy-start.42 = (f32[1,1,512]{2,1,0:T(1,128)S(1)}, f32[1,1,512]{2,1,0:T(1,128)}, u32[]{:S(2)}) copy-start(f32[1,1,512]{2,1,0:T(1,128)} %copy-done.41) | copy-start | bytes 6148
  64.5 3.3 %copy-start.44 = (f32[1,1,512]{2,1,0:T(1,128)S(1)}, f32[1,1,512]{2,1,0:T(1,128)}, u32[]{:S(2)}) copy-start(f32[1,1,512]{2,1,0:T(1,128)} %copy-done.43) | copy-start | bytes 6148
  64.5 3.3 %copy-start.46 = (f32[1,1,512]{2,1,0:T(1,128)S(1)}, f32[1,1,512]{2,1,0:T(1,128)}, u32[]{:S(2)}) copy-start(f32[1,1,512]{2,1,0:T(1,128)} %copy-done.45) | copy-start | bytes 6148
  64.5 3.3 %copy-start.48 = (f32[1,1,512]{2,1,0:T(1,128)S(1)}, f32[1,1,512]{2,1,0:T(1,128)}, u32[]{:S(2)}) copy-start(f32[1,1,512]{2,1,0:T(1,128)} %copy-done.47) | copy-start | bytes 6148
  64.5 3.3 %copy-start.50 = (f32[1,1,512]{2,1,0:T(1,128)S(1)}, f32[1,1,512]{2,1,0:T(1,128)}, u32[]{:S(2)}) copy-start(f32[1,1,512]{2,1,0:T(1,128)} %copy-done.49) | copy-start | bytes 6148
  64.5 4.2 %copy-start.24 = (f32[1,1,512]{2,1,0:T(1,128)S(1)}, f32[1,1,512]{2,1,0:T(1,128)}, u32[]{:S(2)}) copy-start(f32[1,1,512]{2,1,0:T(1,128)} %copy-done.23) | copy-start | bytes 6148
  64.5 4.2 %copy-start.26 = (f32[1,1,512]{2,1,0:T(1,128)S(1)}, f32[1,1,512]{2,1,0:T(1,128)}, u32[]{:S(2)}) copy-start(f32[1,1,512]{2,1,0:T(1,128)} %copy-done.25) | copy-start | bytes 6148
  64.5 4.2 %copy-start.28 = (f32[1,1,512]{2,1,0:T(1,128)S(1)}, f32[1,1,512]{2,1,0:T(1,128)}, u32[]{:S(2)}) copy-start(f32[1,1,512]{2,1,0:T(1,128)} %copy-done.27) | copy-start | bytes 6148
  64.6 4.2 %copy-start.30 = (f32[1,1,512]{2,1,0:T(1,128)S(1)}, f32[1,1,512]{2,1,0:T(1,128)}, u32[]{:S(2)}) copy-start(f32[1,1,512]{2,1,0:T(1,128)} %copy-done.29) | copy-start | bytes 6148
  64.6 4.2 %copy-start.32 = (f32[1,1,512]{2,1,0:T(1,128)S(1)}, f32[1,1,512]{2,1,0:T(1,128)}, u32[]{:S(2)}) copy-start(f32[1,1,512]{2,1,0:T(1,128)} %copy-done.31) | copy-start | bytes 6148
  64.6 4.2 %copy-start.34 = (f32[1,1,512]{2,1,0:T(1,128)S(1)}, f32[1,1,512]{2,1,0:T(1,128)}, u32[]{:S(2)}) copy-start(f32[1,1,512]{2,1,0:T(1,128)} %copy-done.33) | copy-start | bytes 6148
  64.6 4.2 %copy-start.36 = (f32[1,1,512]{2,1,0:T(1,128)S(1)}, f32[1,1,512]{2,1,0:T(1,128)}, u32[]{:S(2)}) copy-start(f32[1,1,512]{2,1,0:T(1,128)} %copy-done.35) | copy-start | bytes 6148
  (9 other events, 18.5 us)

commit v15 on v14

--- a/solution.py
+++ b/solution.py
@@ -21,6 +21,10 @@
 
 def rounded(values):
     return lax.optimization_barrier(values.astype(jnp.bfloat16))
+
+
+def to_bf16(values):
+    return lax.reduce_precision(values, exponent_bits=8, mantissa_bits=7).astype(jnp.bfloat16)
 
 
 def short_causal(prior_rows, inputs, filter_taps):
@@ -102,9 +106,9 @@
         ]
     )
     before = from_behind(rim_rows, ("zl", "xc"), 1)
-    q_short = short_causal(before[0], u_query, short_filter[0]).astype(jnp.bfloat16)
-    k_short = short_causal(before[1], u_key, short_filter[1]).astype(jnp.bfloat16)
-    v_short = short_causal(before[2], u_value, short_filter[2]).astype(jnp.bfloat16)
+    q_short = to_bf16(short_causal(before[0], u_query, short_filter[0]))
+    k_short = to_bf16(short_causal(before[1], u_key, short_filter[1]))
+    v_short = to_bf16(short_causal(before[2], u_value, short_filter[2]))
     product = rounded(k_short.astype(jnp.float32) * v_short.astype(jnp.float32))
     grad_conv = rounded(grad_out.astype(jnp.float32) * q_short.astype(jnp.float32))
 

time: 71 us -> 71 us (level)
  no operation moved by 1% of the time
where the time goes in v15:
time: 71 us; the launch traced here: 69.7 us
  starting transfers between devices  34.2 us (48%)
  other arithmetic  10.1 us (14%)
  matrix products  9.64 us (14%)
  waiting for transfers between devices  8.06 us (11%)
  local copies, waits for them, and re-layouts  5.65 us (8%)
  between operations  2.05 us (3%)
    ppermute x6, starting transfers between devices, cube_scan(): lax.ppermute(window, axis, [(source, source ^ shift) for source in range(...  23.9 us
    ppermute x2, starting transfers between devices, from_behind(): lax.ppermute(value, axis, [(source, source + steps) for source in range(l...  10.3 us
    ppermute x6, waiting for transfers between devices, cube_scan(): lax.ppermute(window, axis, [(source, source ^ shift) for source in range(...  7.04 us
    dot_general x1, matrix products, shards(): toeplitz = jnp.einsum('gtm,gms->gts', falling, rising, precision=precise)  3.65 us
    slice x2, local copies, waits for them, and re-layouts, short_causal(): filter_taps[offset] * padded[SHORT - 1 - offset:SHORT - 1 - offset + length]  1.97 us
    dot_general x4, matrix products, split_dot(): jnp.einsum(spec, low, values, preferred_element_type=jnp.float32)  1.63 us
    dot_general x4, matrix products, split_dot(): jnp.einsum(spec, high.astype(jnp.bfloat16), values, preferred_element_typ...  1.56 us
    convert_element_type x6, other arithmetic, rounded(): return lax.optimization_barrier(values.astype(jnp.bfloat16))  1.55 us
  transfers between devices with their start and end apart: 8, of which 4 were waited for; matrix products, arithmetic and copies ran while one was open for 20% of the time, Pallas kernels for 0%

profile of v15, /device:TPU:1, one launch (start us, length us, event | category | flops | bytes accessed | tf_op | source)
XLA Modules:
  0.0 69.7 jit_solution(16370548836060587590)
XLA Ops:
  0.6 0.7 %slice_bitcast_fusion.6 = bf16[1,6,512]{2,1,0:T(8,128)(2,1)S(1)} fusion(bf16[128,512]{1,0:T(8,128)(2,1)} %param.7), kind=kLoop, calls=%fused_computation.313 | loop fusion | bytes 12288 | tf_op jit(solution)/shard_map/stack | solution.py:101
  1.4 0.7 %slice_bitcast_fusion.4 = (bf16[1,6,512]{2,1,0:T(8,128)(2,1)S(1)}, bf16[1,6,512]{2,1,0:T(8,128)(2,1)S(1)}) fusion(bf16[128,512]{1,0:T(8,128)(2,1)} %param.9, bf16[128,512]{1,0:T(8,128)(2,1)} %param.8), kind=kLoop, calls=%fused_computation.311 | loop fusion | bytes 24576 | tf_op jit(solution)/shard_map/stack | solution.py:101
  2.1 4.5 %collective-permute-start = (bf16[3,6,512]{2,1,0:T(8,128)(2,1)S(1)}, bf16[3,6,512]{2,1,0:T(8,128)(2,1)S(1)}, u32[]{:S(2)}, u32[]{:S(2)}) collective-permute-start(bf16[3,6,512]{2,1,0:T(8,128)(2,1)S(1)} %pad_maximum_fusion.7), channel_id=1, source_target_pairs={{0,8},{8,16},{16,24},{24,32},{32,40},{40,48},{48,56},{56,64},{64,7... | collective-permute-start | bytes 55304 | tf_op jit(solution)/shard_map/ppermute | solution.py:19
  6.6 1.2 %fusion.187 = (f32[1,1,512]{2,1,0:T(1,128)S(1)}, f32[1,1,512]{2,1,0:T(1,128)S(1)}, f32[1,1,512]{2,1,0:T(1,128)S(1)}, f32[1,1,512]{2,1,0:T(1,128)S(1)}, f32[1,1,5...) fusion(f32[3,7,512]{2,1,0:T(8,128)} %param.10), kind=kLoop, calls=%fused_computation.330 | loop fusion | bytes 77824 | tf_op jit(solution)/shard_map/slice | solution.py:36
  8.0 0.8 %fusion.188 = (f32[1,1,512]{2,1,0:T(1,128)S(1)}, f32[1,1,512]{2,1,0:T(1,128)S(1)}) fusion(f32[3,7,512]{2,1,0:T(8,128)} %param.10), kind=kLoop, calls=%fused_computation.331 | loop fusion | bytes 8192 | tf_op jit(solution)/shard_map/slice | solution.py:36
  8.8 0.7 %negate_bitcast_fusion = (f32[16,32]{1,0:T(8,128)S(1)}, f32[32,16]{0,1:T(8,128)S(1)}, f32[32,16]{0,1:T(8,128)S(1)}) fusion(f32[32,16]{0,1:T(8,128)} %param.11, f32[32,16]{0,1:T(8,128)} %param.12), kind=kLoop, calls=%fused_computation.309 | loop fusion | flops 3072 | bytes 10240 | tf_op jit(solution)/shard_map/neg | solution.py:145
  9.6 0.1 copy.25
  9.6 0.1 multiply_exponential_fusion.1
  9.8 0.1 rev.6
  10.2 0.1 broadcast_in_dim.12
  10.4 0.2 neg.35
  10.5 0.1 stack.155
  10.6 0.2 multiply_exponential_fusion
  10.8 0.7 %slice_select_fusion.6 = (f32[1,16,512]{2,1,0:T(8,128)}, f32[1,16,512]{2,1,0:T(8,128)}, f32[1,16,512]{2,1,0:T(8,128)}, f32[1,16,512]{2,1,0:T(8,128)}, f32[1,16,5...) fusion(f32[22,16,512]{2,1,0:T(8,128)S(1)} %multiply_exponential, ...), kind=kLoop, calls=%fused_computation.273 | loop fusion | flops 73728 | bytes 589828 | tf_op jit(solution)/shard_map/jit(_where)/select_n | solution.py:78
  11.5 0.7 %slice_select_fusion.7 = (f32[1,16,512]{2,1,0:T(8,128)}, f32[1,16,512]{2,1,0:T(8,128)}, f32[1,16,512]{2,1,0:T(8,128)}, f32[1,16,512]{2,1,0:T(8,128)S(1)}, f32[1,...) fusion(f32[22,16,512]{2,1,0:T(8,128)S(1)} %multiply_exponential, ...), kind=kLoop, calls=%fused_computation.274 | loop fusion | flops 106496 | bytes 753670 | tf_op jit(solution)/shard_map/jit(_where)/select_n | solution.py:78
  12.5 0.5 fusion.13
  13.1 0.3 fusion.14
  13.4 0.3 fusion.189
  13.7 0.3 convolution_add_fusion.1
  14.0 0.3 fusion.190
  14.2 0.3 convolution_add_fusion
  14.5 0.3 multiply_reduce_fusion.1
  14.8 5.6 %collective-permute-start.1 = (f32[2,16,512]{2,1,0:T(8,128)S(1)}, f32[2,16,512]{2,1,0:T(8,128)S(1)}, u32[]{:S(2)}, u32[]{:S(2)}) collective-permute-start(f32[2,16,512]{2,1,0:T(8,128)S(1)} %pad_maximum_fusion.6), channel_id=1, source_target_pairs={{0,8},{8,0},{16,24},{24,16},{32,40},{40,32},{48,56},{56,48},{1,9},... | collective-permute-start | bytes 196616 | tf_op jit(solution)/shard_map/ppermute | solution.py:89
  20.4 0.6 slice_convert_fusion.1
  21.0 0.1 copy.33
  21.1 0.1 copy.24
  21.2 0.0 collective-permute-done.1
  21.3 0.1 copy.26
  21.3 0.1 copy.27
  21.4 1.9 %collective-permute-start.2 = (f32[2,16,512]{2,1,0:T(8,128)S(1)}, f32[2,16,512]{2,1,0:T(8,128)S(1)}, u32[]{:S(2)}, u32[]{:S(2)}) collective-permute-start(f32[2,16,512]{2,1,0:T(8,128)S(1)} %fusion.151), channel_id=1, source_target_pairs={{0,16},{8,24},{16,0},{24,8},{32,48},{40,56},{48,32},{56,40},{1,17}... | collective-permute-start | bytes 196616 | tf_op jit(solution)/shard_map/ppermute | solution.py:89
  23.4 3.7 %fusion.136 = f32[32,128,128]{2,1,0:T(8,128)S(1)} fusion(f32[32,16]{1,0:T(8,128)S(1)} %copy.27, f32[128]{0:T(128)S(1)} %get-tuple-element.89, f32[128]{0:T(128)S(1)} %get-tuple-element.90, f32[32,16]{1,0:T(8,128)S(1)} %copy.26), kind=kOutput, calls=%fused_computation.214 | convolution fusion | flops 100859904 | bytes 2102272 | tf_op jit(solution)/shard_map/gtm,gms->gts/dot_general | solution.py:158
  27.0 0.4 fusion.11
  27.4 0.4 convolution_add_fusion.2
  28.0 2.6 %collective-permute-start.3 = (f32[2,16,512]{2,1,0:T(8,128)S(1)}, f32[2,16,512]{2,1,0:T(8,128)S(1)}, u32[]{:S(2)}, u32[]{:S(2)}) collective-permute-start(f32[2,16,512]{2,1,0:T(8,128)S(1)} %fusion.152), channel_id=1, source_target_pairs={{0,32},{8,40},{16,48},{24,56},{32,0},{40,8},{48,16},{56,24},{1,33}... | collective-permute-start | bytes 196616 | tf_op jit(solution)/shard_map/ppermute | solution.py:89
  30.5 0.6 fusion.12
  31.2 3.3 %collective-permute-done.3 = f32[2,16,512]{2,1,0:T(8,128)S(1)} collective-permute-done((f32[2,16,512]{2,1,0:T(8,128)S(1)}, f32[2,16,512]{2,1,0:T(8,128)S(1)}, u32[]{:S(2)}, u32[]{:S(2)}) %collective-permute-start.3) | collective-permute-done | bytes 65568 | tf_op jit(solution)/shard_map/ppermute | solution.py:89
  34.6 1.9 %collective-permute-start.4 = (f32[2,16,512]{2,1,0:T(8,128)S(1)}, f32[2,16,512]{2,1,0:T(8,128)S(1)}, u32[]{:S(2)}, u32[]{:S(2)}) collective-permute-start(f32[2,16,512]{2,1,0:T(8,128)S(1)} %get-tuple-element.59), channel_id=1, source_target_pairs={{0,64},{64,0},{128,192},{192,128},{256,320},{320,256},{384,448},{4... | collective-permute-start | bytes 196616 | tf_op jit(solution)/shard_map/ppermute | solution.py:89
  36.5 0.7 convolution_add_fusion.3
  37.2 2.4 %collective-permute-done.4 = f32[2,16,512]{2,1,0:T(8,128)S(1)} collective-permute-done((f32[2,16,512]{2,1,0:T(8,128)S(1)}, f32[2,16,512]{2,1,0:T(8,128)S(1)}, u32[]{:S(2)}, u32[]{:S(2)}) %collective-permute-start.4) | collective-permute-done | bytes 65568 | tf_op jit(solution)/shard_map/ppermute | solution.py:89
  39.7 4.6 %collective-permute-start.5 = (f32[2,16,512]{2,1,0:T(8,128)S(1)}, f32[2,16,512]{2,1,0:T(8,128)S(1)}, u32[]{:S(2)}, u32[]{:S(2)}) collective-permute-start(f32[2,16,512]{2,1,0:T(8,128)S(1)} %fusion.156), channel_id=1, source_target_pairs={{0,128},{64,192},{128,0},{192,64},{256,384},{320,448},{384,256},{4... | collective-permute-start | bytes 196616 | tf_op jit(solution)/shard_map/ppermute | solution.py:89
  44.2 0.2 fusion.186
  44.4 0.1 rev.7
  44.6 1.3 %collective-permute-done.5 = f32[2,16,512]{2,1,0:T(8,128)S(1)} collective-permute-done((f32[2,16,512]{2,1,0:T(8,128)S(1)}, f32[2,16,512]{2,1,0:T(8,128)S(1)}, u32[]{:S(2)}, u32[]{:S(2)}) %collective-permute-start.5) | collective-permute-done | bytes 65568 | tf_op jit(solution)/shard_map/ppermute | solution.py:89
  45.9 0.6 fusion.157
  46.5 7.3 %collective-permute-start.6 = (f32[2,16,512]{2,1,0:T(8,128)}, f32[2,16,512]{2,1,0:T(8,128)}, u32[]{:S(2)}, u32[]{:S(2)}) collective-permute-start(f32[2,16,512]{2,1,0:T(8,128)} %fusion.157), channel_id=1, source_target_pairs={{0,256},{64,320},{128,384},{192,448},{256,0},{320,64},{384,128},{4... | collective-permute-start | bytes 196616 | tf_op jit(solution)/shard_map/ppermute | solution.py:89
  53.9 0.1 broadcast_multiply_fusion.2
  54.0 0.1 copy.43
  54.1 0.1 copy.35
  54.2 0.3 concatenate.24
  54.6 5.8 %collective-permute-start.7 = (f32[46,512]{1,0:T(8,128)S(1)}, f32[46,512]{1,0:T(8,128)S(1)}, u32[]{:S(2)}, u32[]{:S(2)}) collective-permute-start(f32[46,512]{1,0:T(8,128)S(1)} %concatenate.24), channel_id=1, source_target_pairs={{8,0},{16,8},{24,16},{32,24},{40,32},{48,40},{56,48},{64,56},{72,6... | collective-permute-start | bytes 282632 | tf_op jit(solution)/shard_map/ppermute | solution.py:19
  60.4 0.1 copy.38
  60.5 0.1 copy.32
  60.7 0.9 %fusion.154 = f32[2,16,512]{2,1,0:T(8,128)S(1)} fusion(f32[2,16,512]{2,1,0:T(8,128)S(1)} %collective-permute-done.4, f32[1,16,512]{2,1,0:T(8,128)S(1)} %copy-done.4, f32[1,16,512]{2,1,0:T(8,128)S(1)} %copy-done.5, f32[2,16,512]{2,1,0:T(8,128)S(1)} %collective-permute-done.5, f32[1,16,512]{2,1,0:T(8,128)S(1)} %copy-done.8, f32[1,16,512]{2,1,0:T(8,128)S(1)} %copy-done.9, ...), kind=kLoop, calls=%fused_computation.241 | loop fusion | flops 131072 | bytes 458752 | tf_op jit(solution)/shard_map/add | solution.py:92
  61.6 1.0 %collective-permute-done.7 = f32[46,512]{1,0:T(8,128)S(1)} collective-permute-done((f32[46,512]{1,0:T(8,128)S(1)}, f32[46,512]{1,0:T(8,128)S(1)}, u32[]{:S(2)}, u32[]{:S(2)}) %collective-permute-start.7) | collective-permute-done | bytes 94240 | tf_op jit(solution)/shard_map/ppermute | solution.py:19
  62.7 0.8 %fusion.3 = bf16[128,512]{1,0:T(8,128)(2,1)S(1)} fusion(f32[128,512]{1,0:T(8,128)S(1)} %copy.38, f32[32,16,128]{2,1,0:T(8,128)S(1)} %broadcast_multiply_fusion.2, f32[16,512]{1,0:T(8,128)S(1)} %get-tuple-element.13, f32[32,512]{1,0:T(8,128)S(1)} %fusion.158), kind=kOutput, calls=%fused_computation.11 | convolution fusion | flops 403046400 | bytes 753664 | tf_op jit(solution)/shard_map/ks,kc->sc/dot_general | solution.py:168
  63.5 0.1 fusion.18
  63.5 0.3 broadcast_multiply_fusion
  63.8 0.6 fusion.167
  64.6 0.6 fusion.131
  65.3 0.8 %fusion.4 = bf16[128,512]{1,0:T(8,128)(2,1)S(1)} fusion(f32[128,512]{1,0:T(8,128)S(1)} %copy.32, f32[32,16,128]{2,1,0:T(8,128)S(1)} %get-tuple-element.44, f32[16,512]{1,0:T(8,128)S(1)} %get-tuple-element.20, f32[32,512]{1,0:T(8,128)S(1)} %fusion.158), kind=kOutput, calls=%fused_computation.12 | convolution fusion | flops 403046400 | bytes 753664 | tf_op jit(solution)/shard_map/kt,kc->tc/dot_general | solution.py:167
  66.1 0.7 %fusion.16 = (bf16[128,512]{1,0:T(8,128)(2,1)S(1)}, bf16[128,512]{1,0:T(8,128)(2,1)}) fusion(bf16[128,512]{1,0:T(8,128)(2,1)S(1)} %fusion.4, bf16[128,512]{1,0:T(8,128)(2,1)S(1)} %copy-done, bf16[128,512]{1,0:T(8,128)(2,1)S(1)} %get-tuple-element.15), kind=kLoop, calls=%fused_computation.70 | loop fusion | flops 458752 | bytes 655360 | tf_op jit(solution)/shard_map/convert_element_type | solution.py:23
  66.9 0.9 %fusion.25 = bf16[128,512]{1,0:T(8,128)(2,1)} fusion(f32[6,512]{1,0:T(8,128)S(1)} %convert_element_type.273, f32[128,512]{1,0:T(8,128)S(1)} %convert_element_type.271, f32[512]{0:T(512)S(1)} %bitcast.181, f32[512]{0:T(512)S(1)} %bitcast.179, f32[512]{0:T(512)S(1)} %bitcast.169, f32[512]{0:T(512)S(1)} %bitcast.171, f32[512]{0:T(512)S(1)} %bitcast.173, ...), kind=kLoop, calls=%fused_computation.79 | loop fusion | flops 1310720 | bytes 419840 | tf_op jit(solution)/shard_map/convert_element_type | solution.py:206
  67.9 0.9 %fusion.42 = bf16[128,512]{1,0:T(8,128)(2,1)} fusion(f32[6,512]{1,0:T(8,128)S(1)} %convert_element_type.268, f32[128,512]{1,0:T(8,128)S(1)} %convert_element_type.264, f32[512]{0:T(512)S(1)} %bitcast.155, f32[512]{0:T(512)S(1)} %bitcast.157, f32[512]{0:T(512)S(1)} %bitcast.159, f32[512]{0:T(512)S(1)} %bitcast.161, f32[512]{0:T(512)S(1)} %bitcast.163, ...), kind=kLoop, calls=%fused_computation.96 | loop fusion | flops 1310720 | bytes 419840 | tf_op jit(solution)/shard_map/convert_element_type | solution.py:205
  68.8 0.9 %fusion.59 = bf16[128,512]{1,0:T(8,128)(2,1)} fusion(f32[6,512]{1,0:T(8,128)S(1)} %convert_element_type.259, f32[128,512]{1,0:T(8,128)S(1)} %convert_element_type.252, f32[512]{0:T(512)S(1)} %bitcast.143, f32[512]{0:T(512)S(1)} %bitcast.145, f32[512]{0:T(512)S(1)} %bitcast.147, f32[512]{0:T(512)S(1)} %bitcast.149, f32[512]{0:T(512)S(1)} %bitcast.151, ...), kind=kLoop, calls=%fused_computation.113 | loop fusion | flops 1310720 | bytes 419840 | tf_op jit(solution)/shard_map/convert_element_type | solution.py:204
  (163 shorter events, 0.8 us)
Async XLA Ops:
  0.6 9.5 %copy-start = (bf16[128,512]{1,0:T(8,128)(2,1)S(1)}, bf16[128,512]{1,0:T(8,128)(2,1)}, u32[]{:S(2)}) copy-start(bf16[128,512]{1,0:T(8,128)(2,1)} %param.13) | copy-start | bytes 393220
  2.1 10.3 %collective-permute-start = (bf16[3,6,512]{2,1,0:T(8,128)(2,1)S(1)}, bf16[3,6,512]{2,1,0:T(8,128)(2,1)S(1)}, u32[]{:S(2)}, u32[]{:S(2)}) collective-permute-start(bf16[3,6,512]{2,1,0:T(8,128)(2,1)S(1)} %pad_maximum_fusion.7), channel_id=1, source_target_pairs={{0,8},{8,16},{16,24},{24,32},{32,40},{40,48},{48,56},{56,64},{64,7... | collective-permute-start | bytes 55304 | tf_op jit(solution)/shard_map/ppermute | solution.py:19
  7.8 4.6 %copy-start.37 = (f32[1,1,512]{2,1,0:T(1,128)}, f32[1,1,512]{2,1,0:T(1,128)S(1)}, u32[]{:S(2)}) copy-start(f32[1,1,512]{2,1,0:T(1,128)S(1)} %get-tuple-element.66) | copy-start | bytes 6148
  7.8 4.6 %copy-start.39 = (f32[1,1,512]{2,1,0:T(1,128)}, f32[1,1,512]{2,1,0:T(1,128)S(1)}, u32[]{:S(2)}) copy-start(f32[1,1,512]{2,1,0:T(1,128)S(1)} %get-tuple-element.67) | copy-start | bytes 6148
  7.8 4.6 %copy-start.41 = (f32[1,1,512]{2,1,0:T(1,128)}, f32[1,1,512]{2,1,0:T(1,128)S(1)}, u32[]{:S(2)}) copy-start(f32[1,1,512]{2,1,0:T(1,128)S(1)} %get-tuple-element.68) | copy-start | bytes 6148
  7.8 4.6 %copy-start.43 = (f32[1,1,512]{2,1,0:T(1,128)}, f32[1,1,512]{2,1,0:T(1,128)S(1)}, u32[]{:S(2)}) copy-start(f32[1,1,512]{2,1,0:T(1,128)S(1)} %get-tuple-element.69) | copy-start | bytes 6148
  7.8 4.6 %copy-start.45 = (f32[1,1,512]{2,1,0:T(1,128)}, f32[1,1,512]{2,1,0:T(1,128)S(1)}, u32[]{:S(2)}) copy-start(f32[1,1,512]{2,1,0:T(1,128)S(1)} %get-tuple-element.70) | copy-start | bytes 6148
  7.9 4.6 %copy-start.47 = (f32[1,1,512]{2,1,0:T(1,128)}, f32[1,1,512]{2,1,0:T(1,128)S(1)}, u32[]{:S(2)}) copy-start(f32[1,1,512]{2,1,0:T(1,128)S(1)} %get-tuple-element.71) | copy-start | bytes 6148
  7.9 4.6 %copy-start.49 = (f32[1,1,512]{2,1,0:T(1,128)}, f32[1,1,512]{2,1,0:T(1,128)S(1)}, u32[]{:S(2)}) copy-start(f32[1,1,512]{2,1,0:T(1,128)S(1)} %get-tuple-element.72) | copy-start | bytes 6148
  7.9 4.6 %copy-start.51 = (f32[1,1,512]{2,1,0:T(1,128)}, f32[1,1,512]{2,1,0:T(1,128)S(1)}, u32[]{:S(2)}) copy-start(f32[1,1,512]{2,1,0:T(1,128)S(1)} %get-tuple-element.61) | copy-start | bytes 6148
  7.9 4.6 %copy-start.53 = (f32[1,1,512]{2,1,0:T(1,128)}, f32[1,1,512]{2,1,0:T(1,128)S(1)}, u32[]{:S(2)}) copy-start(f32[1,1,512]{2,1,0:T(1,128)S(1)} %get-tuple-element.62) | copy-start | bytes 6148
  7.9 4.6 %copy-start.55 = (f32[1,1,512]{2,1,0:T(1,128)}, f32[1,1,512]{2,1,0:T(1,128)S(1)}, u32[]{:S(2)}) copy-start(f32[1,1,512]{2,1,0:T(1,128)S(1)} %get-tuple-element.63) | copy-start | bytes 6148
  7.9 4.6 %copy-start.57 = (f32[1,1,512]{2,1,0:T(1,128)}, f32[1,1,512]{2,1,0:T(1,128)S(1)}, u32[]{:S(2)}) copy-start(f32[1,1,512]{2,1,0:T(1,128)S(1)} %get-tuple-element.64) | copy-start | bytes 6148
  7.9 4.6 %copy-start.59 = (f32[1,1,512]{2,1,0:T(1,128)}, f32[1,1,512]{2,1,0:T(1,128)S(1)}, u32[]{:S(2)}) copy-start(f32[1,1,512]{2,1,0:T(1,128)S(1)} %get-tuple-element.65) | copy-start | bytes 6148
  7.9 5.1 %copy-start.23 = (f32[1,1,512]{2,1,0:T(1,128)}, f32[1,1,512]{2,1,0:T(1,128)S(1)}, u32[]{:S(2)}) copy-start(f32[1,1,512]{2,1,0:T(1,128)S(1)} %get-tuple-element.60) | copy-start | bytes 6148
  7.9 5.1 %copy-start.25 = (f32[1,1,512]{2,1,0:T(1,128)}, f32[1,1,512]{2,1,0:T(1,128)S(1)}, u32[]{:S(2)}) copy-start(f32[1,1,512]{2,1,0:T(1,128)S(1)} %get-tuple-element.73) | copy-start | bytes 6148
  7.9 5.1 %copy-start.27 = (f32[1,1,512]{2,1,0:T(1,128)}, f32[1,1,512]{2,1,0:T(1,128)S(1)}, u32[]{:S(2)}) copy-start(f32[1,1,512]{2,1,0:T(1,128)S(1)} %get-tuple-element.74) | copy-start | bytes 6148
  8.0 5.1 %copy-start.29 = (f32[1,1,512]{2,1,0:T(1,128)}, f32[1,1,512]{2,1,0:T(1,128)S(1)}, u32[]{:S(2)}) copy-start(f32[1,1,512]{2,1,0:T(1,128)S(1)} %get-tuple-element.75) | copy-start | bytes 6148
  8.0 5.1 %copy-start.31 = (f32[1,1,512]{2,1,0:T(1,128)}, f32[1,1,512]{2,1,0:T(1,128)S(1)}, u32[]{:S(2)}) copy-start(f32[1,1,512]{2,1,0:T(1,128)S(1)} %get-tuple-element.76) | copy-start | bytes 6148
  8.0 5.1 %copy-start.33 = (f32[1,1,512]{2,1,0:T(1,128)}, f32[1,1,512]{2,1,0:T(1,128)S(1)}, u32[]{:S(2)}) copy-start(f32[1,1,512]{2,1,0:T(1,128)S(1)} %get-tuple-element.77) | copy-start | bytes 6148
  8.0 5.1 %copy-start.35 = (f32[1,1,512]{2,1,0:T(1,128)}, f32[1,1,512]{2,1,0:T(1,128)S(1)}, u32[]{:S(2)}) copy-start(f32[1,1,512]{2,1,0:T(1,128)S(1)} %get-tuple-element.78) | copy-start | bytes 6148
  8.8 3.7 %copy-start.61 = (f32[1,1,512]{2,1,0:T(1,128)}, f32[1,1,512]{2,1,0:T(1,128)S(1)}, u32[]{:S(2)}) copy-start(f32[1,1,512]{2,1,0:T(1,128)S(1)} %get-tuple-element.79) | copy-start | bytes 6148
  8.8 3.7 %copy-start.63 = (f32[1,1,512]{2,1,0:T(1,128)}, f32[1,1,512]{2,1,0:T(1,128)S(1)}, u32[]{:S(2)}) copy-start(f32[1,1,512]{2,1,0:T(1,128)S(1)} %get-tuple-element.80) | copy-start | bytes 6148
  14.2 7.1 %copy-start.22 = (f32[32,16]{0,1:T(8,128)S(1)}, f32[32,16]{0,1:T(8,128)}, u32[]{:S(2)}) copy-start(f32[32,16]{0,1:T(8,128)} %param.11) | copy-start | bytes 6148
  14.8 6.4 %collective-permute-start.1 = (f32[2,16,512]{2,1,0:T(8,128)S(1)}, f32[2,16,512]{2,1,0:T(8,128)S(1)}, u32[]{:S(2)}, u32[]{:S(2)}) collective-permute-start(f32[2,16,512]{2,1,0:T(8,128)S(1)} %pad_maximum_fusion.6), channel_id=1, source_target_pairs={{0,8},{8,0},{16,24},{24,16},{32,40},{40,32},{48,56},{56,48},{1,9},... | collective-permute-start | bytes 196616 | tf_op jit(solution)/shard_map/ppermute | solution.py:89
  21.4 6.5 %collective-permute-start.2 = (f32[2,16,512]{2,1,0:T(8,128)S(1)}, f32[2,16,512]{2,1,0:T(8,128)S(1)}, u32[]{:S(2)}, u32[]{:S(2)}) collective-permute-start(f32[2,16,512]{2,1,0:T(8,128)S(1)} %fusion.151), channel_id=1, source_target_pairs={{0,16},{8,24},{16,0},{24,8},{32,48},{40,56},{48,32},{56,40},{1,17}... | collective-permute-start | bytes 196616 | tf_op jit(solution)/shard_map/ppermute | solution.py:89
  27.8 6.6 %copy-start.10 = (f32[1,16,512]{2,1,0:T(8,128)S(1)}, f32[1,16,512]{2,1,0:T(8,128)}, u32[]{:S(2)}) copy-start(f32[1,16,512]{2,1,0:T(8,128)} %get-tuple-element.34) | copy-start | bytes 98308
  27.8 6.6 %copy-start.11 = (f32[1,16,512]{2,1,0:T(8,128)S(1)}, f32[1,16,512]{2,1,0:T(8,128)}, u32[]{:S(2)}) copy-start(f32[1,16,512]{2,1,0:T(8,128)} %get-tuple-element.39) | copy-start | bytes 98308
  27.8 6.6 %copy-start.12 = (f32[1,16,512]{2,1,0:T(8,128)S(1)}, f32[1,16,512]{2,1,0:T(8,128)}, u32[]{:S(2)}) copy-start(f32[1,16,512]{2,1,0:T(8,128)} %get-tuple-element.40) | copy-start | bytes 98308
  27.8 6.6 %copy-start.13 = (f32[1,16,512]{2,1,0:T(8,128)S(1)}, f32[1,16,512]{2,1,0:T(8,128)}, u32[]{:S(2)}) copy-start(f32[1,16,512]{2,1,0:T(8,128)} %get-tuple-element.41) | copy-start | bytes 98308
  27.8 6.6 %copy-start.14 = (f32[1,16,512]{2,1,0:T(8,128)S(1)}, f32[1,16,512]{2,1,0:T(8,128)}, u32[]{:S(2)}) copy-start(f32[1,16,512]{2,1,0:T(8,128)} %get-tuple-element.42) | copy-start | bytes 98308
  27.9 6.6 %copy-start.15 = (f32[1,16,512]{2,1,0:T(8,128)S(1)}, f32[1,16,512]{2,1,0:T(8,128)}, u32[]{:S(2)}) copy-start(f32[1,16,512]{2,1,0:T(8,128)} %get-tuple-element.21) | copy-start | bytes 98308
  27.9 6.6 %copy-start.16 = (f32[1,16,512]{2,1,0:T(8,128)S(1)}, f32[1,16,512]{2,1,0:T(8,128)}, u32[]{:S(2)}) copy-start(f32[1,16,512]{2,1,0:T(8,128)} %get-tuple-element.23) | copy-start | bytes 98308
  27.9 6.6 %copy-start.17 = (f32[1,16,512]{2,1,0:T(8,128)S(1)}, f32[1,16,512]{2,1,0:T(8,128)}, u32[]{:S(2)}) copy-start(f32[1,16,512]{2,1,0:T(8,128)} %get-tuple-element.33) | copy-start | bytes 98308
  28.0 6.5 %collective-permute-start.3 = (f32[2,16,512]{2,1,0:T(8,128)S(1)}, f32[2,16,512]{2,1,0:T(8,128)S(1)}, u32[]{:S(2)}, u32[]{:S(2)}) collective-permute-start(f32[2,16,512]{2,1,0:T(8,128)S(1)} %fusion.152), channel_id=1, source_target_pairs={{0,32},{8,40},{16,48},{24,56},{32,0},{40,8},{48,16},{56,24},{1,33}... | collective-permute-start | bytes 196616 | tf_op jit(solution)/shard_map/ppermute | solution.py:89
  34.6 11.3 %copy-start.20 = (f32[1,16,512]{2,1,0:T(8,128)S(1)}, f32[1,16,512]{2,1,0:T(8,128)}, u32[]{:S(2)}) copy-start(f32[1,16,512]{2,1,0:T(8,128)} %get-tuple-element.25) | copy-start | bytes 98308
  34.6 5.0 %collective-permute-start.4 = (f32[2,16,512]{2,1,0:T(8,128)S(1)}, f32[2,16,512]{2,1,0:T(8,128)S(1)}, u32[]{:S(2)}, u32[]{:S(2)}) collective-permute-start(f32[2,16,512]{2,1,0:T(8,128)S(1)} %get-tuple-element.59), channel_id=1, source_target_pairs={{0,64},{64,0},{128,192},{192,128},{256,320},{320,256},{384,448},{4... | collective-permute-start | bytes 196616 | tf_op jit(solution)/shard_map/ppermute | solution.py:89
  37.2 17.1 %copy-start.21 = (f32[6,512]{1,0:T(8,128)S(1)}, f32[6,512]{1,0:T(8,128)}, u32[]{:S(2)}) copy-start(f32[6,512]{1,0:T(8,128)} %slice_convert_fusion.1) | copy-start | bytes 36868
  39.6 21.1 %copy-start.4 = (f32[1,16,512]{2,1,0:T(8,128)S(1)}, f32[1,16,512]{2,1,0:T(8,128)}, u32[]{:S(2)}) copy-start(f32[1,16,512]{2,1,0:T(8,128)} %get-tuple-element.35) | copy-start | bytes 98308
  39.6 21.1 %copy-start.5 = (f32[1,16,512]{2,1,0:T(8,128)S(1)}, f32[1,16,512]{2,1,0:T(8,128)}, u32[]{:S(2)}) copy-start(f32[1,16,512]{2,1,0:T(8,128)} %get-tuple-element.36) | copy-start | bytes 98308
  39.6 21.1 %copy-start.6 = (f32[1,16,512]{2,1,0:T(8,128)S(1)}, f32[1,16,512]{2,1,0:T(8,128)}, u32[]{:S(2)}) copy-start(f32[1,16,512]{2,1,0:T(8,128)} %get-tuple-element.28) | copy-start | bytes 98308
  39.6 21.1 %copy-start.7 = (f32[1,16,512]{2,1,0:T(8,128)S(1)}, f32[1,16,512]{2,1,0:T(8,128)}, u32[]{:S(2)}) copy-start(f32[1,16,512]{2,1,0:T(8,128)} %get-tuple-element.29) | copy-start | bytes 98308
  39.6 21.1 %copy-start.8 = (f32[1,16,512]{2,1,0:T(8,128)S(1)}, f32[1,16,512]{2,1,0:T(8,128)}, u32[]{:S(2)}) copy-start(f32[1,16,512]{2,1,0:T(8,128)} %get-tuple-element.31) | copy-start | bytes 98308
  39.6 21.1 %copy-start.9 = (f32[1,16,512]{2,1,0:T(8,128)S(1)}, f32[1,16,512]{2,1,0:T(8,128)}, u32[]{:S(2)}) copy-start(f32[1,16,512]{2,1,0:T(8,128)} %get-tuple-element.32) | copy-start | bytes 98308
  39.7 6.2 %collective-permute-start.5 = (f32[2,16,512]{2,1,0:T(8,128)S(1)}, f32[2,16,512]{2,1,0:T(8,128)S(1)}, u32[]{:S(2)}, u32[]{:S(2)}) collective-permute-start(f32[2,16,512]{2,1,0:T(8,128)S(1)} %fusion.156), channel_id=1, source_target_pairs={{0,128},{64,192},{128,0},{192,64},{256,384},{320,448},{384,256},{4... | collective-permute-start | bytes 196616 | tf_op jit(solution)/shard_map/ppermute | solution.py:89
  46.5 14.1 %collective-permute-start.6 = (f32[2,16,512]{2,1,0:T(8,128)}, f32[2,16,512]{2,1,0:T(8,128)}, u32[]{:S(2)}, u32[]{:S(2)}) collective-permute-start(f32[2,16,512]{2,1,0:T(8,128)} %fusion.157), channel_id=1, source_target_pairs={{0,256},{64,320},{128,384},{192,448},{256,0},{320,64},{384,128},{4... | collective-permute-start | bytes 196616 | tf_op jit(solution)/shard_map/ppermute | solution.py:89
  54.6 8.0 %collective-permute-start.7 = (f32[46,512]{1,0:T(8,128)S(1)}, f32[46,512]{1,0:T(8,128)S(1)}, u32[]{:S(2)}, u32[]{:S(2)}) collective-permute-start(f32[46,512]{1,0:T(8,128)S(1)} %concatenate.24), channel_id=1, source_target_pairs={{8,0},{16,8},{24,16},{32,24},{40,32},{48,40},{56,48},{64,56},{72,6... | collective-permute-start | bytes 282632 | tf_op jit(solution)/shard_map/ppermute | solution.py:19
  64.4 2.5 %copy-start.56 = (f32[1,1,512]{2,1,0:T(1,128)S(1)}, f32[1,1,512]{2,1,0:T(1,128)}, u32[]{:S(2)}) copy-start(f32[1,1,512]{2,1,0:T(1,128)} %copy-done.55) | copy-start | bytes 6148
  64.4 2.5 %copy-start.58 = (f32[1,1,512]{2,1,0:T(1,128)S(1)}, f32[1,1,512]{2,1,0:T(1,128)}, u32[]{:S(2)}) copy-start(f32[1,1,512]{2,1,0:T(1,128)} %copy-done.57) | copy-start | bytes 6148
  64.5 2.5 %copy-start.60 = (f32[1,1,512]{2,1,0:T(1,128)S(1)}, f32[1,1,512]{2,1,0:T(1,128)}, u32[]{:S(2)}) copy-start(f32[1,1,512]{2,1,0:T(1,128)} %copy-done.59) | copy-start | bytes 6148
  64.5 3.3 %copy-start.38 = (f32[1,1,512]{2,1,0:T(1,128)S(1)}, f32[1,1,512]{2,1,0:T(1,128)}, u32[]{:S(2)}) copy-start(f32[1,1,512]{2,1,0:T(1,128)} %copy-done.37) | copy-start | bytes 6148
  64.5 3.3 %copy-start.40 = (f32[1,1,512]{2,1,0:T(1,128)S(1)}, f32[1,1,512]{2,1,0:T(1,128)}, u32[]{:S(2)}) copy-start(f32[1,1,512]{2,1,0:T(1,128)} %copy-done.39) | copy-start | bytes 6148
  64.5 3.3 %copy-start.42 = (f32[1,1,512]{2,1,0:T(1,128)S(1)}, f32[1,1,512]{2,1,0:T(1,128)}, u32[]{:S(2)}) copy-start(f32[1,1,512]{2,1,0:T(1,128)} %copy-done.41) | copy-start | bytes 6148
  64.5 3.3 %copy-start.44 = (f32[1,1,512]{2,1,0:T(1,128)S(1)}, f32[1,1,512]{2,1,0:T(1,128)}, u32[]{:S(2)}) copy-start(f32[1,1,512]{2,1,0:T(1,128)} %copy-done.43) | copy-start | bytes 6148
  64.5 3.3 %copy-start.46 = (f32[1,1,512]{2,1,0:T(1,128)S(1)}, f32[1,1,512]{2,1,0:T(1,128)}, u32[]{:S(2)}) copy-start(f32[1,1,512]{2,1,0:T(1,128)} %copy-done.45) | copy-start | bytes 6148
  64.5 3.3 %copy-start.48 = (f32[1,1,512]{2,1,0:T(1,128)S(1)}, f32[1,1,512]{2,1,0:T(1,128)}, u32[]{:S(2)}) copy-start(f32[1,1,512]{2,1,0:T(1,128)} %copy-done.47) | copy-start | bytes 6148
  64.5 3.3 %copy-start.50 = (f32[1,1,512]{2,1,0:T(1,128)S(1)}, f32[1,1,512]{2,1,0:T(1,128)}, u32[]{:S(2)}) copy-start(f32[1,1,512]{2,1,0:T(1,128)} %copy-done.49) | copy-start | bytes 6148
  64.6 4.2 %copy-start.24 = (f32[1,1,512]{2,1,0:T(1,128)S(1)}, f32[1,1,512]{2,1,0:T(1,128)}, u32[]{:S(2)}) copy-start(f32[1,1,512]{2,1,0:T(1,128)} %copy-done.23) | copy-start | bytes 6148
  64.6 4.2 %copy-start.26 = (f32[1,1,512]{2,1,0:T(1,128)S(1)}, f32[1,1,512]{2,1,0:T(1,128)}, u32[]{:S(2)}) copy-start(f32[1,1,512]{2,1,0:T(1,128)} %copy-done.25) | copy-start | bytes 6148
  64.6 4.2 %copy-start.28 = (f32[1,1,512]{2,1,0:T(1,128)S(1)}, f32[1,1,512]{2,1,0:T(1,128)}, u32[]{:S(2)}) copy-start(f32[1,1,512]{2,1,0:T(1,128)} %copy-done.27) | copy-start | bytes 6148
  64.6 4.2 %copy-start.30 = (f32[1,1,512]{2,1,0:T(1,128)S(1)}, f32[1,1,512]{2,1,0:T(1,128)}, u32[]{:S(2)}) copy-start(f32[1,1,512]{2,1,0:T(1,128)} %copy-done.29) | copy-start | bytes 6148
  64.6 4.2 %copy-start.32 = (f32[1,1,512]{2,1,0:T(1,128)S(1)}, f32[1,1,512]{2,1,0:T(1,128)}, u32[]{:S(2)}) copy-start(f32[1,1,512]{2,1,0:T(1,128)} %copy-done.31) | copy-start | bytes 6148
  64.6 4.2 %copy-start.34 = (f32[1,1,512]{2,1,0:T(1,128)S(1)}, f32[1,1,512]{2,1,0:T(1,128)}, u32[]{:S(2)}) copy-start(f32[1,1,512]{2,1,0:T(1,128)} %copy-done.33) | copy-start | bytes 6148
  64.6 4.2 %copy-start.36 = (f32[1,1,512]{2,1,0:T(1,128)S(1)}, f32[1,1,512]{2,1,0:T(1,128)}, u32[]{:S(2)}) copy-start(f32[1,1,512]{2,1,0:T(1,128)} %copy-done.35) | copy-start | bytes 6148
  (9 other events, 18.5 us)

commit v16 on v15

--- a/solution.py
+++ b/solution.py
@@ -198,9 +198,9 @@
     )
 
     mixer_out = (q_short.astype(jnp.float32) * conv_out.astype(jnp.float32)).astype(jnp.bfloat16)
-    grad_qshort = rounded(grad_out.astype(jnp.float32) * conv_out.astype(jnp.float32))
-    grad_kshort = rounded(grad_prod.astype(jnp.float32) * v_short.astype(jnp.float32))
-    grad_vshort = rounded(grad_prod.astype(jnp.float32) * k_short.astype(jnp.float32))
+    grad_qshort = to_bf16(grad_out.astype(jnp.float32) * conv_out.astype(jnp.float32))
+    grad_kshort = to_bf16(grad_prod.astype(jnp.float32) * v_short.astype(jnp.float32))
+    grad_vshort = to_bf16(grad_prod.astype(jnp.float32) * k_short.astype(jnp.float32))
     grad_query = short_reverse(grad_qshort, next_rows[0], short_filter[0]).astype(jnp.bfloat16)
     grad_key = short_reverse(grad_kshort, next_rows[1], short_filter[1]).astype(jnp.bfloat16)
     grad_value = short_reverse(grad_vshort, next_rows[2], short_filter[2]).astype(jnp.bfloat16)

time: 71 us -> 74 us (1.042)
  waiting for transfers between devices: 8.06 us -> 11.6 us
  starting transfers between devices: 34.2 us -> 31.5 us
  other arithmetic: 10.1 us -> 11.6 us
    ppermute x6, starting transfers between devices: 23.9 us -> 20.9 us  [cube_scan(): lax.ppermute(window, axis, [(source, source ^ shift) for source in range(...]
    ppermute x6, waiting for transfers between devices: 7.04 us -> 9.81 us  [cube_scan(): lax.ppermute(window, axis, [(source, source ^ shift) for source in range(...]
    add x2, other arithmetic: 0.91 us -> 0.07 us  [cube_scan(): entering = entering + add * arrived]
    ppermute x2, waiting for transfers between devices: 1.02 us -> 1.83 us  [from_behind(): lax.ppermute(value, axis, [(source, source + steps) for source in range(l...]
    convert_element_type x6 -> x4, other arithmetic: 1.55 us -> 0.78 us  [rounded(): return lax.optimization_barrier(values.astype(jnp.bfloat16))]
  transfers between devices with their start and end apart: 8 -> 8, of which waited for: 4 -> 4; matrix products, arithmetic and copies ran while one was open for 20% -> 22% of each run, Pallas kernels for 0% -> 0%
where the time goes in v16:
time: 74 us; the launch traced here: 72.7 us
  starting transfers between devices  31.5 us (43%)
  other arithmetic  11.6 us (16%)
  waiting for transfers between devices  11.6 us (16%)
  matrix products  9.61 us (13%)
  local copies, waits for them, and re-layouts  6.28 us (8%)
  between operations  2.06 us (3%)
    ppermute x6, starting transfers between devices, cube_scan(): lax.ppermute(window, axis, [(source, source ^ shift) for source in range(...  20.9 us
    ppermute x2, starting transfers between devices, from_behind(): lax.ppermute(value, axis, [(source, source + steps) for source in range(l...  10.7 us
    ppermute x6, waiting for transfers between devices, cube_scan(): lax.ppermute(window, axis, [(source, source ^ shift) for source in range(...  9.81 us
    dot_general x1, matrix products, shards(): toeplitz = jnp.einsum('gtm,gms->gts', falling, rising, precision=precise)  3.65 us
    slice x2, local copies, waits for them, and re-layouts, short_causal(): filter_taps[offset] * padded[SHORT - 1 - offset:SHORT - 1 - offset + length]  2.55 us
    ppermute x2, waiting for transfers between devices, from_behind(): lax.ppermute(value, axis, [(source, source + steps) for source in range(l...  1.83 us
    dot_general x4, matrix products, split_dot(): jnp.einsum(spec, low, values, preferred_element_type=jnp.float32)  1.62 us
    dot_general x4, matrix products, split_dot(): jnp.einsum(spec, high.astype(jnp.bfloat16), values, preferred_element_typ...  1.54 us
  transfers between devices with their start and end apart: 8, of which 4 were waited for; matrix products, arithmetic and copies ran while one was open for 22% of the time, Pallas kernels for 0%

profile of v16, /device:TPU:1, one launch (start us, length us, event | category | flops | bytes accessed | tf_op | source)
XLA Modules:
  0.0 72.7 jit_solution(2183024861354516825)
XLA Ops:
  0.6 0.7 %slice_bitcast_fusion.6 = bf16[1,6,512]{2,1,0:T(8,128)(2,1)S(1)} fusion(bf16[128,512]{1,0:T(8,128)(2,1)} %param.7), kind=kLoop, calls=%fused_computation.319 | loop fusion | bytes 12288 | tf_op jit(solution)/shard_map/stack | solution.py:101
  1.4 0.7 slice_bitcast_fusion.4
  2.1 4.5 %collective-permute-start = (bf16[3,6,512]{2,1,0:T(8,128)(2,1)S(1)}, bf16[3,6,512]{2,1,0:T(8,128)(2,1)S(1)}, u32[]{:S(2)}, u32[]{:S(2)}) collective-permute-start(bf16[3,6,512]{2,1,0:T(8,128)(2,1)S(1)} %pad_maximum_fusion.7), channel_id=1, source_target_pairs={{0,8},{8,16},{16,24},{24,32},{32,40},{40,48},{48,56},{56,64},{64,7... | collective-permute-start | bytes 55304 | tf_op jit(solution)/shard_map/ppermute | solution.py:19
  6.6 1.7 %fusion.193 = (f32[1,1,512]{2,1,0:T(1,128)S(1)}, f32[1,1,512]{2,1,0:T(1,128)S(1)}, f32[1,1,512]{2,1,0:T(1,128)S(1)}, f32[1,1,512]{2,1,0:T(1,128)S(1)}, f32[1,1,5...) fusion(f32[3,7,512]{2,1,0:T(8,128)} %param.10), kind=kLoop, calls=%fused_computation.336 | loop fusion | bytes 77824 | tf_op jit(solution)/shard_map/slice | solution.py:36
  8.5 0.8 %fusion.194 = (f32[1,1,512]{2,1,0:T(1,128)S(1)}, f32[1,1,512]{2,1,0:T(1,128)S(1)}) fusion(f32[3,7,512]{2,1,0:T(8,128)} %param.10), kind=kLoop, calls=%fused_computation.337 | loop fusion | bytes 8192 | tf_op jit(solution)/shard_map/slice | solution.py:36
  9.3 1.3 %negate_bitcast_fusion = (f32[16,32]{1,0:T(8,128)S(1)}, f32[32,16]{0,1:T(8,128)S(1)}, f32[32,16]{0,1:T(8,128)}) fusion(f32[32,16]{0,1:T(8,128)} %param.11, f32[32,16]{0,1:T(8,128)} %param.12), kind=kLoop, calls=%fused_computation.315 | loop fusion | flops 3072 | bytes 10240 | tf_op jit(solution)/shard_map/neg | solution.py:145
  10.7 0.1 copy.25
  10.7 0.1 multiply_exponential_fusion.1
  10.9 0.1 rev.6
  11.3 0.6 slice_convert_fusion.2
  11.9 0.1 broadcast_in_dim.12
  12.0 0.2 neg.35
  12.2 0.1 stack.155
  12.3 0.2 multiply_exponential_fusion
  12.5 0.7 slice_select_fusion.6
  13.2 0.8 %slice_select_fusion.7 = (f32[1,16,512]{2,1,0:T(8,128)}, f32[1,16,512]{2,1,0:T(8,128)}, f32[1,16,512]{2,1,0:T(8,128)}, f32[1,16,512]{2,1,0:T(8,128)}, f32[1,16,5...) fusion(f32[22,16,512]{2,1,0:T(8,128)S(1)} %multiply_exponential, ...), kind=kLoop, calls=%fused_computation.280 | loop fusion | flops 106496 | bytes 753670 | tf_op jit(solution)/shard_map/jit(_where)/select_n | solution.py:78
  14.0 0.5 convert_add_fusion
  14.8 0.5 fusion.13
  15.4 0.3 fusion.14
  15.6 0.3 fusion.195
  15.9 0.3 convolution_add_fusion.1
  16.2 0.3 fusion.196
  16.5 0.3 convolution_add_fusion
  16.8 0.3 multiply_reduce_fusion.1
  17.1 5.6 %collective-permute-start.1 = (f32[2,16,512]{2,1,0:T(8,128)S(1)}, f32[2,16,512]{2,1,0:T(8,128)S(1)}, u32[]{:S(2)}, u32[]{:S(2)}) collective-permute-start(f32[2,16,512]{2,1,0:T(8,128)S(1)} %pad_maximum_fusion.6), channel_id=1, source_target_pairs={{0,8},{8,0},{16,24},{24,16},{32,40},{40,32},{48,56},{56,48},{1,9},... | collective-permute-start | bytes 196616 | tf_op jit(solution)/shard_map/ppermute | solution.py:89
  22.7 0.6 slice_convert_fusion
  23.3 0.6 slice_convert_fusion.1
  23.9 0.1 copy.33
  24.0 0.1 copy.24
  24.2 0.1 copy.26
  24.2 0.1 copy.27
  24.3 1.9 %collective-permute-start.2 = (f32[2,16,512]{2,1,0:T(8,128)S(1)}, f32[2,16,512]{2,1,0:T(8,128)S(1)}, u32[]{:S(2)}, u32[]{:S(2)}) collective-permute-start(f32[2,16,512]{2,1,0:T(8,128)S(1)} %fusion.157), channel_id=1, source_target_pairs={{0,16},{8,24},{16,0},{24,8},{32,48},{40,56},{48,32},{56,40},{1,17}... | collective-permute-start | bytes 196616 | tf_op jit(solution)/shard_map/ppermute | solution.py:89
  26.3 3.7 %fusion.139 = f32[32,128,128]{2,1,0:T(8,128)S(1)} fusion(f32[32,16]{1,0:T(8,128)S(1)} %copy.27, f32[128]{0:T(128)S(1)} %copy-done.71, f32[128]{0:T(128)S(1)} %copy-done.72, f32[32,16]{1,0:T(8,128)S(1)} %copy.26), kind=kOutput, calls=%fused_computation.217 | convolution fusion | flops 100859904 | bytes 2102272 | tf_op jit(solution)/shard_map/gtm,gms->gts/dot_general | solution.py:158
  30.0 0.4 fusion.11
  30.3 0.4 convolution_add_fusion.2
  30.9 2.2 %collective-permute-start.3 = (f32[2,16,512]{2,1,0:T(8,128)S(1)}, f32[2,16,512]{2,1,0:T(8,128)S(1)}, u32[]{:S(2)}, u32[]{:S(2)}) collective-permute-start(f32[2,16,512]{2,1,0:T(8,128)S(1)} %fusion.158), channel_id=1, source_target_pairs={{0,32},{8,40},{16,48},{24,56},{32,0},{40,8},{48,16},{56,24},{1,33}... | collective-permute-start | bytes 196616 | tf_op jit(solution)/shard_map/ppermute | solution.py:89
  33.1 0.6 fusion.12
  33.8 4.2 %collective-permute-done.3 = f32[2,16,512]{2,1,0:T(8,128)S(1)} collective-permute-done((f32[2,16,512]{2,1,0:T(8,128)S(1)}, f32[2,16,512]{2,1,0:T(8,128)S(1)}, u32[]{:S(2)}, u32[]{:S(2)}) %collective-permute-start.3) | collective-permute-done | bytes 65568 | tf_op jit(solution)/shard_map/ppermute | solution.py:89
  38.1 2.1 %collective-permute-start.4 = (f32[2,16,512]{2,1,0:T(8,128)S(1)}, f32[2,16,512]{2,1,0:T(8,128)S(1)}, u32[]{:S(2)}, u32[]{:S(2)}) collective-permute-start(f32[2,16,512]{2,1,0:T(8,128)S(1)} %get-tuple-element.59), channel_id=1, source_target_pairs={{0,64},{64,0},{128,192},{192,128},{256,320},{320,256},{384,448},{4... | collective-permute-start | bytes 196616 | tf_op jit(solution)/shard_map/ppermute | solution.py:89
  40.2 0.7 convolution_add_fusion.3
  40.9 2.4 %collective-permute-done.4 = f32[2,16,512]{2,1,0:T(8,128)S(1)} collective-permute-done((f32[2,16,512]{2,1,0:T(8,128)S(1)}, f32[2,16,512]{2,1,0:T(8,128)S(1)}, u32[]{:S(2)}, u32[]{:S(2)}) %collective-permute-start.4) | collective-permute-done | bytes 65568 | tf_op jit(solution)/shard_map/ppermute | solution.py:89
  43.3 3.2 %collective-permute-start.5 = (f32[2,16,512]{2,1,0:T(8,128)S(1)}, f32[2,16,512]{2,1,0:T(8,128)S(1)}, u32[]{:S(2)}, u32[]{:S(2)}) collective-permute-start(f32[2,16,512]{2,1,0:T(8,128)S(1)} %fusion.162), channel_id=1, source_target_pairs={{0,128},{64,192},{128,0},{192,64},{256,384},{320,448},{384,256},{4... | collective-permute-start | bytes 196616 | tf_op jit(solution)/shard_map/ppermute | solution.py:89
  46.5 0.2 fusion.192
  46.7 0.1 rev.7
  46.9 3.2 %collective-permute-done.5 = f32[2,16,512]{2,1,0:T(8,128)S(1)} collective-permute-done((f32[2,16,512]{2,1,0:T(8,128)S(1)}, f32[2,16,512]{2,1,0:T(8,128)S(1)}, u32[]{:S(2)}, u32[]{:S(2)}) %collective-permute-start.5) | collective-permute-done | bytes 65568 | tf_op jit(solution)/shard_map/ppermute | solution.py:89
  50.1 0.6 fusion.163
  50.7 5.9 %collective-permute-start.6 = (f32[2,16,512]{2,1,0:T(8,128)}, f32[2,16,512]{2,1,0:T(8,128)S(1)}, u32[]{:S(2)}, u32[]{:S(2)}) collective-permute-start(f32[2,16,512]{2,1,0:T(8,128)} %fusion.163), channel_id=1, source_target_pairs={{0,256},{64,320},{128,384},{192,448},{256,0},{320,64},{384,128},{4... | collective-permute-start | bytes 196616 | tf_op jit(solution)/shard_map/ppermute | solution.py:89
  56.6 0.1 broadcast_multiply_fusion.2
  56.7 0.1 copy.43
  56.9 0.1 copy.35
  57.0 0.4 concatenate.24
  57.4 6.1 %collective-permute-start.7 = (f32[46,512]{1,0:T(8,128)S(1)}, f32[46,512]{1,0:T(8,128)S(1)}, u32[]{:S(2)}, u32[]{:S(2)}) collective-permute-start(f32[46,512]{1,0:T(8,128)S(1)} %concatenate.24), channel_id=1, source_target_pairs={{8,0},{16,8},{24,16},{32,24},{40,32},{48,40},{56,48},{64,56},{72,6... | collective-permute-start | bytes 282632 | tf_op jit(solution)/shard_map/ppermute | solution.py:19
  63.5 0.1 copy.38
  63.6 0.1 copy.32
  63.9 1.8 %collective-permute-done.7 = f32[46,512]{1,0:T(8,128)S(1)} collective-permute-done((f32[46,512]{1,0:T(8,128)S(1)}, f32[46,512]{1,0:T(8,128)S(1)}, u32[]{:S(2)}, u32[]{:S(2)}) %collective-permute-start.7) | collective-permute-done | bytes 94240 | tf_op jit(solution)/shard_map/ppermute | solution.py:19
  65.8 0.8 %fusion.3 = bf16[128,512]{1,0:T(8,128)(2,1)S(1)} fusion(f32[128,512]{1,0:T(8,128)S(1)} %copy.38, f32[32,16,128]{2,1,0:T(8,128)S(1)} %broadcast_multiply_fusion.2, f32[16,512]{1,0:T(8,128)S(1)} %get-tuple-element.13, f32[32,512]{1,0:T(8,128)S(1)} %fusion.164), kind=kOutput, calls=%fused_computation.11 | convolution fusion | flops 403046400 | bytes 753664 | tf_op jit(solution)/shard_map/ks,kc->sc/dot_general | solution.py:168
  66.6 0.3 broadcast_multiply_fusion
  67.0 0.6 fusion.173
  67.7 0.6 fusion.134
  68.4 0.8 %fusion.4 = bf16[128,512]{1,0:T(8,128)(2,1)S(1)} fusion(f32[128,512]{1,0:T(8,128)S(1)} %copy.32, f32[32,16,128]{2,1,0:T(8,128)S(1)} %get-tuple-element.44, f32[16,512]{1,0:T(8,128)S(1)} %get-tuple-element.20, f32[32,512]{1,0:T(8,128)S(1)} %fusion.164), kind=kOutput, calls=%fused_computation.12 | convolution fusion | flops 403046400 | bytes 753664 | tf_op jit(solution)/shard_map/kt,kc->tc/dot_general | solution.py:167
  69.2 0.9 %fusion.28 = bf16[128,512]{1,0:T(8,128)(2,1)} fusion(f32[6,512]{1,0:T(8,128)S(1)} %convert_element_type.273, f32[128,512]{1,0:T(8,128)S(1)} %get-tuple-element.49, f32[512]{0:T(512)S(1)} %bitcast.181, f32[512]{0:T(512)S(1)} %bitcast.179, f32[512]{0:T(512)S(1)} %bitcast.169, f32[512]{0:T(512)S(1)} %bitcast.171, f32[512]{0:T(512)S(1)} %bitcast.173, ...), kind=kLoop, calls=%fused_computation.82 | loop fusion | flops 1310720 | bytes 419840 | tf_op jit(solution)/shard_map/convert_element_type | solution.py:206
  70.2 0.9 %fusion.45 = bf16[128,512]{1,0:T(8,128)(2,1)} fusion(f32[6,512]{1,0:T(8,128)S(1)} %convert_element_type.268, f32[128,512]{1,0:T(8,128)S(1)} %get-tuple-element.50, f32[512]{0:T(512)S(1)} %bitcast.155, f32[512]{0:T(512)S(1)} %bitcast.157, f32[512]{0:T(512)S(1)} %bitcast.159, f32[512]{0:T(512)S(1)} %bitcast.161, f32[512]{0:T(512)S(1)} %bitcast.163, ...), kind=kLoop, calls=%fused_computation.99 | loop fusion | flops 1310720 | bytes 419840 | tf_op jit(solution)/shard_map/convert_element_type | solution.py:205
  71.1 0.7 fusion.149
  71.8 0.9 %fusion.62 = bf16[128,512]{1,0:T(8,128)(2,1)} fusion(f32[6,512]{1,0:T(8,128)S(1)} %convert_element_type.259, f32[128,512]{1,0:T(8,128)S(1)} %get-tuple-element.51, f32[512]{0:T(512)S(1)} %bitcast.143, f32[512]{0:T(512)S(1)} %bitcast.145, f32[512]{0:T(512)S(1)} %bitcast.147, f32[512]{0:T(512)S(1)} %bitcast.149, f32[512]{0:T(512)S(1)} %bitcast.151, ...), kind=kLoop, calls=%fused_computation.116 | loop fusion | flops 1310720 | bytes 419840 | tf_op jit(solution)/shard_map/convert_element_type | solution.py:204
  (176 shorter events, 0.8 us)
Async XLA Ops:
  0.6 10.6 %copy-start = (bf16[128,512]{1,0:T(8,128)(2,1)S(1)}, bf16[128,512]{1,0:T(8,128)(2,1)}, u32[]{:S(2)}) copy-start(bf16[128,512]{1,0:T(8,128)(2,1)} %param.13) | copy-start | bytes 393220
  2.1 12.5 %collective-permute-start = (bf16[3,6,512]{2,1,0:T(8,128)(2,1)S(1)}, bf16[3,6,512]{2,1,0:T(8,128)(2,1)S(1)}, u32[]{:S(2)}, u32[]{:S(2)}) collective-permute-start(bf16[3,6,512]{2,1,0:T(8,128)(2,1)S(1)} %pad_maximum_fusion.7), channel_id=1, source_target_pairs={{0,8},{8,16},{16,24},{24,32},{32,40},{40,48},{48,56},{56,64},{64,7... | collective-permute-start | bytes 55304 | tf_op jit(solution)/shard_map/ppermute | solution.py:19
  8.4 6.3 %copy-start.43 = (f32[1,1,512]{2,1,0:T(1,128)}, f32[1,1,512]{2,1,0:T(1,128)S(1)}, u32[]{:S(2)}) copy-start(f32[1,1,512]{2,1,0:T(1,128)S(1)} %get-tuple-element.66) | copy-start | bytes 6148
  8.4 6.3 %copy-start.45 = (f32[1,1,512]{2,1,0:T(1,128)}, f32[1,1,512]{2,1,0:T(1,128)S(1)}, u32[]{:S(2)}) copy-start(f32[1,1,512]{2,1,0:T(1,128)S(1)} %get-tuple-element.67) | copy-start | bytes 6148
  8.4 6.3 %copy-start.47 = (f32[1,1,512]{2,1,0:T(1,128)}, f32[1,1,512]{2,1,0:T(1,128)S(1)}, u32[]{:S(2)}) copy-start(f32[1,1,512]{2,1,0:T(1,128)S(1)} %get-tuple-element.68) | copy-start | bytes 6148
  8.4 6.3 %copy-start.49 = (f32[1,1,512]{2,1,0:T(1,128)}, f32[1,1,512]{2,1,0:T(1,128)S(1)}, u32[]{:S(2)}) copy-start(f32[1,1,512]{2,1,0:T(1,128)S(1)} %get-tuple-element.69) | copy-start | bytes 6148
  8.4 6.3 %copy-start.51 = (f32[1,1,512]{2,1,0:T(1,128)}, f32[1,1,512]{2,1,0:T(1,128)S(1)}, u32[]{:S(2)}) copy-start(f32[1,1,512]{2,1,0:T(1,128)S(1)} %get-tuple-element.70) | copy-start | bytes 6148
  8.4 6.3 %copy-start.53 = (f32[1,1,512]{2,1,0:T(1,128)}, f32[1,1,512]{2,1,0:T(1,128)S(1)}, u32[]{:S(2)}) copy-start(f32[1,1,512]{2,1,0:T(1,128)S(1)} %get-tuple-element.71) | copy-start | bytes 6148
  8.4 6.3 %copy-start.55 = (f32[1,1,512]{2,1,0:T(1,128)}, f32[1,1,512]{2,1,0:T(1,128)S(1)}, u32[]{:S(2)}) copy-start(f32[1,1,512]{2,1,0:T(1,128)S(1)} %get-tuple-element.72) | copy-start | bytes 6148
  8.4 6.3 %copy-start.57 = (f32[1,1,512]{2,1,0:T(1,128)}, f32[1,1,512]{2,1,0:T(1,128)S(1)}, u32[]{:S(2)}) copy-start(f32[1,1,512]{2,1,0:T(1,128)S(1)} %get-tuple-element.61) | copy-start | bytes 6148
  8.5 6.3 %copy-start.59 = (f32[1,1,512]{2,1,0:T(1,128)}, f32[1,1,512]{2,1,0:T(1,128)S(1)}, u32[]{:S(2)}) copy-start(f32[1,1,512]{2,1,0:T(1,128)S(1)} %get-tuple-element.62) | copy-start | bytes 6148
  8.5 6.3 %copy-start.61 = (f32[1,1,512]{2,1,0:T(1,128)}, f32[1,1,512]{2,1,0:T(1,128)S(1)}, u32[]{:S(2)}) copy-start(f32[1,1,512]{2,1,0:T(1,128)S(1)} %get-tuple-element.63) | copy-start | bytes 6148
  8.5 6.3 %copy-start.63 = (f32[1,1,512]{2,1,0:T(1,128)}, f32[1,1,512]{2,1,0:T(1,128)S(1)}, u32[]{:S(2)}) copy-start(f32[1,1,512]{2,1,0:T(1,128)S(1)} %get-tuple-element.64) | copy-start | bytes 6148
  8.5 6.3 %copy-start.65 = (f32[1,1,512]{2,1,0:T(1,128)}, f32[1,1,512]{2,1,0:T(1,128)S(1)}, u32[]{:S(2)}) copy-start(f32[1,1,512]{2,1,0:T(1,128)S(1)} %get-tuple-element.65) | copy-start | bytes 6148
  8.5 6.8 %copy-start.29 = (f32[1,1,512]{2,1,0:T(1,128)}, f32[1,1,512]{2,1,0:T(1,128)S(1)}, u32[]{:S(2)}) copy-start(f32[1,1,512]{2,1,0:T(1,128)S(1)} %get-tuple-element.60) | copy-start | bytes 6148
  8.5 6.8 %copy-start.31 = (f32[1,1,512]{2,1,0:T(1,128)}, f32[1,1,512]{2,1,0:T(1,128)S(1)}, u32[]{:S(2)}) copy-start(f32[1,1,512]{2,1,0:T(1,128)S(1)} %get-tuple-element.73) | copy-start | bytes 6148
  9.3 5.5 %copy-start.67 = (f32[1,1,512]{2,1,0:T(1,128)}, f32[1,1,512]{2,1,0:T(1,128)S(1)}, u32[]{:S(2)}) copy-start(f32[1,1,512]{2,1,0:T(1,128)S(1)} %get-tuple-element.79) | copy-start | bytes 6148
  9.3 5.5 %copy-start.69 = (f32[1,1,512]{2,1,0:T(1,128)}, f32[1,1,512]{2,1,0:T(1,128)S(1)}, u32[]{:S(2)}) copy-start(f32[1,1,512]{2,1,0:T(1,128)S(1)} %get-tuple-element.80) | copy-start | bytes 6148
  11.1 3.5 %copy-start.1 = (bf16[128,512]{1,0:T(8,128)(2,1)S(1)}, bf16[128,512]{1,0:T(8,128)(2,1)}, u32[]{:S(2)}) copy-start(bf16[128,512]{1,0:T(8,128)(2,1)} %param.8) | copy-start | bytes 393220
  11.1 3.5 %copy-start.2 = (bf16[128,512]{1,0:T(8,128)(2,1)S(1)}, bf16[128,512]{1,0:T(8,128)(2,1)}, u32[]{:S(2)}) copy-start(bf16[128,512]{1,0:T(8,128)(2,1)} %param.9) | copy-start | bytes 393220
  11.2 3.4 %copy-start.3 = (bf16[128,512]{1,0:T(8,128)(2,1)S(1)}, bf16[128,512]{1,0:T(8,128)(2,1)}, u32[]{:S(2)}) copy-start(bf16[128,512]{1,0:T(8,128)(2,1)} %param.7) | copy-start | bytes 393220
  16.5 7.7 %copy-start.28 = (f32[32,16]{0,1:T(8,128)S(1)}, f32[32,16]{0,1:T(8,128)}, u32[]{:S(2)}) copy-start(f32[32,16]{0,1:T(8,128)} %get-tuple-element.7) | copy-start | bytes 6148
  16.5 7.8 %copy-start.27 = (f32[32,16]{0,1:T(8,128)S(1)}, f32[32,16]{0,1:T(8,128)}, u32[]{:S(2)}) copy-start(f32[32,16]{0,1:T(8,128)} %param.11) | copy-start | bytes 6148
  16.8 9.5 %copy-start.71 = (f32[128]{0:T(128)S(1)}, f32[128]{0:T(128)}, u32[]{:S(2)}) copy-start(f32[128]{0:T(128)} %get-tuple-element.89) | copy-start | bytes 1540
  16.8 9.5 %copy-start.72 = (f32[128]{0:T(128)S(1)}, f32[128]{0:T(128)}, u32[]{:S(2)}) copy-start(f32[128]{0:T(128)} %get-tuple-element.90) | copy-start | bytes 1540
  17.1 7.1 %collective-permute-start.1 = (f32[2,16,512]{2,1,0:T(8,128)S(1)}, f32[2,16,512]{2,1,0:T(8,128)S(1)}, u32[]{:S(2)}, u32[]{:S(2)}) collective-permute-start(f32[2,16,512]{2,1,0:T(8,128)S(1)} %pad_maximum_fusion.6), channel_id=1, source_target_pairs={{0,8},{8,0},{16,24},{24,16},{32,40},{40,32},{48,56},{56,48},{1,9},... | collective-permute-start | bytes 196616 | tf_op jit(solution)/shard_map/ppermute | solution.py:89
  24.3 6.5 %collective-permute-start.2 = (f32[2,16,512]{2,1,0:T(8,128)S(1)}, f32[2,16,512]{2,1,0:T(8,128)S(1)}, u32[]{:S(2)}, u32[]{:S(2)}) collective-permute-start(f32[2,16,512]{2,1,0:T(8,128)S(1)} %fusion.157), channel_id=1, source_target_pairs={{0,16},{8,24},{16,0},{24,8},{32,48},{40,56},{48,32},{56,40},{1,17}... | collective-permute-start | bytes 196616 | tf_op jit(solution)/shard_map/ppermute | solution.py:89
  30.8 7.2 %copy-start.10 = (f32[1,16,512]{2,1,0:T(8,128)S(1)}, f32[1,16,512]{2,1,0:T(8,128)}, u32[]{:S(2)}) copy-start(f32[1,16,512]{2,1,0:T(8,128)} %get-tuple-element.34) | copy-start | bytes 98308
  30.8 7.2 %copy-start.11 = (f32[1,16,512]{2,1,0:T(8,128)S(1)}, f32[1,16,512]{2,1,0:T(8,128)}, u32[]{:S(2)}) copy-start(f32[1,16,512]{2,1,0:T(8,128)} %get-tuple-element.39) | copy-start | bytes 98308
  30.8 7.2 %copy-start.12 = (f32[1,16,512]{2,1,0:T(8,128)S(1)}, f32[1,16,512]{2,1,0:T(8,128)}, u32[]{:S(2)}) copy-start(f32[1,16,512]{2,1,0:T(8,128)} %get-tuple-element.40) | copy-start | bytes 98308
  30.8 7.2 %copy-start.13 = (f32[1,16,512]{2,1,0:T(8,128)S(1)}, f32[1,16,512]{2,1,0:T(8,128)}, u32[]{:S(2)}) copy-start(f32[1,16,512]{2,1,0:T(8,128)} %get-tuple-element.41) | copy-start | bytes 98308
  30.8 7.2 %copy-start.14 = (f32[1,16,512]{2,1,0:T(8,128)S(1)}, f32[1,16,512]{2,1,0:T(8,128)}, u32[]{:S(2)}) copy-start(f32[1,16,512]{2,1,0:T(8,128)} %get-tuple-element.42) | copy-start | bytes 98308
  30.8 7.2 %copy-start.15 = (f32[1,16,512]{2,1,0:T(8,128)S(1)}, f32[1,16,512]{2,1,0:T(8,128)}, u32[]{:S(2)}) copy-start(f32[1,16,512]{2,1,0:T(8,128)} %get-tuple-element.21) | copy-start | bytes 98308
  30.8 7.2 %copy-start.16 = (f32[1,16,512]{2,1,0:T(8,128)S(1)}, f32[1,16,512]{2,1,0:T(8,128)}, u32[]{:S(2)}) copy-start(f32[1,16,512]{2,1,0:T(8,128)} %get-tuple-element.23) | copy-start | bytes 98308
  30.8 7.2 %copy-start.17 = (f32[1,16,512]{2,1,0:T(8,128)S(1)}, f32[1,16,512]{2,1,0:T(8,128)}, u32[]{:S(2)}) copy-start(f32[1,16,512]{2,1,0:T(8,128)} %get-tuple-element.33) | copy-start | bytes 98308
  30.9 7.1 %collective-permute-start.3 = (f32[2,16,512]{2,1,0:T(8,128)S(1)}, f32[2,16,512]{2,1,0:T(8,128)S(1)}, u32[]{:S(2)}, u32[]{:S(2)}) collective-permute-start(f32[2,16,512]{2,1,0:T(8,128)S(1)} %fusion.158), channel_id=1, source_target_pairs={{0,32},{8,40},{16,48},{24,56},{32,0},{40,8},{48,16},{56,24},{1,33}... | collective-permute-start | bytes 196616 | tf_op jit(solution)/shard_map/ppermute | solution.py:89
  33.8 9.5 %copy-start.22 = (f32[1,16,512]{2,1,0:T(8,128)S(1)}, f32[1,16,512]{2,1,0:T(8,128)}, u32[]{:S(2)}) copy-start(f32[1,16,512]{2,1,0:T(8,128)} %get-tuple-element.24) | copy-start | bytes 98308
  33.8 9.5 %copy-start.23 = (f32[1,16,512]{2,1,0:T(8,128)S(1)}, f32[1,16,512]{2,1,0:T(8,128)}, u32[]{:S(2)}) copy-start(f32[1,16,512]{2,1,0:T(8,128)} %get-tuple-element.30) | copy-start | bytes 98308
  38.1 12.0 %copy-start.20 = (f32[1,16,512]{2,1,0:T(8,128)S(1)}, f32[1,16,512]{2,1,0:T(8,128)}, u32[]{:S(2)}) copy-start(f32[1,16,512]{2,1,0:T(8,128)} %get-tuple-element.25) | copy-start | bytes 98308
  38.1 11.9 %copy-start.21 = (f32[1,16,512]{2,1,0:T(8,128)S(1)}, f32[1,16,512]{2,1,0:T(8,128)}, u32[]{:S(2)}) copy-start(f32[1,16,512]{2,1,0:T(8,128)} %get-tuple-element.27) | copy-start | bytes 98308
  38.1 5.1 %collective-permute-start.4 = (f32[2,16,512]{2,1,0:T(8,128)S(1)}, f32[2,16,512]{2,1,0:T(8,128)S(1)}, u32[]{:S(2)}, u32[]{:S(2)}) collective-permute-start(f32[2,16,512]{2,1,0:T(8,128)S(1)} %get-tuple-element.59), channel_id=1, source_target_pairs={{0,64},{64,0},{128,192},{192,128},{256,320},{320,256},{384,448},{4... | collective-permute-start | bytes 196616 | tf_op jit(solution)/shard_map/ppermute | solution.py:89
  40.8 16.1 %copy-start.24 = (f32[6,512]{1,0:T(8,128)S(1)}, f32[6,512]{1,0:T(8,128)}, u32[]{:S(2)}) copy-start(f32[6,512]{1,0:T(8,128)} %slice_convert_fusion.2) | copy-start | bytes 36868
  40.8 16.1 %copy-start.25 = (f32[6,512]{1,0:T(8,128)S(1)}, f32[6,512]{1,0:T(8,128)}, u32[]{:S(2)}) copy-start(f32[6,512]{1,0:T(8,128)} %slice_convert_fusion) | copy-start | bytes 36868
  40.8 16.1 %copy-start.26 = (f32[6,512]{1,0:T(8,128)S(1)}, f32[6,512]{1,0:T(8,128)}, u32[]{:S(2)}) copy-start(f32[6,512]{1,0:T(8,128)} %slice_convert_fusion.1) | copy-start | bytes 36868
  43.3 20.5 %copy-start.4 = (f32[1,16,512]{2,1,0:T(8,128)S(1)}, f32[1,16,512]{2,1,0:T(8,128)}, u32[]{:S(2)}) copy-start(f32[1,16,512]{2,1,0:T(8,128)} %get-tuple-element.35) | copy-start | bytes 98308
  43.3 20.5 %copy-start.5 = (f32[1,16,512]{2,1,0:T(8,128)S(1)}, f32[1,16,512]{2,1,0:T(8,128)}, u32[]{:S(2)}) copy-start(f32[1,16,512]{2,1,0:T(8,128)} %get-tuple-element.36) | copy-start | bytes 98308
  43.3 20.5 %copy-start.6 = (f32[1,16,512]{2,1,0:T(8,128)S(1)}, f32[1,16,512]{2,1,0:T(8,128)}, u32[]{:S(2)}) copy-start(f32[1,16,512]{2,1,0:T(8,128)} %get-tuple-element.28) | copy-start | bytes 98308
  43.3 20.5 %copy-start.7 = (f32[1,16,512]{2,1,0:T(8,128)S(1)}, f32[1,16,512]{2,1,0:T(8,128)}, u32[]{:S(2)}) copy-start(f32[1,16,512]{2,1,0:T(8,128)} %get-tuple-element.29) | copy-start | bytes 98308
  43.3 20.5 %copy-start.8 = (f32[1,16,512]{2,1,0:T(8,128)S(1)}, f32[1,16,512]{2,1,0:T(8,128)}, u32[]{:S(2)}) copy-start(f32[1,16,512]{2,1,0:T(8,128)} %get-tuple-element.31) | copy-start | bytes 98308
  43.3 20.5 %copy-start.9 = (f32[1,16,512]{2,1,0:T(8,128)S(1)}, f32[1,16,512]{2,1,0:T(8,128)}, u32[]{:S(2)}) copy-start(f32[1,16,512]{2,1,0:T(8,128)} %get-tuple-element.32) | copy-start | bytes 98308
  43.3 6.7 %collective-permute-start.5 = (f32[2,16,512]{2,1,0:T(8,128)S(1)}, f32[2,16,512]{2,1,0:T(8,128)S(1)}, u32[]{:S(2)}, u32[]{:S(2)}) collective-permute-start(f32[2,16,512]{2,1,0:T(8,128)S(1)} %fusion.162), channel_id=1, source_target_pairs={{0,128},{64,192},{128,0},{192,64},{256,384},{320,448},{384,256},{4... | collective-permute-start | bytes 196616 | tf_op jit(solution)/shard_map/ppermute | solution.py:89
  50.7 13.1 %collective-permute-start.6 = (f32[2,16,512]{2,1,0:T(8,128)}, f32[2,16,512]{2,1,0:T(8,128)S(1)}, u32[]{:S(2)}, u32[]{:S(2)}) collective-permute-start(f32[2,16,512]{2,1,0:T(8,128)} %fusion.163), channel_id=1, source_target_pairs={{0,256},{64,320},{128,384},{192,448},{256,0},{320,64},{384,128},{4... | collective-permute-start | bytes 196616 | tf_op jit(solution)/shard_map/ppermute | solution.py:89
  57.4 8.4 %collective-permute-start.7 = (f32[46,512]{1,0:T(8,128)S(1)}, f32[46,512]{1,0:T(8,128)S(1)}, u32[]{:S(2)}, u32[]{:S(2)}) collective-permute-start(f32[46,512]{1,0:T(8,128)S(1)} %concatenate.24), channel_id=1, source_target_pairs={{8,0},{16,8},{24,16},{32,24},{40,32},{48,40},{56,48},{64,56},{72,6... | collective-permute-start | bytes 282632 | tf_op jit(solution)/shard_map/ppermute | solution.py:19
  67.0 3.2 %copy-start.44 = (f32[1,1,512]{2,1,0:T(1,128)S(1)}, f32[1,1,512]{2,1,0:T(1,128)}, u32[]{:S(2)}) copy-start(f32[1,1,512]{2,1,0:T(1,128)} %copy-done.43) | copy-start | bytes 6148
  67.0 3.2 %copy-start.46 = (f32[1,1,512]{2,1,0:T(1,128)S(1)}, f32[1,1,512]{2,1,0:T(1,128)}, u32[]{:S(2)}) copy-start(f32[1,1,512]{2,1,0:T(1,128)} %copy-done.45) | copy-start | bytes 6148
  67.0 3.2 %copy-start.48 = (f32[1,1,512]{2,1,0:T(1,128)S(1)}, f32[1,1,512]{2,1,0:T(1,128)}, u32[]{:S(2)}) copy-start(f32[1,1,512]{2,1,0:T(1,128)} %copy-done.47) | copy-start | bytes 6148
  67.0 3.2 %copy-start.50 = (f32[1,1,512]{2,1,0:T(1,128)S(1)}, f32[1,1,512]{2,1,0:T(1,128)}, u32[]{:S(2)}) copy-start(f32[1,1,512]{2,1,0:T(1,128)} %copy-done.49) | copy-start | bytes 6148
  67.6 4.1 %copy-start.30 = (f32[1,1,512]{2,1,0:T(1,128)S(1)}, f32[1,1,512]{2,1,0:T(1,128)}, u32[]{:S(2)}) copy-start(f32[1,1,512]{2,1,0:T(1,128)} %copy-done.29) | copy-start | bytes 6148
  67.6 4.1 %copy-start.32 = (f32[1,1,512]{2,1,0:T(1,128)S(1)}, f32[1,1,512]{2,1,0:T(1,128)}, u32[]{:S(2)}) copy-start(f32[1,1,512]{2,1,0:T(1,128)} %copy-done.31) | copy-start | bytes 6148
  67.6 4.1 %copy-start.34 = (f32[1,1,512]{2,1,0:T(1,128)S(1)}, f32[1,1,512]{2,1,0:T(1,128)}, u32[]{:S(2)}) copy-start(f32[1,1,512]{2,1,0:T(1,128)} %get-tuple-element.74) | copy-start | bytes 6148
  67.7 4.1 %copy-start.36 = (f32[1,1,512]{2,1,0:T(1,128)S(1)}, f32[1,1,512]{2,1,0:T(1,128)}, u32[]{:S(2)}) copy-start(f32[1,1,512]{2,1,0:T(1,128)} %get-tuple-element.75) | copy-start | bytes 6148
  67.7 4.1 %copy-start.38 = (f32[1,1,512]{2,1,0:T(1,128)S(1)}, f32[1,1,512]{2,1,0:T(1,128)}, u32[]{:S(2)}) copy-start(f32[1,1,512]{2,1,0:T(1,128)} %get-tuple-element.76) | copy-start | bytes 6148
  67.7 4.1 %copy-start.40 = (f32[1,1,512]{2,1,0:T(1,128)S(1)}, f32[1,1,512]{2,1,0:T(1,128)}, u32[]{:S(2)}) copy-start(f32[1,1,512]{2,1,0:T(1,128)} %get-tuple-element.77) | copy-start | bytes 6148
  67.7 4.1 %copy-start.42 = (f32[1,1,512]{2,1,0:T(1,128)S(1)}, f32[1,1,512]{2,1,0:T(1,128)}, u32[]{:S(2)}) copy-start(f32[1,1,512]{2,1,0:T(1,128)} %get-tuple-element.78) | copy-start | bytes 6148
  (17 other events, 42.4 us)

commit v17 on v15

--- a/solution.py
+++ b/solution.py
@@ -166,8 +166,8 @@
     )
     carried_conv = jnp.einsum("kt,kc->tc", lead_fwd, spread(entering), precision=precise)
     carried_grad = jnp.einsum("ks,kc->sc", lead_bwd, spread(leaving), precision=precise)
-    conv_out = rounded(local_conv + carried_conv)
-    grad_prod = rounded(local_grad + carried_grad)
+    conv_out = to_bf16(local_conv + carried_conv)
+    grad_prod = to_bf16(local_grad + carried_grad)
 
     edge = SHORT - 1
     ahead = jnp.concatenate(

time: 71 us -> 70.9 us (level)
  other arithmetic: 10.1 us -> 9.33 us
  matrix products: 9.64 us -> 10.4 us
    convert_element_type x6 -> x4, other arithmetic: 1.55 us -> 0.78 us  [rounded(): return lax.optimization_barrier(values.astype(jnp.bfloat16))]
where the time goes in v17:
time: 70.9 us; the launch traced here: 69.6 us
  starting transfers between devices  34.2 us (48%)
  matrix products  10.4 us (15%)
  other arithmetic  9.33 us (13%)
  waiting for transfers between devices  8.06 us (11%)
  local copies, waits for them, and re-layouts  5.65 us (8%)
  between operations  2.04 us (3%)
    ppermute x6, starting transfers between devices, cube_scan(): lax.ppermute(window, axis, [(source, source ^ shift) for source in range(...  23.9 us
    ppermute x2, starting transfers between devices, from_behind(): lax.ppermute(value, axis, [(source, source + steps) for source in range(l...  10.3 us
    ppermute x6, waiting for transfers between devices, cube_scan(): lax.ppermute(window, axis, [(source, source ^ shift) for source in range(...  7.04 us
    dot_general x1, matrix products, shards(): toeplitz = jnp.einsum('gtm,gms->gts', falling, rising, precision=precise)  3.65 us
    slice x2, local copies, waits for them, and re-layouts, short_causal(): filter_taps[offset] * padded[SHORT - 1 - offset:SHORT - 1 - offset + length]  1.97 us
    dot_general x4, matrix products, split_dot(): jnp.einsum(spec, low, values, preferred_element_type=jnp.float32)  1.63 us
    dot_general x4, matrix products, split_dot(): jnp.einsum(spec, high.astype(jnp.bfloat16), values, preferred_element_typ...  1.56 us
    dot_general x1, matrix products, shards(): jnp.einsum('kt,kc->tc', lead_fwd, spread(entering), precision=precise)  1.48 us
  transfers between devices with their start and end apart: 8, of which 4 were waited for; matrix products, arithmetic and copies ran while one was open for 20% of the time, Pallas kernels for 0%

profile of v17, /device:TPU:1, one launch (start us, length us, event | category | flops | bytes accessed | tf_op | source)
XLA Modules:
  0.0 69.6 jit_solution(10864912565377537104)
XLA Ops:
  0.6 0.7 %slice_bitcast_fusion.6 = bf16[1,6,512]{2,1,0:T(8,128)(2,1)S(1)} fusion(bf16[128,512]{1,0:T(8,128)(2,1)} %param.7), kind=kLoop, calls=%fused_computation.317 | loop fusion | bytes 12288 | tf_op jit(solution)/shard_map/stack | solution.py:101
  1.4 0.7 %slice_bitcast_fusion.4 = (bf16[1,6,512]{2,1,0:T(8,128)(2,1)S(1)}, bf16[1,6,512]{2,1,0:T(8,128)(2,1)S(1)}) fusion(bf16[128,512]{1,0:T(8,128)(2,1)} %param.9, bf16[128,512]{1,0:T(8,128)(2,1)} %param.8), kind=kLoop, calls=%fused_computation.315 | loop fusion | bytes 24576 | tf_op jit(solution)/shard_map/stack | solution.py:101
  2.1 4.5 %collective-permute-start = (bf16[3,6,512]{2,1,0:T(8,128)(2,1)S(1)}, bf16[3,6,512]{2,1,0:T(8,128)(2,1)S(1)}, u32[]{:S(2)}, u32[]{:S(2)}) collective-permute-start(bf16[3,6,512]{2,1,0:T(8,128)(2,1)S(1)} %pad_maximum_fusion.7), channel_id=1, source_target_pairs={{0,8},{8,16},{16,24},{24,32},{32,40},{40,48},{48,56},{56,64},{64,7... | collective-permute-start | bytes 55304 | tf_op jit(solution)/shard_map/ppermute | solution.py:19
  6.6 1.2 %fusion.191 = (f32[1,1,512]{2,1,0:T(1,128)S(1)}, f32[1,1,512]{2,1,0:T(1,128)S(1)}, f32[1,1,512]{2,1,0:T(1,128)S(1)}, f32[1,1,512]{2,1,0:T(1,128)S(1)}, f32[1,1,5...) fusion(f32[3,7,512]{2,1,0:T(8,128)} %param.10), kind=kLoop, calls=%fused_computation.334 | loop fusion | bytes 77824 | tf_op jit(solution)/shard_map/slice | solution.py:36
  8.0 0.8 %fusion.192 = (f32[1,1,512]{2,1,0:T(1,128)S(1)}, f32[1,1,512]{2,1,0:T(1,128)S(1)}) fusion(f32[3,7,512]{2,1,0:T(8,128)} %param.10), kind=kLoop, calls=%fused_computation.335 | loop fusion | bytes 8192 | tf_op jit(solution)/shard_map/slice | solution.py:36
  8.8 0.7 %negate_bitcast_fusion = (f32[16,32]{1,0:T(8,128)S(1)}, f32[32,16]{0,1:T(8,128)S(1)}, f32[32,16]{0,1:T(8,128)S(1)}) fusion(f32[32,16]{0,1:T(8,128)} %param.11, f32[32,16]{0,1:T(8,128)} %param.12), kind=kLoop, calls=%fused_computation.313 | loop fusion | flops 3072 | bytes 10240 | tf_op jit(solution)/shard_map/neg | solution.py:145
  9.6 0.1 copy.25
  9.6 0.1 multiply_exponential_fusion.1
  9.8 0.1 rev.6
  9.9 0.0 copy-start.1
  9.9 0.0 copy-start.2
  10.2 0.1 broadcast_in_dim.12
  10.4 0.2 neg.35
  10.5 0.1 stack.155
  10.6 0.2 multiply_exponential_fusion
  10.8 0.7 %slice_select_fusion.6 = (f32[1,16,512]{2,1,0:T(8,128)}, f32[1,16,512]{2,1,0:T(8,128)}, f32[1,16,512]{2,1,0:T(8,128)}, f32[1,16,512]{2,1,0:T(8,128)}, f32[1,16,5...) fusion(f32[22,16,512]{2,1,0:T(8,128)S(1)} %multiply_exponential, ...), kind=kLoop, calls=%fused_computation.277 | loop fusion | flops 73728 | bytes 589828 | tf_op jit(solution)/shard_map/jit(_where)/select_n | solution.py:78
  11.5 0.7 %slice_select_fusion.7 = (f32[1,16,512]{2,1,0:T(8,128)}, f32[1,16,512]{2,1,0:T(8,128)}, f32[1,16,512]{2,1,0:T(8,128)}, f32[1,16,512]{2,1,0:T(8,128)S(1)}, f32[1,...) fusion(f32[22,16,512]{2,1,0:T(8,128)S(1)} %multiply_exponential, ...), kind=kLoop, calls=%fused_computation.278 | loop fusion | flops 106496 | bytes 753670 | tf_op jit(solution)/shard_map/jit(_where)/select_n | solution.py:78
  12.5 0.5 fusion.19
  13.1 0.3 fusion.21
  13.4 0.3 fusion.193
  13.7 0.3 convolution_add_fusion.1
  14.0 0.3 fusion.194
  14.2 0.3 convolution_add_fusion
  14.5 0.3 multiply_reduce_fusion.1
  14.8 5.6 %collective-permute-start.1 = (f32[2,16,512]{2,1,0:T(8,128)S(1)}, f32[2,16,512]{2,1,0:T(8,128)S(1)}, u32[]{:S(2)}, u32[]{:S(2)}) collective-permute-start(f32[2,16,512]{2,1,0:T(8,128)S(1)} %pad_maximum_fusion.6), channel_id=1, source_target_pairs={{0,8},{8,0},{16,24},{24,16},{32,40},{40,32},{48,56},{56,48},{1,9},... | collective-permute-start | bytes 196616 | tf_op jit(solution)/shard_map/ppermute | solution.py:89
  20.4 0.6 slice_convert_fusion.1
  21.0 0.1 copy.33
  21.1 0.1 copy.24
  21.2 0.0 collective-permute-done.1
  21.3 0.1 copy.26
  21.3 0.1 copy.27
  21.4 1.9 %collective-permute-start.2 = (f32[2,16,512]{2,1,0:T(8,128)S(1)}, f32[2,16,512]{2,1,0:T(8,128)S(1)}, u32[]{:S(2)}, u32[]{:S(2)}) collective-permute-start(f32[2,16,512]{2,1,0:T(8,128)S(1)} %fusion.155), channel_id=1, source_target_pairs={{0,16},{8,24},{16,0},{24,8},{32,48},{40,56},{48,32},{56,40},{1,17}... | collective-permute-start | bytes 196616 | tf_op jit(solution)/shard_map/ppermute | solution.py:89
  23.4 3.7 %fusion.140 = f32[32,128,128]{2,1,0:T(8,128)S(1)} fusion(f32[32,16]{1,0:T(8,128)S(1)} %copy.27, f32[128]{0:T(128)S(1)} %get-tuple-element.89, f32[128]{0:T(128)S(1)} %get-tuple-element.90, f32[32,16]{1,0:T(8,128)S(1)} %copy.26), kind=kOutput, calls=%fused_computation.218 | convolution fusion | flops 100859904 | bytes 2102272 | tf_op jit(solution)/shard_map/gtm,gms->gts/dot_general | solution.py:158
  27.0 0.4 fusion.15
  27.4 0.4 convolution_add_fusion.2
  28.0 2.6 %collective-permute-start.3 = (f32[2,16,512]{2,1,0:T(8,128)S(1)}, f32[2,16,512]{2,1,0:T(8,128)S(1)}, u32[]{:S(2)}, u32[]{:S(2)}) collective-permute-start(f32[2,16,512]{2,1,0:T(8,128)S(1)} %fusion.156), channel_id=1, source_target_pairs={{0,32},{8,40},{16,48},{24,56},{32,0},{40,8},{48,16},{56,24},{1,33}... | collective-permute-start | bytes 196616 | tf_op jit(solution)/shard_map/ppermute | solution.py:89
  30.5 0.6 fusion.16
  31.2 3.3 %collective-permute-done.3 = f32[2,16,512]{2,1,0:T(8,128)S(1)} collective-permute-done((f32[2,16,512]{2,1,0:T(8,128)S(1)}, f32[2,16,512]{2,1,0:T(8,128)S(1)}, u32[]{:S(2)}, u32[]{:S(2)}) %collective-permute-start.3) | collective-permute-done | bytes 65568 | tf_op jit(solution)/shard_map/ppermute | solution.py:89
  34.6 1.9 %collective-permute-start.4 = (f32[2,16,512]{2,1,0:T(8,128)S(1)}, f32[2,16,512]{2,1,0:T(8,128)S(1)}, u32[]{:S(2)}, u32[]{:S(2)}) collective-permute-start(f32[2,16,512]{2,1,0:T(8,128)S(1)} %get-tuple-element.59), channel_id=1, source_target_pairs={{0,64},{64,0},{128,192},{192,128},{256,320},{320,256},{384,448},{4... | collective-permute-start | bytes 196616 | tf_op jit(solution)/shard_map/ppermute | solution.py:89
  36.5 0.7 convolution_add_fusion.3
  37.2 2.4 %collective-permute-done.4 = f32[2,16,512]{2,1,0:T(8,128)S(1)} collective-permute-done((f32[2,16,512]{2,1,0:T(8,128)S(1)}, f32[2,16,512]{2,1,0:T(8,128)S(1)}, u32[]{:S(2)}, u32[]{:S(2)}) %collective-permute-start.4) | collective-permute-done | bytes 65568 | tf_op jit(solution)/shard_map/ppermute | solution.py:89
  39.7 4.6 %collective-permute-start.5 = (f32[2,16,512]{2,1,0:T(8,128)S(1)}, f32[2,16,512]{2,1,0:T(8,128)S(1)}, u32[]{:S(2)}, u32[]{:S(2)}) collective-permute-start(f32[2,16,512]{2,1,0:T(8,128)S(1)} %fusion.160), channel_id=1, source_target_pairs={{0,128},{64,192},{128,0},{192,64},{256,384},{320,448},{384,256},{4... | collective-permute-start | bytes 196616 | tf_op jit(solution)/shard_map/ppermute | solution.py:89
  44.2 0.2 fusion.190
  44.4 0.1 rev.7
  44.6 1.3 %collective-permute-done.5 = f32[2,16,512]{2,1,0:T(8,128)S(1)} collective-permute-done((f32[2,16,512]{2,1,0:T(8,128)S(1)}, f32[2,16,512]{2,1,0:T(8,128)S(1)}, u32[]{:S(2)}, u32[]{:S(2)}) %collective-permute-start.5) | collective-permute-done | bytes 65568 | tf_op jit(solution)/shard_map/ppermute | solution.py:89
  45.9 0.6 fusion.161
  46.5 7.3 %collective-permute-start.6 = (f32[2,16,512]{2,1,0:T(8,128)}, f32[2,16,512]{2,1,0:T(8,128)}, u32[]{:S(2)}, u32[]{:S(2)}) collective-permute-start(f32[2,16,512]{2,1,0:T(8,128)} %fusion.161), channel_id=1, source_target_pairs={{0,256},{64,320},{128,384},{192,448},{256,0},{320,64},{384,128},{4... | collective-permute-start | bytes 196616 | tf_op jit(solution)/shard_map/ppermute | solution.py:89
  53.9 0.1 broadcast_multiply_fusion.2
  54.0 0.1 copy.43
  54.1 0.1 copy.35
  54.2 0.3 concatenate.24
  54.6 5.8 %collective-permute-start.7 = (f32[46,512]{1,0:T(8,128)S(1)}, f32[46,512]{1,0:T(8,128)S(1)}, u32[]{:S(2)}, u32[]{:S(2)}) collective-permute-start(f32[46,512]{1,0:T(8,128)S(1)} %concatenate.24), channel_id=1, source_target_pairs={{8,0},{16,8},{24,16},{32,24},{40,32},{48,40},{56,48},{64,56},{72,6... | collective-permute-start | bytes 282632 | tf_op jit(solution)/shard_map/ppermute | solution.py:19
  60.4 0.1 copy.38
  60.5 0.1 copy.32
  60.7 0.9 %fusion.158 = f32[2,16,512]{2,1,0:T(8,128)S(1)} fusion(f32[2,16,512]{2,1,0:T(8,128)S(1)} %collective-permute-done.4, f32[1,16,512]{2,1,0:T(8,128)S(1)} %copy-done.4, f32[1,16,512]{2,1,0:T(8,128)S(1)} %copy-done.5, f32[2,16,512]{2,1,0:T(8,128)S(1)} %collective-permute-done.5, f32[1,16,512]{2,1,0:T(8,128)S(1)} %copy-done.8, f32[1,16,512]{2,1,0:T(8,128)S(1)} %copy-done.9, ...), kind=kLoop, calls=%fused_computation.245 | loop fusion | flops 131072 | bytes 458752 | tf_op jit(solution)/shard_map/add | solution.py:92
  61.6 1.0 %collective-permute-done.7 = f32[46,512]{1,0:T(8,128)S(1)} collective-permute-done((f32[46,512]{1,0:T(8,128)S(1)}, f32[46,512]{1,0:T(8,128)S(1)}, u32[]{:S(2)}, u32[]{:S(2)}) %collective-permute-start.7) | collective-permute-done | bytes 94240 | tf_op jit(solution)/shard_map/ppermute | solution.py:19
  62.7 0.8 %fusion.18 = (bf16[128,512]{1,0:T(8,128)(2,1)S(1)}, bf16[128,512]{1,0:T(8,128)(2,1)S(1)}) fusion(bf16[128,512]{1,0:T(8,128)(2,1)S(1)} %get-tuple-element.17, bf16[128,512]{1,0:T(8,128)(2,1)S(1)} %get-tuple-element.18, f32[128,512]{1,0:T(8,128)S(1)} %copy.38, f32[32,16,128]{2,1,0:T(8,128)S(1)} %broadcast_multiply_fusion.2, ...), kind=kOutput, calls=%fused_computation.72 | convolution fusion | flops 403570688 | bytes 1146880 | tf_op jit(solution)/shard_map/ks,kc->sc/dot_general | solution.py:168
  63.5 0.3 broadcast_multiply_fusion
  63.9 0.6 fusion.171
  64.6 0.6 fusion.135
  65.3 1.5 %fusion.22 = (bf16[128,512]{1,0:T(8,128)(2,1)S(1)}, bf16[128,512]{1,0:T(8,128)(2,1)}) fusion(bf16[128,512]{1,0:T(8,128)(2,1)S(1)} %copy-done, bf16[128,512]{1,0:T(8,128)(2,1)S(1)} %get-tuple-element.15, f32[128,512]{1,0:T(8,128)S(1)} %copy.32, f32[32,16,128]{2,1,0:T(8,128)S(1)} %get-tuple-element.44, f32[16,512]{1,0:T(8,128)S(1)} %get-tuple-element.20, ...), kind=kOutput, calls=%fused_computation.76 | convolution fusion | flops 403570688 | bytes 1146880 | tf_op jit(solution)/shard_map/kt,kc->tc/dot_general | solution.py:167
  66.9 0.9 %fusion.29 = bf16[128,512]{1,0:T(8,128)(2,1)} fusion(f32[6,512]{1,0:T(8,128)S(1)} %convert_element_type.273, f32[128,512]{1,0:T(8,128)S(1)} %convert_element_type.271, f32[512]{0:T(512)S(1)} %bitcast.189, f32[512]{0:T(512)S(1)} %bitcast.187, f32[512]{0:T(512)S(1)} %bitcast.177, f32[512]{0:T(512)S(1)} %bitcast.179, f32[512]{0:T(512)S(1)} %bitcast.181, ...), kind=kLoop, calls=%fused_computation.83 | loop fusion | flops 1310720 | bytes 419840 | tf_op jit(solution)/shard_map/convert_element_type | solution.py:206
  67.8 0.9 %fusion.46 = bf16[128,512]{1,0:T(8,128)(2,1)} fusion(f32[6,512]{1,0:T(8,128)S(1)} %convert_element_type.268, f32[128,512]{1,0:T(8,128)S(1)} %convert_element_type.264, f32[512]{0:T(512)S(1)} %bitcast.163, f32[512]{0:T(512)S(1)} %bitcast.165, f32[512]{0:T(512)S(1)} %bitcast.167, f32[512]{0:T(512)S(1)} %bitcast.169, f32[512]{0:T(512)S(1)} %bitcast.171, ...), kind=kLoop, calls=%fused_computation.100 | loop fusion | flops 1310720 | bytes 419840 | tf_op jit(solution)/shard_map/convert_element_type | solution.py:205
  68.7 0.9 %fusion.63 = bf16[128,512]{1,0:T(8,128)(2,1)} fusion(f32[6,512]{1,0:T(8,128)S(1)} %convert_element_type.259, f32[128,512]{1,0:T(8,128)S(1)} %convert_element_type.252, f32[512]{0:T(512)S(1)} %bitcast.151, f32[512]{0:T(512)S(1)} %bitcast.153, f32[512]{0:T(512)S(1)} %bitcast.155, f32[512]{0:T(512)S(1)} %bitcast.157, f32[512]{0:T(512)S(1)} %bitcast.159, ...), kind=kLoop, calls=%fused_computation.117 | loop fusion | flops 1310720 | bytes 419840 | tf_op jit(solution)/shard_map/convert_element_type | solution.py:204
  (161 shorter events, 0.7 us)
Async XLA Ops:
  0.6 9.5 %copy-start = (bf16[128,512]{1,0:T(8,128)(2,1)S(1)}, bf16[128,512]{1,0:T(8,128)(2,1)}, u32[]{:S(2)}) copy-start(bf16[128,512]{1,0:T(8,128)(2,1)} %param.13) | copy-start | bytes 393220
  2.1 10.3 %collective-permute-start = (bf16[3,6,512]{2,1,0:T(8,128)(2,1)S(1)}, bf16[3,6,512]{2,1,0:T(8,128)(2,1)S(1)}, u32[]{:S(2)}, u32[]{:S(2)}) collective-permute-start(bf16[3,6,512]{2,1,0:T(8,128)(2,1)S(1)} %pad_maximum_fusion.7), channel_id=1, source_target_pairs={{0,8},{8,16},{16,24},{24,32},{32,40},{40,48},{48,56},{56,64},{64,7... | collective-permute-start | bytes 55304 | tf_op jit(solution)/shard_map/ppermute | solution.py:19
  7.8 4.6 %copy-start.37 = (f32[1,1,512]{2,1,0:T(1,128)}, f32[1,1,512]{2,1,0:T(1,128)S(1)}, u32[]{:S(2)}) copy-start(f32[1,1,512]{2,1,0:T(1,128)S(1)} %get-tuple-element.66) | copy-start | bytes 6148
  7.8 4.6 %copy-start.39 = (f32[1,1,512]{2,1,0:T(1,128)}, f32[1,1,512]{2,1,0:T(1,128)S(1)}, u32[]{:S(2)}) copy-start(f32[1,1,512]{2,1,0:T(1,128)S(1)} %get-tuple-element.67) | copy-start | bytes 6148
  7.8 4.6 %copy-start.41 = (f32[1,1,512]{2,1,0:T(1,128)}, f32[1,1,512]{2,1,0:T(1,128)S(1)}, u32[]{:S(2)}) copy-start(f32[1,1,512]{2,1,0:T(1,128)S(1)} %get-tuple-element.68) | copy-start | bytes 6148
  7.8 4.6 %copy-start.43 = (f32[1,1,512]{2,1,0:T(1,128)}, f32[1,1,512]{2,1,0:T(1,128)S(1)}, u32[]{:S(2)}) copy-start(f32[1,1,512]{2,1,0:T(1,128)S(1)} %get-tuple-element.69) | copy-start | bytes 6148
  7.8 4.6 %copy-start.45 = (f32[1,1,512]{2,1,0:T(1,128)}, f32[1,1,512]{2,1,0:T(1,128)S(1)}, u32[]{:S(2)}) copy-start(f32[1,1,512]{2,1,0:T(1,128)S(1)} %get-tuple-element.70) | copy-start | bytes 6148
  7.9 4.6 %copy-start.47 = (f32[1,1,512]{2,1,0:T(1,128)}, f32[1,1,512]{2,1,0:T(1,128)S(1)}, u32[]{:S(2)}) copy-start(f32[1,1,512]{2,1,0:T(1,128)S(1)} %get-tuple-element.71) | copy-start | bytes 6148
  7.9 4.6 %copy-start.49 = (f32[1,1,512]{2,1,0:T(1,128)}, f32[1,1,512]{2,1,0:T(1,128)S(1)}, u32[]{:S(2)}) copy-start(f32[1,1,512]{2,1,0:T(1,128)S(1)} %get-tuple-element.72) | copy-start | bytes 6148
  7.9 4.6 %copy-start.51 = (f32[1,1,512]{2,1,0:T(1,128)}, f32[1,1,512]{2,1,0:T(1,128)S(1)}, u32[]{:S(2)}) copy-start(f32[1,1,512]{2,1,0:T(1,128)S(1)} %get-tuple-element.61) | copy-start | bytes 6148
  7.9 4.6 %copy-start.53 = (f32[1,1,512]{2,1,0:T(1,128)}, f32[1,1,512]{2,1,0:T(1,128)S(1)}, u32[]{:S(2)}) copy-start(f32[1,1,512]{2,1,0:T(1,128)S(1)} %get-tuple-element.62) | copy-start | bytes 6148
  7.9 4.6 %copy-start.55 = (f32[1,1,512]{2,1,0:T(1,128)}, f32[1,1,512]{2,1,0:T(1,128)S(1)}, u32[]{:S(2)}) copy-start(f32[1,1,512]{2,1,0:T(1,128)S(1)} %get-tuple-element.63) | copy-start | bytes 6148
  7.9 4.6 %copy-start.57 = (f32[1,1,512]{2,1,0:T(1,128)}, f32[1,1,512]{2,1,0:T(1,128)S(1)}, u32[]{:S(2)}) copy-start(f32[1,1,512]{2,1,0:T(1,128)S(1)} %get-tuple-element.64) | copy-start | bytes 6148
  7.9 4.6 %copy-start.59 = (f32[1,1,512]{2,1,0:T(1,128)}, f32[1,1,512]{2,1,0:T(1,128)S(1)}, u32[]{:S(2)}) copy-start(f32[1,1,512]{2,1,0:T(1,128)S(1)} %get-tuple-element.65) | copy-start | bytes 6148
  7.9 5.1 %copy-start.23 = (f32[1,1,512]{2,1,0:T(1,128)}, f32[1,1,512]{2,1,0:T(1,128)S(1)}, u32[]{:S(2)}) copy-start(f32[1,1,512]{2,1,0:T(1,128)S(1)} %get-tuple-element.60) | copy-start | bytes 6148
  7.9 5.1 %copy-start.25 = (f32[1,1,512]{2,1,0:T(1,128)}, f32[1,1,512]{2,1,0:T(1,128)S(1)}, u32[]{:S(2)}) copy-start(f32[1,1,512]{2,1,0:T(1,128)S(1)} %get-tuple-element.73) | copy-start | bytes 6148
  7.9 5.1 %copy-start.27 = (f32[1,1,512]{2,1,0:T(1,128)}, f32[1,1,512]{2,1,0:T(1,128)S(1)}, u32[]{:S(2)}) copy-start(f32[1,1,512]{2,1,0:T(1,128)S(1)} %get-tuple-element.74) | copy-start | bytes 6148
  8.0 5.1 %copy-start.29 = (f32[1,1,512]{2,1,0:T(1,128)}, f32[1,1,512]{2,1,0:T(1,128)S(1)}, u32[]{:S(2)}) copy-start(f32[1,1,512]{2,1,0:T(1,128)S(1)} %get-tuple-element.75) | copy-start | bytes 6148
  8.0 5.1 %copy-start.31 = (f32[1,1,512]{2,1,0:T(1,128)}, f32[1,1,512]{2,1,0:T(1,128)S(1)}, u32[]{:S(2)}) copy-start(f32[1,1,512]{2,1,0:T(1,128)S(1)} %get-tuple-element.76) | copy-start | bytes 6148
  8.0 5.1 %copy-start.33 = (f32[1,1,512]{2,1,0:T(1,128)}, f32[1,1,512]{2,1,0:T(1,128)S(1)}, u32[]{:S(2)}) copy-start(f32[1,1,512]{2,1,0:T(1,128)S(1)} %get-tuple-element.77) | copy-start | bytes 6148
  8.0 5.1 %copy-start.35 = (f32[1,1,512]{2,1,0:T(1,128)}, f32[1,1,512]{2,1,0:T(1,128)S(1)}, u32[]{:S(2)}) copy-start(f32[1,1,512]{2,1,0:T(1,128)S(1)} %get-tuple-element.78) | copy-start | bytes 6148
  8.8 3.7 %copy-start.61 = (f32[1,1,512]{2,1,0:T(1,128)}, f32[1,1,512]{2,1,0:T(1,128)S(1)}, u32[]{:S(2)}) copy-start(f32[1,1,512]{2,1,0:T(1,128)S(1)} %get-tuple-element.79) | copy-start | bytes 6148
  8.8 3.7 %copy-start.63 = (f32[1,1,512]{2,1,0:T(1,128)}, f32[1,1,512]{2,1,0:T(1,128)S(1)}, u32[]{:S(2)}) copy-start(f32[1,1,512]{2,1,0:T(1,128)S(1)} %get-tuple-element.80) | copy-start | bytes 6148
  14.2 7.1 %copy-start.22 = (f32[32,16]{0,1:T(8,128)S(1)}, f32[32,16]{0,1:T(8,128)}, u32[]{:S(2)}) copy-start(f32[32,16]{0,1:T(8,128)} %param.11) | copy-start | bytes 6148
  14.8 6.4 %collective-permute-start.1 = (f32[2,16,512]{2,1,0:T(8,128)S(1)}, f32[2,16,512]{2,1,0:T(8,128)S(1)}, u32[]{:S(2)}, u32[]{:S(2)}) collective-permute-start(f32[2,16,512]{2,1,0:T(8,128)S(1)} %pad_maximum_fusion.6), channel_id=1, source_target_pairs={{0,8},{8,0},{16,24},{24,16},{32,40},{40,32},{48,56},{56,48},{1,9},... | collective-permute-start | bytes 196616 | tf_op jit(solution)/shard_map/ppermute | solution.py:89
  21.4 6.5 %collective-permute-start.2 = (f32[2,16,512]{2,1,0:T(8,128)S(1)}, f32[2,16,512]{2,1,0:T(8,128)S(1)}, u32[]{:S(2)}, u32[]{:S(2)}) collective-permute-start(f32[2,16,512]{2,1,0:T(8,128)S(1)} %fusion.155), channel_id=1, source_target_pairs={{0,16},{8,24},{16,0},{24,8},{32,48},{40,56},{48,32},{56,40},{1,17}... | collective-permute-start | bytes 196616 | tf_op jit(solution)/shard_map/ppermute | solution.py:89
  27.8 6.6 %copy-start.10 = (f32[1,16,512]{2,1,0:T(8,128)S(1)}, f32[1,16,512]{2,1,0:T(8,128)}, u32[]{:S(2)}) copy-start(f32[1,16,512]{2,1,0:T(8,128)} %get-tuple-element.34) | copy-start | bytes 98308
  27.8 6.6 %copy-start.11 = (f32[1,16,512]{2,1,0:T(8,128)S(1)}, f32[1,16,512]{2,1,0:T(8,128)}, u32[]{:S(2)}) copy-start(f32[1,16,512]{2,1,0:T(8,128)} %get-tuple-element.39) | copy-start | bytes 98308
  27.8 6.6 %copy-start.12 = (f32[1,16,512]{2,1,0:T(8,128)S(1)}, f32[1,16,512]{2,1,0:T(8,128)}, u32[]{:S(2)}) copy-start(f32[1,16,512]{2,1,0:T(8,128)} %get-tuple-element.40) | copy-start | bytes 98308
  27.8 6.6 %copy-start.13 = (f32[1,16,512]{2,1,0:T(8,128)S(1)}, f32[1,16,512]{2,1,0:T(8,128)}, u32[]{:S(2)}) copy-start(f32[1,16,512]{2,1,0:T(8,128)} %get-tuple-element.41) | copy-start | bytes 98308
  27.8 6.6 %copy-start.14 = (f32[1,16,512]{2,1,0:T(8,128)S(1)}, f32[1,16,512]{2,1,0:T(8,128)}, u32[]{:S(2)}) copy-start(f32[1,16,512]{2,1,0:T(8,128)} %get-tuple-element.42) | copy-start | bytes 98308
  27.9 6.6 %copy-start.15 = (f32[1,16,512]{2,1,0:T(8,128)S(1)}, f32[1,16,512]{2,1,0:T(8,128)}, u32[]{:S(2)}) copy-start(f32[1,16,512]{2,1,0:T(8,128)} %get-tuple-element.21) | copy-start | bytes 98308
  27.9 6.6 %copy-start.16 = (f32[1,16,512]{2,1,0:T(8,128)S(1)}, f32[1,16,512]{2,1,0:T(8,128)}, u32[]{:S(2)}) copy-start(f32[1,16,512]{2,1,0:T(8,128)} %get-tuple-element.23) | copy-start | bytes 98308
  27.9 6.6 %copy-start.17 = (f32[1,16,512]{2,1,0:T(8,128)S(1)}, f32[1,16,512]{2,1,0:T(8,128)}, u32[]{:S(2)}) copy-start(f32[1,16,512]{2,1,0:T(8,128)} %get-tuple-element.33) | copy-start | bytes 98308
  28.0 6.5 %collective-permute-start.3 = (f32[2,16,512]{2,1,0:T(8,128)S(1)}, f32[2,16,512]{2,1,0:T(8,128)S(1)}, u32[]{:S(2)}, u32[]{:S(2)}) collective-permute-start(f32[2,16,512]{2,1,0:T(8,128)S(1)} %fusion.156), channel_id=1, source_target_pairs={{0,32},{8,40},{16,48},{24,56},{32,0},{40,8},{48,16},{56,24},{1,33}... | collective-permute-start | bytes 196616 | tf_op jit(solution)/shard_map/ppermute | solution.py:89
  34.6 11.3 %copy-start.20 = (f32[1,16,512]{2,1,0:T(8,128)S(1)}, f32[1,16,512]{2,1,0:T(8,128)}, u32[]{:S(2)}) copy-start(f32[1,16,512]{2,1,0:T(8,128)} %get-tuple-element.25) | copy-start | bytes 98308
  34.6 5.0 %collective-permute-start.4 = (f32[2,16,512]{2,1,0:T(8,128)S(1)}, f32[2,16,512]{2,1,0:T(8,128)S(1)}, u32[]{:S(2)}, u32[]{:S(2)}) collective-permute-start(f32[2,16,512]{2,1,0:T(8,128)S(1)} %get-tuple-element.59), channel_id=1, source_target_pairs={{0,64},{64,0},{128,192},{192,128},{256,320},{320,256},{384,448},{4... | collective-permute-start | bytes 196616 | tf_op jit(solution)/shard_map/ppermute | solution.py:89
  37.2 17.1 %copy-start.21 = (f32[6,512]{1,0:T(8,128)S(1)}, f32[6,512]{1,0:T(8,128)}, u32[]{:S(2)}) copy-start(f32[6,512]{1,0:T(8,128)} %slice_convert_fusion.1) | copy-start | bytes 36868
  39.6 21.1 %copy-start.4 = (f32[1,16,512]{2,1,0:T(8,128)S(1)}, f32[1,16,512]{2,1,0:T(8,128)}, u32[]{:S(2)}) copy-start(f32[1,16,512]{2,1,0:T(8,128)} %get-tuple-element.35) | copy-start | bytes 98308
  39.6 21.1 %copy-start.5 = (f32[1,16,512]{2,1,0:T(8,128)S(1)}, f32[1,16,512]{2,1,0:T(8,128)}, u32[]{:S(2)}) copy-start(f32[1,16,512]{2,1,0:T(8,128)} %get-tuple-element.36) | copy-start | bytes 98308
  39.6 21.1 %copy-start.6 = (f32[1,16,512]{2,1,0:T(8,128)S(1)}, f32[1,16,512]{2,1,0:T(8,128)}, u32[]{:S(2)}) copy-start(f32[1,16,512]{2,1,0:T(8,128)} %get-tuple-element.28) | copy-start | bytes 98308
  39.6 21.1 %copy-start.7 = (f32[1,16,512]{2,1,0:T(8,128)S(1)}, f32[1,16,512]{2,1,0:T(8,128)}, u32[]{:S(2)}) copy-start(f32[1,16,512]{2,1,0:T(8,128)} %get-tuple-element.29) | copy-start | bytes 98308
  39.6 21.1 %copy-start.8 = (f32[1,16,512]{2,1,0:T(8,128)S(1)}, f32[1,16,512]{2,1,0:T(8,128)}, u32[]{:S(2)}) copy-start(f32[1,16,512]{2,1,0:T(8,128)} %get-tuple-element.31) | copy-start | bytes 98308
  39.6 21.1 %copy-start.9 = (f32[1,16,512]{2,1,0:T(8,128)S(1)}, f32[1,16,512]{2,1,0:T(8,128)}, u32[]{:S(2)}) copy-start(f32[1,16,512]{2,1,0:T(8,128)} %get-tuple-element.32) | copy-start | bytes 98308
  39.7 6.2 %collective-permute-start.5 = (f32[2,16,512]{2,1,0:T(8,128)S(1)}, f32[2,16,512]{2,1,0:T(8,128)S(1)}, u32[]{:S(2)}, u32[]{:S(2)}) collective-permute-start(f32[2,16,512]{2,1,0:T(8,128)S(1)} %fusion.160), channel_id=1, source_target_pairs={{0,128},{64,192},{128,0},{192,64},{256,384},{320,448},{384,256},{4... | collective-permute-start | bytes 196616 | tf_op jit(solution)/shard_map/ppermute | solution.py:89
  46.5 14.1 %collective-permute-start.6 = (f32[2,16,512]{2,1,0:T(8,128)}, f32[2,16,512]{2,1,0:T(8,128)}, u32[]{:S(2)}, u32[]{:S(2)}) collective-permute-start(f32[2,16,512]{2,1,0:T(8,128)} %fusion.161), channel_id=1, source_target_pairs={{0,256},{64,320},{128,384},{192,448},{256,0},{320,64},{384,128},{4... | collective-permute-start | bytes 196616 | tf_op jit(solution)/shard_map/ppermute | solution.py:89
  54.6 8.0 %collective-permute-start.7 = (f32[46,512]{1,0:T(8,128)S(1)}, f32[46,512]{1,0:T(8,128)S(1)}, u32[]{:S(2)}, u32[]{:S(2)}) collective-permute-start(f32[46,512]{1,0:T(8,128)S(1)} %concatenate.24), channel_id=1, source_target_pairs={{8,0},{16,8},{24,16},{32,24},{40,32},{48,40},{56,48},{64,56},{72,6... | collective-permute-start | bytes 282632 | tf_op jit(solution)/shard_map/ppermute | solution.py:19
  63.8 3.0 %copy-start.52 = (f32[1,1,512]{2,1,0:T(1,128)S(1)}, f32[1,1,512]{2,1,0:T(1,128)}, u32[]{:S(2)}) copy-start(f32[1,1,512]{2,1,0:T(1,128)} %copy-done.51) | copy-start | bytes 6148
  63.8 3.0 %copy-start.54 = (f32[1,1,512]{2,1,0:T(1,128)S(1)}, f32[1,1,512]{2,1,0:T(1,128)}, u32[]{:S(2)}) copy-start(f32[1,1,512]{2,1,0:T(1,128)} %copy-done.53) | copy-start | bytes 6148
  63.8 3.0 %copy-start.56 = (f32[1,1,512]{2,1,0:T(1,128)S(1)}, f32[1,1,512]{2,1,0:T(1,128)}, u32[]{:S(2)}) copy-start(f32[1,1,512]{2,1,0:T(1,128)} %copy-done.55) | copy-start | bytes 6148
  64.5 3.3 %copy-start.38 = (f32[1,1,512]{2,1,0:T(1,128)S(1)}, f32[1,1,512]{2,1,0:T(1,128)}, u32[]{:S(2)}) copy-start(f32[1,1,512]{2,1,0:T(1,128)} %copy-done.37) | copy-start | bytes 6148
  64.5 3.3 %copy-start.40 = (f32[1,1,512]{2,1,0:T(1,128)S(1)}, f32[1,1,512]{2,1,0:T(1,128)}, u32[]{:S(2)}) copy-start(f32[1,1,512]{2,1,0:T(1,128)} %copy-done.39) | copy-start | bytes 6148
  64.5 3.3 %copy-start.42 = (f32[1,1,512]{2,1,0:T(1,128)S(1)}, f32[1,1,512]{2,1,0:T(1,128)}, u32[]{:S(2)}) copy-start(f32[1,1,512]{2,1,0:T(1,128)} %copy-done.41) | copy-start | bytes 6148
  64.5 3.3 %copy-start.44 = (f32[1,1,512]{2,1,0:T(1,128)S(1)}, f32[1,1,512]{2,1,0:T(1,128)}, u32[]{:S(2)}) copy-start(f32[1,1,512]{2,1,0:T(1,128)} %copy-done.43) | copy-start | bytes 6148
  64.5 3.3 %copy-start.46 = (f32[1,1,512]{2,1,0:T(1,128)S(1)}, f32[1,1,512]{2,1,0:T(1,128)}, u32[]{:S(2)}) copy-start(f32[1,1,512]{2,1,0:T(1,128)} %copy-done.45) | copy-start | bytes 6148
  64.5 3.3 %copy-start.48 = (f32[1,1,512]{2,1,0:T(1,128)S(1)}, f32[1,1,512]{2,1,0:T(1,128)}, u32[]{:S(2)}) copy-start(f32[1,1,512]{2,1,0:T(1,128)} %copy-done.47) | copy-start | bytes 6148
  64.5 3.3 %copy-start.50 = (f32[1,1,512]{2,1,0:T(1,128)S(1)}, f32[1,1,512]{2,1,0:T(1,128)}, u32[]{:S(2)}) copy-start(f32[1,1,512]{2,1,0:T(1,128)} %copy-done.49) | copy-start | bytes 6148
  64.5 4.2 %copy-start.24 = (f32[1,1,512]{2,1,0:T(1,128)S(1)}, f32[1,1,512]{2,1,0:T(1,128)}, u32[]{:S(2)}) copy-start(f32[1,1,512]{2,1,0:T(1,128)} %copy-done.23) | copy-start | bytes 6148
  64.5 4.2 %copy-start.26 = (f32[1,1,512]{2,1,0:T(1,128)S(1)}, f32[1,1,512]{2,1,0:T(1,128)}, u32[]{:S(2)}) copy-start(f32[1,1,512]{2,1,0:T(1,128)} %copy-done.25) | copy-start | bytes 6148
  64.5 4.2 %copy-start.28 = (f32[1,1,512]{2,1,0:T(1,128)S(1)}, f32[1,1,512]{2,1,0:T(1,128)}, u32[]{:S(2)}) copy-start(f32[1,1,512]{2,1,0:T(1,128)} %copy-done.27) | copy-start | bytes 6148
  64.6 4.2 %copy-start.30 = (f32[1,1,512]{2,1,0:T(1,128)S(1)}, f32[1,1,512]{2,1,0:T(1,128)}, u32[]{:S(2)}) copy-start(f32[1,1,512]{2,1,0:T(1,128)} %copy-done.29) | copy-start | bytes 6148
  64.6 4.2 %copy-start.32 = (f32[1,1,512]{2,1,0:T(1,128)S(1)}, f32[1,1,512]{2,1,0:T(1,128)}, u32[]{:S(2)}) copy-start(f32[1,1,512]{2,1,0:T(1,128)} %copy-done.31) | copy-start | bytes 6148
  64.6 4.2 %copy-start.34 = (f32[1,1,512]{2,1,0:T(1,128)S(1)}, f32[1,1,512]{2,1,0:T(1,128)}, u32[]{:S(2)}) copy-start(f32[1,1,512]{2,1,0:T(1,128)} %copy-done.33) | copy-start | bytes 6148
  64.6 4.2 %copy-start.36 = (f32[1,1,512]{2,1,0:T(1,128)S(1)}, f32[1,1,512]{2,1,0:T(1,128)}, u32[]{:S(2)}) copy-start(f32[1,1,512]{2,1,0:T(1,128)} %copy-done.35) | copy-start | bytes 6148
  (9 other events, 20.8 us)

commit v18 on v17

--- a/solution.py
+++ b/solution.py
@@ -109,8 +109,8 @@
     q_short = to_bf16(short_causal(before[0], u_query, short_filter[0]))
     k_short = to_bf16(short_causal(before[1], u_key, short_filter[1]))
     v_short = to_bf16(short_causal(before[2], u_value, short_filter[2]))
-    product = rounded(k_short.astype(jnp.float32) * v_short.astype(jnp.float32))
-    grad_conv = rounded(grad_out.astype(jnp.float32) * q_short.astype(jnp.float32))
+    product = to_bf16(k_short.astype(jnp.float32) * v_short.astype(jnp.float32))
+    grad_conv = to_bf16(grad_out.astype(jnp.float32) * q_short.astype(jnp.float32))
 
     rates = decay_rate
     weights = residue * jnp.sqrt(-jnp.expm1(-2.0 * rates))

time: 70.9 us -> 70.7 us (level)
    convert_element_type x0 -> x2, other arithmetic: none -> 0.76 us  [to_bf16(): lax.reduce_precision(values, exponent_bits=8, mantissa_bits=7)]
    convert_element_type x4 -> x2, other arithmetic: 0.78 us -> 0.02 us  [rounded(): return lax.optimization_barrier(values.astype(jnp.bfloat16))]
where the time goes in v18:
time: 70.7 us; the launch traced here: 69.4 us
  starting transfers between devices  34.1 us (48%)
  matrix products  10.4 us (15%)
  other arithmetic  9.26 us (13%)
  waiting for transfers between devices  8.07 us (11%)
  local copies, waits for them, and re-layouts  5.63 us (8%)
  between operations  1.94 us (3%)
    ppermute x6, starting transfers between devices, cube_scan(): lax.ppermute(window, axis, [(source, source ^ shift) for source in range(...  23.8 us
    ppermute x2, starting transfers between devices, from_behind(): lax.ppermute(value, axis, [(source, source + steps) for source in range(l...  10.3 us
    ppermute x6, waiting for transfers between devices, cube_scan(): lax.ppermute(window, axis, [(source, source ^ shift) for source in range(...  7.02 us
    dot_general x1, matrix products, shards(): toeplitz = jnp.einsum('gtm,gms->gts', falling, rising, precision=precise)  3.65 us
    slice x2, local copies, waits for them, and re-layouts, short_causal(): filter_taps[offset] * padded[SHORT - 1 - offset:SHORT - 1 - offset + length]  1.97 us
    dot_general x4, matrix products, split_dot(): jnp.einsum(spec, low, values, preferred_element_type=jnp.float32)  1.63 us
    dot_general x4, matrix products, split_dot(): jnp.einsum(spec, high.astype(jnp.bfloat16), values, preferred_element_typ...  1.55 us
    dot_general x1, matrix products, shards(): jnp.einsum('kt,kc->tc', lead_fwd, spread(entering), precision=precise)  1.48 us
  transfers between devices with their start and end apart: 8, of which 4 were waited for; matrix products, arithmetic and copies ran while one was open for 20% of the time, Pallas kernels for 0%

profile of v18, /device:TPU:1, one launch (start us, length us, event | category | flops | bytes accessed | tf_op | source)
XLA Modules:
  0.0 69.4 jit_solution(13865584842196764437)
XLA Ops:
  0.6 0.7 %slice_bitcast_fusion.6 = bf16[1,6,512]{2,1,0:T(8,128)(2,1)S(1)} fusion(bf16[128,512]{1,0:T(8,128)(2,1)} %param.7), kind=kLoop, calls=%fused_computation.319 | loop fusion | bytes 12288 | tf_op jit(solution)/shard_map/stack | solution.py:101
  1.4 0.7 %slice_bitcast_fusion.4 = (bf16[1,6,512]{2,1,0:T(8,128)(2,1)S(1)}, bf16[1,6,512]{2,1,0:T(8,128)(2,1)S(1)}) fusion(bf16[128,512]{1,0:T(8,128)(2,1)} %param.9, bf16[128,512]{1,0:T(8,128)(2,1)} %param.8), kind=kLoop, calls=%fused_computation.317 | loop fusion | bytes 24576 | tf_op jit(solution)/shard_map/stack | solution.py:101
  2.1 4.5 %collective-permute-start = (bf16[3,6,512]{2,1,0:T(8,128)(2,1)S(1)}, bf16[3,6,512]{2,1,0:T(8,128)(2,1)S(1)}, u32[]{:S(2)}, u32[]{:S(2)}) collective-permute-start(bf16[3,6,512]{2,1,0:T(8,128)(2,1)S(1)} %pad_maximum_fusion.7), channel_id=1, source_target_pairs={{0,8},{8,16},{16,24},{24,32},{32,40},{40,48},{48,56},{56,64},{64,7... | collective-permute-start | bytes 55304 | tf_op jit(solution)/shard_map/ppermute | solution.py:19
  6.6 1.2 %fusion.193 = (f32[1,1,512]{2,1,0:T(1,128)S(1)}, f32[1,1,512]{2,1,0:T(1,128)S(1)}, f32[1,1,512]{2,1,0:T(1,128)S(1)}, f32[1,1,512]{2,1,0:T(1,128)S(1)}, f32[1,1,5...) fusion(f32[3,7,512]{2,1,0:T(8,128)} %param.10), kind=kLoop, calls=%fused_computation.336 | loop fusion | bytes 77824 | tf_op jit(solution)/shard_map/slice | solution.py:36
  8.0 0.8 %fusion.194 = (f32[1,1,512]{2,1,0:T(1,128)S(1)}, f32[1,1,512]{2,1,0:T(1,128)S(1)}) fusion(f32[3,7,512]{2,1,0:T(8,128)} %param.10), kind=kLoop, calls=%fused_computation.337 | loop fusion | bytes 8192 | tf_op jit(solution)/shard_map/slice | solution.py:36
  8.8 0.7 %negate_bitcast_fusion = (f32[16,32]{1,0:T(8,128)S(1)}, f32[32,16]{0,1:T(8,128)S(1)}, f32[32,16]{0,1:T(8,128)S(1)}) fusion(f32[32,16]{0,1:T(8,128)} %param.11, f32[32,16]{0,1:T(8,128)} %param.12), kind=kLoop, calls=%fused_computation.315 | loop fusion | flops 3072 | bytes 10240 | tf_op jit(solution)/shard_map/neg | solution.py:145
  9.6 0.1 copy.25
  9.6 0.1 multiply_exponential_fusion.1
  9.8 0.1 rev.6
  10.1 0.0 copy-start.3
  10.2 0.1 broadcast_in_dim.12
  10.4 0.2 neg.35
  10.5 0.1 stack.155
  10.6 0.2 multiply_exponential_fusion
  10.8 0.7 slice_select_fusion.6
  11.5 0.7 %slice_select_fusion.7 = (f32[1,16,512]{2,1,0:T(8,128)}, f32[1,16,512]{2,1,0:T(8,128)}, f32[1,16,512]{2,1,0:T(8,128)}, f32[1,16,512]{2,1,0:T(8,128)S(1)}, f32[1,...) fusion(f32[22,16,512]{2,1,0:T(8,128)S(1)} %multiply_exponential, ...), kind=kLoop, calls=%fused_computation.280 | loop fusion | flops 106496 | bytes 753670 | tf_op jit(solution)/shard_map/jit(_where)/select_n | solution.py:78
  12.5 0.5 fusion.20
  13.0 0.3 fusion.195
  13.2 0.3 convolution_add_fusion.1
  13.6 0.3 fusion.23
  13.9 0.3 fusion.196
  14.2 0.3 convolution_add_fusion
  14.4 0.3 multiply_reduce_fusion.1
  14.7 5.6 %collective-permute-start.1 = (f32[2,16,512]{2,1,0:T(8,128)S(1)}, f32[2,16,512]{2,1,0:T(8,128)S(1)}, u32[]{:S(2)}, u32[]{:S(2)}) collective-permute-start(f32[2,16,512]{2,1,0:T(8,128)S(1)} %pad_maximum_fusion.6), channel_id=1, source_target_pairs={{0,8},{8,0},{16,24},{24,16},{32,40},{40,32},{48,56},{56,48},{1,9},... | collective-permute-start | bytes 196616 | tf_op jit(solution)/shard_map/ppermute | solution.py:89
  20.3 0.6 slice_convert_fusion.1
  20.9 0.1 copy.33
  21.0 0.1 copy.24
  21.2 0.0 collective-permute-done.1
  21.2 0.1 copy.26
  21.3 0.1 copy.27
  21.4 1.9 %collective-permute-start.2 = (f32[2,16,512]{2,1,0:T(8,128)S(1)}, f32[2,16,512]{2,1,0:T(8,128)S(1)}, u32[]{:S(2)}, u32[]{:S(2)}) collective-permute-start(f32[2,16,512]{2,1,0:T(8,128)S(1)} %fusion.157), channel_id=1, source_target_pairs={{0,16},{8,24},{16,0},{24,8},{32,48},{40,56},{48,32},{56,40},{1,17}... | collective-permute-start | bytes 196616 | tf_op jit(solution)/shard_map/ppermute | solution.py:89
  23.3 3.7 %fusion.142 = f32[32,128,128]{2,1,0:T(8,128)S(1)} fusion(f32[32,16]{1,0:T(8,128)S(1)} %copy.27, f32[128]{0:T(128)S(1)} %get-tuple-element.89, f32[128]{0:T(128)S(1)} %get-tuple-element.90, f32[32,16]{1,0:T(8,128)S(1)} %copy.26), kind=kOutput, calls=%fused_computation.220 | convolution fusion | flops 100859904 | bytes 2102272 | tf_op jit(solution)/shard_map/gtm,gms->gts/dot_general | solution.py:158
  27.0 0.4 fusion.15
  27.3 0.4 convolution_add_fusion.2
  27.8 0.0 copy-start.7
  27.9 2.6 %collective-permute-start.3 = (f32[2,16,512]{2,1,0:T(8,128)S(1)}, f32[2,16,512]{2,1,0:T(8,128)S(1)}, u32[]{:S(2)}, u32[]{:S(2)}) collective-permute-start(f32[2,16,512]{2,1,0:T(8,128)S(1)} %fusion.158), channel_id=1, source_target_pairs={{0,32},{8,40},{16,48},{24,56},{32,0},{40,8},{48,16},{56,24},{1,33}... | collective-permute-start | bytes 196616 | tf_op jit(solution)/shard_map/ppermute | solution.py:89
  30.5 0.6 fusion.16
  31.1 3.3 %collective-permute-done.3 = f32[2,16,512]{2,1,0:T(8,128)S(1)} collective-permute-done((f32[2,16,512]{2,1,0:T(8,128)S(1)}, f32[2,16,512]{2,1,0:T(8,128)S(1)}, u32[]{:S(2)}, u32[]{:S(2)}) %collective-permute-start.3) | collective-permute-done | bytes 65568 | tf_op jit(solution)/shard_map/ppermute | solution.py:89
  34.5 1.9 %collective-permute-start.4 = (f32[2,16,512]{2,1,0:T(8,128)S(1)}, f32[2,16,512]{2,1,0:T(8,128)S(1)}, u32[]{:S(2)}, u32[]{:S(2)}) collective-permute-start(f32[2,16,512]{2,1,0:T(8,128)S(1)} %get-tuple-element.59), channel_id=1, source_target_pairs={{0,64},{64,0},{128,192},{192,128},{256,320},{320,256},{384,448},{4... | collective-permute-start | bytes 196616 | tf_op jit(solution)/shard_map/ppermute | solution.py:89
  36.4 0.7 convolution_add_fusion.3
  37.1 2.4 %collective-permute-done.4 = f32[2,16,512]{2,1,0:T(8,128)S(1)} collective-permute-done((f32[2,16,512]{2,1,0:T(8,128)S(1)}, f32[2,16,512]{2,1,0:T(8,128)S(1)}, u32[]{:S(2)}, u32[]{:S(2)}) %collective-permute-start.4) | collective-permute-done | bytes 65568 | tf_op jit(solution)/shard_map/ppermute | solution.py:89
  39.5 4.5 %collective-permute-start.5 = (f32[2,16,512]{2,1,0:T(8,128)S(1)}, f32[2,16,512]{2,1,0:T(8,128)S(1)}, u32[]{:S(2)}, u32[]{:S(2)}) collective-permute-start(f32[2,16,512]{2,1,0:T(8,128)S(1)} %fusion.162), channel_id=1, source_target_pairs={{0,128},{64,192},{128,0},{192,64},{256,384},{320,448},{384,256},{4... | collective-permute-start | bytes 196616 | tf_op jit(solution)/shard_map/ppermute | solution.py:89
  44.0 0.2 fusion.192
  44.2 0.1 rev.7
  44.3 1.3 %collective-permute-done.5 = f32[2,16,512]{2,1,0:T(8,128)S(1)} collective-permute-done((f32[2,16,512]{2,1,0:T(8,128)S(1)}, f32[2,16,512]{2,1,0:T(8,128)S(1)}, u32[]{:S(2)}, u32[]{:S(2)}) %collective-permute-start.5) | collective-permute-done | bytes 65568 | tf_op jit(solution)/shard_map/ppermute | solution.py:89
  45.6 0.6 fusion.163
  46.3 7.3 %collective-permute-start.6 = (f32[2,16,512]{2,1,0:T(8,128)}, f32[2,16,512]{2,1,0:T(8,128)}, u32[]{:S(2)}, u32[]{:S(2)}) collective-permute-start(f32[2,16,512]{2,1,0:T(8,128)} %fusion.163), channel_id=1, source_target_pairs={{0,256},{64,320},{128,384},{192,448},{256,0},{320,64},{384,128},{4... | collective-permute-start | bytes 196616 | tf_op jit(solution)/shard_map/ppermute | solution.py:89
  53.6 0.1 broadcast_multiply_fusion.2
  53.7 0.1 copy.43
  53.8 0.1 copy.35
  54.0 0.3 concatenate.24
  54.3 5.8 %collective-permute-start.7 = (f32[46,512]{1,0:T(8,128)S(1)}, f32[46,512]{1,0:T(8,128)S(1)}, u32[]{:S(2)}, u32[]{:S(2)}) collective-permute-start(f32[46,512]{1,0:T(8,128)S(1)} %concatenate.24), channel_id=1, source_target_pairs={{8,0},{16,8},{24,16},{32,24},{40,32},{48,40},{56,48},{64,56},{72,6... | collective-permute-start | bytes 282632 | tf_op jit(solution)/shard_map/ppermute | solution.py:19
  60.1 0.1 copy.38
  60.3 0.1 copy.32
  60.4 0.9 %fusion.160 = f32[2,16,512]{2,1,0:T(8,128)S(1)} fusion(f32[2,16,512]{2,1,0:T(8,128)S(1)} %collective-permute-done.4, f32[1,16,512]{2,1,0:T(8,128)S(1)} %get-tuple-element.35, f32[1,16,512]{2,1,0:T(8,128)S(1)} %get-tuple-element.36, f32[2,16,512]{2,1,0:T(8,128)S(1)} %collective-permute-done.5, f32[1,16,512]{2,1,0:T(8,128)S(1)} %get-tuple-element.31, ...), kind=kLoop, calls=%fused_computation.247 | loop fusion | flops 131072 | bytes 458752 | tf_op jit(solution)/shard_map/add | solution.py:92
  61.3 1.0 %collective-permute-done.7 = f32[46,512]{1,0:T(8,128)S(1)} collective-permute-done((f32[46,512]{1,0:T(8,128)S(1)}, f32[46,512]{1,0:T(8,128)S(1)}, u32[]{:S(2)}, u32[]{:S(2)}) %collective-permute-start.7) | collective-permute-done | bytes 94240 | tf_op jit(solution)/shard_map/ppermute | solution.py:19
  62.4 0.8 %fusion.18 = (bf16[128,512]{1,0:T(8,128)(2,1)S(1)}, bf16[128,512]{1,0:T(8,128)(2,1)S(1)}) fusion(bf16[128,512]{1,0:T(8,128)(2,1)S(1)} %get-tuple-element.17, bf16[128,512]{1,0:T(8,128)(2,1)S(1)} %get-tuple-element.18, f32[128,512]{1,0:T(8,128)S(1)} %copy.38, f32[32,16,128]{2,1,0:T(8,128)S(1)} %broadcast_multiply_fusion.2, ...), kind=kOutput, calls=%fused_computation.72 | convolution fusion | flops 403570688 | bytes 1146880 | tf_op jit(solution)/shard_map/ks,kc->sc/dot_general | solution.py:168
  63.2 0.3 broadcast_multiply_fusion
  63.6 0.6 fusion.173
  64.3 0.6 fusion.137
  65.0 1.5 %fusion.24 = (bf16[128,512]{1,0:T(8,128)(2,1)S(1)}, bf16[128,512]{1,0:T(8,128)(2,1)}) fusion(bf16[128,512]{1,0:T(8,128)(2,1)S(1)} %copy-done, bf16[128,512]{1,0:T(8,128)(2,1)S(1)} %get-tuple-element.15, f32[128,512]{1,0:T(8,128)S(1)} %copy.32, f32[32,16,128]{2,1,0:T(8,128)S(1)} %get-tuple-element.44, f32[16,512]{1,0:T(8,128)S(1)} %get-tuple-element.20, ...), kind=kOutput, calls=%fused_computation.78 | convolution fusion | flops 403570688 | bytes 1146880 | tf_op jit(solution)/shard_map/kt,kc->tc/dot_general | solution.py:167
  66.6 0.9 %fusion.31 = bf16[128,512]{1,0:T(8,128)(2,1)} fusion(f32[6,512]{1,0:T(8,128)S(1)} %convert_element_type.273, f32[128,512]{1,0:T(8,128)S(1)} %convert_element_type.271, f32[512]{0:T(512)S(1)} %bitcast.189, f32[512]{0:T(512)S(1)} %bitcast.187, f32[512]{0:T(512)S(1)} %bitcast.177, f32[512]{0:T(512)S(1)} %bitcast.179, f32[512]{0:T(512)S(1)} %bitcast.181, ...), kind=kLoop, calls=%fused_computation.85 | loop fusion | flops 1310720 | bytes 419840 | tf_op jit(solution)/shard_map/convert_element_type | solution.py:206
  67.5 0.9 %fusion.48 = bf16[128,512]{1,0:T(8,128)(2,1)} fusion(f32[6,512]{1,0:T(8,128)S(1)} %convert_element_type.268, f32[128,512]{1,0:T(8,128)S(1)} %convert_element_type.264, f32[512]{0:T(512)S(1)} %bitcast.163, f32[512]{0:T(512)S(1)} %bitcast.165, f32[512]{0:T(512)S(1)} %bitcast.167, f32[512]{0:T(512)S(1)} %bitcast.169, f32[512]{0:T(512)S(1)} %bitcast.171, ...), kind=kLoop, calls=%fused_computation.102 | loop fusion | flops 1310720 | bytes 419840 | tf_op jit(solution)/shard_map/convert_element_type | solution.py:205
  68.5 0.9 %fusion.65 = bf16[128,512]{1,0:T(8,128)(2,1)} fusion(f32[6,512]{1,0:T(8,128)S(1)} %convert_element_type.259, f32[128,512]{1,0:T(8,128)S(1)} %convert_element_type.252, f32[512]{0:T(512)S(1)} %bitcast.151, f32[512]{0:T(512)S(1)} %bitcast.153, f32[512]{0:T(512)S(1)} %bitcast.155, f32[512]{0:T(512)S(1)} %bitcast.157, f32[512]{0:T(512)S(1)} %bitcast.159, ...), kind=kLoop, calls=%fused_computation.119 | loop fusion | flops 1310720 | bytes 419840 | tf_op jit(solution)/shard_map/convert_element_type | solution.py:204
  (147 shorter events, 0.7 us)
Async XLA Ops:
  0.6 9.5 %copy-start = (bf16[128,512]{1,0:T(8,128)(2,1)S(1)}, bf16[128,512]{1,0:T(8,128)(2,1)}, u32[]{:S(2)}) copy-start(bf16[128,512]{1,0:T(8,128)(2,1)} %param.13) | copy-start | bytes 393220
  2.1 10.2 %collective-permute-start = (bf16[3,6,512]{2,1,0:T(8,128)(2,1)S(1)}, bf16[3,6,512]{2,1,0:T(8,128)(2,1)S(1)}, u32[]{:S(2)}, u32[]{:S(2)}) collective-permute-start(bf16[3,6,512]{2,1,0:T(8,128)(2,1)S(1)} %pad_maximum_fusion.7), channel_id=1, source_target_pairs={{0,8},{8,16},{16,24},{24,32},{32,40},{40,48},{48,56},{56,64},{64,7... | collective-permute-start | bytes 55304 | tf_op jit(solution)/shard_map/ppermute | solution.py:19
  7.8 4.5 %copy-start.30 = (f32[1,1,512]{2,1,0:T(1,128)}, f32[1,1,512]{2,1,0:T(1,128)S(1)}, u32[]{:S(2)}) copy-start(f32[1,1,512]{2,1,0:T(1,128)S(1)} %get-tuple-element.66) | copy-start | bytes 6148
  7.8 4.5 %copy-start.32 = (f32[1,1,512]{2,1,0:T(1,128)}, f32[1,1,512]{2,1,0:T(1,128)S(1)}, u32[]{:S(2)}) copy-start(f32[1,1,512]{2,1,0:T(1,128)S(1)} %get-tuple-element.67) | copy-start | bytes 6148
  7.8 4.5 %copy-start.34 = (f32[1,1,512]{2,1,0:T(1,128)}, f32[1,1,512]{2,1,0:T(1,128)S(1)}, u32[]{:S(2)}) copy-start(f32[1,1,512]{2,1,0:T(1,128)S(1)} %get-tuple-element.68) | copy-start | bytes 6148
  7.8 4.5 %copy-start.36 = (f32[1,1,512]{2,1,0:T(1,128)}, f32[1,1,512]{2,1,0:T(1,128)S(1)}, u32[]{:S(2)}) copy-start(f32[1,1,512]{2,1,0:T(1,128)S(1)} %get-tuple-element.69) | copy-start | bytes 6148
  7.8 4.5 %copy-start.38 = (f32[1,1,512]{2,1,0:T(1,128)}, f32[1,1,512]{2,1,0:T(1,128)S(1)}, u32[]{:S(2)}) copy-start(f32[1,1,512]{2,1,0:T(1,128)S(1)} %get-tuple-element.70) | copy-start | bytes 6148
  7.9 4.5 %copy-start.40 = (f32[1,1,512]{2,1,0:T(1,128)}, f32[1,1,512]{2,1,0:T(1,128)S(1)}, u32[]{:S(2)}) copy-start(f32[1,1,512]{2,1,0:T(1,128)S(1)} %get-tuple-element.71) | copy-start | bytes 6148
  7.9 4.5 %copy-start.42 = (f32[1,1,512]{2,1,0:T(1,128)}, f32[1,1,512]{2,1,0:T(1,128)S(1)}, u32[]{:S(2)}) copy-start(f32[1,1,512]{2,1,0:T(1,128)S(1)} %get-tuple-element.72) | copy-start | bytes 6148
  7.9 4.5 %copy-start.44 = (f32[1,1,512]{2,1,0:T(1,128)}, f32[1,1,512]{2,1,0:T(1,128)S(1)}, u32[]{:S(2)}) copy-start(f32[1,1,512]{2,1,0:T(1,128)S(1)} %get-tuple-element.61) | copy-start | bytes 6148
  7.9 4.5 %copy-start.46 = (f32[1,1,512]{2,1,0:T(1,128)}, f32[1,1,512]{2,1,0:T(1,128)S(1)}, u32[]{:S(2)}) copy-start(f32[1,1,512]{2,1,0:T(1,128)S(1)} %get-tuple-element.62) | copy-start | bytes 6148
  7.9 4.5 %copy-start.48 = (f32[1,1,512]{2,1,0:T(1,128)}, f32[1,1,512]{2,1,0:T(1,128)S(1)}, u32[]{:S(2)}) copy-start(f32[1,1,512]{2,1,0:T(1,128)S(1)} %get-tuple-element.63) | copy-start | bytes 6148
  7.9 4.5 %copy-start.50 = (f32[1,1,512]{2,1,0:T(1,128)}, f32[1,1,512]{2,1,0:T(1,128)S(1)}, u32[]{:S(2)}) copy-start(f32[1,1,512]{2,1,0:T(1,128)S(1)} %get-tuple-element.64) | copy-start | bytes 6148
  7.9 4.5 %copy-start.52 = (f32[1,1,512]{2,1,0:T(1,128)}, f32[1,1,512]{2,1,0:T(1,128)S(1)}, u32[]{:S(2)}) copy-start(f32[1,1,512]{2,1,0:T(1,128)S(1)} %get-tuple-element.65) | copy-start | bytes 6148
  7.9 5.6 %copy-start.16 = (f32[1,1,512]{2,1,0:T(1,128)}, f32[1,1,512]{2,1,0:T(1,128)S(1)}, u32[]{:S(2)}) copy-start(f32[1,1,512]{2,1,0:T(1,128)S(1)} %get-tuple-element.60) | copy-start | bytes 6148
  7.9 5.6 %copy-start.18 = (f32[1,1,512]{2,1,0:T(1,128)}, f32[1,1,512]{2,1,0:T(1,128)S(1)}, u32[]{:S(2)}) copy-start(f32[1,1,512]{2,1,0:T(1,128)S(1)} %get-tuple-element.73) | copy-start | bytes 6148
  7.9 5.6 %copy-start.20 = (f32[1,1,512]{2,1,0:T(1,128)}, f32[1,1,512]{2,1,0:T(1,128)S(1)}, u32[]{:S(2)}) copy-start(f32[1,1,512]{2,1,0:T(1,128)S(1)} %get-tuple-element.74) | copy-start | bytes 6148
  8.0 5.6 %copy-start.22 = (f32[1,1,512]{2,1,0:T(1,128)}, f32[1,1,512]{2,1,0:T(1,128)S(1)}, u32[]{:S(2)}) copy-start(f32[1,1,512]{2,1,0:T(1,128)S(1)} %get-tuple-element.75) | copy-start | bytes 6148
  8.0 5.6 %copy-start.24 = (f32[1,1,512]{2,1,0:T(1,128)}, f32[1,1,512]{2,1,0:T(1,128)S(1)}, u32[]{:S(2)}) copy-start(f32[1,1,512]{2,1,0:T(1,128)S(1)} %get-tuple-element.76) | copy-start | bytes 6148
  8.0 5.6 %copy-start.26 = (f32[1,1,512]{2,1,0:T(1,128)}, f32[1,1,512]{2,1,0:T(1,128)S(1)}, u32[]{:S(2)}) copy-start(f32[1,1,512]{2,1,0:T(1,128)S(1)} %get-tuple-element.77) | copy-start | bytes 6148
  8.0 5.6 %copy-start.28 = (f32[1,1,512]{2,1,0:T(1,128)}, f32[1,1,512]{2,1,0:T(1,128)S(1)}, u32[]{:S(2)}) copy-start(f32[1,1,512]{2,1,0:T(1,128)S(1)} %get-tuple-element.78) | copy-start | bytes 6148
  8.8 3.6 %copy-start.54 = (f32[1,1,512]{2,1,0:T(1,128)}, f32[1,1,512]{2,1,0:T(1,128)S(1)}, u32[]{:S(2)}) copy-start(f32[1,1,512]{2,1,0:T(1,128)S(1)} %get-tuple-element.79) | copy-start | bytes 6148
  8.8 3.6 %copy-start.56 = (f32[1,1,512]{2,1,0:T(1,128)}, f32[1,1,512]{2,1,0:T(1,128)S(1)}, u32[]{:S(2)}) copy-start(f32[1,1,512]{2,1,0:T(1,128)S(1)} %get-tuple-element.80) | copy-start | bytes 6148
  9.9 2.3 %copy-start.1 = (bf16[128,512]{1,0:T(8,128)(2,1)S(1)}, bf16[128,512]{1,0:T(8,128)(2,1)}, u32[]{:S(2)}) copy-start(bf16[128,512]{1,0:T(8,128)(2,1)} %param.8) | copy-start | bytes 393220
  9.9 2.3 %copy-start.2 = (bf16[128,512]{1,0:T(8,128)(2,1)S(1)}, bf16[128,512]{1,0:T(8,128)(2,1)}, u32[]{:S(2)}) copy-start(bf16[128,512]{1,0:T(8,128)(2,1)} %param.9) | copy-start | bytes 393220
  10.1 2.2 %copy-start.3 = (bf16[128,512]{1,0:T(8,128)(2,1)S(1)}, bf16[128,512]{1,0:T(8,128)(2,1)}, u32[]{:S(2)}) copy-start(bf16[128,512]{1,0:T(8,128)(2,1)} %param.7) | copy-start | bytes 393220
  14.1 7.1 %copy-start.15 = (f32[32,16]{0,1:T(8,128)S(1)}, f32[32,16]{0,1:T(8,128)}, u32[]{:S(2)}) copy-start(f32[32,16]{0,1:T(8,128)} %param.11) | copy-start | bytes 6148
  14.7 6.5 %collective-permute-start.1 = (f32[2,16,512]{2,1,0:T(8,128)S(1)}, f32[2,16,512]{2,1,0:T(8,128)S(1)}, u32[]{:S(2)}, u32[]{:S(2)}) collective-permute-start(f32[2,16,512]{2,1,0:T(8,128)S(1)} %pad_maximum_fusion.6), channel_id=1, source_target_pairs={{0,8},{8,0},{16,24},{24,16},{32,40},{40,32},{48,56},{56,48},{1,9},... | collective-permute-start | bytes 196616 | tf_op jit(solution)/shard_map/ppermute | solution.py:89
  21.4 6.4 %collective-permute-start.2 = (f32[2,16,512]{2,1,0:T(8,128)S(1)}, f32[2,16,512]{2,1,0:T(8,128)S(1)}, u32[]{:S(2)}, u32[]{:S(2)}) collective-permute-start(f32[2,16,512]{2,1,0:T(8,128)S(1)} %fusion.157), channel_id=1, source_target_pairs={{0,16},{8,24},{16,0},{24,8},{32,48},{40,56},{48,32},{56,40},{1,17}... | collective-permute-start | bytes 196616 | tf_op jit(solution)/shard_map/ppermute | solution.py:89
  27.8 6.6 %copy-start.5 = (f32[1,16,512]{2,1,0:T(8,128)S(1)}, f32[1,16,512]{2,1,0:T(8,128)}, u32[]{:S(2)}) copy-start(f32[1,16,512]{2,1,0:T(8,128)} %get-tuple-element.40) | copy-start | bytes 98308
  27.8 6.6 %copy-start.6 = (f32[1,16,512]{2,1,0:T(8,128)S(1)}, f32[1,16,512]{2,1,0:T(8,128)}, u32[]{:S(2)}) copy-start(f32[1,16,512]{2,1,0:T(8,128)} %get-tuple-element.41) | copy-start | bytes 98308
  27.8 6.6 %copy-start.7 = (f32[1,16,512]{2,1,0:T(8,128)S(1)}, f32[1,16,512]{2,1,0:T(8,128)}, u32[]{:S(2)}) copy-start(f32[1,16,512]{2,1,0:T(8,128)} %get-tuple-element.42) | copy-start | bytes 98308
  27.8 6.6 %copy-start.8 = (f32[1,16,512]{2,1,0:T(8,128)S(1)}, f32[1,16,512]{2,1,0:T(8,128)}, u32[]{:S(2)}) copy-start(f32[1,16,512]{2,1,0:T(8,128)} %get-tuple-element.21) | copy-start | bytes 98308
  27.8 6.6 %copy-start.9 = (f32[1,16,512]{2,1,0:T(8,128)S(1)}, f32[1,16,512]{2,1,0:T(8,128)}, u32[]{:S(2)}) copy-start(f32[1,16,512]{2,1,0:T(8,128)} %get-tuple-element.23) | copy-start | bytes 98308
  27.8 6.6 %copy-start.10 = (f32[1,16,512]{2,1,0:T(8,128)S(1)}, f32[1,16,512]{2,1,0:T(8,128)}, u32[]{:S(2)}) copy-start(f32[1,16,512]{2,1,0:T(8,128)} %get-tuple-element.33) | copy-start | bytes 98308
  27.9 6.5 %collective-permute-start.3 = (f32[2,16,512]{2,1,0:T(8,128)S(1)}, f32[2,16,512]{2,1,0:T(8,128)S(1)}, u32[]{:S(2)}, u32[]{:S(2)}) collective-permute-start(f32[2,16,512]{2,1,0:T(8,128)S(1)} %fusion.158), channel_id=1, source_target_pairs={{0,32},{8,40},{16,48},{24,56},{32,0},{40,8},{48,16},{56,24},{1,33}... | collective-permute-start | bytes 196616 | tf_op jit(solution)/shard_map/ppermute | solution.py:89
  34.5 11.1 %copy-start.13 = (f32[1,16,512]{2,1,0:T(8,128)S(1)}, f32[1,16,512]{2,1,0:T(8,128)}, u32[]{:S(2)}) copy-start(f32[1,16,512]{2,1,0:T(8,128)} %get-tuple-element.25) | copy-start | bytes 98308
  34.5 5.0 %collective-permute-start.4 = (f32[2,16,512]{2,1,0:T(8,128)S(1)}, f32[2,16,512]{2,1,0:T(8,128)S(1)}, u32[]{:S(2)}, u32[]{:S(2)}) collective-permute-start(f32[2,16,512]{2,1,0:T(8,128)S(1)} %get-tuple-element.59), channel_id=1, source_target_pairs={{0,64},{64,0},{128,192},{192,128},{256,320},{320,256},{384,448},{4... | collective-permute-start | bytes 196616 | tf_op jit(solution)/shard_map/ppermute | solution.py:89
  37.1 16.9 %copy-start.14 = (f32[6,512]{1,0:T(8,128)S(1)}, f32[6,512]{1,0:T(8,128)}, u32[]{:S(2)}) copy-start(f32[6,512]{1,0:T(8,128)} %slice_convert_fusion.1) | copy-start | bytes 36868
  39.5 20.9 %copy-start.4 = (f32[1,16,512]{2,1,0:T(8,128)S(1)}, f32[1,16,512]{2,1,0:T(8,128)}, u32[]{:S(2)}) copy-start(f32[1,16,512]{2,1,0:T(8,128)} %get-tuple-element.32) | copy-start | bytes 98308
  39.5 6.1 %collective-permute-start.5 = (f32[2,16,512]{2,1,0:T(8,128)S(1)}, f32[2,16,512]{2,1,0:T(8,128)S(1)}, u32[]{:S(2)}, u32[]{:S(2)}) collective-permute-start(f32[2,16,512]{2,1,0:T(8,128)S(1)} %fusion.162), channel_id=1, source_target_pairs={{0,128},{64,192},{128,0},{192,64},{256,384},{320,448},{384,256},{4... | collective-permute-start | bytes 196616 | tf_op jit(solution)/shard_map/ppermute | solution.py:89
  46.3 14.1 %collective-permute-start.6 = (f32[2,16,512]{2,1,0:T(8,128)}, f32[2,16,512]{2,1,0:T(8,128)}, u32[]{:S(2)}, u32[]{:S(2)}) collective-permute-start(f32[2,16,512]{2,1,0:T(8,128)} %fusion.163), channel_id=1, source_target_pairs={{0,256},{64,320},{128,384},{192,448},{256,0},{320,64},{384,128},{4... | collective-permute-start | bytes 196616 | tf_op jit(solution)/shard_map/ppermute | solution.py:89
  54.3 8.0 %collective-permute-start.7 = (f32[46,512]{1,0:T(8,128)S(1)}, f32[46,512]{1,0:T(8,128)S(1)}, u32[]{:S(2)}, u32[]{:S(2)}) collective-permute-start(f32[46,512]{1,0:T(8,128)S(1)} %concatenate.24), channel_id=1, source_target_pairs={{8,0},{16,8},{24,16},{32,24},{40,32},{48,40},{56,48},{64,56},{72,6... | collective-permute-start | bytes 282632 | tf_op jit(solution)/shard_map/ppermute | solution.py:19
  63.5 3.0 %copy-start.45 = (f32[1,1,512]{2,1,0:T(1,128)S(1)}, f32[1,1,512]{2,1,0:T(1,128)}, u32[]{:S(2)}) copy-start(f32[1,1,512]{2,1,0:T(1,128)} %copy-done.44) | copy-start | bytes 6148
  63.5 3.0 %copy-start.47 = (f32[1,1,512]{2,1,0:T(1,128)S(1)}, f32[1,1,512]{2,1,0:T(1,128)}, u32[]{:S(2)}) copy-start(f32[1,1,512]{2,1,0:T(1,128)} %copy-done.46) | copy-start | bytes 6148
  63.5 3.0 %copy-start.49 = (f32[1,1,512]{2,1,0:T(1,128)S(1)}, f32[1,1,512]{2,1,0:T(1,128)}, u32[]{:S(2)}) copy-start(f32[1,1,512]{2,1,0:T(1,128)} %copy-done.48) | copy-start | bytes 6148
  63.5 3.0 %copy-start.51 = (f32[1,1,512]{2,1,0:T(1,128)S(1)}, f32[1,1,512]{2,1,0:T(1,128)}, u32[]{:S(2)}) copy-start(f32[1,1,512]{2,1,0:T(1,128)} %copy-done.50) | copy-start | bytes 6148
  63.5 3.0 %copy-start.53 = (f32[1,1,512]{2,1,0:T(1,128)S(1)}, f32[1,1,512]{2,1,0:T(1,128)}, u32[]{:S(2)}) copy-start(f32[1,1,512]{2,1,0:T(1,128)} %copy-done.52) | copy-start | bytes 6148
  63.5 3.0 %copy-start.55 = (f32[1,1,512]{2,1,0:T(1,128)S(1)}, f32[1,1,512]{2,1,0:T(1,128)}, u32[]{:S(2)}) copy-start(f32[1,1,512]{2,1,0:T(1,128)} %copy-done.54) | copy-start | bytes 6148
  63.6 3.0 %copy-start.57 = (f32[1,1,512]{2,1,0:T(1,128)S(1)}, f32[1,1,512]{2,1,0:T(1,128)}, u32[]{:S(2)}) copy-start(f32[1,1,512]{2,1,0:T(1,128)} %copy-done.56) | copy-start | bytes 6148
  64.2 3.3 %copy-start.31 = (f32[1,1,512]{2,1,0:T(1,128)S(1)}, f32[1,1,512]{2,1,0:T(1,128)}, u32[]{:S(2)}) copy-start(f32[1,1,512]{2,1,0:T(1,128)} %copy-done.30) | copy-start | bytes 6148
  64.2 3.3 %copy-start.33 = (f32[1,1,512]{2,1,0:T(1,128)S(1)}, f32[1,1,512]{2,1,0:T(1,128)}, u32[]{:S(2)}) copy-start(f32[1,1,512]{2,1,0:T(1,128)} %copy-done.32) | copy-start | bytes 6148
  64.2 3.3 %copy-start.35 = (f32[1,1,512]{2,1,0:T(1,128)S(1)}, f32[1,1,512]{2,1,0:T(1,128)}, u32[]{:S(2)}) copy-start(f32[1,1,512]{2,1,0:T(1,128)} %copy-done.34) | copy-start | bytes 6148
  64.2 3.3 %copy-start.37 = (f32[1,1,512]{2,1,0:T(1,128)S(1)}, f32[1,1,512]{2,1,0:T(1,128)}, u32[]{:S(2)}) copy-start(f32[1,1,512]{2,1,0:T(1,128)} %copy-done.36) | copy-start | bytes 6148
  64.2 3.3 %copy-start.39 = (f32[1,1,512]{2,1,0:T(1,128)S(1)}, f32[1,1,512]{2,1,0:T(1,128)}, u32[]{:S(2)}) copy-start(f32[1,1,512]{2,1,0:T(1,128)} %copy-done.38) | copy-start | bytes 6148
  64.2 3.3 %copy-start.41 = (f32[1,1,512]{2,1,0:T(1,128)S(1)}, f32[1,1,512]{2,1,0:T(1,128)}, u32[]{:S(2)}) copy-start(f32[1,1,512]{2,1,0:T(1,128)} %copy-done.40) | copy-start | bytes 6148
  64.2 3.3 %copy-start.43 = (f32[1,1,512]{2,1,0:T(1,128)S(1)}, f32[1,1,512]{2,1,0:T(1,128)}, u32[]{:S(2)}) copy-start(f32[1,1,512]{2,1,0:T(1,128)} %copy-done.42) | copy-start | bytes 6148
  64.2 4.2 %copy-start.17 = (f32[1,1,512]{2,1,0:T(1,128)S(1)}, f32[1,1,512]{2,1,0:T(1,128)}, u32[]{:S(2)}) copy-start(f32[1,1,512]{2,1,0:T(1,128)} %copy-done.16) | copy-start | bytes 6148
  64.2 4.2 %copy-start.19 = (f32[1,1,512]{2,1,0:T(1,128)S(1)}, f32[1,1,512]{2,1,0:T(1,128)}, u32[]{:S(2)}) copy-start(f32[1,1,512]{2,1,0:T(1,128)} %copy-done.18) | copy-start | bytes 6148
  64.3 4.2 %copy-start.21 = (f32[1,1,512]{2,1,0:T(1,128)S(1)}, f32[1,1,512]{2,1,0:T(1,128)}, u32[]{:S(2)}) copy-start(f32[1,1,512]{2,1,0:T(1,128)} %copy-done.20) | copy-start | bytes 6148
  64.3 4.2 %copy-start.23 = (f32[1,1,512]{2,1,0:T(1,128)S(1)}, f32[1,1,512]{2,1,0:T(1,128)}, u32[]{:S(2)}) copy-start(f32[1,1,512]{2,1,0:T(1,128)} %copy-done.22) | copy-start | bytes 6148
  64.3 4.2 %copy-start.25 = (f32[1,1,512]{2,1,0:T(1,128)S(1)}, f32[1,1,512]{2,1,0:T(1,128)}, u32[]{:S(2)}) copy-start(f32[1,1,512]{2,1,0:T(1,128)} %copy-done.24) | copy-start | bytes 6148
  64.3 4.2 %copy-start.27 = (f32[1,1,512]{2,1,0:T(1,128)S(1)}, f32[1,1,512]{2,1,0:T(1,128)}, u32[]{:S(2)}) copy-start(f32[1,1,512]{2,1,0:T(1,128)} %copy-done.26) | copy-start | bytes 6148
  64.3 4.2 %copy-start.29 = (f32[1,1,512]{2,1,0:T(1,128)S(1)}, f32[1,1,512]{2,1,0:T(1,128)}, u32[]{:S(2)}) copy-start(f32[1,1,512]{2,1,0:T(1,128)} %copy-done.28) | copy-start | bytes 6148
  (2 other events, 1.7 us)
